TPU v7x, 32 devices: a whole 2x2x4 slice. The times are simulated.
32 devices in a mesh: ctx: 16 (over z, x, core), tp: 2 (over y).
Axes of the slice: x: 2, y: 2, z: 4, core: 2. Of those that a mesh axis runs over, the one named last changes fastest.
Arguments:
- streams: bfloat16 [4096, 3, 4096], P(('ctx', 'tp')), may hold values from -6 to 6
- short_filter: float32 [3, 3, 4096], replicated, may hold values from -2 to 2
- skip: float32 [4096], replicated, may hold values from 0.5 to 1.5
- rates: float32 [4096, 16], replicated, may hold values from 0 to 0.05, as said below
- residues: float32 [4096, 16], replicated, may hold values from -0.5 to 0.5
Outputs:
- mixed: bfloat16 [4096, 4096], P(('ctx', 'tp'))
Inputs may be any that keep to these rules, and one draw needn't show every extreme that they name: Positive decay rates.
All inputs are finite; a program needn't handle non-finite values.
Results may differ from a plain program's by a relative error of at most 0.0095.
Values may be sent and summed in bfloat16 or wider, within the bound.
No kernel may reach another device: no remote copies, remote signals or barrier semaphores. Data moves between devices by JAX's collectives and lax.ppermute only.
A program may use at most 128 MiB of HBM per device.

v0:
```python
import math

import jax
import jax.numpy as jnp
from jax import lax
from jax.sharding import PartitionSpec as P

SPAN = 256


highest = lax.Precision.HIGHEST


def trig_table(first, second, total):
    product = first[:, None] * second[None, :] % total
    angle = product.astype(jnp.float32) * (2.0 * math.pi / total)
    return (jnp.cos(angle), jnp.sin(angle))


def make_tables(rows, span):
    row_index = jnp.arange(rows, dtype=jnp.int32)
    half_index = jnp.arange(rows // 2, dtype=jnp.int32)
    span_index = jnp.arange(span, dtype=jnp.int32)
    cos_r, sin_r = trig_table(row_index, half_index, rows)
    cos_s, sin_s = trig_table(span_index, span_index, span)
    cos_t, sin_t = trig_table(row_index, span_index, rows * span)
    return (cos_r, sin_r, cos_s, sin_s, cos_t, sin_t)


def forward(signal, tables):
    cos_r, sin_r, cos_s, sin_s, cos_t, sin_t = tables
    first_re = jnp.einsum("kn,cns->cks", cos_r, signal, precision=highest)
    first_im = -jnp.einsum("kn,cns->cks", sin_r, signal, precision=highest)
    turned_re = first_re * cos_t + first_im * sin_t
    turned_im = first_im * cos_t - first_re * sin_t
    out_re = jnp.einsum("cks,sj->ckj", turned_re, cos_s, precision=highest) + jnp.einsum(
        "cks,sj->ckj", turned_im, sin_s, precision=highest
    )
    out_im = jnp.einsum("cks,sj->ckj", turned_im, cos_s, precision=highest) - jnp.einsum(
        "cks,sj->ckj", turned_re, sin_s, precision=highest
    )
    return (out_re, out_im)


def inverse(spec_re, spec_im, tables):
    cos_r, sin_r, cos_s, sin_s, cos_t, sin_t = tables
    back_re = jnp.einsum("ckj,js->cks", spec_re, cos_s, precision=highest) - jnp.einsum(
        "ckj,js->cks", spec_im, sin_s, precision=highest
    )
    back_im = jnp.einsum("ckj,js->cks", spec_im, cos_s, precision=highest) + jnp.einsum(
        "ckj,js->cks", spec_re, sin_s, precision=highest
    )
    turned_re = back_re * cos_t - back_im * sin_t
    turned_im = back_im * cos_t + back_re * sin_t
    result = jnp.einsum("kn,cks->cns", cos_r, turned_re, precision=highest) - jnp.einsum(
        "kn,cks->cns", sin_r, turned_im, precision=highest
    )
    return result / float(cos_t.shape[0] * cos_t.shape[1])


def build_kernel(rate_rows, residue_rows, length):
    times = jnp.arange(length, dtype=jnp.int32).astype(jnp.float32)

    def add_mode(mode, total):
        decay = lax.dynamic_index_in_dim(rate_rows, mode, 1, keepdims=False)
        amplitude = lax.dynamic_index_in_dim(residue_rows, mode, 1, keepdims=False)
        return total + amplitude[:, None] * jnp.exp(-decay[:, None] * times[None, :])

    empty = jnp.zeros((rate_rows.shape[0], length), jnp.float32)
    return lax.fori_loop(0, rate_rows.shape[1], add_mode, empty)


def long_conv(gated, kernel, skip_rows):
    channels, length = gated.shape
    rows = 2 * length // SPAN
    tables = make_tables(rows, SPAN)
    signal = gated.astype(jnp.float32)
    signal_re, signal_im = forward(signal.reshape(channels, rows // 2, SPAN), tables)
    kernel_re, kernel_im = forward(kernel.reshape(channels, rows // 2, SPAN), tables)
    spec_re = signal_re * kernel_re - signal_im * kernel_im
    spec_im = signal_re * kernel_im + signal_im * kernel_re
    conv = inverse(spec_re, spec_im, tables).reshape(channels, length)
    return (conv + skip_rows[:, None] * signal).astype(jnp.bfloat16)


def body(streams, short_filter, skip, rates, residues):
    ctx_count = lax.axis_size("ctx")
    tp_count = lax.axis_size("tp")
    devices = ctx_count * tp_count
    group = lax.axis_index("tp") * ctx_count + lax.axis_index("ctx")
    tok_rows, _, width = streams.shape
    per_dev = width // devices
    length = tok_rows * devices
    taps_count = short_filter.shape[0]
    first_channel = group * per_dev
    rate_rows = lax.dynamic_slice_in_dim(rates, first_channel, per_dev, 0)
    residue_rows = lax.dynamic_slice_in_dim(residues, first_channel, per_dev, 0)
    skip_rows = lax.dynamic_slice_in_dim(skip, first_channel, per_dev, 0)
    kernel = build_kernel(rate_rows, residue_rows, length)
    moved = jnp.transpose(streams, (1, 2, 0)).reshape(3, devices, per_dev, tok_rows)
    whole = lax.all_to_all(
        lax.all_to_all(moved, "tp", split_axis=1, concat_axis=3, tiled=True),
        "ctx",
        split_axis=1,
        concat_axis=3,
        tiled=True,
    ).reshape(3, per_dev, length)
    taps = lax.dynamic_slice_in_dim(short_filter, first_channel, per_dev, 2)
    padded = jnp.pad(whole.astype(jnp.float32), ((0, 0), (0, 0), (taps_count - 1, 0)))
    feat = jnp.zeros((3, per_dev, length), jnp.float32)
    for tap in range(taps_count):
        feat = (
            feat
            + taps[tap][:, :, None]
            * padded[:, :, taps_count - 1 - tap : taps_count - 1 - tap + length]
        )
    gated = (feat[1] * feat[2]).astype(jnp.bfloat16)
    result = long_conv(gated, kernel, skip_rows)
    mixed_rows = (feat[0] * result.astype(jnp.float32)).astype(jnp.bfloat16)
    returned = lax.all_to_all(
        lax.all_to_all(
            mixed_rows.reshape(1, per_dev, length), "ctx", split_axis=2, concat_axis=0, tiled=True
        ),
        "tp",
        split_axis=2,
        concat_axis=0,
        tiled=True,
    )
    return returned.reshape(width, tok_rows).T


def solution(mesh):
    return jax.shard_map(
        body,
        mesh=mesh,
        in_specs=(P(("ctx", "tp"), None, None), P(), P(), P(), P()),
        out_specs=P(("ctx", "tp"), None),
        check_vma=False,
    )
```

profile of v0, /device:TPU:16, one launch (start us, length us, event | category | flops | bytes accessed | tf_op | source)
XLA Modules:
  0.0 367.8 jit_solution(10503142534619687234)
XLA Ops:
  6.3 5.2 %all-to-all-start = ((bf16[3,32,128,128]{2,3,0,1:T(8,128)(2,1)}), bf16[3,32,128,128]{2,3,0,1:T(8,128)(2,1)}, u32[]{:S(2)}, u32[]{:S(2)}) async-start(bf16[3,32,128,128]{2,3,0,1:T(8,128)(2,1)} %copy.70), calls=%async_computation | async-start | bytes 6291456 | tf_op jit(solution)/shard_map/all_to_all | solution.py:102
  12.2 35.7 %all-to-all-done = bf16[3,32,128,128]{2,3,0,1:T(8,128)(2,1)} async-done(((bf16[3,32,128,128]{2,3,0,1:T(8,128)(2,1)}), bf16[3,32,128,128]{2,3,0,1:T(8,128)(2,1)}, u32[]{:S(2)}, u32[]{:S(2)}) %all-to-all-start) | async-done | bytes 3145760 | tf_op jit(solution)/shard_map/all_to_all | solution.py:102
  47.9 8.7 %copy.71 = bf16[3,16,128,2,128]{4,3,2,0,1:T(2,128)(2,1)} copy(bf16[3,16,128,2,128]{2,4,0,1,3:T(8,128)(2,1)} %bitcast.4) | data formatting | bytes 6291456 | tf_op jit(solution)/shard_map/all_to_all | solution.py:102
  56.6 6.0 %all_to_all.47 = bf16[3,16,128,256]{3,2,0,1:T(8,128)(2,1)} reshape(bf16[3,16,128,2,128]{4,3,2,0,1:T(2,128)(2,1)} %copy.71) | data formatting | bytes 6291456 | tf_op jit(solution)/shard_map/all_to_all | solution.py:102
  62.6 6.2 %all-to-all-start.1 = ((bf16[3,16,128,256]{3,2,0,1:T(8,128)(2,1)}), bf16[3,16,128,256]{3,2,0,1:T(8,128)(2,1)}, u32[]{:S(2)}, u32[]{:S(2)}) async-start(bf16[3,16,128,256]{3,2,0,1:T(8,128)(2,1)} %all_to_all.47), calls=%async_computation.1 | async-start | bytes 6291456 | tf_op jit(solution)/shard_map/all_to_all | solution.py:101
  68.7 19.3 %while.14 = (s32[]{:T(128)}, f32[128,4096]{1,0:T(8,128)S(1)}, f32[128,16]{0,1:T(8,128)S(1)}, f32[128,16]{0,1:T(8,128)S(1)}, s32[]{:T(128)}, /*index=5*/s32[]{:T(128)}) while((s32[]{:T(128)}, f32[128,4096]{1,0:T(8,128)S(1)}, f32[128,16]{0,1:T(8,128)S(1)}, f32[128,16]{0,1:T(8,128)S(1)}, s32[]{:T(128)}, /*index=5*/s32[]{:T(128)}) %tuple.44), condition=%wide.region_1.2_spmd.clone, body=%wide.region_0.1_spmd.clone.sunk | while | flops 2101379 | bytes 4230235 | solution.py:70
  96.0 43.0 %all-to-all-done.1 = bf16[3,16,128,256]{3,2,0,1:T(8,128)(2,1)} async-done(((bf16[3,16,128,256]{3,2,0,1:T(8,128)(2,1)}), bf16[3,16,128,256]{3,2,0,1:T(8,128)(2,1)}, u32[]{:S(2)}, u32[]{:S(2)}) %all-to-all-start.1) | async-done | bytes 3145760 | tf_op jit(solution)/shard_map/all_to_all | solution.py:101
  156.8 8.6 %fusion.2 = (f32[128,32,256]{2,1,0:T(8,128)S(1)}, f32[128,32,256]{2,1,0:T(8,128)S(1)}, f32[128,32,256]{2,1,0:T(8,128)S(1)}, f32[128,32,256]{2,1,0:T(8,128)S(1)}) fusion(f32[128,256,32]{1,2,0:T(8,128)} %fusion.109, f32[32,256]{1,0:T(8,128)S(1)} %get-tuple-element.140, f32[32,256]{1,0:T(8,128)S(1)} %get-tuple-element.141, f32[128,256,32]{1,2,0:T(8,128)} %fusion.116, ...), kind=kOutput, calls=%fused_computation.8 | convolution fusion | flops 216013824 | bytes 31522816 | tf_op jit(solution)/shard_map/kn,cns->cks/dot_general | solution.py:32
  165.4 6.5 %fusion.22 = f32[128,32,256]{2,0,1:T(8,128)S(1)} fusion(f32[128,32,256]{2,1,0:T(8,128)S(1)} %get-tuple-element.130), kind=kOutput, calls=%fused_computation.36 | convolution fusion | flops 3222142976 | bytes 8388608 | tf_op jit(solution)/shard_map/cks,sj->ckj/dot_general | solution.py:39
  171.8 18.5 %fusion.24 = f32[128,32,256]{2,0,1:T(8,128)S(1)} fusion(f32[128,32,256]{2,1,0:T(8,128)S(1)} %get-tuple-element.130), kind=kOutput, calls=%fused_computation.38 | convolution fusion | flops 3222142976 | bytes 8388608 | tf_op jit(solution)/shard_map/cks,sj->ckj/dot_general | solution.py:36
  190.4 8.3 %fusion.30 = f32[128,32,256]{2,0,1:T(8,128)} fusion(f32[128,32,256]{2,1,0:T(8,128)S(1)} %get-tuple-element.136), kind=kOutput, calls=%fused_computation.44 | convolution fusion | flops 3222142976 | bytes 8388608 | tf_op jit(solution)/shard_map/cks,sj->ckj/dot_general | solution.py:39
  198.6 6.5 %fusion.32 = f32[128,32,256]{2,0,1:T(8,128)S(1)} fusion(f32[128,32,256]{2,1,0:T(8,128)S(1)} %get-tuple-element.136), kind=kOutput, calls=%fused_computation.46 | convolution fusion | flops 3222142976 | bytes 8388608 | tf_op jit(solution)/shard_map/cks,sj->ckj/dot_general | solution.py:36
  205.2 7.1 %fusion.44 = f32[128,32,256]{2,0,1:T(8,128)S(1)} fusion(f32[128,32,256]{2,0,1:T(8,128)S(1)} %fusion.24, f32[128,32,256]{2,1,0:T(8,128)S(1)} %get-tuple-element.129), kind=kOutput, calls=%fused_computation.55 | convolution fusion | flops 3223191552 | bytes 12582912 | tf_op jit(solution)/shard_map/cks,sj->ckj/dot_general | solution.py:36
  212.3 6.5 %fusion.47 = f32[128,32,256]{2,0,1:T(8,128)S(1)} fusion(f32[128,32,256]{2,0,1:T(8,128)S(1)} %fusion.22, f32[128,32,256]{2,1,0:T(8,128)S(1)} %get-tuple-element.129), kind=kOutput, calls=%fused_computation.56 | convolution fusion | flops 3223191552 | bytes 12582912 | tf_op jit(solution)/shard_map/cks,sj->ckj/dot_general | solution.py:39
  218.8 8.7 %fusion.38 = f32[128,32,256]{2,0,1:T(8,128)} fusion(f32[128,32,256]{2,0,1:T(8,128)S(1)} %fusion.32, f32[128,32,256]{2,1,0:T(8,128)S(1)} %get-tuple-element.137), kind=kOutput, calls=%fused_computation.53 | convolution fusion | flops 3223191552 | bytes 12582912 | tf_op jit(solution)/shard_map/cks,sj->ckj/dot_general | solution.py:36
  227.5 11.3 %multiply_subtract_fusion = (f32[128,32,256]{2,0,1:T(8,128)S(1)}, f32[128,32,256]{2,0,1:T(8,128)S(1)}) fusion(f32[128,32,256]{2,0,1:T(8,128)S(1)} %fusion.47, f32[128,32,256]{2,0,1:T(8,128)} %fusion.38, f32[128,32,256]{2,0,1:T(8,128)S(1)} %fusion.44, f32[128,32,256]{2,0,1:T(8,128)} %fusion.30, f32[128,32,256]{2,1,0:T(8,128)S(1)} %get-tuple-element.137), kind=kOutput, calls=%fused_computation.27 | convolution fusion | flops 3229483008 | bytes 29360128 | tf_op jit(solution)/shard_map/cks,sj->ckj/dot_general | solution.py:39
  238.8 6.7 %fusion.14 = f32[128,32,256]{2,1,0:T(8,128)S(1)} fusion(f32[128,32,256]{2,0,1:T(8,128)S(1)} %get-tuple-element.128), kind=kOutput, calls=%fused_computation.28 | convolution fusion | flops 3222142976 | bytes 8388608 | tf_op jit(solution)/shard_map/ckj,js->cks/dot_general | solution.py:50
  245.5 6.5 %fusion.16 = f32[128,32,256]{2,1,0:T(8,128)S(1)} fusion(f32[128,32,256]{2,0,1:T(8,128)S(1)} %get-tuple-element.128), kind=kOutput, calls=%fused_computation.30 | convolution fusion | flops 3222142976 | bytes 8388608 | tf_op jit(solution)/shard_map/ckj,js->cks/dot_general | solution.py:47
  252.0 6.9 %fusion.53 = f32[128,32,256]{2,1,0:T(8,128)S(1)} fusion(f32[128,32,256]{2,1,0:T(8,128)S(1)} %fusion.14, f32[128,32,256]{2,0,1:T(8,128)S(1)} %get-tuple-element.127), kind=kOutput, calls=%fused_computation.58 | convolution fusion | flops 3223191552 | bytes 12582912 | tf_op jit(solution)/shard_map/ckj,js->cks/dot_general | solution.py:50
  259.0 6.6 %fusion.50 = f32[128,32,256]{2,1,0:T(8,128)S(1)} fusion(f32[128,32,256]{2,1,0:T(8,128)S(1)} %fusion.16, f32[128,32,256]{2,0,1:T(8,128)S(1)} %get-tuple-element.127), kind=kOutput, calls=%fused_computation.57 | convolution fusion | flops 3223191552 | bytes 12582912 | tf_op jit(solution)/shard_map/ckj,js->cks/dot_general | solution.py:47
  277.9 16.7 %copy.142 = bf16[1,128,4096]{1,0,2:T(2,128)(2,1)S(1)} copy(bf16[1,128,4096]{1,2,0:T(8,128)(2,1)S(1)} %fusion.57) | data formatting | bytes 2097152 | tf_op jit(solution)/shard_map/convert_element_type | solution.py:119
  295.2 22.4 %reduce = bf16[4096,128]{1,0:T(8,128)(2,1)S(1)} reduce(bf16[4096,1,128]{2,1,0:T(2,128)(2,1)S(1)} %bitcast.134, bf16[]{:T(256)} %broadcast.159), dimensions={1}, to_apply=%bitcast.125.reduce_sub_computation | reduce | bytes 2097154
  317.9 29.6 %all_to_all.60 = bf16[16,2,16384]{2,1,0:T(2,128)(2,1)S(1)} all-to-all(bf16[16,2,16384]{2,1,0:T(2,128)(2,1)S(1)} %reshape.82), channel_id=1, replica_groups=mesh['ctx'=16,'tp'=2] {'ctx'}, dimensions={0} | all-to-all | bytes 2097152 | tf_op jit(solution)/shard_map/all_to_all | solution.py:121
  349.4 15.9 %all_to_all.61 = bf16[16,128,256]{1,0,2:T(8,128)(2,1)S(1)} all-to-all(bf16[16,128,256]{1,0,2:T(8,128)(2,1)S(1)} %copy.89), channel_id=1, replica_groups=mesh['ctx'=16,'tp'=2] {'tp'}, dimensions={2} | all-to-all | bytes 2097152 | tf_op jit(solution)/shard_map/all_to_all | solution.py:120
  (81 shorter events, 68.7 us)
Async XLA Ops:
  6.3 41.6 %all-to-all-start = ((bf16[3,32,128,128]{2,3,0,1:T(8,128)(2,1)}), bf16[3,32,128,128]{2,3,0,1:T(8,128)(2,1)}, u32[]{:S(2)}, u32[]{:S(2)}) async-start(bf16[3,32,128,128]{2,3,0,1:T(8,128)(2,1)} %copy.70), calls=%async_computation | async-start | bytes 6291456 | tf_op jit(solution)/shard_map/all_to_all | solution.py:102
  62.6 76.4 %all-to-all-start.1 = ((bf16[3,16,128,256]{3,2,0,1:T(8,128)(2,1)}), bf16[3,16,128,256]{3,2,0,1:T(8,128)(2,1)}, u32[]{:S(2)}, u32[]{:S(2)}) async-start(bf16[3,16,128,256]{3,2,0,1:T(8,128)(2,1)} %all_to_all.47), calls=%async_computation.1 | async-start | bytes 6291456 | tf_op jit(solution)/shard_map/all_to_all | solution.py:101
  89.5 1.3 copy-start.1
  145.2 2.7 copy-start
  148.9 7.8 %copy-start.2 = (f32[16,8,16,256]{3,2,1,0:T(8,128)S(1)}, f32[16,8,16,256]{3,2,1,0:T(8,128)}, u32[]{:S(2)}) copy-start(f32[16,8,16,256]{3,2,1,0:T(8,128)} %copy-done.1) | copy-start | bytes 6291460
where the time goes:
time: 374 us; the launch traced here: 368 us
  matrix products  129 us (34%)
  waiting for transfers between devices  78.6 us (21%)
  local copies, waits for them, and re-layouts  54.9 us (15%)
  other arithmetic  47.4 us (13%)
  blocking collectives  45.5 us (12%)
  starting transfers between devices  11.4 us (3%)
    all_to_all x1, waiting for transfers between devices, body(): lax.all_to_all(lax.all_to_all(moved, 'tp', split_axis=1, concat_axis=3, t...  43 us
    all_to_all x1, waiting for transfers between devices, body(): lax.all_to_all(moved, 'tp', split_axis=1, concat_axis=3, tiled=True)  35.7 us
    all_to_all x1, blocking collectives, body(): lax.all_to_all(mixed_rows.reshape(1, per_dev, length), 'ctx', split_axis=...  29.6 us
    dot_general x2, matrix products, forward(): jnp.einsum('cks,sj->ckj', turned_im, sin_s, precision=highest)  25 us
    unnamed x2, other arithmetic  22.4 us
    add x16, other arithmetic, add_mode(): total + amplitude[:, None] * jnp.exp(-decay[:, None] * times[None, :])  18.5 us
    dot_general x2, matrix products, forward(): jnp.einsum('cks,sj->ckj', turned_re, sin_s, precision=highest)  17.8 us
    convert_element_type x1, local copies, waits for them, and re-layouts, body(): mixed_rows = (feat[0] * result.astype(jnp.float32)).astype(jnp.bfloat16)  16.7 us
  transfers between devices with their start and end apart: 2, of which 2 were waited for; matrix products, arithmetic and copies ran while one was open for 7% of the time, Pallas kernels for 0%

commit v1 on v0

v1 whole, which is shorter than its diff:
```python
import functools

import jax
import jax.numpy as jnp
from jax import lax
from jax.experimental import pallas as pl
from jax.experimental.pallas import tpu as pltpu
from jax.sharding import PartitionSpec as P

LANES = 128
GROUPS = 8


def features(x_ref, f_ref, t):
    taps = f_ref.shape[0]
    feats = []
    for s in range(x_ref.shape[0]):
        acc = f_ref[0, s] * x_ref[s, t + taps - 1]
        for tap in range(1, taps):
            acc = acc + f_ref[tap, s] * x_ref[s, t + taps - 1 - tap]
        feats.append(acc)
    return feats


def gate(feats):
    return (feats[1] * feats[2]).astype(jnp.bfloat16).astype(jnp.float32)


def state_kernel(x_ref, f_ref, d_ref, h_ref):
    modes = d_ref.shape[0]
    steps = x_ref.shape[1] - f_ref.shape[0] + 1

    def step(t, states):
        u = gate(features(x_ref, f_ref, t))
        return tuple(d_ref[m] * states[m] + u for m in range(modes))

    zero = jnp.zeros(h_ref.shape[1:], jnp.float32)
    states = lax.fori_loop(0, steps, step, (zero,) * modes, unroll=2)
    for m in range(modes):
        h_ref[m] = states[m]


def out_kernel(x_ref, f_ref, d_ref, r_ref, skip_ref, h_ref, o_ref):
    modes = d_ref.shape[0]
    steps = x_ref.shape[1] - f_ref.shape[0] + 1

    def step(t, states):
        feats = features(x_ref, f_ref, t)
        u = gate(feats)
        new = []
        conv = None
        for m in range(modes):
            sm = d_ref[m] * states[m] + u
            term = r_ref[m] * sm
            conv = term if conv is None else conv + term
            new.append(sm)
        y = (conv + skip_ref[...] * u).astype(jnp.bfloat16).astype(jnp.float32)
        o_ref[t] = feats[0] * y
        return tuple(new)

    lax.fori_loop(0, steps, step, tuple(h_ref[m] for m in range(modes)), unroll=2)


def run_state(x, f, d):
    streams_count, rows, groups, lanes = x.shape
    taps = f.shape[0]
    modes = d.shape[0]
    grid = (groups // GROUPS,)
    return pl.pallas_call(
        state_kernel,
        grid=grid,
        in_specs=[
            pl.BlockSpec((streams_count, rows, GROUPS, lanes), lambda i: (0, 0, i, 0)),
            pl.BlockSpec((taps, streams_count, GROUPS, lanes), lambda i: (0, 0, i, 0)),
            pl.BlockSpec((modes, GROUPS, lanes), lambda i: (0, i, 0)),
        ],
        out_specs=pl.BlockSpec((modes, GROUPS, lanes), lambda i: (0, i, 0)),
        out_shape=jax.ShapeDtypeStruct((modes, groups, lanes), jnp.float32),
    )(x, f, d)


def run_out(x, f, d, r, skip, h):
    streams_count, rows, groups, lanes = x.shape
    taps = f.shape[0]
    modes = d.shape[0]
    steps = rows - taps + 1
    grid = (groups // GROUPS,)
    return pl.pallas_call(
        out_kernel,
        grid=grid,
        in_specs=[
            pl.BlockSpec((streams_count, rows, GROUPS, lanes), lambda i: (0, 0, i, 0)),
            pl.BlockSpec((taps, streams_count, GROUPS, lanes), lambda i: (0, 0, i, 0)),
            pl.BlockSpec((modes, GROUPS, lanes), lambda i: (0, i, 0)),
            pl.BlockSpec((modes, GROUPS, lanes), lambda i: (0, i, 0)),
            pl.BlockSpec((GROUPS, lanes), lambda i: (i, 0)),
            pl.BlockSpec((modes, GROUPS, lanes), lambda i: (0, i, 0)),
        ],
        out_specs=pl.BlockSpec((steps, GROUPS, lanes), lambda i: (0, i, 0)),
        out_shape=jax.ShapeDtypeStruct((steps, groups, lanes), jnp.float32),
    )(x, f, d, r, skip, h)


def body(streams, short_filter, skip, rates, residues):
    axes = ("ctx", "tp")
    devices = lax.axis_size("ctx") * lax.axis_size("tp")
    tok_rows, streams_count, width = streams.shape
    taps = short_filter.shape[0]
    modes = rates.shape[1]
    groups = width // LANES

    def shift(value, offset):
        pairs = [(j, j + offset) for j in range(devices - offset)]
        return lax.ppermute(value, axes, pairs)

    halo = shift(streams[tok_rows - (taps - 1) :], 1)
    padded = jnp.concatenate([halo, streams], axis=0)
    x = jnp.transpose(padded, (1, 0, 2)).astype(jnp.float32)
    x = x.reshape(streams_count, tok_rows + taps - 1, groups, LANES)
    f = short_filter.reshape(taps, streams_count, groups, LANES)
    rate_t = rates.T.reshape(modes, groups, LANES)
    residue_t = residues.T.reshape(modes, groups, LANES)
    decay = jnp.exp(-rate_t)
    local = run_state(x, f, decay)

    carried = shift(local, 1)
    offset = 1
    while offset < devices:
        factor = jnp.exp(-rate_t * float(tok_rows * offset))
        carried = carried + factor * shift(carried, offset)
        offset *= 2

    out = run_out(x, f, decay, residue_t, skip.reshape(groups, LANES), carried)
    return out.reshape(tok_rows, width).astype(jnp.bfloat16)


def solution(mesh):
    return jax.shard_map(
        body,
        mesh=mesh,
        in_specs=(P(("ctx", "tp"), None, None), P(), P(), P(), P()),
        out_specs=P(("ctx", "tp"), None),
        check_vma=False,
    )
```

time: 374 us -> 104 us (0.28)
  the two profiles are of different devices: /device:TPU:16 before, /device:TPU:30 now
where the time goes in v1:
time: 104 us; the launch traced here: 103 us
  waiting for transfers between devices  47 us (45%)
  Pallas kernels  19.7 us (19%)
  starting transfers between devices  14 us (13%)
  local copies, waits for them, and re-layouts  12.8 us (12%)
  other arithmetic  9.61 us (9%)
    ppermute x7, waiting for transfers between devices, shift(): return lax.ppermute(value, axes, pairs)  47 us
    ppermute x7, starting transfers between devices, shift(): return lax.ppermute(value, axes, pairs)  14 us
    pallas_call x1, Pallas kernels, run_out(): pl.pallas_call(out_kernel, grid=grid, in_specs=[pl.BlockSpec((streams_cou...  12.5 us
    pallas_call x1, Pallas kernels, run_state(): pl.pallas_call(state_kernel, grid=grid, in_specs=[pl.BlockSpec((streams_c...  7.14 us
    reshape x1, local copies, waits for them, and re-layouts, body(): x = x.reshape(streams_count, tok_rows + taps - 1, groups, LANES)  6.88 us
    reshape x1, other arithmetic, body(): x = x.reshape(streams_count, tok_rows + taps - 1, groups, LANES)  5.63 us
    unnamed x10, local copies, waits for them, and re-layouts  3.19 us
  transfers between devices with their start and end apart: 7, of which 7 were waited for; matrix products, arithmetic and copies ran while one was open for 4% of the time, Pallas kernels for 0%

profile of v1, /device:TPU:30, one launch (start us, length us, event | category | flops | bytes accessed | tf_op | source)
XLA Modules:
  0.0 103.2 jit_solution(2636405834002690345)
XLA Ops:
  0.0 1.0 slice.3
  1.0 1.9 %collective-permute-start = (bf16[2,3,4096]{2,0,1:T(2,128)(2,1)S(1)}, bf16[2,3,4096]{2,0,1:T(2,128)(2,1)S(1)}, u32[]{:S(2)}, u32[]{:S(2)}) collective-permute-start(bf16[2,3,4096]{2,0,1:T(2,128)(2,1)S(1)} %slice.3), channel_id=1, source_target_pairs={{0,1},{1,2},{2,3},{3,4},{4,5},{5,6},{6,7},{7,8},{8,9},{9,10},{10,1... | collective-permute-start | bytes 147464 | tf_op jit(solution)/shard_map/ppermute | solution.py:114
  2.9 1.2 %exponential_bitcast_fusion = (f32[2,8,32,128]{3,1,2,0:T(8,128)S(1)}, f32[2,8,32,128]{3,1,2,0:T(8,128)S(1)}, f32[2,8,32,128]{3,1,2,0:T(8,128)S(1)}, f32[2,8,32,1...) fusion(f32[4096,16]{0,1:T(8,128)} %param.8), kind=kLoop, calls=%fused_computation.12 | loop fusion | flops 393216 | bytes 1835008
  4.1 1.7 %reshape.36.f_ref = f32[3,3,32,128]{3,2,1,0:T(8,128)} reshape(f32[3,3,4096]{2,1,0:T(4,128)} %param.6) | data formatting | bytes 294912 | tf_op jit(solution)/shard_map/reshape | solution.py:120
  7.0 5.6 %convert_bitcast_fusion = f32[3,130,4096]{2,1,0:T(8,128)} fusion(bf16[128,3,4096]{2,0,1:T(8,128)(2,1)} %param.5, bf16[2,3,4096]{2,0,1:T(2,128)(2,1)S(1)} %collective-permute-done), kind=kLoop, calls=%fused_computation | loop fusion | flops 6389760 | bytes 9584640 | tf_op jit(solution)/shard_map/reshape | solution.py:119
  12.6 6.9 %reshape.40.x_ref = f32[3,130,32,128]{3,2,1,0:T(8,128)} reshape(f32[3,130,4096]{2,1,0:T(8,128)} %convert_bitcast_fusion) | data formatting | bytes 12779520 | tf_op jit(solution)/shard_map/reshape | solution.py:119
  19.5 7.1 %shard_map.55 = f32[16,32,128]{2,1,0:T(8,128)} custom-call(f32[3,130,32,128]{3,2,1,0:T(8,128)} %reshape.40.x_ref, f32[3,3,32,128]{3,2,1,0:T(8,128)} %reshape.36.f_ref, f32[16,32,128]{2,1,0:T(8,128)} %bitcast.50), custom_call_target="tpu_custom_call" | custom-call | tf_op jit(solution)/shard_map/pallas_call | solution.py:69
  26.6 2.6 %collective-permute-start.1 = (f32[16,32,128]{2,1,0:T(8,128)}, f32[16,32,128]{2,1,0:T(8,128)S(1)}, u32[]{:S(2)}, u32[]{:S(2)}) collective-permute-start(f32[16,32,128]{2,1,0:T(8,128)} %shard_map.55), channel_id=1, source_target_pairs={{0,1},{1,2},{2,3},{3,4},{4,5},{5,6},{6,7},{7,8},{8,9},{9,10},{10,1... | collective-permute-start | bytes 786440 | tf_op jit(solution)/shard_map/ppermute | solution.py:114
  29.3 7.1 %collective-permute-done.1 = f32[16,32,128]{2,1,0:T(8,128)S(1)} collective-permute-done((f32[16,32,128]{2,1,0:T(8,128)}, f32[16,32,128]{2,1,0:T(8,128)S(1)}, u32[]{:S(2)}, u32[]{:S(2)}) %collective-permute-start.1) | collective-permute-done | bytes 262176 | tf_op jit(solution)/shard_map/ppermute | solution.py:114
  36.3 3.6 %collective-permute-start.2 = (f32[16,32,128]{2,1,0:T(8,128)S(1)}, f32[16,32,128]{2,1,0:T(8,128)S(1)}, u32[]{:S(2)}, u32[]{:S(2)}) collective-permute-start(f32[16,32,128]{2,1,0:T(8,128)S(1)} %collective-permute-done.1), channel_id=1, source_target_pairs={{0,1},{1,2},{2,3},{3,4},{4,5},{5,6},{6,7},{7,8},{8,9},{9,10},{10,1... | collective-permute-start | bytes 786440 | tf_op jit(solution)/shard_map/ppermute | solution.py:114
  40.0 6.8 %collective-permute-done.2 = f32[16,32,128]{2,1,0:T(8,128)S(1)} collective-permute-done((f32[16,32,128]{2,1,0:T(8,128)S(1)}, f32[16,32,128]{2,1,0:T(8,128)S(1)}, u32[]{:S(2)}, u32[]{:S(2)}) %collective-permute-start.2) | collective-permute-done | bytes 262176 | tf_op jit(solution)/shard_map/ppermute | solution.py:114
  46.9 1.9 %collective-permute-start.3 = (f32[16,32,128]{2,1,0:T(8,128)S(1)}, f32[16,32,128]{2,1,0:T(8,128)S(1)}, u32[]{:S(2)}, u32[]{:S(2)}) collective-permute-start(f32[16,32,128]{2,1,0:T(8,128)S(1)} %fusion.4), channel_id=1, source_target_pairs={{0,2},{1,3},{2,4},{3,5},{4,6},{5,7},{6,8},{7,9},{8,10},{9,11},{10,... | collective-permute-start | bytes 786440 | tf_op jit(solution)/shard_map/ppermute | solution.py:114
  48.9 5.7 %collective-permute-done.3 = f32[16,32,128]{2,1,0:T(8,128)S(1)} collective-permute-done((f32[16,32,128]{2,1,0:T(8,128)S(1)}, f32[16,32,128]{2,1,0:T(8,128)S(1)}, u32[]{:S(2)}, u32[]{:S(2)}) %collective-permute-start.3) | collective-permute-done | bytes 262176 | tf_op jit(solution)/shard_map/ppermute | solution.py:114
  54.6 1.3 %collective-permute-start.4 = (f32[16,32,128]{2,1,0:T(8,128)S(1)}, f32[16,32,128]{2,1,0:T(8,128)S(1)}, u32[]{:S(2)}, u32[]{:S(2)}) collective-permute-start(f32[16,32,128]{2,1,0:T(8,128)S(1)} %fusion.3), channel_id=1, source_target_pairs={{0,4},{1,5},{2,6},{3,7},{4,8},{5,9},{6,10},{7,11},{8,12},{9,13},{1... | collective-permute-start | bytes 786440 | tf_op jit(solution)/shard_map/ppermute | solution.py:114
  56.0 7.5 %collective-permute-done.4 = f32[16,32,128]{2,1,0:T(8,128)S(1)} collective-permute-done((f32[16,32,128]{2,1,0:T(8,128)S(1)}, f32[16,32,128]{2,1,0:T(8,128)S(1)}, u32[]{:S(2)}, u32[]{:S(2)}) %collective-permute-start.4) | collective-permute-done | bytes 262176 | tf_op jit(solution)/shard_map/ppermute | solution.py:114
  63.5 1.3 %collective-permute-start.5 = (f32[16,32,128]{2,1,0:T(8,128)S(1)}, f32[16,32,128]{2,1,0:T(8,128)S(1)}, u32[]{:S(2)}, u32[]{:S(2)}) collective-permute-start(f32[16,32,128]{2,1,0:T(8,128)S(1)} %fusion.2), channel_id=1, source_target_pairs={{0,8},{1,9},{2,10},{3,11},{4,12},{5,13},{6,14},{7,15},{8,16},{9,17... | collective-permute-start | bytes 786440 | tf_op jit(solution)/shard_map/ppermute | solution.py:114
  64.9 7.4 %collective-permute-done.5 = f32[16,32,128]{2,1,0:T(8,128)S(1)} collective-permute-done((f32[16,32,128]{2,1,0:T(8,128)S(1)}, f32[16,32,128]{2,1,0:T(8,128)S(1)}, u32[]{:S(2)}, u32[]{:S(2)}) %collective-permute-start.5) | collective-permute-done | bytes 262176 | tf_op jit(solution)/shard_map/ppermute | solution.py:114
  72.3 1.3 %collective-permute-start.6 = (f32[16,32,128]{2,1,0:T(8,128)S(1)}, f32[16,32,128]{2,1,0:T(8,128)S(1)}, u32[]{:S(2)}, u32[]{:S(2)}) collective-permute-start(f32[16,32,128]{2,1,0:T(8,128)S(1)} %fusion.1), channel_id=1, source_target_pairs={{0,16},{1,17},{2,18},{3,19},{4,20},{5,21},{6,22},{7,23},{8,24},{9,... | collective-permute-start | bytes 786440 | tf_op jit(solution)/shard_map/ppermute | solution.py:114
  73.6 0.8 copy.7
  74.4 12.2 %collective-permute-done.6 = f32[16,32,128]{2,1,0:T(8,128)S(1)} collective-permute-done((f32[16,32,128]{2,1,0:T(8,128)S(1)}, f32[16,32,128]{2,1,0:T(8,128)S(1)}, u32[]{:S(2)}, u32[]{:S(2)}) %collective-permute-start.6) | collective-permute-done | bytes 262176 | tf_op jit(solution)/shard_map/ppermute | solution.py:114
  86.6 0.8 fusion.h_ref
  87.4 12.5 %shard_map.56 = f32[128,32,128]{2,1,0:T(8,128)} custom-call(f32[3,130,32,128]{3,2,1,0:T(8,128)} %reshape.40.x_ref, f32[3,3,32,128]{3,2,1,0:T(8,128)} %reshape.36.f_ref, f32[16,32,128]{2,1,0:T(8,128)} %bitcast.51, f32[16,32,128]{2,1,0:T(8,128)} %bitcast.52, f32[32,128]{1,0:T(8,128)} %bitcast.54, f32[16,32,128]{2,1,0:T(8,128)} %fusion.h_ref), custom_call_target="tpu_custom_call" | custom-call | tf_op jit(solution)/shard_map/pallas_call | solution.py:88
  99.9 1.8 %convert_element_type.11 = bf16[128,32,128]{2,1,0:T(8,128)(2,1)S(1)} convert(f32[128,32,128]{2,1,0:T(8,128)} %shard_map.56) | non-fusion elementwise | flops 524288 | bytes 3145728 | tf_op jit(solution)/shard_map/convert_element_type | solution.py:134
  101.7 1.4 %copy.15 = bf16[16,8,32,128]{3,1,2,0:T(8,128)(2,1)} copy(bf16[16,8,32,128]{3,2,1,0:T(8,128)(2,1)S(1)} %bitcast.49) | data formatting | bytes 2097152
  (13 shorter events, 1.7 us)
Async XLA Ops:
  1.0 6.0 %collective-permute-start = (bf16[2,3,4096]{2,0,1:T(2,128)(2,1)S(1)}, bf16[2,3,4096]{2,0,1:T(2,128)(2,1)S(1)}, u32[]{:S(2)}, u32[]{:S(2)}) collective-permute-start(bf16[2,3,4096]{2,0,1:T(2,128)(2,1)S(1)} %slice.3), channel_id=1, source_target_pairs={{0,1},{1,2},{2,3},{3,4},{4,5},{5,6},{6,7},{7,8},{8,9},{9,10},{10,1... | collective-permute-start | bytes 147464 | tf_op jit(solution)/shard_map/ppermute | solution.py:114
  19.5 54.1 %copy-start = (f32[4096,16]{0,1:T(8,128)S(1)}, f32[4096,16]{0,1:T(8,128)}, u32[]{:S(2)}) copy-start(f32[4096,16]{0,1:T(8,128)} %param.9) | copy-start | bytes 786436
  26.6 9.7 %collective-permute-start.1 = (f32[16,32,128]{2,1,0:T(8,128)}, f32[16,32,128]{2,1,0:T(8,128)S(1)}, u32[]{:S(2)}, u32[]{:S(2)}) collective-permute-start(f32[16,32,128]{2,1,0:T(8,128)} %shard_map.55), channel_id=1, source_target_pairs={{0,1},{1,2},{2,3},{3,4},{4,5},{5,6},{6,7},{7,8},{8,9},{9,10},{10,1... | collective-permute-start | bytes 786440 | tf_op jit(solution)/shard_map/ppermute | solution.py:114
  36.3 10.5 %collective-permute-start.2 = (f32[16,32,128]{2,1,0:T(8,128)S(1)}, f32[16,32,128]{2,1,0:T(8,128)S(1)}, u32[]{:S(2)}, u32[]{:S(2)}) collective-permute-start(f32[16,32,128]{2,1,0:T(8,128)S(1)} %collective-permute-done.1), channel_id=1, source_target_pairs={{0,1},{1,2},{2,3},{3,4},{4,5},{5,6},{6,7},{7,8},{8,9},{9,10},{10,1... | collective-permute-start | bytes 786440 | tf_op jit(solution)/shard_map/ppermute | solution.py:114
  46.9 7.7 %collective-permute-start.3 = (f32[16,32,128]{2,1,0:T(8,128)S(1)}, f32[16,32,128]{2,1,0:T(8,128)S(1)}, u32[]{:S(2)}, u32[]{:S(2)}) collective-permute-start(f32[16,32,128]{2,1,0:T(8,128)S(1)} %fusion.4), channel_id=1, source_target_pairs={{0,2},{1,3},{2,4},{3,5},{4,6},{5,7},{6,8},{7,9},{8,10},{9,11},{10,... | collective-permute-start | bytes 786440 | tf_op jit(solution)/shard_map/ppermute | solution.py:114
  54.6 8.8 %collective-permute-start.4 = (f32[16,32,128]{2,1,0:T(8,128)S(1)}, f32[16,32,128]{2,1,0:T(8,128)S(1)}, u32[]{:S(2)}, u32[]{:S(2)}) collective-permute-start(f32[16,32,128]{2,1,0:T(8,128)S(1)} %fusion.3), channel_id=1, source_target_pairs={{0,4},{1,5},{2,6},{3,7},{4,8},{5,9},{6,10},{7,11},{8,12},{9,13},{1... | collective-permute-start | bytes 786440 | tf_op jit(solution)/shard_map/ppermute | solution.py:114
  63.5 8.7 %collective-permute-start.5 = (f32[16,32,128]{2,1,0:T(8,128)S(1)}, f32[16,32,128]{2,1,0:T(8,128)S(1)}, u32[]{:S(2)}, u32[]{:S(2)}) collective-permute-start(f32[16,32,128]{2,1,0:T(8,128)S(1)} %fusion.2), channel_id=1, source_target_pairs={{0,8},{1,9},{2,10},{3,11},{4,12},{5,13},{6,14},{7,15},{8,16},{9,17... | collective-permute-start | bytes 786440 | tf_op jit(solution)/shard_map/ppermute | solution.py:114
  72.3 14.3 %collective-permute-start.6 = (f32[16,32,128]{2,1,0:T(8,128)S(1)}, f32[16,32,128]{2,1,0:T(8,128)S(1)}, u32[]{:S(2)}, u32[]{:S(2)}) collective-permute-start(f32[16,32,128]{2,1,0:T(8,128)S(1)} %fusion.1), channel_id=1, source_target_pairs={{0,16},{1,17},{2,18},{3,19},{4,20},{5,21},{6,22},{7,23},{8,24},{9,... | collective-permute-start | bytes 786440 | tf_op jit(solution)/shard_map/ppermute | solution.py:114

commit v2 on v1

--- a/solution.py
+++ b/solution.py
@@ -123,11 +123,11 @@
     decay = jnp.exp(-rate_t)
     local = run_state(x, f, decay)
 
-    carried = shift(local, 1)
+    carried = shift(local.astype(jnp.bfloat16), 1).astype(jnp.float32)
     offset = 1
     while offset < devices:
         factor = jnp.exp(-rate_t * float(tok_rows * offset))
-        carried = carried + factor * shift(carried, offset)
+        carried = carried + factor * shift(carried.astype(jnp.bfloat16), offset).astype(jnp.float32)
         offset *= 2
 
     out = run_out(x, f, decay, residue_t, skip.reshape(groups, LANES), carried)

time: 104 us -> 93.2 us (0.90)
  the two profiles are of different devices: /device:TPU:30 before, /device:TPU:16 now
where the time goes in v2:
time: 93.2 us; the launch traced here: 91.5 us
  waiting for transfers between devices  31.8 us (34%)
  Pallas kernels  19.7 us (21%)
  starting transfers between devices  16.5 us (18%)
  local copies, waits for them, and re-layouts  12.8 us (14%)
  other arithmetic  10.6 us (11%)
    ppermute x7, waiting for transfers between devices, shift(): return lax.ppermute(value, axes, pairs)  31.8 us
    ppermute x7, starting transfers between devices, shift(): return lax.ppermute(value, axes, pairs)  16.5 us
    pallas_call x1, Pallas kernels, run_out(): pl.pallas_call(out_kernel, grid=grid, in_specs=[pl.BlockSpec((streams_cou...  12.5 us
    pallas_call x1, Pallas kernels, run_state(): pl.pallas_call(state_kernel, grid=grid, in_specs=[pl.BlockSpec((streams_c...  7.13 us
    reshape x1, local copies, waits for them, and re-layouts, body(): x = x.reshape(streams_count, tok_rows + taps - 1, groups, LANES)  6.91 us
    reshape x1, other arithmetic, body(): x = x.reshape(streams_count, tok_rows + taps - 1, groups, LANES)  5.63 us
    unnamed x10, local copies, waits for them, and re-layouts  3.18 us
  transfers between devices with their start and end apart: 7, of which 7 were waited for; matrix products, arithmetic and copies ran while one was open for 5% of the time, Pallas kernels for 0%

profile of v2, /device:TPU:16, one launch (start us, length us, event | category | flops | bytes accessed | tf_op | source)
XLA Modules:
  0.0 91.5 jit_solution(6925522139508903746)
XLA Ops:
  0.0 1.0 %slice.3 = bf16[2,3,4096]{2,0,1:T(2,128)(2,1)S(1)} slice(bf16[128,3,4096]{2,0,1:T(8,128)(2,1)} %param.5), slice={[126:128], [0:3], [0:4096]} | slice | bytes 98304 | tf_op jit(solution)/shard_map/slice | solution.py:116
  1.0 3.4 %collective-permute-start = (bf16[2,3,4096]{2,0,1:T(2,128)(2,1)S(1)}, bf16[2,3,4096]{2,0,1:T(2,128)(2,1)S(1)}, u32[]{:S(2)}, u32[]{:S(2)}) collective-permute-start(bf16[2,3,4096]{2,0,1:T(2,128)(2,1)S(1)} %slice.3), channel_id=1, source_target_pairs={{0,1},{1,2},{2,3},{3,4},{4,5},{5,6},{6,7},{7,8},{8,9},{9,10},{10,1... | collective-permute-start | bytes 147464 | tf_op jit(solution)/shard_map/ppermute | solution.py:114
  4.4 1.2 %exponential_bitcast_fusion = (f32[2,8,32,128]{3,1,2,0:T(8,128)S(1)}, f32[2,8,32,128]{3,1,2,0:T(8,128)S(1)}, f32[2,8,32,128]{3,1,2,0:T(8,128)S(1)}, f32[2,8,32,1...) fusion(f32[4096,16]{0,1:T(8,128)} %param.8), kind=kLoop, calls=%fused_computation.12 | loop fusion | flops 393216 | bytes 1835008
  5.6 1.7 %reshape.36.f_ref = f32[3,3,32,128]{3,2,1,0:T(8,128)} reshape(f32[3,3,4096]{2,1,0:T(4,128)} %param.6) | data formatting | bytes 294912 | tf_op jit(solution)/shard_map/reshape | solution.py:120
  8.2 5.6 %convert_bitcast_fusion = f32[3,130,4096]{2,1,0:T(8,128)} fusion(bf16[128,3,4096]{2,0,1:T(8,128)(2,1)} %param.5, bf16[2,3,4096]{2,0,1:T(2,128)(2,1)S(1)} %collective-permute-done), kind=kLoop, calls=%fused_computation | loop fusion | flops 6389760 | bytes 9584640 | tf_op jit(solution)/shard_map/reshape | solution.py:119
  13.8 6.9 %reshape.40.x_ref = f32[3,130,32,128]{3,2,1,0:T(8,128)} reshape(f32[3,130,4096]{2,1,0:T(8,128)} %convert_bitcast_fusion) | data formatting | bytes 12779520 | tf_op jit(solution)/shard_map/reshape | solution.py:119
  20.7 7.1 %shard_map.55 = f32[16,32,128]{2,1,0:T(8,128)} custom-call(f32[3,130,32,128]{3,2,1,0:T(8,128)} %reshape.40.x_ref, f32[3,3,32,128]{3,2,1,0:T(8,128)} %reshape.36.f_ref, f32[16,32,128]{2,1,0:T(8,128)} %bitcast.62), custom_call_target="tpu_custom_call" | custom-call | tf_op jit(solution)/shard_map/pallas_call | solution.py:69
  27.9 1.0 %convert_element_type.45 = bf16[16,32,128]{2,1,0:T(8,128)(2,1)S(1)} convert(f32[16,32,128]{2,1,0:T(8,128)} %shard_map.55) | non-fusion elementwise | flops 65536 | bytes 393216 | tf_op jit(solution)/shard_map/convert_element_type | solution.py:126
  28.8 2.2 %collective-permute-start.1 = (bf16[16,32,128]{2,1,0:T(8,128)(2,1)S(1)}, bf16[16,32,128]{2,1,0:T(8,128)(2,1)S(1)}, u32[]{:S(2)}, u32[]{:S(2)}) collective-permute-start(bf16[16,32,128]{2,1,0:T(8,128)(2,1)S(1)} %convert_element_type.45), channel_id=1, source_target_pairs={{0,1},{1,2},{2,3},{3,4},{4,5},{5,6},{6,7},{7,8},{8,9},{9,10},{10,1... | collective-permute-start | bytes 393224 | tf_op jit(solution)/shard_map/ppermute | solution.py:114
  31.0 5.9 %collective-permute-done.1 = bf16[16,32,128]{2,1,0:T(8,128)(2,1)S(1)} collective-permute-done((bf16[16,32,128]{2,1,0:T(8,128)(2,1)S(1)}, bf16[16,32,128]{2,1,0:T(8,128)(2,1)S(1)}, u32[]{:S(2)}, u32[]{:S(2)}) %collective-permute-start.1) | collective-permute-done | bytes 131104 | tf_op jit(solution)/shard_map/ppermute | solution.py:114
  36.9 2.2 %collective-permute-start.2 = (bf16[16,32,128]{2,1,0:T(8,128)(2,1)S(1)}, bf16[16,32,128]{2,1,0:T(8,128)(2,1)S(1)}, u32[]{:S(2)}, u32[]{:S(2)}) collective-permute-start(bf16[16,32,128]{2,1,0:T(8,128)(2,1)S(1)} %collective-permute-done.1), channel_id=1, source_target_pairs={{0,1},{1,2},{2,3},{3,4},{4,5},{5,6},{6,7},{7,8},{8,9},{9,10},{10,1... | collective-permute-start | bytes 393224 | tf_op jit(solution)/shard_map/ppermute | solution.py:114
  39.2 5.8 %collective-permute-done.2 = bf16[16,32,128]{2,1,0:T(8,128)(2,1)S(1)} collective-permute-done((bf16[16,32,128]{2,1,0:T(8,128)(2,1)S(1)}, bf16[16,32,128]{2,1,0:T(8,128)(2,1)S(1)}, u32[]{:S(2)}, u32[]{:S(2)}) %collective-permute-start.2) | collective-permute-done | bytes 131104 | tf_op jit(solution)/shard_map/ppermute | solution.py:114
  45.0 1.9 %collective-permute-start.3 = (bf16[16,32,128]{2,1,0:T(8,128)(2,1)S(1)}, bf16[16,32,128]{2,1,0:T(8,128)(2,1)S(1)}, u32[]{:S(2)}, u32[]{:S(2)}) collective-permute-start(bf16[16,32,128]{2,1,0:T(8,128)(2,1)S(1)} %fusion.5), channel_id=1, source_target_pairs={{0,2},{1,3},{2,4},{3,5},{4,6},{5,7},{6,8},{7,9},{8,10},{9,11},{10,... | collective-permute-start | bytes 393224 | tf_op jit(solution)/shard_map/ppermute | solution.py:114
  47.0 5.2 %collective-permute-done.3 = bf16[16,32,128]{2,1,0:T(8,128)(2,1)S(1)} collective-permute-done((bf16[16,32,128]{2,1,0:T(8,128)(2,1)S(1)}, bf16[16,32,128]{2,1,0:T(8,128)(2,1)S(1)}, u32[]{:S(2)}, u32[]{:S(2)}) %collective-permute-start.3) | collective-permute-done | bytes 131104 | tf_op jit(solution)/shard_map/ppermute | solution.py:114
  52.3 1.9 %collective-permute-start.4 = (bf16[16,32,128]{2,1,0:T(8,128)(2,1)S(1)}, bf16[16,32,128]{2,1,0:T(8,128)(2,1)S(1)}, u32[]{:S(2)}, u32[]{:S(2)}) collective-permute-start(bf16[16,32,128]{2,1,0:T(8,128)(2,1)S(1)} %get-tuple-element.7), channel_id=1, source_target_pairs={{0,4},{1,5},{2,6},{3,7},{4,8},{5,9},{6,10},{7,11},{8,12},{9,13},{1... | collective-permute-start | bytes 393224 | tf_op jit(solution)/shard_map/ppermute | solution.py:114
  54.3 5.8 %collective-permute-done.4 = bf16[16,32,128]{2,1,0:T(8,128)(2,1)S(1)} collective-permute-done((bf16[16,32,128]{2,1,0:T(8,128)(2,1)S(1)}, bf16[16,32,128]{2,1,0:T(8,128)(2,1)S(1)}, u32[]{:S(2)}, u32[]{:S(2)}) %collective-permute-start.4) | collective-permute-done | bytes 131104 | tf_op jit(solution)/shard_map/ppermute | solution.py:114
  60.1 3.5 %collective-permute-start.5 = (bf16[16,32,128]{2,1,0:T(8,128)(2,1)S(1)}, bf16[16,32,128]{2,1,0:T(8,128)(2,1)S(1)}, u32[]{:S(2)}, u32[]{:S(2)}) collective-permute-start(bf16[16,32,128]{2,1,0:T(8,128)(2,1)S(1)} %fusion.6), channel_id=1, source_target_pairs={{0,8},{1,9},{2,10},{3,11},{4,12},{5,13},{6,14},{7,15},{8,16},{9,17... | collective-permute-start | bytes 393224 | tf_op jit(solution)/shard_map/ppermute | solution.py:114
  63.7 3.3 %collective-permute-done.5 = bf16[16,32,128]{2,1,0:T(8,128)(2,1)S(1)} collective-permute-done((bf16[16,32,128]{2,1,0:T(8,128)(2,1)S(1)}, bf16[16,32,128]{2,1,0:T(8,128)(2,1)S(1)}, u32[]{:S(2)}, u32[]{:S(2)}) %collective-permute-start.5) | collective-permute-done | bytes 131104 | tf_op jit(solution)/shard_map/ppermute | solution.py:114
  67.1 1.3 %collective-permute-start.6 = (bf16[16,32,128]{2,1,0:T(8,128)(2,1)S(1)}, bf16[16,32,128]{2,1,0:T(8,128)(2,1)S(1)}, u32[]{:S(2)}, u32[]{:S(2)}) collective-permute-start(bf16[16,32,128]{2,1,0:T(8,128)(2,1)S(1)} %get-tuple-element.5), channel_id=1, source_target_pairs={{0,16},{1,17},{2,18},{3,19},{4,20},{5,21},{6,22},{7,23},{8,24},{9,... | collective-permute-start | bytes 393224 | tf_op jit(solution)/shard_map/ppermute | solution.py:114
  69.2 5.7 %collective-permute-done.6 = bf16[16,32,128]{2,1,0:T(8,128)(2,1)S(1)} collective-permute-done((bf16[16,32,128]{2,1,0:T(8,128)(2,1)S(1)}, bf16[16,32,128]{2,1,0:T(8,128)(2,1)S(1)}, u32[]{:S(2)}, u32[]{:S(2)}) %collective-permute-start.6) | collective-permute-done | bytes 131104 | tf_op jit(solution)/shard_map/ppermute | solution.py:114
  75.0 0.8 fusion.h_ref
  75.7 12.5 %shard_map.56 = f32[128,32,128]{2,1,0:T(8,128)} custom-call(f32[3,130,32,128]{3,2,1,0:T(8,128)} %reshape.40.x_ref, f32[3,3,32,128]{3,2,1,0:T(8,128)} %reshape.36.f_ref, f32[16,32,128]{2,1,0:T(8,128)} %bitcast.63, f32[16,32,128]{2,1,0:T(8,128)} %bitcast.64, f32[32,128]{1,0:T(8,128)} %bitcast.66, f32[16,32,128]{2,1,0:T(8,128)} %fusion.h_ref), custom_call_target="tpu_custom_call" | custom-call | tf_op jit(solution)/shard_map/pallas_call | solution.py:88
  88.3 1.8 %convert_element_type.56 = bf16[128,32,128]{2,1,0:T(8,128)(2,1)S(1)} convert(f32[128,32,128]{2,1,0:T(8,128)} %shard_map.56) | non-fusion elementwise | flops 524288 | bytes 3145728 | tf_op jit(solution)/shard_map/convert_element_type | solution.py:134
  90.1 1.4 %copy.15 = bf16[16,8,32,128]{3,1,2,0:T(8,128)(2,1)} copy(bf16[16,8,32,128]{3,2,1,0:T(8,128)(2,1)S(1)} %bitcast.61) | data formatting | bytes 2097152
  (14 shorter events, 2.2 us)
Async XLA Ops:
  1.0 7.2 %collective-permute-start = (bf16[2,3,4096]{2,0,1:T(2,128)(2,1)S(1)}, bf16[2,3,4096]{2,0,1:T(2,128)(2,1)S(1)}, u32[]{:S(2)}, u32[]{:S(2)}) collective-permute-start(bf16[2,3,4096]{2,0,1:T(2,128)(2,1)S(1)} %slice.3), channel_id=1, source_target_pairs={{0,1},{1,2},{2,3},{3,4},{4,5},{5,6},{6,7},{7,8},{8,9},{9,10},{10,1... | collective-permute-start | bytes 147464 | tf_op jit(solution)/shard_map/ppermute | solution.py:114
  20.7 47.7 %copy-start = (f32[4096,16]{0,1:T(8,128)S(1)}, f32[4096,16]{0,1:T(8,128)}, u32[]{:S(2)}) copy-start(f32[4096,16]{0,1:T(8,128)} %param.9) | copy-start | bytes 786436
  28.8 8.1 %collective-permute-start.1 = (bf16[16,32,128]{2,1,0:T(8,128)(2,1)S(1)}, bf16[16,32,128]{2,1,0:T(8,128)(2,1)S(1)}, u32[]{:S(2)}, u32[]{:S(2)}) collective-permute-start(bf16[16,32,128]{2,1,0:T(8,128)(2,1)S(1)} %convert_element_type.45), channel_id=1, source_target_pairs={{0,1},{1,2},{2,3},{3,4},{4,5},{5,6},{6,7},{7,8},{8,9},{9,10},{10,1... | collective-permute-start | bytes 393224 | tf_op jit(solution)/shard_map/ppermute | solution.py:114
  36.9 8.1 %collective-permute-start.2 = (bf16[16,32,128]{2,1,0:T(8,128)(2,1)S(1)}, bf16[16,32,128]{2,1,0:T(8,128)(2,1)S(1)}, u32[]{:S(2)}, u32[]{:S(2)}) collective-permute-start(bf16[16,32,128]{2,1,0:T(8,128)(2,1)S(1)} %collective-permute-done.1), channel_id=1, source_target_pairs={{0,1},{1,2},{2,3},{3,4},{4,5},{5,6},{6,7},{7,8},{8,9},{9,10},{10,1... | collective-permute-start | bytes 393224 | tf_op jit(solution)/shard_map/ppermute | solution.py:114
  45.0 7.2 %collective-permute-start.3 = (bf16[16,32,128]{2,1,0:T(8,128)(2,1)S(1)}, bf16[16,32,128]{2,1,0:T(8,128)(2,1)S(1)}, u32[]{:S(2)}, u32[]{:S(2)}) collective-permute-start(bf16[16,32,128]{2,1,0:T(8,128)(2,1)S(1)} %fusion.5), channel_id=1, source_target_pairs={{0,2},{1,3},{2,4},{3,5},{4,6},{5,7},{6,8},{7,9},{8,10},{9,11},{10,... | collective-permute-start | bytes 393224 | tf_op jit(solution)/shard_map/ppermute | solution.py:114
  52.3 7.8 %collective-permute-start.4 = (bf16[16,32,128]{2,1,0:T(8,128)(2,1)S(1)}, bf16[16,32,128]{2,1,0:T(8,128)(2,1)S(1)}, u32[]{:S(2)}, u32[]{:S(2)}) collective-permute-start(bf16[16,32,128]{2,1,0:T(8,128)(2,1)S(1)} %get-tuple-element.7), channel_id=1, source_target_pairs={{0,4},{1,5},{2,6},{3,7},{4,8},{5,9},{6,10},{7,11},{8,12},{9,13},{1... | collective-permute-start | bytes 393224 | tf_op jit(solution)/shard_map/ppermute | solution.py:114
  60.1 6.9 %collective-permute-start.5 = (bf16[16,32,128]{2,1,0:T(8,128)(2,1)S(1)}, bf16[16,32,128]{2,1,0:T(8,128)(2,1)S(1)}, u32[]{:S(2)}, u32[]{:S(2)}) collective-permute-start(bf16[16,32,128]{2,1,0:T(8,128)(2,1)S(1)} %fusion.6), channel_id=1, source_target_pairs={{0,8},{1,9},{2,10},{3,11},{4,12},{5,13},{6,14},{7,15},{8,16},{9,17... | collective-permute-start | bytes 393224 | tf_op jit(solution)/shard_map/ppermute | solution.py:114
  67.1 7.9 %collective-permute-start.6 = (bf16[16,32,128]{2,1,0:T(8,128)(2,1)S(1)}, bf16[16,32,128]{2,1,0:T(8,128)(2,1)S(1)}, u32[]{:S(2)}, u32[]{:S(2)}) collective-permute-start(bf16[16,32,128]{2,1,0:T(8,128)(2,1)S(1)} %get-tuple-element.5), channel_id=1, source_target_pairs={{0,16},{1,17},{2,18},{3,19},{4,20},{5,21},{6,22},{7,23},{8,24},{9,... | collective-permute-start | bytes 393224 | tf_op jit(solution)/shard_map/ppermute | solution.py:114

commit v3 on v2

--- a/solution.py
+++ b/solution.py
@@ -9,6 +9,7 @@
 
 LANES = 128
 GROUPS = 8
+FIRST_WINDOW = 8
 
 
 def features(x_ref, f_ref, t):
@@ -123,12 +124,26 @@
     decay = jnp.exp(-rate_t)
     local = run_state(x, f, decay)
 
-    carried = shift(local.astype(jnp.bfloat16), 1).astype(jnp.float32)
-    offset = 1
-    while offset < devices:
-        factor = jnp.exp(-rate_t * float(tok_rows * offset))
-        carried = carried + factor * shift(carried.astype(jnp.bfloat16), offset).astype(jnp.float32)
-        offset *= 2
+    def decay_pow(steps):
+        return jnp.exp(-rate_t * float(tok_rows * steps))
+
+    def gather_window(value, spacing, count):
+        sent = value.astype(jnp.bfloat16)
+        total = None
+        for k in range(1, count + 1):
+            if k * spacing >= devices:
+                break
+            term = decay_pow((k - 1) * spacing) * shift(sent, k * spacing).astype(jnp.float32)
+            total = term if total is None else total + term
+        return total
+
+    first = min(FIRST_WINDOW, devices - 1)
+    carried = gather_window(local, 1, first)
+    window = first
+    while window < devices - 1:
+        count = min(-(-(devices - 1) // window) - 1, FIRST_WINDOW)
+        carried = carried + decay_pow(window) * gather_window(carried, window, count)
+        window *= count + 1
 
     out = run_out(x, f, decay, residue_t, skip.reshape(groups, LANES), carried)
     return out.reshape(tok_rows, width).astype(jnp.bfloat16)

time: 93.2 us -> 87.5 us (0.939); the launches traced: 91.5 us -> 86.8 us
  waiting for transfers between devices: 31.8 us -> 14.9 us
  starting transfers between devices: 16.5 us -> 28 us
    ppermute x7 -> x12, waiting for transfers between devices: 31.8 us -> 14.9 us  [shift(): return lax.ppermute(value, axes, pairs)]
    ppermute x7 -> x12, starting transfers between devices: 16.5 us -> 28 us  [shift(): return lax.ppermute(value, axes, pairs)]
    unnamed x10 -> x15, local copies, waits for them, and re-layouts: 3.18 us -> 3.46 us
  transfers between devices with their start and end apart: 7 -> 12, of which waited for: 7 -> 5; matrix products, arithmetic and copies ran while one was open for 5% -> 6% of each run, Pallas kernels for 0% -> 0%
where the time goes in v3:
time: 87.5 us; the launch traced here: 86.8 us
  starting transfers between devices  28 us (32%)
  Pallas kernels  19.7 us (23%)
  waiting for transfers between devices  14.9 us (17%)
  local copies, waits for them, and re-layouts  13 us (15%)
  other arithmetic  10.9 us (12%)
    ppermute x12, starting transfers between devices, shift(): return lax.ppermute(value, axes, pairs)  28 us
    ppermute x12, waiting for transfers between devices, shift(): return lax.ppermute(value, axes, pairs)  14.9 us
    pallas_call x1, Pallas kernels, run_out(): pl.pallas_call(out_kernel, grid=grid, in_specs=[pl.BlockSpec((streams_cou...  12.6 us
    pallas_call x1, Pallas kernels, run_state(): pl.pallas_call(state_kernel, grid=grid, in_specs=[pl.BlockSpec((streams_c...  7.13 us
    reshape x1, local copies, waits for them, and re-layouts, body(): x = x.reshape(streams_count, tok_rows + taps - 1, groups, LANES)  6.91 us
    reshape x1, other arithmetic, body(): x = x.reshape(streams_count, tok_rows + taps - 1, groups, LANES)  5.63 us
    unnamed x15, local copies, waits for them, and re-layouts  3.46 us
    convert_element_type x1, other arithmetic, body(): return out.reshape(tok_rows, width).astype(jnp.bfloat16)  1.81 us
  transfers between devices with their start and end apart: 12, of which 5 were waited for; matrix products, arithmetic and copies ran while one was open for 6% of the time, Pallas kernels for 0%

profile of v3, /device:TPU:16, one launch (start us, length us, event | category | flops | bytes accessed | tf_op | source)
XLA Modules:
  0.0 86.8 jit_solution(167547336128365764)
XLA Ops:
  0.0 1.0 %slice.3 = bf16[2,3,4096]{2,0,1:T(2,128)(2,1)S(1)} slice(bf16[128,3,4096]{2,0,1:T(8,128)(2,1)} %param.5), slice={[126:128], [0:3], [0:4096]} | slice | bytes 98304 | tf_op jit(solution)/shard_map/slice | solution.py:117
  1.0 3.4 %collective-permute-start = (bf16[2,3,4096]{2,0,1:T(2,128)(2,1)S(1)}, bf16[2,3,4096]{2,0,1:T(2,128)(2,1)S(1)}, u32[]{:S(2)}, u32[]{:S(2)}) collective-permute-start(bf16[2,3,4096]{2,0,1:T(2,128)(2,1)S(1)} %slice.3), channel_id=1, source_target_pairs={{0,1},{1,2},{2,3},{3,4},{4,5},{5,6},{6,7},{7,8},{8,9},{9,10},{10,1... | collective-permute-start | bytes 147464 | tf_op jit(solution)/shard_map/ppermute | solution.py:115
  4.4 1.3 %exponential_bitcast_fusion.1 = (f32[2,8,32,128]{3,1,2,0:T(8,128)S(1)}, f32[2,8,32,128]{3,1,2,0:T(8,128)S(1)}, f32[2,8,32,128]{3,1,2,0:T(8,128)S(1)}, f32[2,8,32...) fusion(f32[4096,16]{0,1:T(8,128)} %param.8), kind=kLoop, calls=%fused_computation.25 | loop fusion | flops 720896 | bytes 3145728
  5.8 1.7 %reshape.51.f_ref = f32[3,3,32,128]{3,2,1,0:T(8,128)} reshape(f32[3,3,4096]{2,1,0:T(4,128)} %param.6) | data formatting | bytes 294912 | tf_op jit(solution)/shard_map/reshape | solution.py:121
  8.2 5.6 %convert_bitcast_fusion = f32[3,130,4096]{2,1,0:T(8,128)} fusion(bf16[128,3,4096]{2,0,1:T(8,128)(2,1)} %param.5, bf16[2,3,4096]{2,0,1:T(2,128)(2,1)S(1)} %collective-permute-done), kind=kLoop, calls=%fused_computation | loop fusion | flops 6389760 | bytes 9584640 | tf_op jit(solution)/shard_map/reshape | solution.py:120
  13.8 6.9 %reshape.55.x_ref = f32[3,130,32,128]{3,2,1,0:T(8,128)} reshape(f32[3,130,4096]{2,1,0:T(8,128)} %convert_bitcast_fusion) | data formatting | bytes 12779520 | tf_op jit(solution)/shard_map/reshape | solution.py:120
  20.8 7.1 %shard_map.55 = f32[16,32,128]{2,1,0:T(8,128)} custom-call(f32[3,130,32,128]{3,2,1,0:T(8,128)} %reshape.55.x_ref, f32[3,3,32,128]{3,2,1,0:T(8,128)} %reshape.51.f_ref, f32[16,32,128]{2,1,0:T(8,128)} %bitcast.115), custom_call_target="tpu_custom_call" | custom-call | tf_op jit(solution)/shard_map/pallas_call | solution.py:70
  28.9 3.5 %collective-permute-start.8 = (bf16[16,32,128]{2,1,0:T(8,128)(2,1)S(1)}, bf16[16,32,128]{2,1,0:T(8,128)(2,1)S(1)}, u32[]{:S(2)}, u32[]{:S(2)}) collective-permute-start(bf16[16,32,128]{2,1,0:T(8,128)(2,1)S(1)} %convert_element_type.50), channel_id=1, source_target_pairs={{0,8},{1,9},{2,10},{3,11},{4,12},{5,13},{6,14},{7,15},{8,16},{9,17... | collective-permute-start | bytes 393224 | tf_op jit(solution)/shard_map/ppermute | solution.py:115
  32.4 2.5 %collective-permute-start.7 = (bf16[16,32,128]{2,1,0:T(8,128)(2,1)S(1)}, bf16[16,32,128]{2,1,0:T(8,128)(2,1)S(1)}, u32[]{:S(2)}, u32[]{:S(2)}) collective-permute-start(bf16[16,32,128]{2,1,0:T(8,128)(2,1)S(1)} %convert_element_type.50), channel_id=1, source_target_pairs={{0,7},{1,8},{2,9},{3,10},{4,11},{5,12},{6,13},{7,14},{8,15},{9,16}... | collective-permute-start | bytes 393224 | tf_op jit(solution)/shard_map/ppermute | solution.py:115
  34.8 1.9 %collective-permute-start.6 = (bf16[16,32,128]{2,1,0:T(8,128)(2,1)S(1)}, bf16[16,32,128]{2,1,0:T(8,128)(2,1)S(1)}, u32[]{:S(2)}, u32[]{:S(2)}) collective-permute-start(bf16[16,32,128]{2,1,0:T(8,128)(2,1)S(1)} %convert_element_type.50), channel_id=1, source_target_pairs={{0,6},{1,7},{2,8},{3,9},{4,10},{5,11},{6,12},{7,13},{8,14},{9,15},... | collective-permute-start | bytes 393224 | tf_op jit(solution)/shard_map/ppermute | solution.py:115
  36.8 3.1 %collective-permute-start.5 = (bf16[16,32,128]{2,1,0:T(8,128)(2,1)S(1)}, bf16[16,32,128]{2,1,0:T(8,128)(2,1)S(1)}, u32[]{:S(2)}, u32[]{:S(2)}) collective-permute-start(bf16[16,32,128]{2,1,0:T(8,128)(2,1)S(1)} %convert_element_type.50), channel_id=1, source_target_pairs={{0,5},{1,6},{2,7},{3,8},{4,9},{5,10},{6,11},{7,12},{8,13},{9,14},{... | collective-permute-start | bytes 393224 | tf_op jit(solution)/shard_map/ppermute | solution.py:115
  39.9 1.9 %collective-permute-start.4 = (bf16[16,32,128]{2,1,0:T(8,128)(2,1)S(1)}, bf16[16,32,128]{2,1,0:T(8,128)(2,1)S(1)}, u32[]{:S(2)}, u32[]{:S(2)}) collective-permute-start(bf16[16,32,128]{2,1,0:T(8,128)(2,1)S(1)} %convert_element_type.50), channel_id=1, source_target_pairs={{0,4},{1,5},{2,6},{3,7},{4,8},{5,9},{6,10},{7,11},{8,12},{9,13},{1... | collective-permute-start | bytes 393224 | tf_op jit(solution)/shard_map/ppermute | solution.py:115
  41.8 1.9 %collective-permute-start.3 = (bf16[16,32,128]{2,1,0:T(8,128)(2,1)S(1)}, bf16[16,32,128]{2,1,0:T(8,128)(2,1)S(1)}, u32[]{:S(2)}, u32[]{:S(2)}) collective-permute-start(bf16[16,32,128]{2,1,0:T(8,128)(2,1)S(1)} %convert_element_type.50), channel_id=1, source_target_pairs={{0,3},{1,4},{2,5},{3,6},{4,7},{5,8},{6,9},{7,10},{8,11},{9,12},{10... | collective-permute-start | bytes 393224 | tf_op jit(solution)/shard_map/ppermute | solution.py:115
  43.8 2.0 %collective-permute-start.2 = (bf16[16,32,128]{2,1,0:T(8,128)(2,1)S(1)}, bf16[16,32,128]{2,1,0:T(8,128)(2,1)S(1)}, u32[]{:S(2)}, u32[]{:S(2)}) collective-permute-start(bf16[16,32,128]{2,1,0:T(8,128)(2,1)S(1)} %convert_element_type.50), channel_id=1, source_target_pairs={{0,2},{1,3},{2,4},{3,5},{4,6},{5,7},{6,8},{7,9},{8,10},{9,11},{10,... | collective-permute-start | bytes 393224 | tf_op jit(solution)/shard_map/ppermute | solution.py:115
  45.8 3.0 %collective-permute-start.1 = (bf16[16,32,128]{2,1,0:T(8,128)(2,1)S(1)}, bf16[16,32,128]{2,1,0:T(8,128)(2,1)S(1)}, u32[]{:S(2)}, u32[]{:S(2)}) collective-permute-start(bf16[16,32,128]{2,1,0:T(8,128)(2,1)S(1)} %convert_element_type.50), channel_id=1, source_target_pairs={{0,1},{1,2},{2,3},{3,4},{4,5},{5,6},{6,7},{7,8},{8,9},{9,10},{10,1... | collective-permute-start | bytes 393224 | tf_op jit(solution)/shard_map/ppermute | solution.py:115
  49.8 3.1 %collective-permute-done.3 = bf16[16,32,128]{2,1,0:T(8,128)(2,1)S(1)} collective-permute-done((bf16[16,32,128]{2,1,0:T(8,128)(2,1)S(1)}, bf16[16,32,128]{2,1,0:T(8,128)(2,1)S(1)}, u32[]{:S(2)}, u32[]{:S(2)}) %collective-permute-start.3) | collective-permute-done | bytes 131104 | tf_op jit(solution)/shard_map/ppermute | solution.py:115
  53.0 2.1 %collective-permute-done.1 = bf16[16,32,128]{2,1,0:T(8,128)(2,1)S(1)} collective-permute-done((bf16[16,32,128]{2,1,0:T(8,128)(2,1)S(1)}, bf16[16,32,128]{2,1,0:T(8,128)(2,1)S(1)}, u32[]{:S(2)}, u32[]{:S(2)}) %collective-permute-start.1) | collective-permute-done | bytes 131104 | tf_op jit(solution)/shard_map/ppermute | solution.py:115
  56.1 1.3 %collective-permute-start.10 = (bf16[16,32,128]{2,1,0:T(8,128)(2,1)S(1)}, bf16[16,32,128]{2,1,0:T(8,128)(2,1)S(1)}, u32[]{:S(2)}, u32[]{:S(2)}) collective-permute-start(bf16[16,32,128]{2,1,0:T(8,128)(2,1)S(1)} %get-tuple-element.5), channel_id=1, source_target_pairs={{0,16},{1,17},{2,18},{3,19},{4,20},{5,21},{6,22},{7,23},{8,24},{9,... | collective-permute-start | bytes 393224 | tf_op jit(solution)/shard_map/ppermute | solution.py:115
  57.4 2.8 %collective-permute-start.9 = (bf16[16,32,128]{2,1,0:T(8,128)(2,1)S(1)}, bf16[16,32,128]{2,1,0:T(8,128)(2,1)S(1)}, u32[]{:S(2)}, u32[]{:S(2)}) collective-permute-start(bf16[16,32,128]{2,1,0:T(8,128)(2,1)S(1)} %get-tuple-element.5), channel_id=1, source_target_pairs={{0,8},{1,9},{2,10},{3,11},{4,12},{5,13},{6,14},{7,15},{8,16},{9,17... | collective-permute-start | bytes 393224 | tf_op jit(solution)/shard_map/ppermute | solution.py:115
  61.0 6.1 %collective-permute-done.10 = bf16[16,32,128]{2,1,0:T(8,128)(2,1)S(1)} collective-permute-done((bf16[16,32,128]{2,1,0:T(8,128)(2,1)S(1)}, bf16[16,32,128]{2,1,0:T(8,128)(2,1)S(1)}, u32[]{:S(2)}, u32[]{:S(2)}) %collective-permute-start.10) | collective-permute-done | bytes 131104 | tf_op jit(solution)/shard_map/ppermute | solution.py:115
  67.1 3.1 %collective-permute-done.9 = bf16[16,32,128]{2,1,0:T(8,128)(2,1)S(1)} collective-permute-done((bf16[16,32,128]{2,1,0:T(8,128)(2,1)S(1)}, bf16[16,32,128]{2,1,0:T(8,128)(2,1)S(1)}, u32[]{:S(2)}, u32[]{:S(2)}) %collective-permute-start.9) | collective-permute-done | bytes 131104 | tf_op jit(solution)/shard_map/ppermute | solution.py:115
  71.0 12.6 %shard_map.56 = f32[128,32,128]{2,1,0:T(8,128)} custom-call(f32[3,130,32,128]{3,2,1,0:T(8,128)} %reshape.55.x_ref, f32[3,3,32,128]{3,2,1,0:T(8,128)} %reshape.51.f_ref, f32[16,32,128]{2,1,0:T(8,128)} %bitcast.116, f32[16,32,128]{2,1,0:T(8,128)} %bitcast.117, f32[32,128]{1,0:T(8,128)} %bitcast.119, f32[16,32,128]{2,1,0:T(8,128)} %fusion.2.h_ref), custom_call_target="tpu_custom_call" | custom-call | tf_op jit(solution)/shard_map/pallas_call | solution.py:89
  83.6 1.8 %convert_element_type.63 = bf16[128,32,128]{2,1,0:T(8,128)(2,1)S(1)} convert(f32[128,32,128]{2,1,0:T(8,128)} %shard_map.56) | non-fusion elementwise | flops 524288 | bytes 3145728 | tf_op jit(solution)/shard_map/convert_element_type | solution.py:149
  85.4 1.4 %copy.20 = bf16[16,8,32,128]{3,1,2,0:T(8,128)(2,1)} copy(bf16[16,8,32,128]{3,2,1,0:T(8,128)(2,1)S(1)} %bitcast.114) | data formatting | bytes 2097152
  (26 shorter events, 5.4 us)
Async XLA Ops:
  1.0 7.2 %collective-permute-start = (bf16[2,3,4096]{2,0,1:T(2,128)(2,1)S(1)}, bf16[2,3,4096]{2,0,1:T(2,128)(2,1)S(1)}, u32[]{:S(2)}, u32[]{:S(2)}) collective-permute-start(bf16[2,3,4096]{2,0,1:T(2,128)(2,1)S(1)} %slice.3), channel_id=1, source_target_pairs={{0,1},{1,2},{2,3},{3,4},{4,5},{5,6},{6,7},{7,8},{8,9},{9,10},{10,1... | collective-permute-start | bytes 147464 | tf_op jit(solution)/shard_map/ppermute | solution.py:115
  20.8 39.4 %copy-start = (f32[4096,16]{0,1:T(8,128)S(1)}, f32[4096,16]{0,1:T(8,128)}, u32[]{:S(2)}) copy-start(f32[4096,16]{0,1:T(8,128)} %param.9) | copy-start | bytes 786436
  28.9 13.0 %collective-permute-start.8 = (bf16[16,32,128]{2,1,0:T(8,128)(2,1)S(1)}, bf16[16,32,128]{2,1,0:T(8,128)(2,1)S(1)}, u32[]{:S(2)}, u32[]{:S(2)}) collective-permute-start(bf16[16,32,128]{2,1,0:T(8,128)(2,1)S(1)} %convert_element_type.50), channel_id=1, source_target_pairs={{0,8},{1,9},{2,10},{3,11},{4,12},{5,13},{6,14},{7,15},{8,16},{9,17... | collective-permute-start | bytes 393224 | tf_op jit(solution)/shard_map/ppermute | solution.py:115
  32.4 11.4 %collective-permute-start.7 = (bf16[16,32,128]{2,1,0:T(8,128)(2,1)S(1)}, bf16[16,32,128]{2,1,0:T(8,128)(2,1)S(1)}, u32[]{:S(2)}, u32[]{:S(2)}) collective-permute-start(bf16[16,32,128]{2,1,0:T(8,128)(2,1)S(1)} %convert_element_type.50), channel_id=1, source_target_pairs={{0,7},{1,8},{2,9},{3,10},{4,11},{5,12},{6,13},{7,14},{8,15},{9,16}... | collective-permute-start | bytes 393224 | tf_op jit(solution)/shard_map/ppermute | solution.py:115
  34.8 11.0 %collective-permute-start.6 = (bf16[16,32,128]{2,1,0:T(8,128)(2,1)S(1)}, bf16[16,32,128]{2,1,0:T(8,128)(2,1)S(1)}, u32[]{:S(2)}, u32[]{:S(2)}) collective-permute-start(bf16[16,32,128]{2,1,0:T(8,128)(2,1)S(1)} %convert_element_type.50), channel_id=1, source_target_pairs={{0,6},{1,7},{2,8},{3,9},{4,10},{5,11},{6,12},{7,13},{8,14},{9,15},... | collective-permute-start | bytes 393224 | tf_op jit(solution)/shard_map/ppermute | solution.py:115
  36.8 12.5 %collective-permute-start.5 = (bf16[16,32,128]{2,1,0:T(8,128)(2,1)S(1)}, bf16[16,32,128]{2,1,0:T(8,128)(2,1)S(1)}, u32[]{:S(2)}, u32[]{:S(2)}) collective-permute-start(bf16[16,32,128]{2,1,0:T(8,128)(2,1)S(1)} %convert_element_type.50), channel_id=1, source_target_pairs={{0,5},{1,6},{2,7},{3,8},{4,9},{5,10},{6,11},{7,12},{8,13},{9,14},{... | collective-permute-start | bytes 393224 | tf_op jit(solution)/shard_map/ppermute | solution.py:115
  39.9 10.0 %collective-permute-start.4 = (bf16[16,32,128]{2,1,0:T(8,128)(2,1)S(1)}, bf16[16,32,128]{2,1,0:T(8,128)(2,1)S(1)}, u32[]{:S(2)}, u32[]{:S(2)}) collective-permute-start(bf16[16,32,128]{2,1,0:T(8,128)(2,1)S(1)} %convert_element_type.50), channel_id=1, source_target_pairs={{0,4},{1,5},{2,6},{3,7},{4,8},{5,9},{6,10},{7,11},{8,12},{9,13},{1... | collective-permute-start | bytes 393224 | tf_op jit(solution)/shard_map/ppermute | solution.py:115
  41.8 11.2 %collective-permute-start.3 = (bf16[16,32,128]{2,1,0:T(8,128)(2,1)S(1)}, bf16[16,32,128]{2,1,0:T(8,128)(2,1)S(1)}, u32[]{:S(2)}, u32[]{:S(2)}) collective-permute-start(bf16[16,32,128]{2,1,0:T(8,128)(2,1)S(1)} %convert_element_type.50), channel_id=1, source_target_pairs={{0,3},{1,4},{2,5},{3,6},{4,7},{5,8},{6,9},{7,10},{8,11},{9,12},{10... | collective-permute-start | bytes 393224 | tf_op jit(solution)/shard_map/ppermute | solution.py:115
  43.8 9.2 %collective-permute-start.2 = (bf16[16,32,128]{2,1,0:T(8,128)(2,1)S(1)}, bf16[16,32,128]{2,1,0:T(8,128)(2,1)S(1)}, u32[]{:S(2)}, u32[]{:S(2)}) collective-permute-start(bf16[16,32,128]{2,1,0:T(8,128)(2,1)S(1)} %convert_element_type.50), channel_id=1, source_target_pairs={{0,2},{1,3},{2,4},{3,5},{4,6},{5,7},{6,8},{7,9},{8,10},{9,11},{10,... | collective-permute-start | bytes 393224 | tf_op jit(solution)/shard_map/ppermute | solution.py:115
  45.8 9.3 %collective-permute-start.1 = (bf16[16,32,128]{2,1,0:T(8,128)(2,1)S(1)}, bf16[16,32,128]{2,1,0:T(8,128)(2,1)S(1)}, u32[]{:S(2)}, u32[]{:S(2)}) collective-permute-start(bf16[16,32,128]{2,1,0:T(8,128)(2,1)S(1)} %convert_element_type.50), channel_id=1, source_target_pairs={{0,1},{1,2},{2,3},{3,4},{4,5},{5,6},{6,7},{7,8},{8,9},{9,10},{10,1... | collective-permute-start | bytes 393224 | tf_op jit(solution)/shard_map/ppermute | solution.py:115
  55.4 5.6 %collective-permute-start.11 = (bf16[16,32,128]{2,1,0:T(8,128)(2,1)S(1)}, bf16[16,32,128]{2,1,0:T(8,128)(2,1)S(1)}, u32[]{:S(2)}, u32[]{:S(2)}) collective-permute-start(bf16[16,32,128]{2,1,0:T(8,128)(2,1)S(1)} %get-tuple-element.5), channel_id=1, source_target_pairs={{0,24},{1,25},{2,26},{3,27},{4,28},{5,29},{6,30},{7,31}} | collective-permute-start | bytes 393224 | tf_op jit(solution)/shard_map/ppermute | solution.py:115
  56.1 11.0 %collective-permute-start.10 = (bf16[16,32,128]{2,1,0:T(8,128)(2,1)S(1)}, bf16[16,32,128]{2,1,0:T(8,128)(2,1)S(1)}, u32[]{:S(2)}, u32[]{:S(2)}) collective-permute-start(bf16[16,32,128]{2,1,0:T(8,128)(2,1)S(1)} %get-tuple-element.5), channel_id=1, source_target_pairs={{0,16},{1,17},{2,18},{3,19},{4,20},{5,21},{6,22},{7,23},{8,24},{9,... | collective-permute-start | bytes 393224 | tf_op jit(solution)/shard_map/ppermute | solution.py:115
  57.4 12.8 %collective-permute-start.9 = (bf16[16,32,128]{2,1,0:T(8,128)(2,1)S(1)}, bf16[16,32,128]{2,1,0:T(8,128)(2,1)S(1)}, u32[]{:S(2)}, u32[]{:S(2)}) collective-permute-start(bf16[16,32,128]{2,1,0:T(8,128)(2,1)S(1)} %get-tuple-element.5), channel_id=1, source_target_pairs={{0,8},{1,9},{2,10},{3,11},{4,12},{5,13},{6,14},{7,15},{8,16},{9,17... | collective-permute-start | bytes 393224 | tf_op jit(solution)/shard_map/ppermute | solution.py:115

commit v4 on v3

v4 whole, which is shorter than its diff:
```python
import jax
import jax.numpy as jnp
from jax import lax
from jax.experimental import pallas as pl
from jax.experimental.pallas import tpu as pltpu
from jax.sharding import PartitionSpec as P

LANES = 128
SUB = 8
BLOCK = 512
FIRST_WINDOW = 8


def lane_slice(c):
    return pl.ds(pl.multiple_of(c * LANES, LANES), LANES)


def row(ref, index, lanes):
    return jnp.broadcast_to(ref[pl.ds(index, 1), lanes], (SUB, LANES))


def first_prev(xs, halo_ref, c, lanes, seg, taps, sub):
    prev = []
    for back in range(1, taps):
        per_stream = []
        for s in range(xs.shape[0]):
            rows = xs[s, c, pl.ds(seg - back, SUB, stride=seg), :]
            edge = jnp.broadcast_to(halo_ref[s, pl.ds(taps - 1 - back, 1), lanes], (SUB, LANES))
            per_stream.append(jnp.where(sub == 0, edge, pltpu.roll(rows, 1, 0)))
        prev.append(per_stream)
    return prev


def step_features(xs, f_ref, c, lanes, seg, j, prev):
    taps = f_ref.shape[0]
    now = [xs[s, c, pl.ds(j, SUB, stride=seg), :] for s in range(xs.shape[0])]
    feats = []
    for s in range(xs.shape[0]):
        acc = jnp.broadcast_to(f_ref[0, pl.ds(s, 1), lanes], (SUB, LANES)) * now[s]
        for tap in range(1, taps):
            weight = jnp.broadcast_to(f_ref[tap, pl.ds(s, 1), lanes], (SUB, LANES))
            acc = acc + weight * prev[tap - 1][s]
        feats.append(acc)
    new_prev = [now] + prev[:-1]
    return feats, new_prev


def gate(feats):
    return (feats[1] * feats[2]).astype(jnp.bfloat16).astype(jnp.float32)


def state_kernel(x_ref, halo_ref, f_ref, a_ref, seg_ref, h_ref, xs, dsc):
    streams_count, rows, block = x_ref.shape
    taps = f_ref.shape[0]
    modes = a_ref.shape[0]
    seg = rows // SUB
    for c in range(block // LANES):
        xs[:, c] = x_ref[:, :, c * LANES : (c + 1) * LANES].astype(jnp.float32)
    sub = lax.broadcasted_iota(jnp.int32, (SUB, LANES), 0)

    def lane_group(c, carry):
        lanes = lane_slice(c)
        for m in range(modes):
            dsc[m] = jnp.exp(-row(a_ref, m, lanes))

        def step(j, state):
            prev, states = state
            feats, prev = step_features(xs, f_ref, c, lanes, seg, j, prev)
            u = gate(feats)
            return prev, tuple(dsc[m] * states[m] + u for m in range(modes))

        zero = jnp.zeros((SUB, LANES), jnp.float32)
        init = (first_prev(xs, halo_ref, c, lanes, seg, taps, sub), (zero,) * modes)
        _, states = lax.fori_loop(0, seg, step, init, unroll=2)
        later = (SUB - 1 - sub).astype(jnp.float32) * float(seg)
        for m in range(modes):
            seg_ref[m, :, lanes] = states[m]
            weight = jnp.exp(-row(a_ref, m, lanes) * later)
            h_ref[pl.ds(m, 1), lanes] = jnp.sum(weight * states[m], axis=0, keepdims=True)
        return carry

    lax.fori_loop(0, block // LANES, lane_group, 0)


def out_kernel(x_ref, halo_ref, f_ref, a_ref, r_ref, skip_ref, seg_ref, hin_ref, o_ref, xs, ys, dsc, rsc):
    streams_count, rows, block = x_ref.shape
    taps = f_ref.shape[0]
    modes = a_ref.shape[0]
    seg = rows // SUB
    for c in range(block // LANES):
        xs[:, c] = x_ref[:, :, c * LANES : (c + 1) * LANES].astype(jnp.float32)
    sub = lax.broadcasted_iota(jnp.int32, (SUB, LANES), 0)

    def lane_group(c, carry):
        lanes = lane_slice(c)
        starts = []
        for m in range(modes):
            rate = row(a_ref, m, lanes)
            dsc[m] = jnp.exp(-rate)
            rsc[m] = row(r_ref, m, lanes)
            ends = seg_ref[m, :, lanes]
            carried = jnp.where(sub >= 1, pltpu.roll(ends, 1, 0), 0.0)
            offset = 1
            while offset < SUB:
                factor = jnp.exp(-rate * float(seg * offset))
                carried = carried + jnp.where(sub >= offset, factor * pltpu.roll(carried, offset, 0), 0.0)
                offset *= 2
            lead = jnp.exp(-rate * (sub.astype(jnp.float32) * float(seg)))
            starts.append(carried + lead * row(hin_ref, m, lanes))
        skip_rows = row(skip_ref, 0, lanes)

        def step(j, state):
            prev, states = state
            feats, prev = step_features(xs, f_ref, c, lanes, seg, j, prev)
            u = gate(feats)
            new = []
            conv = None
            for m in range(modes):
                sm = dsc[m] * states[m] + u
                term = rsc[m] * sm
                conv = term if conv is None else conv + term
                new.append(sm)
            y = (conv + skip_rows * u).astype(jnp.bfloat16).astype(jnp.float32)
            ys[c, pl.ds(j, SUB, stride=seg), :] = feats[0] * y
            return prev, tuple(new)

        init = (first_prev(xs, halo_ref, c, lanes, seg, taps, sub), tuple(starts))
        lax.fori_loop(0, seg, step, init, unroll=2)
        return carry

    lax.fori_loop(0, block // LANES, lane_group, 0)
    for c in range(block // LANES):
        o_ref[:, c * LANES : (c + 1) * LANES] = ys[c].astype(o_ref.dtype)


def run_state(x, halo, f, rate_t):
    streams_count, rows, width = x.shape
    taps = f.shape[0]
    modes = rate_t.shape[0]
    return pl.pallas_call(
        state_kernel,
        grid=(width // BLOCK,),
        in_specs=[
            pl.BlockSpec((streams_count, rows, BLOCK), lambda i: (0, 0, i)),
            pl.BlockSpec((streams_count, taps - 1, BLOCK), lambda i: (0, 0, i)),
            pl.BlockSpec((taps, streams_count, BLOCK), lambda i: (0, 0, i)),
            pl.BlockSpec((modes, BLOCK), lambda i: (0, i)),
        ],
        out_specs=[
            pl.BlockSpec((modes, SUB, BLOCK), lambda i: (0, 0, i)),
            pl.BlockSpec((modes, BLOCK), lambda i: (0, i)),
        ],
        out_shape=[
            jax.ShapeDtypeStruct((modes, SUB, width), jnp.float32),
            jax.ShapeDtypeStruct((modes, width), jnp.float32),
        ],
        scratch_shapes=[
            pltpu.VMEM((streams_count, BLOCK // LANES, rows, LANES), jnp.float32),
            pltpu.VMEM((modes, SUB, LANES), jnp.float32),
        ],
    )(x, halo, f, rate_t)


def run_out(x, halo, f, rate_t, residue_t, skip, ends, hin):
    streams_count, rows, width = x.shape
    taps = f.shape[0]
    modes = rate_t.shape[0]
    return pl.pallas_call(
        out_kernel,
        grid=(width // BLOCK,),
        in_specs=[
            pl.BlockSpec((streams_count, rows, BLOCK), lambda i: (0, 0, i)),
            pl.BlockSpec((streams_count, taps - 1, BLOCK), lambda i: (0, 0, i)),
            pl.BlockSpec((taps, streams_count, BLOCK), lambda i: (0, 0, i)),
            pl.BlockSpec((modes, BLOCK), lambda i: (0, i)),
            pl.BlockSpec((modes, BLOCK), lambda i: (0, i)),
            pl.BlockSpec((1, BLOCK), lambda i: (0, i)),
            pl.BlockSpec((modes, SUB, BLOCK), lambda i: (0, 0, i)),
            pl.BlockSpec((modes, BLOCK), lambda i: (0, i)),
        ],
        out_specs=pl.BlockSpec((rows, BLOCK), lambda i: (0, i)),
        out_shape=jax.ShapeDtypeStruct((rows, width), jnp.bfloat16),
        scratch_shapes=[
            pltpu.VMEM((streams_count, BLOCK // LANES, rows, LANES), jnp.float32),
            pltpu.VMEM((BLOCK // LANES, rows, LANES), jnp.float32),
            pltpu.VMEM((modes, SUB, LANES), jnp.float32),
            pltpu.VMEM((modes, SUB, LANES), jnp.float32),
        ],
    )(x, halo, f, rate_t, residue_t, skip, ends, hin)


def body(streams, short_filter, skip, rates, residues):
    axes = ("ctx", "tp")
    devices = lax.axis_size("ctx") * lax.axis_size("tp")
    tok_rows, streams_count, width = streams.shape
    taps = short_filter.shape[0]
    modes = rates.shape[1]

    def shift(value, offset):
        pairs = [(j, j + offset) for j in range(devices - offset)]
        return lax.ppermute(value, axes, pairs)

    halo = shift(streams[tok_rows - (taps - 1) :], 1)
    halo = jnp.transpose(halo, (1, 0, 2)).astype(jnp.float32)
    x = jnp.transpose(streams, (1, 0, 2))
    rate_t = rates.T
    residue_t = residues.T
    ends, local = run_state(x, halo, short_filter, rate_t)

    def decay_pow(steps):
        return jnp.exp(-rate_t * float(tok_rows * steps))

    def gather_window(value, spacing, count):
        sent = value.astype(jnp.bfloat16)
        total = None
        for k in range(1, count + 1):
            if k * spacing >= devices:
                break
            term = decay_pow((k - 1) * spacing) * shift(sent, k * spacing).astype(jnp.float32)
            total = term if total is None else total + term
        return total

    first = min(FIRST_WINDOW, devices - 1)
    carried = gather_window(local, 1, first)
    window = first
    while window < devices - 1:
        count = min(-(-(devices - 1) // window) - 1, FIRST_WINDOW)
        carried = carried + decay_pow(window) * gather_window(carried, window, count)
        window *= count + 1

    return run_out(x, halo, short_filter, rate_t, residue_t, skip.reshape(1, width), ends, carried)


def solution(mesh):
    return jax.shard_map(
        body,
        mesh=mesh,
        in_specs=(P(("ctx", "tp"), None, None), P(), P(), P(), P()),
        out_specs=P(("ctx", "tp"), None),
        check_vma=False,
    )
```

time: 87.5 us -> 81 us (0.926)
  local copies, waits for them, and re-layouts: 13 us -> 1.03 us
  Pallas kernels: 19.7 us -> 28.8 us
  other arithmetic: 10.9 us -> 2.94 us
  waiting for transfers between devices: 14.9 us -> 19.9 us
    pallas_call x2, Pallas kernels: 19.7 us -> 28.8 us  [the longest x1 17.9 us: run_out(): pl.pallas_call(out_kernel, grid=(width // BLOCK,), in_specs=[pl.BlockSpec...]
    reshape x2 -> x0, local copies, waits for them, and re-layouts: 8.61 us -> none  [the longest x1 6.91 us: body(): x = x.reshape(streams_count, tok_rows + taps - 1, groups, LANES)]
    reshape x1 -> x0, other arithmetic: 5.63 us -> none  [body(): x = x.reshape(streams_count, tok_rows + taps - 1, groups, LANES)]
    ppermute x12, waiting for transfers between devices: 14.9 us -> 19.9 us  [shift(): return lax.ppermute(value, axes, pairs)]
    unnamed x15 -> x2, local copies, waits for them, and re-layouts: 3.46 us -> 0.01 us
    unnamed x1 -> x0, other arithmetic: 1.34 us -> none
    convert_element_type x1, other arithmetic: 1.81 us -> 0.67 us  [body(): halo = jnp.transpose(halo, (1, 0, 2)).astype(jnp.float32)]
  transfers between devices with their start and end apart: 12 -> 12, of which waited for: 5 -> 6; matrix products, arithmetic and copies ran while one was open for 6% -> 0% of each run, Pallas kernels for 0% -> 0%
where the time goes in v4:
time: 81 us; the launch traced here: 80.2 us
  Pallas kernels  28.8 us (36%)
  starting transfers between devices  27.4 us (34%)
  waiting for transfers between devices  19.9 us (25%)
  other arithmetic  2.94 us (4%)
  local copies, waits for them, and re-layouts  1.03 us (1%)
    ppermute x12, starting transfers between devices, shift(): return lax.ppermute(value, axes, pairs)  27.4 us
    ppermute x12, waiting for transfers between devices, shift(): return lax.ppermute(value, axes, pairs)  19.9 us
    pallas_call x1, Pallas kernels, run_out(): pl.pallas_call(out_kernel, grid=(width // BLOCK,), in_specs=[pl.BlockSpec...  17.9 us
    pallas_call x1, Pallas kernels, run_state(): pl.pallas_call(state_kernel, grid=(width // BLOCK,), in_specs=[pl.BlockSp...  10.9 us
  transfers between devices with their start and end apart: 12, of which 6 were waited for; matrix products, arithmetic and copies ran while one was open for 0% of the time, Pallas kernels for 0%

profile of v4, /device:TPU:16, one launch (start us, length us, event | category | flops | bytes accessed | tf_op | source)
XLA Modules:
  0.0 80.2 jit_solution(5749492888352480125)
XLA Ops:
  0.0 1.0 %slice.3 = bf16[2,3,4096]{2,0,1:T(2,128)(2,1)S(1)} slice(bf16[128,3,4096]{2,0,1:T(8,128)(2,1)} %param.5), slice={[126:128], [0:3], [0:4096]} | slice | bytes 98304 | tf_op jit(solution)/shard_map/slice | solution.py:203
  1.0 3.4 %collective-permute-start = (bf16[2,3,4096]{2,0,1:T(2,128)(2,1)S(1)}, bf16[2,3,4096]{2,0,1:T(2,128)(2,1)S(1)}, u32[]{:S(2)}, u32[]{:S(2)}) collective-permute-start(bf16[2,3,4096]{2,0,1:T(2,128)(2,1)S(1)} %slice.3), channel_id=1, source_target_pairs={{0,1},{1,2},{2,3},{3,4},{4,5},{5,6},{6,7},{7,8},{8,9},{9,10},{10,1... | collective-permute-start | bytes 147464 | tf_op jit(solution)/shard_map/ppermute | solution.py:201
  4.5 3.8 %collective-permute-done = bf16[2,3,4096]{2,0,1:T(2,128)(2,1)S(1)} collective-permute-done((bf16[2,3,4096]{2,0,1:T(2,128)(2,1)S(1)}, bf16[2,3,4096]{2,0,1:T(2,128)(2,1)S(1)}, u32[]{:S(2)}, u32[]{:S(2)}) %collective-permute-start) | collective-permute-done | bytes 49184 | tf_op jit(solution)/shard_map/ppermute | solution.py:201
  8.2 0.7 convert_bitcast_fusion.halo_ref
  8.9 10.9 %shard_map.55 = (f32[16,8,4096]{2,1,0:T(8,128)}, f32[16,4096]{1,0:T(8,128)}) custom-call(bf16[3,128,4096]{2,1,0:T(8,128)(2,1)} %bitcast.9, f32[3,2,4096]{2,1,0:T(2,128)} %convert_bitcast_fusion.halo_ref, f32[3,3,4096]{2,1,0:T(4,128)} %f_ref.3, f32[16,4096]{1,0:T(8,128)} %bitcast.11), custom_call_target="tpu_custom_call" | custom-call | tf_op jit(solution)/shard_map/pallas_call | solution.py:140
  19.8 1.0 %convert_element_type.46 = bf16[16,4096]{1,0:T(8,128)(2,1)S(1)} convert(f32[16,4096]{1,0:T(8,128)} %get-tuple-element.8) | non-fusion elementwise | flops 65536 | bytes 393216 | tf_op jit(solution)/shard_map/convert_element_type | solution.py:214
  20.7 3.5 %collective-permute-start.8 = (bf16[16,4096]{1,0:T(8,128)(2,1)S(1)}, bf16[16,4096]{1,0:T(8,128)(2,1)S(1)}, u32[]{:S(2)}, u32[]{:S(2)}) collective-permute-start(bf16[16,4096]{1,0:T(8,128)(2,1)S(1)} %convert_element_type.46), channel_id=1, source_target_pairs={{0,8},{1,9},{2,10},{3,11},{4,12},{5,13},{6,14},{7,15},{8,16},{9,17... | collective-permute-start | bytes 393224 | tf_op jit(solution)/shard_map/ppermute | solution.py:201
  24.2 1.9 %collective-permute-start.7 = (bf16[16,4096]{1,0:T(8,128)(2,1)S(1)}, bf16[16,4096]{1,0:T(8,128)(2,1)S(1)}, u32[]{:S(2)}, u32[]{:S(2)}) collective-permute-start(bf16[16,4096]{1,0:T(8,128)(2,1)S(1)} %convert_element_type.46), channel_id=1, source_target_pairs={{0,7},{1,8},{2,9},{3,10},{4,11},{5,12},{6,13},{7,14},{8,15},{9,16}... | collective-permute-start | bytes 393224 | tf_op jit(solution)/shard_map/ppermute | solution.py:201
  26.2 2.2 %collective-permute-start.6 = (bf16[16,4096]{1,0:T(8,128)(2,1)S(1)}, bf16[16,4096]{1,0:T(8,128)(2,1)S(1)}, u32[]{:S(2)}, u32[]{:S(2)}) collective-permute-start(bf16[16,4096]{1,0:T(8,128)(2,1)S(1)} %convert_element_type.46), channel_id=1, source_target_pairs={{0,6},{1,7},{2,8},{3,9},{4,10},{5,11},{6,12},{7,13},{8,14},{9,15},... | collective-permute-start | bytes 393224 | tf_op jit(solution)/shard_map/ppermute | solution.py:201
  28.4 2.8 %collective-permute-start.5 = (bf16[16,4096]{1,0:T(8,128)(2,1)S(1)}, bf16[16,4096]{1,0:T(8,128)(2,1)S(1)}, u32[]{:S(2)}, u32[]{:S(2)}) collective-permute-start(bf16[16,4096]{1,0:T(8,128)(2,1)S(1)} %convert_element_type.46), channel_id=1, source_target_pairs={{0,5},{1,6},{2,7},{3,8},{4,9},{5,10},{6,11},{7,12},{8,13},{9,14},{... | collective-permute-start | bytes 393224 | tf_op jit(solution)/shard_map/ppermute | solution.py:201
  31.2 1.9 %collective-permute-start.4 = (bf16[16,4096]{1,0:T(8,128)(2,1)S(1)}, bf16[16,4096]{1,0:T(8,128)(2,1)S(1)}, u32[]{:S(2)}, u32[]{:S(2)}) collective-permute-start(bf16[16,4096]{1,0:T(8,128)(2,1)S(1)} %convert_element_type.46), channel_id=1, source_target_pairs={{0,4},{1,5},{2,6},{3,7},{4,8},{5,9},{6,10},{7,11},{8,12},{9,13},{1... | collective-permute-start | bytes 393224 | tf_op jit(solution)/shard_map/ppermute | solution.py:201
  33.2 1.9 %collective-permute-start.3 = (bf16[16,4096]{1,0:T(8,128)(2,1)S(1)}, bf16[16,4096]{1,0:T(8,128)(2,1)S(1)}, u32[]{:S(2)}, u32[]{:S(2)}) collective-permute-start(bf16[16,4096]{1,0:T(8,128)(2,1)S(1)} %convert_element_type.46), channel_id=1, source_target_pairs={{0,3},{1,4},{2,5},{3,6},{4,7},{5,8},{6,9},{7,10},{8,11},{9,12},{10... | collective-permute-start | bytes 393224 | tf_op jit(solution)/shard_map/ppermute | solution.py:201
  35.1 2.0 %collective-permute-start.2 = (bf16[16,4096]{1,0:T(8,128)(2,1)S(1)}, bf16[16,4096]{1,0:T(8,128)(2,1)S(1)}, u32[]{:S(2)}, u32[]{:S(2)}) collective-permute-start(bf16[16,4096]{1,0:T(8,128)(2,1)S(1)} %convert_element_type.46), channel_id=1, source_target_pairs={{0,2},{1,3},{2,4},{3,5},{4,6},{5,7},{6,8},{7,9},{8,10},{9,11},{10,... | collective-permute-start | bytes 393224 | tf_op jit(solution)/shard_map/ppermute | solution.py:201
  37.1 2.9 %collective-permute-start.1 = (bf16[16,4096]{1,0:T(8,128)(2,1)S(1)}, bf16[16,4096]{1,0:T(8,128)(2,1)S(1)}, u32[]{:S(2)}, u32[]{:S(2)}) collective-permute-start(bf16[16,4096]{1,0:T(8,128)(2,1)S(1)} %convert_element_type.46), channel_id=1, source_target_pairs={{0,1},{1,2},{2,3},{3,4},{4,5},{5,6},{6,7},{7,8},{8,9},{9,10},{10,1... | collective-permute-start | bytes 393224 | tf_op jit(solution)/shard_map/ppermute | solution.py:201
  40.4 3.4 %collective-permute-done.3 = bf16[16,4096]{1,0:T(8,128)(2,1)S(1)} collective-permute-done((bf16[16,4096]{1,0:T(8,128)(2,1)S(1)}, bf16[16,4096]{1,0:T(8,128)(2,1)S(1)}, u32[]{:S(2)}, u32[]{:S(2)}) %collective-permute-start.3) | collective-permute-done | bytes 131104 | tf_op jit(solution)/shard_map/ppermute | solution.py:201
  43.8 2.3 %collective-permute-done.1 = bf16[16,4096]{1,0:T(8,128)(2,1)S(1)} collective-permute-done((bf16[16,4096]{1,0:T(8,128)(2,1)S(1)}, bf16[16,4096]{1,0:T(8,128)(2,1)S(1)}, u32[]{:S(2)}, u32[]{:S(2)}) %collective-permute-start.1) | collective-permute-done | bytes 131104 | tf_op jit(solution)/shard_map/ppermute | solution.py:201
  46.1 0.4 fusion
  46.5 0.7 collective-permute-start.11
  47.2 1.3 %collective-permute-start.10 = (bf16[16,4096]{1,0:T(8,128)(2,1)S(1)}, bf16[16,4096]{1,0:T(8,128)(2,1)S(1)}, u32[]{:S(2)}, u32[]{:S(2)}) collective-permute-start(bf16[16,4096]{1,0:T(8,128)(2,1)S(1)} %get-tuple-element.9), channel_id=1, source_target_pairs={{0,16},{1,17},{2,18},{3,19},{4,20},{5,21},{6,22},{7,23},{8,24},{9,... | collective-permute-start | bytes 393224 | tf_op jit(solution)/shard_map/ppermute | solution.py:201
  48.5 2.8 %collective-permute-start.9 = (bf16[16,4096]{1,0:T(8,128)(2,1)S(1)}, bf16[16,4096]{1,0:T(8,128)(2,1)S(1)}, u32[]{:S(2)}, u32[]{:S(2)}) collective-permute-start(bf16[16,4096]{1,0:T(8,128)(2,1)S(1)} %get-tuple-element.9), channel_id=1, source_target_pairs={{0,8},{1,9},{2,10},{3,11},{4,12},{5,13},{6,14},{7,15},{8,16},{9,17... | collective-permute-start | bytes 393224 | tf_op jit(solution)/shard_map/ppermute | solution.py:201
  51.3 7.0 %collective-permute-done.10 = bf16[16,4096]{1,0:T(8,128)(2,1)S(1)} collective-permute-done((bf16[16,4096]{1,0:T(8,128)(2,1)S(1)}, bf16[16,4096]{1,0:T(8,128)(2,1)S(1)}, u32[]{:S(2)}, u32[]{:S(2)}) %collective-permute-start.10) | collective-permute-done | bytes 131104 | tf_op jit(solution)/shard_map/ppermute | solution.py:201
  58.2 3.2 %collective-permute-done.9 = bf16[16,4096]{1,0:T(8,128)(2,1)S(1)} collective-permute-done((bf16[16,4096]{1,0:T(8,128)(2,1)S(1)}, bf16[16,4096]{1,0:T(8,128)(2,1)S(1)}, u32[]{:S(2)}, u32[]{:S(2)}) %collective-permute-start.9) | collective-permute-done | bytes 131104 | tf_op jit(solution)/shard_map/ppermute | solution.py:201
  61.4 0.9 %multiply_add_fusion.hin_ref = f32[16,4096]{1,0:T(8,128)} fusion(f32[16,4096]{1,0:T(8,128)S(1)} %get-tuple-element.10, bf16[16,4096]{1,0:T(8,128)(2,1)S(1)} %collective-permute-done.11, bf16[16,4096]{1,0:T(8,128)(2,1)S(1)} %collective-permute-done.10, bf16[16,4096]{1,0:T(8,128)(2,1)S(1)} %collective-permute-done.9, f32[4096,16]{0,1:T(8,128)S(1)} %copy-done), kind=kLoop, calls=%fused_computation | loop fusion | flops 917504 | bytes 1179648 | tf_op jit(solution)/shard_map/add | solution.py:228
  62.3 17.9 %shard_map.56 = bf16[128,4096]{1,0:T(8,128)(2,1)} custom-call(bf16[3,128,4096]{2,1,0:T(8,128)(2,1)} %bitcast.10, f32[3,2,4096]{2,1,0:T(2,128)} %convert_bitcast_fusion.halo_ref, f32[3,3,4096]{2,1,0:T(4,128)} %f_ref.3, f32[16,4096]{1,0:T(8,128)} %bitcast.12, f32[16,4096]{1,0:T(8,128)} %bitcast.13, f32[1,4096]{1,0:T(1,128)} %bitcast.14, ...), custom_call_target="tpu_custom_call" | custom-call | tf_op jit(solution)/shard_map/pallas_call | solution.py:168
  (9 shorter events, 0.4 us)
Async XLA Ops:
  0.0 46.1 %copy-start = (f32[4096,16]{0,1:T(8,128)S(1)}, f32[4096,16]{0,1:T(8,128)}, u32[]{:S(2)}) copy-start(f32[4096,16]{0,1:T(8,128)} %param.8) | copy-start | bytes 786436
  1.0 7.2 %collective-permute-start = (bf16[2,3,4096]{2,0,1:T(2,128)(2,1)S(1)}, bf16[2,3,4096]{2,0,1:T(2,128)(2,1)S(1)}, u32[]{:S(2)}, u32[]{:S(2)}) collective-permute-start(bf16[2,3,4096]{2,0,1:T(2,128)(2,1)S(1)} %slice.3), channel_id=1, source_target_pairs={{0,1},{1,2},{2,3},{3,4},{4,5},{5,6},{6,7},{7,8},{8,9},{9,10},{10,1... | collective-permute-start | bytes 147464 | tf_op jit(solution)/shard_map/ppermute | solution.py:201
  20.7 12.4 %collective-permute-start.8 = (bf16[16,4096]{1,0:T(8,128)(2,1)S(1)}, bf16[16,4096]{1,0:T(8,128)(2,1)S(1)}, u32[]{:S(2)}, u32[]{:S(2)}) collective-permute-start(bf16[16,4096]{1,0:T(8,128)(2,1)S(1)} %convert_element_type.46), channel_id=1, source_target_pairs={{0,8},{1,9},{2,10},{3,11},{4,12},{5,13},{6,14},{7,15},{8,16},{9,17... | collective-permute-start | bytes 393224 | tf_op jit(solution)/shard_map/ppermute | solution.py:201
  24.2 10.9 %collective-permute-start.7 = (bf16[16,4096]{1,0:T(8,128)(2,1)S(1)}, bf16[16,4096]{1,0:T(8,128)(2,1)S(1)}, u32[]{:S(2)}, u32[]{:S(2)}) collective-permute-start(bf16[16,4096]{1,0:T(8,128)(2,1)S(1)} %convert_element_type.46), channel_id=1, source_target_pairs={{0,7},{1,8},{2,9},{3,10},{4,11},{5,12},{6,13},{7,14},{8,15},{9,16}... | collective-permute-start | bytes 393224 | tf_op jit(solution)/shard_map/ppermute | solution.py:201
  26.2 11.0 %collective-permute-start.6 = (bf16[16,4096]{1,0:T(8,128)(2,1)S(1)}, bf16[16,4096]{1,0:T(8,128)(2,1)S(1)}, u32[]{:S(2)}, u32[]{:S(2)}) collective-permute-start(bf16[16,4096]{1,0:T(8,128)(2,1)S(1)} %convert_element_type.46), channel_id=1, source_target_pairs={{0,6},{1,7},{2,8},{3,9},{4,10},{5,11},{6,12},{7,13},{8,14},{9,15},... | collective-permute-start | bytes 393224 | tf_op jit(solution)/shard_map/ppermute | solution.py:201
  28.4 11.6 %collective-permute-start.5 = (bf16[16,4096]{1,0:T(8,128)(2,1)S(1)}, bf16[16,4096]{1,0:T(8,128)(2,1)S(1)}, u32[]{:S(2)}, u32[]{:S(2)}) collective-permute-start(bf16[16,4096]{1,0:T(8,128)(2,1)S(1)} %convert_element_type.46), channel_id=1, source_target_pairs={{0,5},{1,6},{2,7},{3,8},{4,9},{5,10},{6,11},{7,12},{8,13},{9,14},{... | collective-permute-start | bytes 393224 | tf_op jit(solution)/shard_map/ppermute | solution.py:201
  31.2 9.2 %collective-permute-start.4 = (bf16[16,4096]{1,0:T(8,128)(2,1)S(1)}, bf16[16,4096]{1,0:T(8,128)(2,1)S(1)}, u32[]{:S(2)}, u32[]{:S(2)}) collective-permute-start(bf16[16,4096]{1,0:T(8,128)(2,1)S(1)} %convert_element_type.46), channel_id=1, source_target_pairs={{0,4},{1,5},{2,6},{3,7},{4,8},{5,9},{6,10},{7,11},{8,12},{9,13},{1... | collective-permute-start | bytes 393224 | tf_op jit(solution)/shard_map/ppermute | solution.py:201
  33.2 10.6 %collective-permute-start.3 = (bf16[16,4096]{1,0:T(8,128)(2,1)S(1)}, bf16[16,4096]{1,0:T(8,128)(2,1)S(1)}, u32[]{:S(2)}, u32[]{:S(2)}) collective-permute-start(bf16[16,4096]{1,0:T(8,128)(2,1)S(1)} %convert_element_type.46), channel_id=1, source_target_pairs={{0,3},{1,4},{2,5},{3,6},{4,7},{5,8},{6,9},{7,10},{8,11},{9,12},{10... | collective-permute-start | bytes 393224 | tf_op jit(solution)/shard_map/ppermute | solution.py:201
  35.1 8.7 %collective-permute-start.2 = (bf16[16,4096]{1,0:T(8,128)(2,1)S(1)}, bf16[16,4096]{1,0:T(8,128)(2,1)S(1)}, u32[]{:S(2)}, u32[]{:S(2)}) collective-permute-start(bf16[16,4096]{1,0:T(8,128)(2,1)S(1)} %convert_element_type.46), channel_id=1, source_target_pairs={{0,2},{1,3},{2,4},{3,5},{4,6},{5,7},{6,8},{7,9},{8,10},{9,11},{10,... | collective-permute-start | bytes 393224 | tf_op jit(solution)/shard_map/ppermute | solution.py:201
  37.1 8.9 %collective-permute-start.1 = (bf16[16,4096]{1,0:T(8,128)(2,1)S(1)}, bf16[16,4096]{1,0:T(8,128)(2,1)S(1)}, u32[]{:S(2)}, u32[]{:S(2)}) collective-permute-start(bf16[16,4096]{1,0:T(8,128)(2,1)S(1)} %convert_element_type.46), channel_id=1, source_target_pairs={{0,1},{1,2},{2,3},{3,4},{4,5},{5,6},{6,7},{7,8},{8,9},{9,10},{10,1... | collective-permute-start | bytes 393224 | tf_op jit(solution)/shard_map/ppermute | solution.py:201
  46.5 4.8 %collective-permute-start.11 = (bf16[16,4096]{1,0:T(8,128)(2,1)S(1)}, bf16[16,4096]{1,0:T(8,128)(2,1)S(1)}, u32[]{:S(2)}, u32[]{:S(2)}) collective-permute-start(bf16[16,4096]{1,0:T(8,128)(2,1)S(1)} %get-tuple-element.9), channel_id=1, source_target_pairs={{0,24},{1,25},{2,26},{3,27},{4,28},{5,29},{6,30},{7,31}} | collective-permute-start | bytes 393224 | tf_op jit(solution)/shard_map/ppermute | solution.py:201
  47.2 11.1 %collective-permute-start.10 = (bf16[16,4096]{1,0:T(8,128)(2,1)S(1)}, bf16[16,4096]{1,0:T(8,128)(2,1)S(1)}, u32[]{:S(2)}, u32[]{:S(2)}) collective-permute-start(bf16[16,4096]{1,0:T(8,128)(2,1)S(1)} %get-tuple-element.9), channel_id=1, source_target_pairs={{0,16},{1,17},{2,18},{3,19},{4,20},{5,21},{6,22},{7,23},{8,24},{9,... | collective-permute-start | bytes 393224 | tf_op jit(solution)/shard_map/ppermute | solution.py:201
  48.5 12.9 %collective-permute-start.9 = (bf16[16,4096]{1,0:T(8,128)(2,1)S(1)}, bf16[16,4096]{1,0:T(8,128)(2,1)S(1)}, u32[]{:S(2)}, u32[]{:S(2)}) collective-permute-start(bf16[16,4096]{1,0:T(8,128)(2,1)S(1)} %get-tuple-element.9), channel_id=1, source_target_pairs={{0,8},{1,9},{2,10},{3,11},{4,12},{5,13},{6,14},{7,15},{8,16},{9,17... | collective-permute-start | bytes 393224 | tf_op jit(solution)/shard_map/ppermute | solution.py:201

commit v5 on v4

--- a/solution.py
+++ b/solution.py
@@ -8,7 +8,8 @@
 LANES = 128
 SUB = 8
 BLOCK = 512
-FIRST_WINDOW = 8
+FIRST_WINDOW = 3
+UNROLL = 4
 
 
 def lane_slice(c):
@@ -31,15 +32,22 @@
     return prev
 
 
-def step_features(xs, f_ref, c, lanes, seg, j, prev):
-    taps = f_ref.shape[0]
-    now = [xs[s, c, pl.ds(j, SUB, stride=seg), :] for s in range(xs.shape[0])]
+def fill_filters(f_ref, fsc, lanes):
+    streams_count = f_ref.shape[1]
+    for tap in range(f_ref.shape[0]):
+        for s in range(streams_count):
+            fsc[tap * streams_count + s] = row(f_ref.at[tap], s, lanes)
+
+
+def step_features(xs, fsc, c, seg, j, prev):
+    streams_count = xs.shape[0]
+    taps = len(prev) + 1
+    now = [xs[s, c, pl.ds(j, SUB, stride=seg), :] for s in range(streams_count)]
     feats = []
-    for s in range(xs.shape[0]):
-        acc = jnp.broadcast_to(f_ref[0, pl.ds(s, 1), lanes], (SUB, LANES)) * now[s]
+    for s in range(streams_count):
+        acc = fsc[s] * now[s]
         for tap in range(1, taps):
-            weight = jnp.broadcast_to(f_ref[tap, pl.ds(s, 1), lanes], (SUB, LANES))
-            acc = acc + weight * prev[tap - 1][s]
+            acc = acc + fsc[tap * streams_count + s] * prev[tap - 1][s]
         feats.append(acc)
     new_prev = [now] + prev[:-1]
     return feats, new_prev
@@ -49,7 +57,7 @@
     return (feats[1] * feats[2]).astype(jnp.bfloat16).astype(jnp.float32)
 
 
-def state_kernel(x_ref, halo_ref, f_ref, a_ref, seg_ref, h_ref, xs, dsc):
+def state_kernel(x_ref, halo_ref, f_ref, a_ref, seg_ref, h_ref, xs, dsc, fsc):
     streams_count, rows, block = x_ref.shape
     taps = f_ref.shape[0]
     modes = a_ref.shape[0]
@@ -60,18 +68,19 @@
 
     def lane_group(c, carry):
         lanes = lane_slice(c)
+        fill_filters(f_ref, fsc, lanes)
         for m in range(modes):
             dsc[m] = jnp.exp(-row(a_ref, m, lanes))
 
         def step(j, state):
             prev, states = state
-            feats, prev = step_features(xs, f_ref, c, lanes, seg, j, prev)
+            feats, prev = step_features(xs, fsc, c, seg, j, prev)
             u = gate(feats)
             return prev, tuple(dsc[m] * states[m] + u for m in range(modes))
 
         zero = jnp.zeros((SUB, LANES), jnp.float32)
         init = (first_prev(xs, halo_ref, c, lanes, seg, taps, sub), (zero,) * modes)
-        _, states = lax.fori_loop(0, seg, step, init, unroll=2)
+        _, states = lax.fori_loop(0, seg, step, init, unroll=UNROLL)
         later = (SUB - 1 - sub).astype(jnp.float32) * float(seg)
         for m in range(modes):
             seg_ref[m, :, lanes] = states[m]
@@ -82,7 +91,7 @@
     lax.fori_loop(0, block // LANES, lane_group, 0)
 
 
-def out_kernel(x_ref, halo_ref, f_ref, a_ref, r_ref, skip_ref, seg_ref, hin_ref, o_ref, xs, ys, dsc, rsc):
+def out_kernel(x_ref, halo_ref, f_ref, a_ref, r_ref, skip_ref, seg_ref, hin_ref, o_ref, xs, ys, dsc, rsc, fsc):
     streams_count, rows, block = x_ref.shape
     taps = f_ref.shape[0]
     modes = a_ref.shape[0]
@@ -93,6 +102,7 @@
 
     def lane_group(c, carry):
         lanes = lane_slice(c)
+        fill_filters(f_ref, fsc, lanes)
         starts = []
         for m in range(modes):
             rate = row(a_ref, m, lanes)
@@ -111,7 +121,7 @@
 
         def step(j, state):
             prev, states = state
-            feats, prev = step_features(xs, f_ref, c, lanes, seg, j, prev)
+            feats, prev = step_features(xs, fsc, c, seg, j, prev)
             u = gate(feats)
             new = []
             conv = None
@@ -125,7 +135,7 @@
             return prev, tuple(new)
 
         init = (first_prev(xs, halo_ref, c, lanes, seg, taps, sub), tuple(starts))
-        lax.fori_loop(0, seg, step, init, unroll=2)
+        lax.fori_loop(0, seg, step, init, unroll=UNROLL)
         return carry
 
     lax.fori_loop(0, block // LANES, lane_group, 0)
@@ -157,6 +167,7 @@
         scratch_shapes=[
             pltpu.VMEM((streams_count, BLOCK // LANES, rows, LANES), jnp.float32),
             pltpu.VMEM((modes, SUB, LANES), jnp.float32),
+            pltpu.VMEM((taps * streams_count, SUB, LANES), jnp.float32),
         ],
     )(x, halo, f, rate_t)
 
@@ -185,6 +196,7 @@
             pltpu.VMEM((BLOCK // LANES, rows, LANES), jnp.float32),
             pltpu.VMEM((modes, SUB, LANES), jnp.float32),
             pltpu.VMEM((modes, SUB, LANES), jnp.float32),
+            pltpu.VMEM((taps * streams_count, SUB, LANES), jnp.float32),
         ],
     )(x, halo, f, rate_t, residue_t, skip, ends, hin)
 

time: 81 us -> 77.3 us (0.954)
  starting transfers between devices: 27.4 us -> 20.6 us
  waiting for transfers between devices: 19.9 us -> 26.1 us
  Pallas kernels: 28.8 us -> 25 us
    ppermute x12 -> x9, starting transfers between devices: 27.4 us -> 20.6 us  [shift(): return lax.ppermute(value, axes, pairs)]
    ppermute x12 -> x9, waiting for transfers between devices: 19.9 us -> 26.1 us  [shift(): return lax.ppermute(value, axes, pairs)]
    pallas_call x1, Pallas kernels: 17.9 us -> 15.3 us  [run_out(): pl.pallas_call(out_kernel, grid=(width // BLOCK,), in_specs=[pl.BlockSpec...]
    pallas_call x1, Pallas kernels: 10.9 us -> 9.71 us  [run_state(): pl.pallas_call(state_kernel, grid=(width // BLOCK,), in_specs=[pl.BlockSp...]
  transfers between devices with their start and end apart: 12 -> 9, of which waited for: 6 -> 7; matrix products, arithmetic and copies ran while one was open for 0% -> 0% of each run, Pallas kernels for 0% -> 0%
where the time goes in v5:
time: 77.3 us; the launch traced here: 75.8 us
  waiting for transfers between devices  26.1 us (34%)
  Pallas kernels  25 us (32%)
  starting transfers between devices  20.6 us (27%)
  other arithmetic  2.93 us (4%)
  local copies, waits for them, and re-layouts  1.03 us (1%)
    ppermute x9, waiting for transfers between devices, shift(): return lax.ppermute(value, axes, pairs)  26.1 us
    ppermute x9, starting transfers between devices, shift(): return lax.ppermute(value, axes, pairs)  20.6 us
    pallas_call x1, Pallas kernels, run_out(): pl.pallas_call(out_kernel, grid=(width // BLOCK,), in_specs=[pl.BlockSpec...  15.3 us
    pallas_call x1, Pallas kernels, run_state(): pl.pallas_call(state_kernel, grid=(width // BLOCK,), in_specs=[pl.BlockSp...  9.71 us
  transfers between devices with their start and end apart: 9, of which 7 were waited for; matrix products, arithmetic and copies ran while one was open for 0% of the time, Pallas kernels for 0%

profile of v5, /device:TPU:16, one launch (start us, length us, event | category | flops | bytes accessed | tf_op | source)
XLA Modules:
  0.0 75.8 jit_solution(1234109932327407553)
XLA Ops:
  0.0 1.0 %slice.3 = bf16[2,3,4096]{2,0,1:T(2,128)(2,1)S(1)} slice(bf16[128,3,4096]{2,0,1:T(8,128)(2,1)} %param.5), slice={[126:128], [0:3], [0:4096]} | slice | bytes 98304 | tf_op jit(solution)/shard_map/slice | solution.py:215
  1.0 3.4 %collective-permute-start = (bf16[2,3,4096]{2,0,1:T(2,128)(2,1)S(1)}, bf16[2,3,4096]{2,0,1:T(2,128)(2,1)S(1)}, u32[]{:S(2)}, u32[]{:S(2)}) collective-permute-start(bf16[2,3,4096]{2,0,1:T(2,128)(2,1)S(1)} %slice.3), channel_id=1, source_target_pairs={{0,1},{1,2},{2,3},{3,4},{4,5},{5,6},{6,7},{7,8},{8,9},{9,10},{10,1... | collective-permute-start | bytes 147464 | tf_op jit(solution)/shard_map/ppermute | solution.py:213
  4.5 3.8 %collective-permute-done = bf16[2,3,4096]{2,0,1:T(2,128)(2,1)S(1)} collective-permute-done((bf16[2,3,4096]{2,0,1:T(2,128)(2,1)S(1)}, bf16[2,3,4096]{2,0,1:T(2,128)(2,1)S(1)}, u32[]{:S(2)}, u32[]{:S(2)}) %collective-permute-start) | collective-permute-done | bytes 49184 | tf_op jit(solution)/shard_map/ppermute | solution.py:213
  8.2 0.7 convert_bitcast_fusion.halo_ref
  8.9 9.7 %shard_map.55 = (f32[16,8,4096]{2,1,0:T(8,128)}, f32[16,4096]{1,0:T(8,128)}) custom-call(bf16[3,128,4096]{2,1,0:T(8,128)(2,1)} %bitcast.10, f32[3,2,4096]{2,1,0:T(2,128)} %convert_bitcast_fusion.halo_ref, f32[3,3,4096]{2,1,0:T(4,128)} %f_ref.3, f32[16,4096]{1,0:T(8,128)} %bitcast.12), custom_call_target="tpu_custom_call" | custom-call | tf_op jit(solution)/shard_map/pallas_call | solution.py:150
  18.6 1.0 %convert_element_type.40 = bf16[16,4096]{1,0:T(8,128)(2,1)S(1)} convert(f32[16,4096]{1,0:T(8,128)} %get-tuple-element.8) | non-fusion elementwise | flops 65536 | bytes 393216 | tf_op jit(solution)/shard_map/convert_element_type | solution.py:226
  19.6 1.9 %collective-permute-start.3 = (bf16[16,4096]{1,0:T(8,128)(2,1)S(1)}, bf16[16,4096]{1,0:T(8,128)(2,1)S(1)}, u32[]{:S(2)}, u32[]{:S(2)}) collective-permute-start(bf16[16,4096]{1,0:T(8,128)(2,1)S(1)} %convert_element_type.40), channel_id=1, source_target_pairs={{0,3},{1,4},{2,5},{3,6},{4,7},{5,8},{6,9},{7,10},{8,11},{9,12},{10... | collective-permute-start | bytes 393224 | tf_op jit(solution)/shard_map/ppermute | solution.py:213
  21.5 3.2 %collective-permute-start.2 = (bf16[16,4096]{1,0:T(8,128)(2,1)S(1)}, bf16[16,4096]{1,0:T(8,128)(2,1)S(1)}, u32[]{:S(2)}, u32[]{:S(2)}) collective-permute-start(bf16[16,4096]{1,0:T(8,128)(2,1)S(1)} %convert_element_type.40), channel_id=1, source_target_pairs={{0,2},{1,3},{2,4},{3,5},{4,6},{5,7},{6,8},{7,9},{8,10},{9,11},{10,... | collective-permute-start | bytes 393224 | tf_op jit(solution)/shard_map/ppermute | solution.py:213
  24.8 2.6 %collective-permute-start.1 = (bf16[16,4096]{1,0:T(8,128)(2,1)S(1)}, bf16[16,4096]{1,0:T(8,128)(2,1)S(1)}, u32[]{:S(2)}, u32[]{:S(2)}) collective-permute-start(bf16[16,4096]{1,0:T(8,128)(2,1)S(1)} %convert_element_type.40), channel_id=1, source_target_pairs={{0,1},{1,2},{2,3},{3,4},{4,5},{5,6},{6,7},{7,8},{8,9},{9,10},{10,1... | collective-permute-start | bytes 393224 | tf_op jit(solution)/shard_map/ppermute | solution.py:213
  27.4 0.8 %collective-permute-done.3 = bf16[16,4096]{1,0:T(8,128)(2,1)S(1)} collective-permute-done((bf16[16,4096]{1,0:T(8,128)(2,1)S(1)}, bf16[16,4096]{1,0:T(8,128)(2,1)S(1)}, u32[]{:S(2)}, u32[]{:S(2)}) %collective-permute-start.3) | collective-permute-done | bytes 131104 | tf_op jit(solution)/shard_map/ppermute | solution.py:213
  28.2 0.5 collective-permute-done.2
  28.7 4.1 %collective-permute-done.1 = bf16[16,4096]{1,0:T(8,128)(2,1)S(1)} collective-permute-done((bf16[16,4096]{1,0:T(8,128)(2,1)S(1)}, bf16[16,4096]{1,0:T(8,128)(2,1)S(1)}, u32[]{:S(2)}, u32[]{:S(2)}) %collective-permute-start.1) | collective-permute-done | bytes 131104 | tf_op jit(solution)/shard_map/ppermute | solution.py:213
  32.8 0.2 fusion
  33.0 2.4 %collective-permute-start.6 = (bf16[16,4096]{1,0:T(8,128)(2,1)S(1)}, bf16[16,4096]{1,0:T(8,128)(2,1)S(1)}, u32[]{:S(2)}, u32[]{:S(2)}) collective-permute-start(bf16[16,4096]{1,0:T(8,128)(2,1)S(1)} %fusion), channel_id=1, source_target_pairs={{0,9},{1,10},{2,11},{3,12},{4,13},{5,14},{6,15},{7,16},{8,17},{9,1... | collective-permute-start | bytes 393224 | tf_op jit(solution)/shard_map/ppermute | solution.py:213
  35.5 2.4 %collective-permute-start.5 = (bf16[16,4096]{1,0:T(8,128)(2,1)S(1)}, bf16[16,4096]{1,0:T(8,128)(2,1)S(1)}, u32[]{:S(2)}, u32[]{:S(2)}) collective-permute-start(bf16[16,4096]{1,0:T(8,128)(2,1)S(1)} %fusion), channel_id=1, source_target_pairs={{0,6},{1,7},{2,8},{3,9},{4,10},{5,11},{6,12},{7,13},{8,14},{9,15},... | collective-permute-start | bytes 393224 | tf_op jit(solution)/shard_map/ppermute | solution.py:213
  37.9 1.9 %collective-permute-start.4 = (bf16[16,4096]{1,0:T(8,128)(2,1)S(1)}, bf16[16,4096]{1,0:T(8,128)(2,1)S(1)}, u32[]{:S(2)}, u32[]{:S(2)}) collective-permute-start(bf16[16,4096]{1,0:T(8,128)(2,1)S(1)} %fusion), channel_id=1, source_target_pairs={{0,3},{1,4},{2,5},{3,6},{4,7},{5,8},{6,9},{7,10},{8,11},{9,12},{10... | collective-permute-start | bytes 393224 | tf_op jit(solution)/shard_map/ppermute | solution.py:213
  39.8 2.7 %collective-permute-done.6 = bf16[16,4096]{1,0:T(8,128)(2,1)S(1)} collective-permute-done((bf16[16,4096]{1,0:T(8,128)(2,1)S(1)}, bf16[16,4096]{1,0:T(8,128)(2,1)S(1)}, u32[]{:S(2)}, u32[]{:S(2)}) %collective-permute-start.6) | collective-permute-done | bytes 131104 | tf_op jit(solution)/shard_map/ppermute | solution.py:213
  42.5 6.3 %collective-permute-done.4 = bf16[16,4096]{1,0:T(8,128)(2,1)S(1)} collective-permute-done((bf16[16,4096]{1,0:T(8,128)(2,1)S(1)}, bf16[16,4096]{1,0:T(8,128)(2,1)S(1)}, u32[]{:S(2)}, u32[]{:S(2)}) %collective-permute-start.4) | collective-permute-done | bytes 131104 | tf_op jit(solution)/shard_map/ppermute | solution.py:213
  48.8 0.3 fusion.1
  49.1 0.7 collective-permute-start.8
  49.8 1.9 %collective-permute-start.7 = (bf16[16,4096]{1,0:T(8,128)(2,1)S(1)}, bf16[16,4096]{1,0:T(8,128)(2,1)S(1)}, u32[]{:S(2)}, u32[]{:S(2)}) collective-permute-start(bf16[16,4096]{1,0:T(8,128)(2,1)S(1)} %get-tuple-element.9), channel_id=1, source_target_pairs={{0,12},{1,13},{2,14},{3,15},{4,16},{5,17},{6,18},{7,19},{8,20},{9,... | collective-permute-start | bytes 393224 | tf_op jit(solution)/shard_map/ppermute | solution.py:213
  51.8 7.9 %collective-permute-done.7 = bf16[16,4096]{1,0:T(8,128)(2,1)S(1)} collective-permute-done((bf16[16,4096]{1,0:T(8,128)(2,1)S(1)}, bf16[16,4096]{1,0:T(8,128)(2,1)S(1)}, u32[]{:S(2)}, u32[]{:S(2)}) %collective-permute-start.7) | collective-permute-done | bytes 131104 | tf_op jit(solution)/shard_map/ppermute | solution.py:213
  59.7 0.8 %multiply_add_fusion.hin_ref = f32[16,4096]{1,0:T(8,128)} fusion(f32[16,4096]{1,0:T(8,128)S(1)} %get-tuple-element.10, bf16[16,4096]{1,0:T(8,128)(2,1)S(1)} %collective-permute-done.8, bf16[16,4096]{1,0:T(8,128)(2,1)S(1)} %collective-permute-done.7, f32[4096,16]{0,1:T(8,128)S(1)} %copy-done), kind=kLoop, calls=%fused_computation | loop fusion | flops 655360 | bytes 1048576 | tf_op jit(solution)/shard_map/add | solution.py:240
  60.5 15.3 %shard_map.56 = bf16[128,4096]{1,0:T(8,128)(2,1)} custom-call(bf16[3,128,4096]{2,1,0:T(8,128)(2,1)} %bitcast.11, f32[3,2,4096]{2,1,0:T(2,128)} %convert_bitcast_fusion.halo_ref, f32[3,3,4096]{2,1,0:T(4,128)} %f_ref.3, f32[16,4096]{1,0:T(8,128)} %bitcast.13, f32[16,4096]{1,0:T(8,128)} %bitcast.14, f32[1,4096]{1,0:T(1,128)} %bitcast.15, ...), custom_call_target="tpu_custom_call" | custom-call | tf_op jit(solution)/shard_map/pallas_call | solution.py:179
  (4 shorter events, 0.0 us)
Async XLA Ops:
  0.0 32.8 %copy-start = (f32[4096,16]{0,1:T(8,128)S(1)}, f32[4096,16]{0,1:T(8,128)}, u32[]{:S(2)}) copy-start(f32[4096,16]{0,1:T(8,128)} %param.8) | copy-start | bytes 786436
  1.0 7.2 %collective-permute-start = (bf16[2,3,4096]{2,0,1:T(2,128)(2,1)S(1)}, bf16[2,3,4096]{2,0,1:T(2,128)(2,1)S(1)}, u32[]{:S(2)}, u32[]{:S(2)}) collective-permute-start(bf16[2,3,4096]{2,0,1:T(2,128)(2,1)S(1)} %slice.3), channel_id=1, source_target_pairs={{0,1},{1,2},{2,3},{3,4},{4,5},{5,6},{6,7},{7,8},{8,9},{9,10},{10,1... | collective-permute-start | bytes 147464 | tf_op jit(solution)/shard_map/ppermute | solution.py:213
  19.6 8.7 %collective-permute-start.3 = (bf16[16,4096]{1,0:T(8,128)(2,1)S(1)}, bf16[16,4096]{1,0:T(8,128)(2,1)S(1)}, u32[]{:S(2)}, u32[]{:S(2)}) collective-permute-start(bf16[16,4096]{1,0:T(8,128)(2,1)S(1)} %convert_element_type.40), channel_id=1, source_target_pairs={{0,3},{1,4},{2,5},{3,6},{4,7},{5,8},{6,9},{7,10},{8,11},{9,12},{10... | collective-permute-start | bytes 393224 | tf_op jit(solution)/shard_map/ppermute | solution.py:213
  21.5 7.2 %collective-permute-start.2 = (bf16[16,4096]{1,0:T(8,128)(2,1)S(1)}, bf16[16,4096]{1,0:T(8,128)(2,1)S(1)}, u32[]{:S(2)}, u32[]{:S(2)}) collective-permute-start(bf16[16,4096]{1,0:T(8,128)(2,1)S(1)} %convert_element_type.40), channel_id=1, source_target_pairs={{0,2},{1,3},{2,4},{3,5},{4,6},{5,7},{6,8},{7,9},{8,10},{9,11},{10,... | collective-permute-start | bytes 393224 | tf_op jit(solution)/shard_map/ppermute | solution.py:213
  24.8 8.1 %collective-permute-start.1 = (bf16[16,4096]{1,0:T(8,128)(2,1)S(1)}, bf16[16,4096]{1,0:T(8,128)(2,1)S(1)}, u32[]{:S(2)}, u32[]{:S(2)}) collective-permute-start(bf16[16,4096]{1,0:T(8,128)(2,1)S(1)} %convert_element_type.40), channel_id=1, source_target_pairs={{0,1},{1,2},{2,3},{3,4},{4,5},{5,6},{6,7},{7,8},{8,9},{9,10},{10,1... | collective-permute-start | bytes 393224 | tf_op jit(solution)/shard_map/ppermute | solution.py:213
  33.0 9.5 %collective-permute-start.6 = (bf16[16,4096]{1,0:T(8,128)(2,1)S(1)}, bf16[16,4096]{1,0:T(8,128)(2,1)S(1)}, u32[]{:S(2)}, u32[]{:S(2)}) collective-permute-start(bf16[16,4096]{1,0:T(8,128)(2,1)S(1)} %fusion), channel_id=1, source_target_pairs={{0,9},{1,10},{2,11},{3,12},{4,13},{5,14},{6,15},{7,16},{8,17},{9,1... | collective-permute-start | bytes 393224 | tf_op jit(solution)/shard_map/ppermute | solution.py:213
  35.5 7.1 %collective-permute-start.5 = (bf16[16,4096]{1,0:T(8,128)(2,1)S(1)}, bf16[16,4096]{1,0:T(8,128)(2,1)S(1)}, u32[]{:S(2)}, u32[]{:S(2)}) collective-permute-start(bf16[16,4096]{1,0:T(8,128)(2,1)S(1)} %fusion), channel_id=1, source_target_pairs={{0,6},{1,7},{2,8},{3,9},{4,10},{5,11},{6,12},{7,13},{8,14},{9,15},... | collective-permute-start | bytes 393224 | tf_op jit(solution)/shard_map/ppermute | solution.py:213
  37.9 10.9 %collective-permute-start.4 = (bf16[16,4096]{1,0:T(8,128)(2,1)S(1)}, bf16[16,4096]{1,0:T(8,128)(2,1)S(1)}, u32[]{:S(2)}, u32[]{:S(2)}) collective-permute-start(bf16[16,4096]{1,0:T(8,128)(2,1)S(1)} %fusion), channel_id=1, source_target_pairs={{0,3},{1,4},{2,5},{3,6},{4,7},{5,8},{6,9},{7,10},{8,11},{9,12},{10... | collective-permute-start | bytes 393224 | tf_op jit(solution)/shard_map/ppermute | solution.py:213
  49.1 2.6 %collective-permute-start.8 = (bf16[16,4096]{1,0:T(8,128)(2,1)S(1)}, bf16[16,4096]{1,0:T(8,128)(2,1)S(1)}, u32[]{:S(2)}, u32[]{:S(2)}) collective-permute-start(bf16[16,4096]{1,0:T(8,128)(2,1)S(1)} %get-tuple-element.9), channel_id=1, source_target_pairs={{0,24},{1,25},{2,26},{3,27},{4,28},{5,29},{6,30},{7,31}} | collective-permute-start | bytes 393224 | tf_op jit(solution)/shard_map/ppermute | solution.py:213
  49.8 9.8 %collective-permute-start.7 = (bf16[16,4096]{1,0:T(8,128)(2,1)S(1)}, bf16[16,4096]{1,0:T(8,128)(2,1)S(1)}, u32[]{:S(2)}, u32[]{:S(2)}) collective-permute-start(bf16[16,4096]{1,0:T(8,128)(2,1)S(1)} %get-tuple-element.9), channel_id=1, source_target_pairs={{0,12},{1,13},{2,14},{3,15},{4,16},{5,17},{6,18},{7,19},{8,20},{9,... | collective-permute-start | bytes 393224 | tf_op jit(solution)/shard_map/ppermute | solution.py:213

commit v6 on v5

--- a/solution.py
+++ b/solution.py
@@ -91,7 +91,9 @@
     lax.fori_loop(0, block // LANES, lane_group, 0)
 
 
-def out_kernel(x_ref, halo_ref, f_ref, a_ref, r_ref, skip_ref, seg_ref, hin_ref, o_ref, xs, ys, dsc, rsc, fsc):
+def out_kernel(
+    x_ref, halo_ref, f_ref, a_ref, r_ref, skip_ref, seg_ref, fix_ref, hin_ref, o_ref, xs, ys, dsc, rsc, fsc
+):
     streams_count, rows, block = x_ref.shape
     taps = f_ref.shape[0]
     modes = a_ref.shape[0]
@@ -108,7 +110,7 @@
             rate = row(a_ref, m, lanes)
             dsc[m] = jnp.exp(-rate)
             rsc[m] = row(r_ref, m, lanes)
-            ends = seg_ref[m, :, lanes]
+            ends = seg_ref[m, :, lanes] + jnp.where(sub == 0, row(fix_ref, m, lanes), 0.0)
             carried = jnp.where(sub >= 1, pltpu.roll(ends, 1, 0), 0.0)
             offset = 1
             while offset < SUB:
@@ -172,7 +174,7 @@
     )(x, halo, f, rate_t)
 
 
-def run_out(x, halo, f, rate_t, residue_t, skip, ends, hin):
+def run_out(x, halo, f, rate_t, residue_t, skip, ends, fix, hin):
     streams_count, rows, width = x.shape
     taps = f.shape[0]
     modes = rate_t.shape[0]
@@ -188,6 +190,7 @@
             pl.BlockSpec((1, BLOCK), lambda i: (0, i)),
             pl.BlockSpec((modes, SUB, BLOCK), lambda i: (0, 0, i)),
             pl.BlockSpec((modes, BLOCK), lambda i: (0, i)),
+            pl.BlockSpec((modes, BLOCK), lambda i: (0, i)),
         ],
         out_specs=pl.BlockSpec((rows, BLOCK), lambda i: (0, i)),
         out_shape=jax.ShapeDtypeStruct((rows, width), jnp.bfloat16),
@@ -198,7 +201,7 @@
             pltpu.VMEM((modes, SUB, LANES), jnp.float32),
             pltpu.VMEM((taps * streams_count, SUB, LANES), jnp.float32),
         ],
-    )(x, halo, f, rate_t, residue_t, skip, ends, hin)
+    )(x, halo, f, rate_t, residue_t, skip, ends, fix, hin)
 
 
 def body(streams, short_filter, skip, rates, residues):
@@ -212,12 +215,37 @@
         pairs = [(j, j + offset) for j in range(devices - offset)]
         return lax.ppermute(value, axes, pairs)
 
-    halo = shift(streams[tok_rows - (taps - 1) :], 1)
-    halo = jnp.transpose(halo, (1, 0, 2)).astype(jnp.float32)
+    halo_rows = shift(streams[tok_rows - (taps - 1) :], 1).astype(jnp.float32)
+    halo = jnp.transpose(halo_rows, (1, 0, 2))
     x = jnp.transpose(streams, (1, 0, 2))
     rate_t = rates.T
     residue_t = residues.T
-    ends, local = run_state(x, halo, short_filter, rate_t)
+    ends, local = run_state(x, jnp.zeros_like(halo), short_filter, rate_t)
+
+    head = streams[: taps - 1].astype(jnp.float32)
+
+    def head_gate(before):
+        rows = jnp.concatenate([before, head], axis=0)
+        gated = []
+        for t in range(taps - 1):
+            feat = short_filter[0] * rows[t + taps - 1]
+            for tap in range(1, taps):
+                feat = feat + short_filter[tap] * rows[t + taps - 1 - tap]
+            gated.append((feat[1] * feat[2]).astype(jnp.bfloat16).astype(jnp.float32))
+        return gated
+
+    seg = tok_rows // SUB
+    true_head = head_gate(halo_rows)
+    zero_head = head_gate(jnp.zeros_like(halo_rows))
+    local_fix = None
+    ends_fix = None
+    for t in range(taps - 1):
+        delta = (true_head[t] - zero_head[t])[None, :]
+        to_end = jnp.exp(-rate_t * float(tok_rows - 1 - t)) * delta
+        to_seg = jnp.exp(-rate_t * float(seg - 1 - t)) * delta
+        local_fix = to_end if local_fix is None else local_fix + to_end
+        ends_fix = to_seg if ends_fix is None else ends_fix + to_seg
+    local = local + local_fix
 
     def decay_pow(steps):
         return jnp.exp(-rate_t * float(tok_rows * steps))
@@ -240,7 +268,7 @@
         carried = carried + decay_pow(window) * gather_window(carried, window, count)
         window *= count + 1
 
-    return run_out(x, halo, short_filter, rate_t, residue_t, skip.reshape(1, width), ends, carried)
+    return run_out(x, halo, short_filter, rate_t, residue_t, skip.reshape(1, width), ends, ends_fix, carried)
 
 
 def solution(mesh):

time: 77.3 us -> 76.9 us (level)
  waiting for transfers between devices: 26.1 us -> 21.7 us
  other arithmetic: 2.93 us -> 5.36 us
  starting transfers between devices: 20.6 us -> 21.8 us
    ppermute x9, waiting for transfers between devices: 26.1 us -> 21.7 us  [shift(): return lax.ppermute(value, axes, pairs)]
    ppermute x9, starting transfers between devices: 20.6 us -> 21.8 us  [shift(): return lax.ppermute(value, axes, pairs)]
    convert_element_type x1 -> x2, other arithmetic: 0.67 us -> 1.82 us  [the longest x1 1.13 us: body(): head = streams[:taps - 1].astype(jnp.float32)]
    convert_element_type x3, other arithmetic: 1.44 us -> 2.32 us  [gather_window(): sent = value.astype(jnp.bfloat16)]
  transfers between devices with their start and end apart: 9 -> 9, of which waited for: 7 -> 5; matrix products, arithmetic and copies ran while one was open for 0% -> 2% of each run, Pallas kernels for 0% -> 13%
where the time goes in v6:
time: 76.9 us; the launch traced here: 75.8 us
  Pallas kernels  25.1 us (33%)
  starting transfers between devices  21.8 us (28%)
  waiting for transfers between devices  21.7 us (28%)
  other arithmetic  5.36 us (7%)
  local copies, waits for them, and re-layouts  1.6 us (2%)
    ppermute x9, starting transfers between devices, shift(): return lax.ppermute(value, axes, pairs)  21.8 us
    ppermute x9, waiting for transfers between devices, shift(): return lax.ppermute(value, axes, pairs)  21.7 us
    pallas_call x1, Pallas kernels, run_out(): pl.pallas_call(out_kernel, grid=(width // BLOCK,), in_specs=[pl.BlockSpec...  15.4 us
    pallas_call x1, Pallas kernels, run_state(): pl.pallas_call(state_kernel, grid=(width // BLOCK,), in_specs=[pl.BlockSp...  9.67 us
    convert_element_type x3, other arithmetic, gather_window(): sent = value.astype(jnp.bfloat16)  2.32 us
  transfers between devices with their start and end apart: 9, of which 5 were waited for; matrix products, arithmetic and copies ran while one was open for 2% of the time, Pallas kernels for 13%

profile of v6, /device:TPU:16, one launch (start us, length us, event | category | flops | bytes accessed | tf_op | source)
XLA Modules:
  0.0 75.8 jit_solution(1508106989462552970)
XLA Ops:
  0.0 1.1 %slice_convert_fusion = (f32[2,3,4096]{2,0,1:T(2,128)S(1)}, bf16[2,3,4096]{2,0,1:T(2,128)(2,1)S(1)}) fusion(bf16[128,3,4096]{2,0,1:T(8,128)(2,1)} %param.5), kind=kLoop, calls=%fused_computation.12 | loop fusion | flops 24576 | bytes 245760 | tf_op jit(solution)/shard_map/convert_element_type | solution.py:225
  1.1 3.4 %collective-permute-start = (bf16[2,3,4096]{2,0,1:T(2,128)(2,1)S(1)}, bf16[2,3,4096]{2,0,1:T(2,128)(2,1)S(1)}, u32[]{:S(2)}, u32[]{:S(2)}) collective-permute-start(bf16[2,3,4096]{2,0,1:T(2,128)(2,1)S(1)} %get-tuple-element.14), channel_id=1, source_target_pairs={{0,1},{1,2},{2,3},{3,4},{4,5},{5,6},{6,7},{7,8},{8,9},{9,10},{10,1... | collective-permute-start | bytes 147464 | tf_op jit(solution)/shard_map/ppermute | solution.py:216
  4.6 0.9 %fusion.15 = (f32[1,3,4096]{2,1,0:T(4,128)S(1)}, f32[1,3,4096]{2,1,0:T(4,128)S(1)}, f32[1,3,4096]{2,1,0:T(4,128)S(1)}) fusion(f32[3,3,4096]{2,1,0:T(4,128)} %f_ref.3), kind=kLoop, calls=%fused_computation.32 | loop fusion | bytes 294912 | tf_op jit(solution)/shard_map/slice | solution.py:231
  5.5 0.7 broadcast_in_dim.2.halo_ref
  6.2 9.7 %shard_map.55 = (f32[16,8,4096]{2,1,0:T(8,128)}, f32[16,4096]{1,0:T(8,128)}) custom-call(bf16[3,128,4096]{2,1,0:T(8,128)(2,1)} %bitcast.14, f32[3,2,4096]{2,1,0:T(2,128)} %broadcast_in_dim.2.halo_ref, f32[3,3,4096]{2,1,0:T(4,128)} %f_ref.3, f32[16,4096]{1,0:T(8,128)} %bitcast.16), custom_call_target="tpu_custom_call" | custom-call | tf_op jit(solution)/shard_map/pallas_call | solution.py:152
  15.9 0.7 fusion.16
  16.5 0.2 multiply_add_fusion.4
  17.0 1.8 %add_convert_fusion = (bf16[16,4096]{1,0:T(8,128)(2,1)S(1)}, f32[16,4096]{1,0:T(8,128)}) fusion(f32[16,4096]{1,0:T(8,128)} %get-tuple-element.8, f32[4096]{0:T(1024)S(1)} %bitcast.19, f32[4096]{0:T(1024)S(1)} %bitcast.20, f32[4096,16]{0,1:T(8,128)S(1)} %copy-done), kind=kLoop, calls=%fused_computation.3 | loop fusion | flops 851968 | bytes 950272 | tf_op jit(solution)/shard_map/convert_element_type | solution.py:254
  18.8 3.0 %collective-permute-start.3 = (bf16[16,4096]{1,0:T(8,128)(2,1)S(1)}, bf16[16,4096]{1,0:T(8,128)(2,1)S(1)}, u32[]{:S(2)}, u32[]{:S(2)}) collective-permute-start(bf16[16,4096]{1,0:T(8,128)(2,1)S(1)} %get-tuple-element.16), channel_id=1, source_target_pairs={{0,3},{1,4},{2,5},{3,6},{4,7},{5,8},{6,9},{7,10},{8,11},{9,12},{10... | collective-permute-start | bytes 393224 | tf_op jit(solution)/shard_map/ppermute | solution.py:216
  21.9 1.9 %collective-permute-start.2 = (bf16[16,4096]{1,0:T(8,128)(2,1)S(1)}, bf16[16,4096]{1,0:T(8,128)(2,1)S(1)}, u32[]{:S(2)}, u32[]{:S(2)}) collective-permute-start(bf16[16,4096]{1,0:T(8,128)(2,1)S(1)} %get-tuple-element.16), channel_id=1, source_target_pairs={{0,2},{1,3},{2,4},{3,5},{4,6},{5,7},{6,8},{7,9},{8,10},{9,11},{10,... | collective-permute-start | bytes 393224 | tf_op jit(solution)/shard_map/ppermute | solution.py:216
  23.8 3.7 %collective-permute-start.1 = (bf16[16,4096]{1,0:T(8,128)(2,1)S(1)}, bf16[16,4096]{1,0:T(8,128)(2,1)S(1)}, u32[]{:S(2)}, u32[]{:S(2)}) collective-permute-start(bf16[16,4096]{1,0:T(8,128)(2,1)S(1)} %get-tuple-element.16), channel_id=1, source_target_pairs={{0,1},{1,2},{2,3},{3,4},{4,5},{5,6},{6,7},{7,8},{8,9},{9,10},{10,1... | collective-permute-start | bytes 393224 | tf_op jit(solution)/shard_map/ppermute | solution.py:216
  27.5 1.5 %collective-permute-done.2 = bf16[16,4096]{1,0:T(8,128)(2,1)S(1)} collective-permute-done((bf16[16,4096]{1,0:T(8,128)(2,1)S(1)}, bf16[16,4096]{1,0:T(8,128)(2,1)S(1)}, u32[]{:S(2)}, u32[]{:S(2)}) %collective-permute-start.2) | collective-permute-done | bytes 131104 | tf_op jit(solution)/shard_map/ppermute | solution.py:216
  29.0 3.3 %collective-permute-done.1 = bf16[16,4096]{1,0:T(8,128)(2,1)S(1)} collective-permute-done((bf16[16,4096]{1,0:T(8,128)(2,1)S(1)}, bf16[16,4096]{1,0:T(8,128)(2,1)S(1)}, u32[]{:S(2)}, u32[]{:S(2)}) %collective-permute-start.1) | collective-permute-done | bytes 131104 | tf_op jit(solution)/shard_map/ppermute | solution.py:216
  32.5 3.1 %collective-permute-start.6 = (bf16[16,4096]{1,0:T(8,128)(2,1)S(1)}, bf16[16,4096]{1,0:T(8,128)(2,1)S(1)}, u32[]{:S(2)}, u32[]{:S(2)}) collective-permute-start(bf16[16,4096]{1,0:T(8,128)(2,1)S(1)} %fusion.12), channel_id=1, source_target_pairs={{0,9},{1,10},{2,11},{3,12},{4,13},{5,14},{6,15},{7,16},{8,17},{9,1... | collective-permute-start | bytes 393224 | tf_op jit(solution)/shard_map/ppermute | solution.py:216
  35.5 2.1 %collective-permute-start.5 = (bf16[16,4096]{1,0:T(8,128)(2,1)S(1)}, bf16[16,4096]{1,0:T(8,128)(2,1)S(1)}, u32[]{:S(2)}, u32[]{:S(2)}) collective-permute-start(bf16[16,4096]{1,0:T(8,128)(2,1)S(1)} %fusion.12), channel_id=1, source_target_pairs={{0,6},{1,7},{2,8},{3,9},{4,10},{5,11},{6,12},{7,13},{8,14},{9,15},... | collective-permute-start | bytes 393224 | tf_op jit(solution)/shard_map/ppermute | solution.py:216
  37.7 1.9 %collective-permute-start.4 = (bf16[16,4096]{1,0:T(8,128)(2,1)S(1)}, bf16[16,4096]{1,0:T(8,128)(2,1)S(1)}, u32[]{:S(2)}, u32[]{:S(2)}) collective-permute-start(bf16[16,4096]{1,0:T(8,128)(2,1)S(1)} %fusion.12), channel_id=1, source_target_pairs={{0,3},{1,4},{2,5},{3,6},{4,7},{5,8},{6,9},{7,10},{8,11},{9,12},{10... | collective-permute-start | bytes 393224 | tf_op jit(solution)/shard_map/ppermute | solution.py:216
  39.6 2.9 %collective-permute-done.6 = bf16[16,4096]{1,0:T(8,128)(2,1)S(1)} collective-permute-done((bf16[16,4096]{1,0:T(8,128)(2,1)S(1)}, bf16[16,4096]{1,0:T(8,128)(2,1)S(1)}, u32[]{:S(2)}, u32[]{:S(2)}) %collective-permute-start.6) | collective-permute-done | bytes 131104 | tf_op jit(solution)/shard_map/ppermute | solution.py:216
  42.5 6.6 %collective-permute-done.4 = bf16[16,4096]{1,0:T(8,128)(2,1)S(1)} collective-permute-done((bf16[16,4096]{1,0:T(8,128)(2,1)S(1)}, bf16[16,4096]{1,0:T(8,128)(2,1)S(1)}, u32[]{:S(2)}, u32[]{:S(2)}) %collective-permute-start.4) | collective-permute-done | bytes 131104 | tf_op jit(solution)/shard_map/ppermute | solution.py:216
  49.1 0.3 fusion.13
  49.4 0.7 collective-permute-start.8
  50.1 1.9 %collective-permute-start.7 = (bf16[16,4096]{1,0:T(8,128)(2,1)S(1)}, bf16[16,4096]{1,0:T(8,128)(2,1)S(1)}, u32[]{:S(2)}, u32[]{:S(2)}) collective-permute-start(bf16[16,4096]{1,0:T(8,128)(2,1)S(1)} %get-tuple-element.9), channel_id=1, source_target_pairs={{0,12},{1,13},{2,14},{3,15},{4,16},{5,17},{6,18},{7,19},{8,20},{9,... | collective-permute-start | bytes 393224 | tf_op jit(solution)/shard_map/ppermute | solution.py:216
  52.1 7.4 %collective-permute-done.7 = bf16[16,4096]{1,0:T(8,128)(2,1)S(1)} collective-permute-done((bf16[16,4096]{1,0:T(8,128)(2,1)S(1)}, bf16[16,4096]{1,0:T(8,128)(2,1)S(1)}, u32[]{:S(2)}, u32[]{:S(2)}) %collective-permute-start.7) | collective-permute-done | bytes 131104 | tf_op jit(solution)/shard_map/ppermute | solution.py:216
  59.5 0.8 %multiply_add_fusion.hin_ref = f32[16,4096]{1,0:T(8,128)} fusion(f32[16,4096]{1,0:T(8,128)S(1)} %get-tuple-element.10, bf16[16,4096]{1,0:T(8,128)(2,1)S(1)} %collective-permute-done.8, bf16[16,4096]{1,0:T(8,128)(2,1)S(1)} %collective-permute-done.7, f32[4096,16]{0,1:T(8,128)S(1)} %copy-done), kind=kLoop, calls=%fused_computation | loop fusion | flops 655360 | bytes 1048576 | tf_op jit(solution)/shard_map/add | solution.py:268
  60.3 15.4 %shard_map.56 = bf16[128,4096]{1,0:T(8,128)(2,1)} custom-call(bf16[3,128,4096]{2,1,0:T(8,128)(2,1)} %bitcast.15, f32[3,2,4096]{2,1,0:T(2,128)} %get-tuple-element.23.halo_ref, f32[3,3,4096]{2,1,0:T(4,128)} %f_ref.3, f32[16,4096]{1,0:T(8,128)} %bitcast.17, f32[16,4096]{1,0:T(8,128)} %bitcast.18, f32[1,4096]{1,0:T(1,128)} %bitcast.21, ...), custom_call_target="tpu_custom_call" | custom-call | tf_op jit(solution)/shard_map/pallas_call | solution.py:181
  (9 shorter events, 0.3 us)
Async XLA Ops:
  0.0 16.9 %copy-start = (f32[4096,16]{0,1:T(8,128)S(1)}, f32[4096,16]{0,1:T(8,128)}, u32[]{:S(2)}) copy-start(f32[4096,16]{0,1:T(8,128)} %param.8) | copy-start | bytes 786436
  1.1 14.7 %collective-permute-start = (bf16[2,3,4096]{2,0,1:T(2,128)(2,1)S(1)}, bf16[2,3,4096]{2,0,1:T(2,128)(2,1)S(1)}, u32[]{:S(2)}, u32[]{:S(2)}) collective-permute-start(bf16[2,3,4096]{2,0,1:T(2,128)(2,1)S(1)} %get-tuple-element.14), channel_id=1, source_target_pairs={{0,1},{1,2},{2,3},{3,4},{4,5},{5,6},{6,7},{7,8},{8,9},{9,10},{10,1... | collective-permute-start | bytes 147464 | tf_op jit(solution)/shard_map/ppermute | solution.py:216
  18.8 8.7 %collective-permute-start.3 = (bf16[16,4096]{1,0:T(8,128)(2,1)S(1)}, bf16[16,4096]{1,0:T(8,128)(2,1)S(1)}, u32[]{:S(2)}, u32[]{:S(2)}) collective-permute-start(bf16[16,4096]{1,0:T(8,128)(2,1)S(1)} %get-tuple-element.16), channel_id=1, source_target_pairs={{0,3},{1,4},{2,5},{3,6},{4,7},{5,8},{6,9},{7,10},{8,11},{9,12},{10... | collective-permute-start | bytes 393224 | tf_op jit(solution)/shard_map/ppermute | solution.py:216
  21.9 7.2 %collective-permute-start.2 = (bf16[16,4096]{1,0:T(8,128)(2,1)S(1)}, bf16[16,4096]{1,0:T(8,128)(2,1)S(1)}, u32[]{:S(2)}, u32[]{:S(2)}) collective-permute-start(bf16[16,4096]{1,0:T(8,128)(2,1)S(1)} %get-tuple-element.16), channel_id=1, source_target_pairs={{0,2},{1,3},{2,4},{3,5},{4,6},{5,7},{6,8},{7,9},{8,10},{9,11},{10,... | collective-permute-start | bytes 393224 | tf_op jit(solution)/shard_map/ppermute | solution.py:216
  23.8 8.5 %collective-permute-start.1 = (bf16[16,4096]{1,0:T(8,128)(2,1)S(1)}, bf16[16,4096]{1,0:T(8,128)(2,1)S(1)}, u32[]{:S(2)}, u32[]{:S(2)}) collective-permute-start(bf16[16,4096]{1,0:T(8,128)(2,1)S(1)} %get-tuple-element.16), channel_id=1, source_target_pairs={{0,1},{1,2},{2,3},{3,4},{4,5},{5,6},{6,7},{7,8},{8,9},{9,10},{10,1... | collective-permute-start | bytes 393224 | tf_op jit(solution)/shard_map/ppermute | solution.py:216
  32.5 10.0 %collective-permute-start.6 = (bf16[16,4096]{1,0:T(8,128)(2,1)S(1)}, bf16[16,4096]{1,0:T(8,128)(2,1)S(1)}, u32[]{:S(2)}, u32[]{:S(2)}) collective-permute-start(bf16[16,4096]{1,0:T(8,128)(2,1)S(1)} %fusion.12), channel_id=1, source_target_pairs={{0,9},{1,10},{2,11},{3,12},{4,13},{5,14},{6,15},{7,16},{8,17},{9,1... | collective-permute-start | bytes 393224 | tf_op jit(solution)/shard_map/ppermute | solution.py:216
  35.5 7.0 %collective-permute-start.5 = (bf16[16,4096]{1,0:T(8,128)(2,1)S(1)}, bf16[16,4096]{1,0:T(8,128)(2,1)S(1)}, u32[]{:S(2)}, u32[]{:S(2)}) collective-permute-start(bf16[16,4096]{1,0:T(8,128)(2,1)S(1)} %fusion.12), channel_id=1, source_target_pairs={{0,6},{1,7},{2,8},{3,9},{4,10},{5,11},{6,12},{7,13},{8,14},{9,15},... | collective-permute-start | bytes 393224 | tf_op jit(solution)/shard_map/ppermute | solution.py:216
  37.7 11.4 %collective-permute-start.4 = (bf16[16,4096]{1,0:T(8,128)(2,1)S(1)}, bf16[16,4096]{1,0:T(8,128)(2,1)S(1)}, u32[]{:S(2)}, u32[]{:S(2)}) collective-permute-start(bf16[16,4096]{1,0:T(8,128)(2,1)S(1)} %fusion.12), channel_id=1, source_target_pairs={{0,3},{1,4},{2,5},{3,6},{4,7},{5,8},{6,9},{7,10},{8,11},{9,12},{10... | collective-permute-start | bytes 393224 | tf_op jit(solution)/shard_map/ppermute | solution.py:216
  49.4 2.6 %collective-permute-start.8 = (bf16[16,4096]{1,0:T(8,128)(2,1)S(1)}, bf16[16,4096]{1,0:T(8,128)(2,1)S(1)}, u32[]{:S(2)}, u32[]{:S(2)}) collective-permute-start(bf16[16,4096]{1,0:T(8,128)(2,1)S(1)} %get-tuple-element.9), channel_id=1, source_target_pairs={{0,24},{1,25},{2,26},{3,27},{4,28},{5,29},{6,30},{7,31}} | collective-permute-start | bytes 393224 | tf_op jit(solution)/shard_map/ppermute | solution.py:216
  50.1 9.4 %collective-permute-start.7 = (bf16[16,4096]{1,0:T(8,128)(2,1)S(1)}, bf16[16,4096]{1,0:T(8,128)(2,1)S(1)}, u32[]{:S(2)}, u32[]{:S(2)}) collective-permute-start(bf16[16,4096]{1,0:T(8,128)(2,1)S(1)} %get-tuple-element.9), channel_id=1, source_target_pairs={{0,12},{1,13},{2,14},{3,15},{4,16},{5,17},{6,18},{7,19},{8,20},{9,... | collective-permute-start | bytes 393224 | tf_op jit(solution)/shard_map/ppermute | solution.py:216

commit v7 on v6

--- a/solution.py
+++ b/solution.py
@@ -9,7 +9,7 @@
 SUB = 8
 BLOCK = 512
 FIRST_WINDOW = 3
-UNROLL = 4
+UNROLL = 8
 
 
 def lane_slice(c):
@@ -125,13 +125,12 @@
             prev, states = state
             feats, prev = step_features(xs, fsc, c, seg, j, prev)
             u = gate(feats)
-            new = []
-            conv = None
-            for m in range(modes):
-                sm = dsc[m] * states[m] + u
-                term = rsc[m] * sm
-                conv = term if conv is None else conv + term
-                new.append(sm)
+            new = [dsc[m] * states[m] + u for m in range(modes)]
+            terms = [rsc[m] * new[m] for m in range(modes)]
+            while len(terms) > 1:
+                paired = [terms[i] + terms[i + 1] for i in range(0, len(terms) - 1, 2)]
+                terms = paired + terms[len(terms) - len(terms) % 2 :]
+            conv = terms[0]
             y = (conv + skip_rows * u).astype(jnp.bfloat16).astype(jnp.float32)
             ys[c, pl.ds(j, SUB, stride=seg), :] = feats[0] * y
             return prev, tuple(new)

time: 76.9 us -> 75.4 us (0.980)
  Pallas kernels: 25.1 us -> 23.7 us
    pallas_call x1, Pallas kernels: 15.4 us -> 14.3 us  [run_out(): pl.pallas_call(out_kernel, grid=(width // BLOCK,), in_specs=[pl.BlockSpec...]
where the time goes in v7:
time: 75.4 us; the launch traced here: 74.3 us
  Pallas kernels  23.7 us (31%)
  starting transfers between devices  21.8 us (29%)
  waiting for transfers between devices  21.7 us (29%)
  other arithmetic  5.36 us (7%)
  local copies, waits for them, and re-layouts  1.6 us (2%)
    ppermute x9, starting transfers between devices, shift(): return lax.ppermute(value, axes, pairs)  21.8 us
    ppermute x9, waiting for transfers between devices, shift(): return lax.ppermute(value, axes, pairs)  21.7 us
    pallas_call x1, Pallas kernels, run_out(): pl.pallas_call(out_kernel, grid=(width // BLOCK,), in_specs=[pl.BlockSpec...  14.3 us
    pallas_call x1, Pallas kernels, run_state(): pl.pallas_call(state_kernel, grid=(width // BLOCK,), in_specs=[pl.BlockSp...  9.32 us
    convert_element_type x3, other arithmetic, gather_window(): sent = value.astype(jnp.bfloat16)  2.32 us
  transfers between devices with their start and end apart: 9, of which 5 were waited for; matrix products, arithmetic and copies ran while one was open for 2% of the time, Pallas kernels for 13%

profile of v7, /device:TPU:16, one launch (start us, length us, event | category | flops | bytes accessed | tf_op | source)
XLA Modules:
  0.0 74.3 jit_solution(10582729813930610363)
XLA Ops:
  0.0 1.1 %slice_convert_fusion = (f32[2,3,4096]{2,0,1:T(2,128)S(1)}, bf16[2,3,4096]{2,0,1:T(2,128)(2,1)S(1)}) fusion(bf16[128,3,4096]{2,0,1:T(8,128)(2,1)} %param.5), kind=kLoop, calls=%fused_computation.12 | loop fusion | flops 24576 | bytes 245760 | tf_op jit(solution)/shard_map/convert_element_type | solution.py:224
  1.1 3.4 %collective-permute-start = (bf16[2,3,4096]{2,0,1:T(2,128)(2,1)S(1)}, bf16[2,3,4096]{2,0,1:T(2,128)(2,1)S(1)}, u32[]{:S(2)}, u32[]{:S(2)}) collective-permute-start(bf16[2,3,4096]{2,0,1:T(2,128)(2,1)S(1)} %get-tuple-element.14), channel_id=1, source_target_pairs={{0,1},{1,2},{2,3},{3,4},{4,5},{5,6},{6,7},{7,8},{8,9},{9,10},{10,1... | collective-permute-start | bytes 147464 | tf_op jit(solution)/shard_map/ppermute | solution.py:215
  4.6 0.9 %fusion.15 = (f32[1,3,4096]{2,1,0:T(4,128)S(1)}, f32[1,3,4096]{2,1,0:T(4,128)S(1)}, f32[1,3,4096]{2,1,0:T(4,128)S(1)}) fusion(f32[3,3,4096]{2,1,0:T(4,128)} %f_ref.3), kind=kLoop, calls=%fused_computation.32 | loop fusion | bytes 294912 | tf_op jit(solution)/shard_map/slice | solution.py:230
  5.5 0.7 broadcast_in_dim.2.halo_ref
  6.2 9.3 %shard_map.55 = (f32[16,8,4096]{2,1,0:T(8,128)}, f32[16,4096]{1,0:T(8,128)}) custom-call(bf16[3,128,4096]{2,1,0:T(8,128)(2,1)} %bitcast.14, f32[3,2,4096]{2,1,0:T(2,128)} %broadcast_in_dim.2.halo_ref, f32[3,3,4096]{2,1,0:T(4,128)} %f_ref.3, f32[16,4096]{1,0:T(8,128)} %bitcast.16), custom_call_target="tpu_custom_call" | custom-call | tf_op jit(solution)/shard_map/pallas_call | solution.py:151
  15.5 0.7 fusion.16
  16.2 0.2 multiply_add_fusion.4
  16.6 1.8 %add_convert_fusion = (bf16[16,4096]{1,0:T(8,128)(2,1)S(1)}, f32[16,4096]{1,0:T(8,128)}) fusion(f32[16,4096]{1,0:T(8,128)} %get-tuple-element.8, f32[4096]{0:T(1024)S(1)} %bitcast.19, f32[4096]{0:T(1024)S(1)} %bitcast.20, f32[4096,16]{0,1:T(8,128)S(1)} %copy-done), kind=kLoop, calls=%fused_computation.3 | loop fusion | flops 851968 | bytes 950272 | tf_op jit(solution)/shard_map/convert_element_type | solution.py:253
  18.4 3.0 %collective-permute-start.3 = (bf16[16,4096]{1,0:T(8,128)(2,1)S(1)}, bf16[16,4096]{1,0:T(8,128)(2,1)S(1)}, u32[]{:S(2)}, u32[]{:S(2)}) collective-permute-start(bf16[16,4096]{1,0:T(8,128)(2,1)S(1)} %get-tuple-element.16), channel_id=1, source_target_pairs={{0,3},{1,4},{2,5},{3,6},{4,7},{5,8},{6,9},{7,10},{8,11},{9,12},{10... | collective-permute-start | bytes 393224 | tf_op jit(solution)/shard_map/ppermute | solution.py:215
  21.5 1.9 %collective-permute-start.2 = (bf16[16,4096]{1,0:T(8,128)(2,1)S(1)}, bf16[16,4096]{1,0:T(8,128)(2,1)S(1)}, u32[]{:S(2)}, u32[]{:S(2)}) collective-permute-start(bf16[16,4096]{1,0:T(8,128)(2,1)S(1)} %get-tuple-element.16), channel_id=1, source_target_pairs={{0,2},{1,3},{2,4},{3,5},{4,6},{5,7},{6,8},{7,9},{8,10},{9,11},{10,... | collective-permute-start | bytes 393224 | tf_op jit(solution)/shard_map/ppermute | solution.py:215
  23.4 3.7 %collective-permute-start.1 = (bf16[16,4096]{1,0:T(8,128)(2,1)S(1)}, bf16[16,4096]{1,0:T(8,128)(2,1)S(1)}, u32[]{:S(2)}, u32[]{:S(2)}) collective-permute-start(bf16[16,4096]{1,0:T(8,128)(2,1)S(1)} %get-tuple-element.16), channel_id=1, source_target_pairs={{0,1},{1,2},{2,3},{3,4},{4,5},{5,6},{6,7},{7,8},{8,9},{9,10},{10,1... | collective-permute-start | bytes 393224 | tf_op jit(solution)/shard_map/ppermute | solution.py:215
  27.2 1.5 %collective-permute-done.2 = bf16[16,4096]{1,0:T(8,128)(2,1)S(1)} collective-permute-done((bf16[16,4096]{1,0:T(8,128)(2,1)S(1)}, bf16[16,4096]{1,0:T(8,128)(2,1)S(1)}, u32[]{:S(2)}, u32[]{:S(2)}) %collective-permute-start.2) | collective-permute-done | bytes 131104 | tf_op jit(solution)/shard_map/ppermute | solution.py:215
  28.7 3.3 %collective-permute-done.1 = bf16[16,4096]{1,0:T(8,128)(2,1)S(1)} collective-permute-done((bf16[16,4096]{1,0:T(8,128)(2,1)S(1)}, bf16[16,4096]{1,0:T(8,128)(2,1)S(1)}, u32[]{:S(2)}, u32[]{:S(2)}) %collective-permute-start.1) | collective-permute-done | bytes 131104 | tf_op jit(solution)/shard_map/ppermute | solution.py:215
  32.1 3.1 %collective-permute-start.6 = (bf16[16,4096]{1,0:T(8,128)(2,1)S(1)}, bf16[16,4096]{1,0:T(8,128)(2,1)S(1)}, u32[]{:S(2)}, u32[]{:S(2)}) collective-permute-start(bf16[16,4096]{1,0:T(8,128)(2,1)S(1)} %fusion.12), channel_id=1, source_target_pairs={{0,9},{1,10},{2,11},{3,12},{4,13},{5,14},{6,15},{7,16},{8,17},{9,1... | collective-permute-start | bytes 393224 | tf_op jit(solution)/shard_map/ppermute | solution.py:215
  35.2 2.1 %collective-permute-start.5 = (bf16[16,4096]{1,0:T(8,128)(2,1)S(1)}, bf16[16,4096]{1,0:T(8,128)(2,1)S(1)}, u32[]{:S(2)}, u32[]{:S(2)}) collective-permute-start(bf16[16,4096]{1,0:T(8,128)(2,1)S(1)} %fusion.12), channel_id=1, source_target_pairs={{0,6},{1,7},{2,8},{3,9},{4,10},{5,11},{6,12},{7,13},{8,14},{9,15},... | collective-permute-start | bytes 393224 | tf_op jit(solution)/shard_map/ppermute | solution.py:215
  37.4 1.9 %collective-permute-start.4 = (bf16[16,4096]{1,0:T(8,128)(2,1)S(1)}, bf16[16,4096]{1,0:T(8,128)(2,1)S(1)}, u32[]{:S(2)}, u32[]{:S(2)}) collective-permute-start(bf16[16,4096]{1,0:T(8,128)(2,1)S(1)} %fusion.12), channel_id=1, source_target_pairs={{0,3},{1,4},{2,5},{3,6},{4,7},{5,8},{6,9},{7,10},{8,11},{9,12},{10... | collective-permute-start | bytes 393224 | tf_op jit(solution)/shard_map/ppermute | solution.py:215
  39.3 2.9 %collective-permute-done.6 = bf16[16,4096]{1,0:T(8,128)(2,1)S(1)} collective-permute-done((bf16[16,4096]{1,0:T(8,128)(2,1)S(1)}, bf16[16,4096]{1,0:T(8,128)(2,1)S(1)}, u32[]{:S(2)}, u32[]{:S(2)}) %collective-permute-start.6) | collective-permute-done | bytes 131104 | tf_op jit(solution)/shard_map/ppermute | solution.py:215
  42.2 6.6 %collective-permute-done.4 = bf16[16,4096]{1,0:T(8,128)(2,1)S(1)} collective-permute-done((bf16[16,4096]{1,0:T(8,128)(2,1)S(1)}, bf16[16,4096]{1,0:T(8,128)(2,1)S(1)}, u32[]{:S(2)}, u32[]{:S(2)}) %collective-permute-start.4) | collective-permute-done | bytes 131104 | tf_op jit(solution)/shard_map/ppermute | solution.py:215
  48.8 0.3 fusion.13
  49.1 0.7 collective-permute-start.8
  49.8 1.9 %collective-permute-start.7 = (bf16[16,4096]{1,0:T(8,128)(2,1)S(1)}, bf16[16,4096]{1,0:T(8,128)(2,1)S(1)}, u32[]{:S(2)}, u32[]{:S(2)}) collective-permute-start(bf16[16,4096]{1,0:T(8,128)(2,1)S(1)} %get-tuple-element.9), channel_id=1, source_target_pairs={{0,12},{1,13},{2,14},{3,15},{4,16},{5,17},{6,18},{7,19},{8,20},{9,... | collective-permute-start | bytes 393224 | tf_op jit(solution)/shard_map/ppermute | solution.py:215
  51.7 7.4 %collective-permute-done.7 = bf16[16,4096]{1,0:T(8,128)(2,1)S(1)} collective-permute-done((bf16[16,4096]{1,0:T(8,128)(2,1)S(1)}, bf16[16,4096]{1,0:T(8,128)(2,1)S(1)}, u32[]{:S(2)}, u32[]{:S(2)}) %collective-permute-start.7) | collective-permute-done | bytes 131104 | tf_op jit(solution)/shard_map/ppermute | solution.py:215
  59.1 0.8 %multiply_add_fusion.hin_ref = f32[16,4096]{1,0:T(8,128)} fusion(f32[16,4096]{1,0:T(8,128)S(1)} %get-tuple-element.10, bf16[16,4096]{1,0:T(8,128)(2,1)S(1)} %collective-permute-done.8, bf16[16,4096]{1,0:T(8,128)(2,1)S(1)} %collective-permute-done.7, f32[4096,16]{0,1:T(8,128)S(1)} %copy-done), kind=kLoop, calls=%fused_computation | loop fusion | flops 655360 | bytes 1048576 | tf_op jit(solution)/shard_map/add | solution.py:267
  60.0 14.3 %shard_map.56 = bf16[128,4096]{1,0:T(8,128)(2,1)} custom-call(bf16[3,128,4096]{2,1,0:T(8,128)(2,1)} %bitcast.15, f32[3,2,4096]{2,1,0:T(2,128)} %get-tuple-element.23.halo_ref, f32[3,3,4096]{2,1,0:T(4,128)} %f_ref.3, f32[16,4096]{1,0:T(8,128)} %bitcast.17, f32[16,4096]{1,0:T(8,128)} %bitcast.18, f32[1,4096]{1,0:T(1,128)} %bitcast.21, ...), custom_call_target="tpu_custom_call" | custom-call | tf_op jit(solution)/shard_map/pallas_call | solution.py:180
  (9 shorter events, 0.3 us)
Async XLA Ops:
  0.0 16.6 %copy-start = (f32[4096,16]{0,1:T(8,128)S(1)}, f32[4096,16]{0,1:T(8,128)}, u32[]{:S(2)}) copy-start(f32[4096,16]{0,1:T(8,128)} %param.8) | copy-start | bytes 786436
  1.1 14.4 %collective-permute-start = (bf16[2,3,4096]{2,0,1:T(2,128)(2,1)S(1)}, bf16[2,3,4096]{2,0,1:T(2,128)(2,1)S(1)}, u32[]{:S(2)}, u32[]{:S(2)}) collective-permute-start(bf16[2,3,4096]{2,0,1:T(2,128)(2,1)S(1)} %get-tuple-element.14), channel_id=1, source_target_pairs={{0,1},{1,2},{2,3},{3,4},{4,5},{5,6},{6,7},{7,8},{8,9},{9,10},{10,1... | collective-permute-start | bytes 147464 | tf_op jit(solution)/shard_map/ppermute | solution.py:215
  18.4 8.7 %collective-permute-start.3 = (bf16[16,4096]{1,0:T(8,128)(2,1)S(1)}, bf16[16,4096]{1,0:T(8,128)(2,1)S(1)}, u32[]{:S(2)}, u32[]{:S(2)}) collective-permute-start(bf16[16,4096]{1,0:T(8,128)(2,1)S(1)} %get-tuple-element.16), channel_id=1, source_target_pairs={{0,3},{1,4},{2,5},{3,6},{4,7},{5,8},{6,9},{7,10},{8,11},{9,12},{10... | collective-permute-start | bytes 393224 | tf_op jit(solution)/shard_map/ppermute | solution.py:215
  21.5 7.2 %collective-permute-start.2 = (bf16[16,4096]{1,0:T(8,128)(2,1)S(1)}, bf16[16,4096]{1,0:T(8,128)(2,1)S(1)}, u32[]{:S(2)}, u32[]{:S(2)}) collective-permute-start(bf16[16,4096]{1,0:T(8,128)(2,1)S(1)} %get-tuple-element.16), channel_id=1, source_target_pairs={{0,2},{1,3},{2,4},{3,5},{4,6},{5,7},{6,8},{7,9},{8,10},{9,11},{10,... | collective-permute-start | bytes 393224 | tf_op jit(solution)/shard_map/ppermute | solution.py:215
  23.4 8.5 %collective-permute-start.1 = (bf16[16,4096]{1,0:T(8,128)(2,1)S(1)}, bf16[16,4096]{1,0:T(8,128)(2,1)S(1)}, u32[]{:S(2)}, u32[]{:S(2)}) collective-permute-start(bf16[16,4096]{1,0:T(8,128)(2,1)S(1)} %get-tuple-element.16), channel_id=1, source_target_pairs={{0,1},{1,2},{2,3},{3,4},{4,5},{5,6},{6,7},{7,8},{8,9},{9,10},{10,1... | collective-permute-start | bytes 393224 | tf_op jit(solution)/shard_map/ppermute | solution.py:215
  32.1 10.0 %collective-permute-start.6 = (bf16[16,4096]{1,0:T(8,128)(2,1)S(1)}, bf16[16,4096]{1,0:T(8,128)(2,1)S(1)}, u32[]{:S(2)}, u32[]{:S(2)}) collective-permute-start(bf16[16,4096]{1,0:T(8,128)(2,1)S(1)} %fusion.12), channel_id=1, source_target_pairs={{0,9},{1,10},{2,11},{3,12},{4,13},{5,14},{6,15},{7,16},{8,17},{9,1... | collective-permute-start | bytes 393224 | tf_op jit(solution)/shard_map/ppermute | solution.py:215
  35.2 7.0 %collective-permute-start.5 = (bf16[16,4096]{1,0:T(8,128)(2,1)S(1)}, bf16[16,4096]{1,0:T(8,128)(2,1)S(1)}, u32[]{:S(2)}, u32[]{:S(2)}) collective-permute-start(bf16[16,4096]{1,0:T(8,128)(2,1)S(1)} %fusion.12), channel_id=1, source_target_pairs={{0,6},{1,7},{2,8},{3,9},{4,10},{5,11},{6,12},{7,13},{8,14},{9,15},... | collective-permute-start | bytes 393224 | tf_op jit(solution)/shard_map/ppermute | solution.py:215
  37.4 11.4 %collective-permute-start.4 = (bf16[16,4096]{1,0:T(8,128)(2,1)S(1)}, bf16[16,4096]{1,0:T(8,128)(2,1)S(1)}, u32[]{:S(2)}, u32[]{:S(2)}) collective-permute-start(bf16[16,4096]{1,0:T(8,128)(2,1)S(1)} %fusion.12), channel_id=1, source_target_pairs={{0,3},{1,4},{2,5},{3,6},{4,7},{5,8},{6,9},{7,10},{8,11},{9,12},{10... | collective-permute-start | bytes 393224 | tf_op jit(solution)/shard_map/ppermute | solution.py:215
  49.1 2.6 %collective-permute-start.8 = (bf16[16,4096]{1,0:T(8,128)(2,1)S(1)}, bf16[16,4096]{1,0:T(8,128)(2,1)S(1)}, u32[]{:S(2)}, u32[]{:S(2)}) collective-permute-start(bf16[16,4096]{1,0:T(8,128)(2,1)S(1)} %get-tuple-element.9), channel_id=1, source_target_pairs={{0,24},{1,25},{2,26},{3,27},{4,28},{5,29},{6,30},{7,31}} | collective-permute-start | bytes 393224 | tf_op jit(solution)/shard_map/ppermute | solution.py:215
  49.8 9.4 %collective-permute-start.7 = (bf16[16,4096]{1,0:T(8,128)(2,1)S(1)}, bf16[16,4096]{1,0:T(8,128)(2,1)S(1)}, u32[]{:S(2)}, u32[]{:S(2)}) collective-permute-start(bf16[16,4096]{1,0:T(8,128)(2,1)S(1)} %get-tuple-element.9), channel_id=1, source_target_pairs={{0,12},{1,13},{2,14},{3,15},{4,16},{5,17},{6,18},{7,19},{8,20},{9,... | collective-permute-start | bytes 393224 | tf_op jit(solution)/shard_map/ppermute | solution.py:215

commit v8 on v7

--- a/solution.py
+++ b/solution.py
@@ -39,12 +39,15 @@
             fsc[tap * streams_count + s] = row(f_ref.at[tap], s, lanes)
 
 
-def step_features(xs, fsc, c, seg, j, prev):
+def step_features(xs, fsc, c, seg, j, prev, first=0):
     streams_count = xs.shape[0]
     taps = len(prev) + 1
-    now = [xs[s, c, pl.ds(j, SUB, stride=seg), :] for s in range(streams_count)]
+    now = [xs[s, c, pl.ds(j, SUB, stride=seg), :] if s >= first else prev[0][s] for s in range(streams_count)]
     feats = []
     for s in range(streams_count):
+        if s < first:
+            feats.append(None)
+            continue
         acc = fsc[s] * now[s]
         for tap in range(1, taps):
             acc = acc + fsc[tap * streams_count + s] * prev[tap - 1][s]
@@ -57,7 +60,7 @@
     return (feats[1] * feats[2]).astype(jnp.bfloat16).astype(jnp.float32)
 
 
-def state_kernel(x_ref, halo_ref, f_ref, a_ref, seg_ref, h_ref, xs, dsc, fsc):
+def state_kernel(x_ref, halo_ref, f_ref, a_ref, decay_ref, seg_ref, h_ref, xs, dsc, fsc):
     streams_count, rows, block = x_ref.shape
     taps = f_ref.shape[0]
     modes = a_ref.shape[0]
@@ -70,11 +73,11 @@
         lanes = lane_slice(c)
         fill_filters(f_ref, fsc, lanes)
         for m in range(modes):
-            dsc[m] = jnp.exp(-row(a_ref, m, lanes))
+            dsc[m] = row(decay_ref, m, lanes)
 
         def step(j, state):
             prev, states = state
-            feats, prev = step_features(xs, fsc, c, seg, j, prev)
+            feats, prev = step_features(xs, fsc, c, seg, j, prev, first=1)
             u = gate(feats)
             return prev, tuple(dsc[m] * states[m] + u for m in range(modes))
 
@@ -92,7 +95,7 @@
 
 
 def out_kernel(
-    x_ref, halo_ref, f_ref, a_ref, r_ref, skip_ref, seg_ref, fix_ref, hin_ref, o_ref, xs, ys, dsc, rsc, fsc
+    x_ref, halo_ref, f_ref, a_ref, decay_ref, r_ref, skip_ref, seg_ref, fix_ref, hin_ref, o_ref, xs, ys, dsc, rsc, fsc
 ):
     streams_count, rows, block = x_ref.shape
     taps = f_ref.shape[0]
@@ -108,7 +111,7 @@
         starts = []
         for m in range(modes):
             rate = row(a_ref, m, lanes)
-            dsc[m] = jnp.exp(-rate)
+            dsc[m] = row(decay_ref, m, lanes)
             rsc[m] = row(r_ref, m, lanes)
             ends = seg_ref[m, :, lanes] + jnp.where(sub == 0, row(fix_ref, m, lanes), 0.0)
             carried = jnp.where(sub >= 1, pltpu.roll(ends, 1, 0), 0.0)
@@ -144,7 +147,7 @@
         o_ref[:, c * LANES : (c + 1) * LANES] = ys[c].astype(o_ref.dtype)
 
 
-def run_state(x, halo, f, rate_t):
+def run_state(x, halo, f, rate_t, decay):
     streams_count, rows, width = x.shape
     taps = f.shape[0]
     modes = rate_t.shape[0]
@@ -156,6 +159,7 @@
             pl.BlockSpec((streams_count, taps - 1, BLOCK), lambda i: (0, 0, i)),
             pl.BlockSpec((taps, streams_count, BLOCK), lambda i: (0, 0, i)),
             pl.BlockSpec((modes, BLOCK), lambda i: (0, i)),
+            pl.BlockSpec((modes, BLOCK), lambda i: (0, i)),
         ],
         out_specs=[
             pl.BlockSpec((modes, SUB, BLOCK), lambda i: (0, 0, i)),
@@ -170,10 +174,10 @@
             pltpu.VMEM((modes, SUB, LANES), jnp.float32),
             pltpu.VMEM((taps * streams_count, SUB, LANES), jnp.float32),
         ],
-    )(x, halo, f, rate_t)
-
-
-def run_out(x, halo, f, rate_t, residue_t, skip, ends, fix, hin):
+    )(x, halo, f, rate_t, decay)
+
+
+def run_out(x, halo, f, rate_t, decay, residue_t, skip, ends, fix, hin):
     streams_count, rows, width = x.shape
     taps = f.shape[0]
     modes = rate_t.shape[0]
@@ -186,6 +190,7 @@
             pl.BlockSpec((taps, streams_count, BLOCK), lambda i: (0, 0, i)),
             pl.BlockSpec((modes, BLOCK), lambda i: (0, i)),
             pl.BlockSpec((modes, BLOCK), lambda i: (0, i)),
+            pl.BlockSpec((modes, BLOCK), lambda i: (0, i)),
             pl.BlockSpec((1, BLOCK), lambda i: (0, i)),
             pl.BlockSpec((modes, SUB, BLOCK), lambda i: (0, 0, i)),
             pl.BlockSpec((modes, BLOCK), lambda i: (0, i)),
@@ -200,7 +205,7 @@
             pltpu.VMEM((modes, SUB, LANES), jnp.float32),
             pltpu.VMEM((taps * streams_count, SUB, LANES), jnp.float32),
         ],
-    )(x, halo, f, rate_t, residue_t, skip, ends, fix, hin)
+    )(x, halo, f, rate_t, decay, residue_t, skip, ends, fix, hin)
 
 
 def body(streams, short_filter, skip, rates, residues):
@@ -219,7 +224,8 @@
     x = jnp.transpose(streams, (1, 0, 2))
     rate_t = rates.T
     residue_t = residues.T
-    ends, local = run_state(x, jnp.zeros_like(halo), short_filter, rate_t)
+    decay = jnp.exp(-rate_t)
+    ends, local = run_state(x, jnp.zeros_like(halo), short_filter, rate_t, decay)
 
     head = streams[: taps - 1].astype(jnp.float32)
 
@@ -267,7 +273,7 @@
         carried = carried + decay_pow(window) * gather_window(carried, window, count)
         window *= count + 1
 
-    return run_out(x, halo, short_filter, rate_t, residue_t, skip.reshape(1, width), ends, ends_fix, carried)
+    return run_out(x, halo, short_filter, rate_t, decay, residue_t, skip.reshape(1, width), ends, ends_fix, carried)
 
 
 def solution(mesh):

time: 75.4 us -> 76.8 us (1.019)
  other arithmetic: 5.36 us -> 7.03 us
    exp x0 -> x1, other arithmetic: none -> 1.7 us  [body(): decay = jnp.exp(-rate_t)]
  transfers between devices with their start and end apart: 9 -> 9, of which waited for: 5 -> 5; matrix products, arithmetic and copies ran while one was open for 2% -> 4% of each run, Pallas kernels for 13% -> 12%
where the time goes in v8:
time: 76.8 us; the launch traced here: 75.6 us
  Pallas kernels  23.2 us (30%)
  starting transfers between devices  21.9 us (29%)
  waiting for transfers between devices  21.7 us (28%)
  other arithmetic  7.03 us (9%)
  local copies, waits for them, and re-layouts  1.6 us (2%)
    ppermute x9, starting transfers between devices, shift(): return lax.ppermute(value, axes, pairs)  21.9 us
    ppermute x9, waiting for transfers between devices, shift(): return lax.ppermute(value, axes, pairs)  21.7 us
    pallas_call x1, Pallas kernels, run_out(): pl.pallas_call(out_kernel, grid=(width // BLOCK,), in_specs=[pl.BlockSpec...  13.9 us
    pallas_call x1, Pallas kernels, run_state(): pl.pallas_call(state_kernel, grid=(width // BLOCK,), in_specs=[pl.BlockSp...  9.26 us
    convert_element_type x3, other arithmetic, gather_window(): sent = value.astype(jnp.bfloat16)  2.32 us
    exp x1, other arithmetic, body(): decay = jnp.exp(-rate_t)  1.7 us
  transfers between devices with their start and end apart: 9, of which 5 were waited for; matrix products, arithmetic and copies ran while one was open for 4% of the time, Pallas kernels for 12%

profile of v8, /device:TPU:16, one launch (start us, length us, event | category | flops | bytes accessed | tf_op | source)
XLA Modules:
  0.0 75.6 jit_solution(17633868265754414310)
XLA Ops:
  0.0 1.1 %slice_convert_fusion = (f32[2,3,4096]{2,0,1:T(2,128)S(1)}, bf16[2,3,4096]{2,0,1:T(2,128)(2,1)S(1)}) fusion(bf16[128,3,4096]{2,0,1:T(8,128)(2,1)} %param.5), kind=kLoop, calls=%fused_computation.13 | loop fusion | flops 24576 | bytes 245760 | tf_op jit(solution)/shard_map/convert_element_type | solution.py:230
  1.1 3.6 %collective-permute-start = (bf16[2,3,4096]{2,0,1:T(2,128)(2,1)S(1)}, bf16[2,3,4096]{2,0,1:T(2,128)(2,1)S(1)}, u32[]{:S(2)}, u32[]{:S(2)}) collective-permute-start(bf16[2,3,4096]{2,0,1:T(2,128)(2,1)S(1)} %get-tuple-element.14), channel_id=1, source_target_pairs={{0,1},{1,2},{2,3},{3,4},{4,5},{5,6},{6,7},{7,8},{8,9},{9,10},{10,1... | collective-permute-start | bytes 147464 | tf_op jit(solution)/shard_map/ppermute | solution.py:220
  4.7 1.7 %negate_exponential_fusion.decay_ref = f32[16,4096]{1,0:T(8,128)} fusion(f32[4096,16]{0,1:T(8,128)} %param.8), kind=kLoop, calls=%fused_computation.6 | loop fusion | flops 65536 | bytes 524288 | tf_op jit(solution)/shard_map/exp | solution.py:227
  6.4 0.9 %fusion.15 = (f32[1,3,4096]{2,1,0:T(4,128)S(1)}, f32[1,3,4096]{2,1,0:T(4,128)S(1)}, f32[1,3,4096]{2,1,0:T(4,128)S(1)}) fusion(f32[3,3,4096]{2,1,0:T(4,128)} %f_ref.3), kind=kLoop, calls=%fused_computation.33 | loop fusion | bytes 294912 | tf_op jit(solution)/shard_map/slice | solution.py:236
  7.3 0.7 broadcast_in_dim.2.halo_ref
  8.0 9.3 %shard_map.55 = (f32[16,8,4096]{2,1,0:T(8,128)}, f32[16,4096]{1,0:T(8,128)}) custom-call(bf16[3,128,4096]{2,1,0:T(8,128)(2,1)} %bitcast.15, f32[3,2,4096]{2,1,0:T(2,128)} %broadcast_in_dim.2.halo_ref, f32[3,3,4096]{2,1,0:T(4,128)} %f_ref.3, f32[16,4096]{1,0:T(8,128)} %bitcast.17, f32[16,4096]{1,0:T(8,128)} %negate_exponential_fusion.decay_ref), custom_call_target="tpu_custom_call" | custom-call | tf_op jit(solution)/shard_map/pallas_call | solution.py:154
  17.2 0.7 fusion.16
  18.3 1.8 %add_convert_fusion = (bf16[16,4096]{1,0:T(8,128)(2,1)S(1)}, f32[16,4096]{1,0:T(8,128)}) fusion(f32[16,4096]{1,0:T(8,128)} %get-tuple-element.8, f32[4096]{0:T(1024)S(1)} %bitcast.20, f32[4096]{0:T(1024)S(1)} %bitcast.21, f32[4096,16]{0,1:T(8,128)S(1)} %copy-done), kind=kLoop, calls=%fused_computation.3 | loop fusion | flops 851968 | bytes 950272 | tf_op jit(solution)/shard_map/convert_element_type | solution.py:259
  20.2 3.0 %collective-permute-start.3 = (bf16[16,4096]{1,0:T(8,128)(2,1)S(1)}, bf16[16,4096]{1,0:T(8,128)(2,1)S(1)}, u32[]{:S(2)}, u32[]{:S(2)}) collective-permute-start(bf16[16,4096]{1,0:T(8,128)(2,1)S(1)} %get-tuple-element.16), channel_id=1, source_target_pairs={{0,3},{1,4},{2,5},{3,6},{4,7},{5,8},{6,9},{7,10},{8,11},{9,12},{10... | collective-permute-start | bytes 393224 | tf_op jit(solution)/shard_map/ppermute | solution.py:220
  23.2 1.9 %collective-permute-start.2 = (bf16[16,4096]{1,0:T(8,128)(2,1)S(1)}, bf16[16,4096]{1,0:T(8,128)(2,1)S(1)}, u32[]{:S(2)}, u32[]{:S(2)}) collective-permute-start(bf16[16,4096]{1,0:T(8,128)(2,1)S(1)} %get-tuple-element.16), channel_id=1, source_target_pairs={{0,2},{1,3},{2,4},{3,5},{4,6},{5,7},{6,8},{7,9},{8,10},{9,11},{10,... | collective-permute-start | bytes 393224 | tf_op jit(solution)/shard_map/ppermute | solution.py:220
  25.2 3.7 %collective-permute-start.1 = (bf16[16,4096]{1,0:T(8,128)(2,1)S(1)}, bf16[16,4096]{1,0:T(8,128)(2,1)S(1)}, u32[]{:S(2)}, u32[]{:S(2)}) collective-permute-start(bf16[16,4096]{1,0:T(8,128)(2,1)S(1)} %get-tuple-element.16), channel_id=1, source_target_pairs={{0,1},{1,2},{2,3},{3,4},{4,5},{5,6},{6,7},{7,8},{8,9},{9,10},{10,1... | collective-permute-start | bytes 393224 | tf_op jit(solution)/shard_map/ppermute | solution.py:220
  28.9 1.5 %collective-permute-done.2 = bf16[16,4096]{1,0:T(8,128)(2,1)S(1)} collective-permute-done((bf16[16,4096]{1,0:T(8,128)(2,1)S(1)}, bf16[16,4096]{1,0:T(8,128)(2,1)S(1)}, u32[]{:S(2)}, u32[]{:S(2)}) %collective-permute-start.2) | collective-permute-done | bytes 131104 | tf_op jit(solution)/shard_map/ppermute | solution.py:220
  30.4 3.3 %collective-permute-done.1 = bf16[16,4096]{1,0:T(8,128)(2,1)S(1)} collective-permute-done((bf16[16,4096]{1,0:T(8,128)(2,1)S(1)}, bf16[16,4096]{1,0:T(8,128)(2,1)S(1)}, u32[]{:S(2)}, u32[]{:S(2)}) %collective-permute-start.1) | collective-permute-done | bytes 131104 | tf_op jit(solution)/shard_map/ppermute | solution.py:220
  33.9 3.1 %collective-permute-start.6 = (bf16[16,4096]{1,0:T(8,128)(2,1)S(1)}, bf16[16,4096]{1,0:T(8,128)(2,1)S(1)}, u32[]{:S(2)}, u32[]{:S(2)}) collective-permute-start(bf16[16,4096]{1,0:T(8,128)(2,1)S(1)} %fusion.12), channel_id=1, source_target_pairs={{0,9},{1,10},{2,11},{3,12},{4,13},{5,14},{6,15},{7,16},{8,17},{9,1... | collective-permute-start | bytes 393224 | tf_op jit(solution)/shard_map/ppermute | solution.py:220
  36.9 2.1 %collective-permute-start.5 = (bf16[16,4096]{1,0:T(8,128)(2,1)S(1)}, bf16[16,4096]{1,0:T(8,128)(2,1)S(1)}, u32[]{:S(2)}, u32[]{:S(2)}) collective-permute-start(bf16[16,4096]{1,0:T(8,128)(2,1)S(1)} %fusion.12), channel_id=1, source_target_pairs={{0,6},{1,7},{2,8},{3,9},{4,10},{5,11},{6,12},{7,13},{8,14},{9,15},... | collective-permute-start | bytes 393224 | tf_op jit(solution)/shard_map/ppermute | solution.py:220
  39.1 1.9 %collective-permute-start.4 = (bf16[16,4096]{1,0:T(8,128)(2,1)S(1)}, bf16[16,4096]{1,0:T(8,128)(2,1)S(1)}, u32[]{:S(2)}, u32[]{:S(2)}) collective-permute-start(bf16[16,4096]{1,0:T(8,128)(2,1)S(1)} %fusion.12), channel_id=1, source_target_pairs={{0,3},{1,4},{2,5},{3,6},{4,7},{5,8},{6,9},{7,10},{8,11},{9,12},{10... | collective-permute-start | bytes 393224 | tf_op jit(solution)/shard_map/ppermute | solution.py:220
  41.0 2.9 %collective-permute-done.6 = bf16[16,4096]{1,0:T(8,128)(2,1)S(1)} collective-permute-done((bf16[16,4096]{1,0:T(8,128)(2,1)S(1)}, bf16[16,4096]{1,0:T(8,128)(2,1)S(1)}, u32[]{:S(2)}, u32[]{:S(2)}) %collective-permute-start.6) | collective-permute-done | bytes 131104 | tf_op jit(solution)/shard_map/ppermute | solution.py:220
  43.9 6.6 %collective-permute-done.4 = bf16[16,4096]{1,0:T(8,128)(2,1)S(1)} collective-permute-done((bf16[16,4096]{1,0:T(8,128)(2,1)S(1)}, bf16[16,4096]{1,0:T(8,128)(2,1)S(1)}, u32[]{:S(2)}, u32[]{:S(2)}) %collective-permute-start.4) | collective-permute-done | bytes 131104 | tf_op jit(solution)/shard_map/ppermute | solution.py:220
  50.5 0.3 fusion.13
  50.8 0.7 collective-permute-start.8
  51.5 1.9 %collective-permute-start.7 = (bf16[16,4096]{1,0:T(8,128)(2,1)S(1)}, bf16[16,4096]{1,0:T(8,128)(2,1)S(1)}, u32[]{:S(2)}, u32[]{:S(2)}) collective-permute-start(bf16[16,4096]{1,0:T(8,128)(2,1)S(1)} %get-tuple-element.9), channel_id=1, source_target_pairs={{0,12},{1,13},{2,14},{3,15},{4,16},{5,17},{6,18},{7,19},{8,20},{9,... | collective-permute-start | bytes 393224 | tf_op jit(solution)/shard_map/ppermute | solution.py:220
  53.4 7.4 %collective-permute-done.7 = bf16[16,4096]{1,0:T(8,128)(2,1)S(1)} collective-permute-done((bf16[16,4096]{1,0:T(8,128)(2,1)S(1)}, bf16[16,4096]{1,0:T(8,128)(2,1)S(1)}, u32[]{:S(2)}, u32[]{:S(2)}) %collective-permute-start.7) | collective-permute-done | bytes 131104 | tf_op jit(solution)/shard_map/ppermute | solution.py:220
  60.9 0.9 %multiply_add_fusion.hin_ref = f32[16,4096]{1,0:T(8,128)} fusion(f32[16,4096]{1,0:T(8,128)S(1)} %get-tuple-element.10, bf16[16,4096]{1,0:T(8,128)(2,1)S(1)} %collective-permute-done.8, bf16[16,4096]{1,0:T(8,128)(2,1)S(1)} %collective-permute-done.7, f32[4096,16]{0,1:T(8,128)S(1)} %copy-done), kind=kLoop, calls=%fused_computation | loop fusion | flops 655360 | bytes 1048576 | tf_op jit(solution)/shard_map/add | solution.py:273
  61.7 13.9 %shard_map.56 = bf16[128,4096]{1,0:T(8,128)(2,1)} custom-call(bf16[3,128,4096]{2,1,0:T(8,128)(2,1)} %bitcast.16, f32[3,2,4096]{2,1,0:T(2,128)} %get-tuple-element.23.halo_ref, f32[3,3,4096]{2,1,0:T(4,128)} %f_ref.3, f32[16,4096]{1,0:T(8,128)} %bitcast.18, f32[16,4096]{1,0:T(8,128)} %negate_exponential_fusion.decay_ref, f32[16,4096]{1,0:T(8,128)} %bitcast.19, ...), custom_call_target="tpu_custom_call" | custom-call | tf_op jit(solution)/shard_map/pallas_call | solution.py:184
  (10 shorter events, 0.6 us)
Async XLA Ops:
  1.1 17.2 %copy-start = (f32[4096,16]{0,1:T(8,128)S(1)}, f32[4096,16]{0,1:T(8,128)}, u32[]{:S(2)}) copy-start(f32[4096,16]{0,1:T(8,128)} %param.8) | copy-start | bytes 786436
  1.1 16.1 %collective-permute-start = (bf16[2,3,4096]{2,0,1:T(2,128)(2,1)S(1)}, bf16[2,3,4096]{2,0,1:T(2,128)(2,1)S(1)}, u32[]{:S(2)}, u32[]{:S(2)}) collective-permute-start(bf16[2,3,4096]{2,0,1:T(2,128)(2,1)S(1)} %get-tuple-element.14), channel_id=1, source_target_pairs={{0,1},{1,2},{2,3},{3,4},{4,5},{5,6},{6,7},{7,8},{8,9},{9,10},{10,1... | collective-permute-start | bytes 147464 | tf_op jit(solution)/shard_map/ppermute | solution.py:220
  20.2 8.7 %collective-permute-start.3 = (bf16[16,4096]{1,0:T(8,128)(2,1)S(1)}, bf16[16,4096]{1,0:T(8,128)(2,1)S(1)}, u32[]{:S(2)}, u32[]{:S(2)}) collective-permute-start(bf16[16,4096]{1,0:T(8,128)(2,1)S(1)} %get-tuple-element.16), channel_id=1, source_target_pairs={{0,3},{1,4},{2,5},{3,6},{4,7},{5,8},{6,9},{7,10},{8,11},{9,12},{10... | collective-permute-start | bytes 393224 | tf_op jit(solution)/shard_map/ppermute | solution.py:220
  23.2 7.2 %collective-permute-start.2 = (bf16[16,4096]{1,0:T(8,128)(2,1)S(1)}, bf16[16,4096]{1,0:T(8,128)(2,1)S(1)}, u32[]{:S(2)}, u32[]{:S(2)}) collective-permute-start(bf16[16,4096]{1,0:T(8,128)(2,1)S(1)} %get-tuple-element.16), channel_id=1, source_target_pairs={{0,2},{1,3},{2,4},{3,5},{4,6},{5,7},{6,8},{7,9},{8,10},{9,11},{10,... | collective-permute-start | bytes 393224 | tf_op jit(solution)/shard_map/ppermute | solution.py:220
  25.2 8.5 %collective-permute-start.1 = (bf16[16,4096]{1,0:T(8,128)(2,1)S(1)}, bf16[16,4096]{1,0:T(8,128)(2,1)S(1)}, u32[]{:S(2)}, u32[]{:S(2)}) collective-permute-start(bf16[16,4096]{1,0:T(8,128)(2,1)S(1)} %get-tuple-element.16), channel_id=1, source_target_pairs={{0,1},{1,2},{2,3},{3,4},{4,5},{5,6},{6,7},{7,8},{8,9},{9,10},{10,1... | collective-permute-start | bytes 393224 | tf_op jit(solution)/shard_map/ppermute | solution.py:220
  33.9 10.0 %collective-permute-start.6 = (bf16[16,4096]{1,0:T(8,128)(2,1)S(1)}, bf16[16,4096]{1,0:T(8,128)(2,1)S(1)}, u32[]{:S(2)}, u32[]{:S(2)}) collective-permute-start(bf16[16,4096]{1,0:T(8,128)(2,1)S(1)} %fusion.12), channel_id=1, source_target_pairs={{0,9},{1,10},{2,11},{3,12},{4,13},{5,14},{6,15},{7,16},{8,17},{9,1... | collective-permute-start | bytes 393224 | tf_op jit(solution)/shard_map/ppermute | solution.py:220
  36.9 7.0 %collective-permute-start.5 = (bf16[16,4096]{1,0:T(8,128)(2,1)S(1)}, bf16[16,4096]{1,0:T(8,128)(2,1)S(1)}, u32[]{:S(2)}, u32[]{:S(2)}) collective-permute-start(bf16[16,4096]{1,0:T(8,128)(2,1)S(1)} %fusion.12), channel_id=1, source_target_pairs={{0,6},{1,7},{2,8},{3,9},{4,10},{5,11},{6,12},{7,13},{8,14},{9,15},... | collective-permute-start | bytes 393224 | tf_op jit(solution)/shard_map/ppermute | solution.py:220
  39.1 11.4 %collective-permute-start.4 = (bf16[16,4096]{1,0:T(8,128)(2,1)S(1)}, bf16[16,4096]{1,0:T(8,128)(2,1)S(1)}, u32[]{:S(2)}, u32[]{:S(2)}) collective-permute-start(bf16[16,4096]{1,0:T(8,128)(2,1)S(1)} %fusion.12), channel_id=1, source_target_pairs={{0,3},{1,4},{2,5},{3,6},{4,7},{5,8},{6,9},{7,10},{8,11},{9,12},{10... | collective-permute-start | bytes 393224 | tf_op jit(solution)/shard_map/ppermute | solution.py:220
  50.8 2.6 %collective-permute-start.8 = (bf16[16,4096]{1,0:T(8,128)(2,1)S(1)}, bf16[16,4096]{1,0:T(8,128)(2,1)S(1)}, u32[]{:S(2)}, u32[]{:S(2)}) collective-permute-start(bf16[16,4096]{1,0:T(8,128)(2,1)S(1)} %get-tuple-element.9), channel_id=1, source_target_pairs={{0,24},{1,25},{2,26},{3,27},{4,28},{5,29},{6,30},{7,31}} | collective-permute-start | bytes 393224 | tf_op jit(solution)/shard_map/ppermute | solution.py:220
  51.5 9.4 %collective-permute-start.7 = (bf16[16,4096]{1,0:T(8,128)(2,1)S(1)}, bf16[16,4096]{1,0:T(8,128)(2,1)S(1)}, u32[]{:S(2)}, u32[]{:S(2)}) collective-permute-start(bf16[16,4096]{1,0:T(8,128)(2,1)S(1)} %get-tuple-element.9), channel_id=1, source_target_pairs={{0,12},{1,13},{2,14},{3,15},{4,16},{5,17},{6,18},{7,19},{8,20},{9,... | collective-permute-start | bytes 393224 | tf_op jit(solution)/shard_map/ppermute | solution.py:220

commit v9 on v7

--- a/solution.py
+++ b/solution.py
@@ -7,7 +7,7 @@
 
 LANES = 128
 SUB = 8
-BLOCK = 512
+BLOCK = 1024
 FIRST_WINDOW = 3
 UNROLL = 8
 

time: 75.4 us -> 74.6 us (0.989)
    pallas_call x1, Pallas kernels: 9.32 us -> 8.53 us  [run_state(): pl.pallas_call(state_kernel, grid=(width // BLOCK,), in_specs=[pl.BlockSp...]
  transfers between devices with their start and end apart: 9 -> 9, of which waited for: 5 -> 5; matrix products, arithmetic and copies ran while one was open for 2% -> 2% of each run, Pallas kernels for 13% -> 12%
where the time goes in v9:
time: 74.6 us; the launch traced here: 73.7 us
  Pallas kernels  23 us (31%)
  starting transfers between devices  21.8 us (29%)
  waiting for transfers between devices  21.7 us (29%)
  other arithmetic  5.36 us (7%)
  local copies, waits for them, and re-layouts  1.6 us (2%)
    ppermute x9, starting transfers between devices, shift(): return lax.ppermute(value, axes, pairs)  21.8 us
    ppermute x9, waiting for transfers between devices, shift(): return lax.ppermute(value, axes, pairs)  21.7 us
    pallas_call x1, Pallas kernels, run_out(): pl.pallas_call(out_kernel, grid=(width // BLOCK,), in_specs=[pl.BlockSpec...  14.5 us
    pallas_call x1, Pallas kernels, run_state(): pl.pallas_call(state_kernel, grid=(width // BLOCK,), in_specs=[pl.BlockSp...  8.53 us
    convert_element_type x3, other arithmetic, gather_window(): sent = value.astype(jnp.bfloat16)  2.32 us
  transfers between devices with their start and end apart: 9, of which 5 were waited for; matrix products, arithmetic and copies ran while one was open for 2% of the time, Pallas kernels for 12%

profile of v9, /device:TPU:16, one launch (start us, length us, event | category | flops | bytes accessed | tf_op | source)
XLA Modules:
  0.0 73.7 jit_solution(900444565548655857)
XLA Ops:
  0.0 1.1 %slice_convert_fusion = (f32[2,3,4096]{2,0,1:T(2,128)S(1)}, bf16[2,3,4096]{2,0,1:T(2,128)(2,1)S(1)}) fusion(bf16[128,3,4096]{2,0,1:T(8,128)(2,1)} %param.5), kind=kLoop, calls=%fused_computation.12 | loop fusion | flops 24576 | bytes 245760 | tf_op jit(solution)/shard_map/convert_element_type | solution.py:224
  1.1 3.4 %collective-permute-start = (bf16[2,3,4096]{2,0,1:T(2,128)(2,1)S(1)}, bf16[2,3,4096]{2,0,1:T(2,128)(2,1)S(1)}, u32[]{:S(2)}, u32[]{:S(2)}) collective-permute-start(bf16[2,3,4096]{2,0,1:T(2,128)(2,1)S(1)} %get-tuple-element.14), channel_id=1, source_target_pairs={{0,1},{1,2},{2,3},{3,4},{4,5},{5,6},{6,7},{7,8},{8,9},{9,10},{10,1... | collective-permute-start | bytes 147464 | tf_op jit(solution)/shard_map/ppermute | solution.py:215
  4.6 0.9 %fusion.15 = (f32[1,3,4096]{2,1,0:T(4,128)S(1)}, f32[1,3,4096]{2,1,0:T(4,128)S(1)}, f32[1,3,4096]{2,1,0:T(4,128)S(1)}) fusion(f32[3,3,4096]{2,1,0:T(4,128)} %f_ref.3), kind=kLoop, calls=%fused_computation.32 | loop fusion | bytes 294912 | tf_op jit(solution)/shard_map/slice | solution.py:230
  5.5 0.7 broadcast_in_dim.2.halo_ref
  6.2 8.5 %shard_map.55 = (f32[16,8,4096]{2,1,0:T(8,128)}, f32[16,4096]{1,0:T(8,128)}) custom-call(bf16[3,128,4096]{2,1,0:T(8,128)(2,1)} %bitcast.14, f32[3,2,4096]{2,1,0:T(2,128)} %broadcast_in_dim.2.halo_ref, f32[3,3,4096]{2,1,0:T(4,128)} %f_ref.3, f32[16,4096]{1,0:T(8,128)} %bitcast.16), custom_call_target="tpu_custom_call" | custom-call | tf_op jit(solution)/shard_map/pallas_call | solution.py:151
  14.7 0.7 fusion.16
  15.4 0.2 multiply_add_fusion.4
  15.8 1.8 %add_convert_fusion = (bf16[16,4096]{1,0:T(8,128)(2,1)S(1)}, f32[16,4096]{1,0:T(8,128)}) fusion(f32[16,4096]{1,0:T(8,128)} %get-tuple-element.8, f32[4096]{0:T(1024)S(1)} %bitcast.19, f32[4096]{0:T(1024)S(1)} %bitcast.20, f32[4096,16]{0,1:T(8,128)S(1)} %copy-done), kind=kLoop, calls=%fused_computation.3 | loop fusion | flops 851968 | bytes 950272 | tf_op jit(solution)/shard_map/convert_element_type | solution.py:253
  17.7 3.0 %collective-permute-start.3 = (bf16[16,4096]{1,0:T(8,128)(2,1)S(1)}, bf16[16,4096]{1,0:T(8,128)(2,1)S(1)}, u32[]{:S(2)}, u32[]{:S(2)}) collective-permute-start(bf16[16,4096]{1,0:T(8,128)(2,1)S(1)} %get-tuple-element.16), channel_id=1, source_target_pairs={{0,3},{1,4},{2,5},{3,6},{4,7},{5,8},{6,9},{7,10},{8,11},{9,12},{10... | collective-permute-start | bytes 393224 | tf_op jit(solution)/shard_map/ppermute | solution.py:215
  20.7 1.9 %collective-permute-start.2 = (bf16[16,4096]{1,0:T(8,128)(2,1)S(1)}, bf16[16,4096]{1,0:T(8,128)(2,1)S(1)}, u32[]{:S(2)}, u32[]{:S(2)}) collective-permute-start(bf16[16,4096]{1,0:T(8,128)(2,1)S(1)} %get-tuple-element.16), channel_id=1, source_target_pairs={{0,2},{1,3},{2,4},{3,5},{4,6},{5,7},{6,8},{7,9},{8,10},{9,11},{10,... | collective-permute-start | bytes 393224 | tf_op jit(solution)/shard_map/ppermute | solution.py:215
  22.6 3.7 %collective-permute-start.1 = (bf16[16,4096]{1,0:T(8,128)(2,1)S(1)}, bf16[16,4096]{1,0:T(8,128)(2,1)S(1)}, u32[]{:S(2)}, u32[]{:S(2)}) collective-permute-start(bf16[16,4096]{1,0:T(8,128)(2,1)S(1)} %get-tuple-element.16), channel_id=1, source_target_pairs={{0,1},{1,2},{2,3},{3,4},{4,5},{5,6},{6,7},{7,8},{8,9},{9,10},{10,1... | collective-permute-start | bytes 393224 | tf_op jit(solution)/shard_map/ppermute | solution.py:215
  26.4 1.5 %collective-permute-done.2 = bf16[16,4096]{1,0:T(8,128)(2,1)S(1)} collective-permute-done((bf16[16,4096]{1,0:T(8,128)(2,1)S(1)}, bf16[16,4096]{1,0:T(8,128)(2,1)S(1)}, u32[]{:S(2)}, u32[]{:S(2)}) %collective-permute-start.2) | collective-permute-done | bytes 131104 | tf_op jit(solution)/shard_map/ppermute | solution.py:215
  27.9 3.3 %collective-permute-done.1 = bf16[16,4096]{1,0:T(8,128)(2,1)S(1)} collective-permute-done((bf16[16,4096]{1,0:T(8,128)(2,1)S(1)}, bf16[16,4096]{1,0:T(8,128)(2,1)S(1)}, u32[]{:S(2)}, u32[]{:S(2)}) %collective-permute-start.1) | collective-permute-done | bytes 131104 | tf_op jit(solution)/shard_map/ppermute | solution.py:215
  31.3 3.1 %collective-permute-start.6 = (bf16[16,4096]{1,0:T(8,128)(2,1)S(1)}, bf16[16,4096]{1,0:T(8,128)(2,1)S(1)}, u32[]{:S(2)}, u32[]{:S(2)}) collective-permute-start(bf16[16,4096]{1,0:T(8,128)(2,1)S(1)} %fusion.12), channel_id=1, source_target_pairs={{0,9},{1,10},{2,11},{3,12},{4,13},{5,14},{6,15},{7,16},{8,17},{9,1... | collective-permute-start | bytes 393224 | tf_op jit(solution)/shard_map/ppermute | solution.py:215
  34.4 2.1 %collective-permute-start.5 = (bf16[16,4096]{1,0:T(8,128)(2,1)S(1)}, bf16[16,4096]{1,0:T(8,128)(2,1)S(1)}, u32[]{:S(2)}, u32[]{:S(2)}) collective-permute-start(bf16[16,4096]{1,0:T(8,128)(2,1)S(1)} %fusion.12), channel_id=1, source_target_pairs={{0,6},{1,7},{2,8},{3,9},{4,10},{5,11},{6,12},{7,13},{8,14},{9,15},... | collective-permute-start | bytes 393224 | tf_op jit(solution)/shard_map/ppermute | solution.py:215
  36.6 1.9 %collective-permute-start.4 = (bf16[16,4096]{1,0:T(8,128)(2,1)S(1)}, bf16[16,4096]{1,0:T(8,128)(2,1)S(1)}, u32[]{:S(2)}, u32[]{:S(2)}) collective-permute-start(bf16[16,4096]{1,0:T(8,128)(2,1)S(1)} %fusion.12), channel_id=1, source_target_pairs={{0,3},{1,4},{2,5},{3,6},{4,7},{5,8},{6,9},{7,10},{8,11},{9,12},{10... | collective-permute-start | bytes 393224 | tf_op jit(solution)/shard_map/ppermute | solution.py:215
  38.5 2.9 %collective-permute-done.6 = bf16[16,4096]{1,0:T(8,128)(2,1)S(1)} collective-permute-done((bf16[16,4096]{1,0:T(8,128)(2,1)S(1)}, bf16[16,4096]{1,0:T(8,128)(2,1)S(1)}, u32[]{:S(2)}, u32[]{:S(2)}) %collective-permute-start.6) | collective-permute-done | bytes 131104 | tf_op jit(solution)/shard_map/ppermute | solution.py:215
  41.4 6.6 %collective-permute-done.4 = bf16[16,4096]{1,0:T(8,128)(2,1)S(1)} collective-permute-done((bf16[16,4096]{1,0:T(8,128)(2,1)S(1)}, bf16[16,4096]{1,0:T(8,128)(2,1)S(1)}, u32[]{:S(2)}, u32[]{:S(2)}) %collective-permute-start.4) | collective-permute-done | bytes 131104 | tf_op jit(solution)/shard_map/ppermute | solution.py:215
  48.0 0.3 fusion.13
  48.3 0.7 collective-permute-start.8
  49.0 1.9 %collective-permute-start.7 = (bf16[16,4096]{1,0:T(8,128)(2,1)S(1)}, bf16[16,4096]{1,0:T(8,128)(2,1)S(1)}, u32[]{:S(2)}, u32[]{:S(2)}) collective-permute-start(bf16[16,4096]{1,0:T(8,128)(2,1)S(1)} %get-tuple-element.9), channel_id=1, source_target_pairs={{0,12},{1,13},{2,14},{3,15},{4,16},{5,17},{6,18},{7,19},{8,20},{9,... | collective-permute-start | bytes 393224 | tf_op jit(solution)/shard_map/ppermute | solution.py:215
  50.9 7.4 %collective-permute-done.7 = bf16[16,4096]{1,0:T(8,128)(2,1)S(1)} collective-permute-done((bf16[16,4096]{1,0:T(8,128)(2,1)S(1)}, bf16[16,4096]{1,0:T(8,128)(2,1)S(1)}, u32[]{:S(2)}, u32[]{:S(2)}) %collective-permute-start.7) | collective-permute-done | bytes 131104 | tf_op jit(solution)/shard_map/ppermute | solution.py:215
  58.3 0.8 %multiply_add_fusion.hin_ref = f32[16,4096]{1,0:T(8,128)} fusion(f32[16,4096]{1,0:T(8,128)S(1)} %get-tuple-element.10, bf16[16,4096]{1,0:T(8,128)(2,1)S(1)} %collective-permute-done.8, bf16[16,4096]{1,0:T(8,128)(2,1)S(1)} %collective-permute-done.7, f32[4096,16]{0,1:T(8,128)S(1)} %copy-done), kind=kLoop, calls=%fused_computation | loop fusion | flops 655360 | bytes 1048576 | tf_op jit(solution)/shard_map/add | solution.py:267
  59.2 14.5 %shard_map.56 = bf16[128,4096]{1,0:T(8,128)(2,1)} custom-call(bf16[3,128,4096]{2,1,0:T(8,128)(2,1)} %bitcast.15, f32[3,2,4096]{2,1,0:T(2,128)} %get-tuple-element.23.halo_ref, f32[3,3,4096]{2,1,0:T(4,128)} %f_ref.3, f32[16,4096]{1,0:T(8,128)} %bitcast.17, f32[16,4096]{1,0:T(8,128)} %bitcast.18, f32[1,4096]{1,0:T(1,128)} %bitcast.21, ...), custom_call_target="tpu_custom_call" | custom-call | tf_op jit(solution)/shard_map/pallas_call | solution.py:180
  (9 shorter events, 0.3 us)
Async XLA Ops:
  0.0 15.8 %copy-start = (f32[4096,16]{0,1:T(8,128)S(1)}, f32[4096,16]{0,1:T(8,128)}, u32[]{:S(2)}) copy-start(f32[4096,16]{0,1:T(8,128)} %param.8) | copy-start | bytes 786436
  1.1 13.6 %collective-permute-start = (bf16[2,3,4096]{2,0,1:T(2,128)(2,1)S(1)}, bf16[2,3,4096]{2,0,1:T(2,128)(2,1)S(1)}, u32[]{:S(2)}, u32[]{:S(2)}) collective-permute-start(bf16[2,3,4096]{2,0,1:T(2,128)(2,1)S(1)} %get-tuple-element.14), channel_id=1, source_target_pairs={{0,1},{1,2},{2,3},{3,4},{4,5},{5,6},{6,7},{7,8},{8,9},{9,10},{10,1... | collective-permute-start | bytes 147464 | tf_op jit(solution)/shard_map/ppermute | solution.py:215
  17.7 8.7 %collective-permute-start.3 = (bf16[16,4096]{1,0:T(8,128)(2,1)S(1)}, bf16[16,4096]{1,0:T(8,128)(2,1)S(1)}, u32[]{:S(2)}, u32[]{:S(2)}) collective-permute-start(bf16[16,4096]{1,0:T(8,128)(2,1)S(1)} %get-tuple-element.16), channel_id=1, source_target_pairs={{0,3},{1,4},{2,5},{3,6},{4,7},{5,8},{6,9},{7,10},{8,11},{9,12},{10... | collective-permute-start | bytes 393224 | tf_op jit(solution)/shard_map/ppermute | solution.py:215
  20.7 7.2 %collective-permute-start.2 = (bf16[16,4096]{1,0:T(8,128)(2,1)S(1)}, bf16[16,4096]{1,0:T(8,128)(2,1)S(1)}, u32[]{:S(2)}, u32[]{:S(2)}) collective-permute-start(bf16[16,4096]{1,0:T(8,128)(2,1)S(1)} %get-tuple-element.16), channel_id=1, source_target_pairs={{0,2},{1,3},{2,4},{3,5},{4,6},{5,7},{6,8},{7,9},{8,10},{9,11},{10,... | collective-permute-start | bytes 393224 | tf_op jit(solution)/shard_map/ppermute | solution.py:215
  22.6 8.5 %collective-permute-start.1 = (bf16[16,4096]{1,0:T(8,128)(2,1)S(1)}, bf16[16,4096]{1,0:T(8,128)(2,1)S(1)}, u32[]{:S(2)}, u32[]{:S(2)}) collective-permute-start(bf16[16,4096]{1,0:T(8,128)(2,1)S(1)} %get-tuple-element.16), channel_id=1, source_target_pairs={{0,1},{1,2},{2,3},{3,4},{4,5},{5,6},{6,7},{7,8},{8,9},{9,10},{10,1... | collective-permute-start | bytes 393224 | tf_op jit(solution)/shard_map/ppermute | solution.py:215
  31.3 10.0 %collective-permute-start.6 = (bf16[16,4096]{1,0:T(8,128)(2,1)S(1)}, bf16[16,4096]{1,0:T(8,128)(2,1)S(1)}, u32[]{:S(2)}, u32[]{:S(2)}) collective-permute-start(bf16[16,4096]{1,0:T(8,128)(2,1)S(1)} %fusion.12), channel_id=1, source_target_pairs={{0,9},{1,10},{2,11},{3,12},{4,13},{5,14},{6,15},{7,16},{8,17},{9,1... | collective-permute-start | bytes 393224 | tf_op jit(solution)/shard_map/ppermute | solution.py:215
  34.4 7.0 %collective-permute-start.5 = (bf16[16,4096]{1,0:T(8,128)(2,1)S(1)}, bf16[16,4096]{1,0:T(8,128)(2,1)S(1)}, u32[]{:S(2)}, u32[]{:S(2)}) collective-permute-start(bf16[16,4096]{1,0:T(8,128)(2,1)S(1)} %fusion.12), channel_id=1, source_target_pairs={{0,6},{1,7},{2,8},{3,9},{4,10},{5,11},{6,12},{7,13},{8,14},{9,15},... | collective-permute-start | bytes 393224 | tf_op jit(solution)/shard_map/ppermute | solution.py:215
  36.6 11.4 %collective-permute-start.4 = (bf16[16,4096]{1,0:T(8,128)(2,1)S(1)}, bf16[16,4096]{1,0:T(8,128)(2,1)S(1)}, u32[]{:S(2)}, u32[]{:S(2)}) collective-permute-start(bf16[16,4096]{1,0:T(8,128)(2,1)S(1)} %fusion.12), channel_id=1, source_target_pairs={{0,3},{1,4},{2,5},{3,6},{4,7},{5,8},{6,9},{7,10},{8,11},{9,12},{10... | collective-permute-start | bytes 393224 | tf_op jit(solution)/shard_map/ppermute | solution.py:215
  48.3 2.6 %collective-permute-start.8 = (bf16[16,4096]{1,0:T(8,128)(2,1)S(1)}, bf16[16,4096]{1,0:T(8,128)(2,1)S(1)}, u32[]{:S(2)}, u32[]{:S(2)}) collective-permute-start(bf16[16,4096]{1,0:T(8,128)(2,1)S(1)} %get-tuple-element.9), channel_id=1, source_target_pairs={{0,24},{1,25},{2,26},{3,27},{4,28},{5,29},{6,30},{7,31}} | collective-permute-start | bytes 393224 | tf_op jit(solution)/shard_map/ppermute | solution.py:215
  49.0 9.4 %collective-permute-start.7 = (bf16[16,4096]{1,0:T(8,128)(2,1)S(1)}, bf16[16,4096]{1,0:T(8,128)(2,1)S(1)}, u32[]{:S(2)}, u32[]{:S(2)}) collective-permute-start(bf16[16,4096]{1,0:T(8,128)(2,1)S(1)} %get-tuple-element.9), channel_id=1, source_target_pairs={{0,12},{1,13},{2,14},{3,15},{4,16},{5,17},{6,18},{7,19},{8,20},{9,... | collective-permute-start | bytes 393224 | tf_op jit(solution)/shard_map/ppermute | solution.py:215

commit v10 on v9

--- a/solution.py
+++ b/solution.py
@@ -7,7 +7,7 @@
 
 LANES = 128
 SUB = 8
-BLOCK = 1024
+BLOCK = 2048
 FIRST_WINDOW = 3
 UNROLL = 8
 

time: 74.6 us -> 75.5 us (1.012)
  Pallas kernels: 23 us -> 24 us
where the time goes in v10:
time: 75.5 us; the launch traced here: 74.6 us
  Pallas kernels  24 us (32%)
  starting transfers between devices  21.8 us (29%)
  waiting for transfers between devices  21.7 us (29%)
  other arithmetic  5.36 us (7%)
  local copies, waits for them, and re-layouts  1.6 us (2%)
    ppermute x9, starting transfers between devices, shift(): return lax.ppermute(value, axes, pairs)  21.8 us
    ppermute x9, waiting for transfers between devices, shift(): return lax.ppermute(value, axes, pairs)  21.7 us
    pallas_call x1, Pallas kernels, run_out(): pl.pallas_call(out_kernel, grid=(width // BLOCK,), in_specs=[pl.BlockSpec...  15 us
    pallas_call x1, Pallas kernels, run_state(): pl.pallas_call(state_kernel, grid=(width // BLOCK,), in_specs=[pl.BlockSp...  8.99 us
    convert_element_type x3, other arithmetic, gather_window(): sent = value.astype(jnp.bfloat16)  2.32 us
  transfers between devices with their start and end apart: 9, of which 5 were waited for; matrix products, arithmetic and copies ran while one was open for 2% of the time, Pallas kernels for 12%

profile of v10, /device:TPU:16, one launch (start us, length us, event | category | flops | bytes accessed | tf_op | source)
XLA Modules:
  0.0 74.6 jit_solution(15595581703498714507)
XLA Ops:
  0.0 1.1 %slice_convert_fusion = (f32[2,3,4096]{2,0,1:T(2,128)S(1)}, bf16[2,3,4096]{2,0,1:T(2,128)(2,1)S(1)}) fusion(bf16[128,3,4096]{2,0,1:T(8,128)(2,1)} %param.5), kind=kLoop, calls=%fused_computation.12 | loop fusion | flops 24576 | bytes 245760 | tf_op jit(solution)/shard_map/convert_element_type | solution.py:224
  1.1 3.4 %collective-permute-start = (bf16[2,3,4096]{2,0,1:T(2,128)(2,1)S(1)}, bf16[2,3,4096]{2,0,1:T(2,128)(2,1)S(1)}, u32[]{:S(2)}, u32[]{:S(2)}) collective-permute-start(bf16[2,3,4096]{2,0,1:T(2,128)(2,1)S(1)} %get-tuple-element.14), channel_id=1, source_target_pairs={{0,1},{1,2},{2,3},{3,4},{4,5},{5,6},{6,7},{7,8},{8,9},{9,10},{10,1... | collective-permute-start | bytes 147464 | tf_op jit(solution)/shard_map/ppermute | solution.py:215
  4.6 0.9 %fusion.15 = (f32[1,3,4096]{2,1,0:T(4,128)S(1)}, f32[1,3,4096]{2,1,0:T(4,128)S(1)}, f32[1,3,4096]{2,1,0:T(4,128)S(1)}) fusion(f32[3,3,4096]{2,1,0:T(4,128)} %f_ref.3), kind=kLoop, calls=%fused_computation.32 | loop fusion | bytes 294912 | tf_op jit(solution)/shard_map/slice | solution.py:230
  5.5 0.7 broadcast_in_dim.2.halo_ref
  6.2 9.0 %shard_map.55 = (f32[16,8,4096]{2,1,0:T(8,128)}, f32[16,4096]{1,0:T(8,128)}) custom-call(bf16[3,128,4096]{2,1,0:T(8,128)(2,1)} %bitcast.14, f32[3,2,4096]{2,1,0:T(2,128)} %broadcast_in_dim.2.halo_ref, f32[3,3,4096]{2,1,0:T(4,128)} %f_ref.3, f32[16,4096]{1,0:T(8,128)} %bitcast.16), custom_call_target="tpu_custom_call" | custom-call | tf_op jit(solution)/shard_map/pallas_call | solution.py:151
  15.2 0.7 fusion.16
  15.9 0.2 multiply_add_fusion.4
  16.3 1.8 %add_convert_fusion = (bf16[16,4096]{1,0:T(8,128)(2,1)S(1)}, f32[16,4096]{1,0:T(8,128)}) fusion(f32[16,4096]{1,0:T(8,128)} %get-tuple-element.8, f32[4096]{0:T(1024)S(1)} %bitcast.19, f32[4096]{0:T(1024)S(1)} %bitcast.20, f32[4096,16]{0,1:T(8,128)S(1)} %copy-done), kind=kLoop, calls=%fused_computation.3 | loop fusion | flops 851968 | bytes 950272 | tf_op jit(solution)/shard_map/convert_element_type | solution.py:253
  18.1 3.0 %collective-permute-start.3 = (bf16[16,4096]{1,0:T(8,128)(2,1)S(1)}, bf16[16,4096]{1,0:T(8,128)(2,1)S(1)}, u32[]{:S(2)}, u32[]{:S(2)}) collective-permute-start(bf16[16,4096]{1,0:T(8,128)(2,1)S(1)} %get-tuple-element.16), channel_id=1, source_target_pairs={{0,3},{1,4},{2,5},{3,6},{4,7},{5,8},{6,9},{7,10},{8,11},{9,12},{10... | collective-permute-start | bytes 393224 | tf_op jit(solution)/shard_map/ppermute | solution.py:215
  21.2 1.9 %collective-permute-start.2 = (bf16[16,4096]{1,0:T(8,128)(2,1)S(1)}, bf16[16,4096]{1,0:T(8,128)(2,1)S(1)}, u32[]{:S(2)}, u32[]{:S(2)}) collective-permute-start(bf16[16,4096]{1,0:T(8,128)(2,1)S(1)} %get-tuple-element.16), channel_id=1, source_target_pairs={{0,2},{1,3},{2,4},{3,5},{4,6},{5,7},{6,8},{7,9},{8,10},{9,11},{10,... | collective-permute-start | bytes 393224 | tf_op jit(solution)/shard_map/ppermute | solution.py:215
  23.1 3.7 %collective-permute-start.1 = (bf16[16,4096]{1,0:T(8,128)(2,1)S(1)}, bf16[16,4096]{1,0:T(8,128)(2,1)S(1)}, u32[]{:S(2)}, u32[]{:S(2)}) collective-permute-start(bf16[16,4096]{1,0:T(8,128)(2,1)S(1)} %get-tuple-element.16), channel_id=1, source_target_pairs={{0,1},{1,2},{2,3},{3,4},{4,5},{5,6},{6,7},{7,8},{8,9},{9,10},{10,1... | collective-permute-start | bytes 393224 | tf_op jit(solution)/shard_map/ppermute | solution.py:215
  26.8 1.5 %collective-permute-done.2 = bf16[16,4096]{1,0:T(8,128)(2,1)S(1)} collective-permute-done((bf16[16,4096]{1,0:T(8,128)(2,1)S(1)}, bf16[16,4096]{1,0:T(8,128)(2,1)S(1)}, u32[]{:S(2)}, u32[]{:S(2)}) %collective-permute-start.2) | collective-permute-done | bytes 131104 | tf_op jit(solution)/shard_map/ppermute | solution.py:215
  28.4 3.3 %collective-permute-done.1 = bf16[16,4096]{1,0:T(8,128)(2,1)S(1)} collective-permute-done((bf16[16,4096]{1,0:T(8,128)(2,1)S(1)}, bf16[16,4096]{1,0:T(8,128)(2,1)S(1)}, u32[]{:S(2)}, u32[]{:S(2)}) %collective-permute-start.1) | collective-permute-done | bytes 131104 | tf_op jit(solution)/shard_map/ppermute | solution.py:215
  31.8 3.1 %collective-permute-start.6 = (bf16[16,4096]{1,0:T(8,128)(2,1)S(1)}, bf16[16,4096]{1,0:T(8,128)(2,1)S(1)}, u32[]{:S(2)}, u32[]{:S(2)}) collective-permute-start(bf16[16,4096]{1,0:T(8,128)(2,1)S(1)} %fusion.12), channel_id=1, source_target_pairs={{0,9},{1,10},{2,11},{3,12},{4,13},{5,14},{6,15},{7,16},{8,17},{9,1... | collective-permute-start | bytes 393224 | tf_op jit(solution)/shard_map/ppermute | solution.py:215
  34.9 2.1 %collective-permute-start.5 = (bf16[16,4096]{1,0:T(8,128)(2,1)S(1)}, bf16[16,4096]{1,0:T(8,128)(2,1)S(1)}, u32[]{:S(2)}, u32[]{:S(2)}) collective-permute-start(bf16[16,4096]{1,0:T(8,128)(2,1)S(1)} %fusion.12), channel_id=1, source_target_pairs={{0,6},{1,7},{2,8},{3,9},{4,10},{5,11},{6,12},{7,13},{8,14},{9,15},... | collective-permute-start | bytes 393224 | tf_op jit(solution)/shard_map/ppermute | solution.py:215
  37.0 1.9 %collective-permute-start.4 = (bf16[16,4096]{1,0:T(8,128)(2,1)S(1)}, bf16[16,4096]{1,0:T(8,128)(2,1)S(1)}, u32[]{:S(2)}, u32[]{:S(2)}) collective-permute-start(bf16[16,4096]{1,0:T(8,128)(2,1)S(1)} %fusion.12), channel_id=1, source_target_pairs={{0,3},{1,4},{2,5},{3,6},{4,7},{5,8},{6,9},{7,10},{8,11},{9,12},{10... | collective-permute-start | bytes 393224 | tf_op jit(solution)/shard_map/ppermute | solution.py:215
  38.9 2.9 %collective-permute-done.6 = bf16[16,4096]{1,0:T(8,128)(2,1)S(1)} collective-permute-done((bf16[16,4096]{1,0:T(8,128)(2,1)S(1)}, bf16[16,4096]{1,0:T(8,128)(2,1)S(1)}, u32[]{:S(2)}, u32[]{:S(2)}) %collective-permute-start.6) | collective-permute-done | bytes 131104 | tf_op jit(solution)/shard_map/ppermute | solution.py:215
  41.8 6.6 %collective-permute-done.4 = bf16[16,4096]{1,0:T(8,128)(2,1)S(1)} collective-permute-done((bf16[16,4096]{1,0:T(8,128)(2,1)S(1)}, bf16[16,4096]{1,0:T(8,128)(2,1)S(1)}, u32[]{:S(2)}, u32[]{:S(2)}) %collective-permute-start.4) | collective-permute-done | bytes 131104 | tf_op jit(solution)/shard_map/ppermute | solution.py:215
  48.5 0.3 fusion.13
  48.8 0.7 collective-permute-start.8
  49.4 1.9 %collective-permute-start.7 = (bf16[16,4096]{1,0:T(8,128)(2,1)S(1)}, bf16[16,4096]{1,0:T(8,128)(2,1)S(1)}, u32[]{:S(2)}, u32[]{:S(2)}) collective-permute-start(bf16[16,4096]{1,0:T(8,128)(2,1)S(1)} %get-tuple-element.9), channel_id=1, source_target_pairs={{0,12},{1,13},{2,14},{3,15},{4,16},{5,17},{6,18},{7,19},{8,20},{9,... | collective-permute-start | bytes 393224 | tf_op jit(solution)/shard_map/ppermute | solution.py:215
  51.4 7.4 %collective-permute-done.7 = bf16[16,4096]{1,0:T(8,128)(2,1)S(1)} collective-permute-done((bf16[16,4096]{1,0:T(8,128)(2,1)S(1)}, bf16[16,4096]{1,0:T(8,128)(2,1)S(1)}, u32[]{:S(2)}, u32[]{:S(2)}) %collective-permute-start.7) | collective-permute-done | bytes 131104 | tf_op jit(solution)/shard_map/ppermute | solution.py:215
  58.8 0.8 %multiply_add_fusion.hin_ref = f32[16,4096]{1,0:T(8,128)} fusion(f32[16,4096]{1,0:T(8,128)S(1)} %get-tuple-element.10, bf16[16,4096]{1,0:T(8,128)(2,1)S(1)} %collective-permute-done.8, bf16[16,4096]{1,0:T(8,128)(2,1)S(1)} %collective-permute-done.7, f32[4096,16]{0,1:T(8,128)S(1)} %copy-done), kind=kLoop, calls=%fused_computation | loop fusion | flops 655360 | bytes 1048576 | tf_op jit(solution)/shard_map/add | solution.py:267
  59.6 15.0 %shard_map.56 = bf16[128,4096]{1,0:T(8,128)(2,1)} custom-call(bf16[3,128,4096]{2,1,0:T(8,128)(2,1)} %bitcast.15, f32[3,2,4096]{2,1,0:T(2,128)} %get-tuple-element.23.halo_ref, f32[3,3,4096]{2,1,0:T(4,128)} %f_ref.3, f32[16,4096]{1,0:T(8,128)} %bitcast.17, f32[16,4096]{1,0:T(8,128)} %bitcast.18, f32[1,4096]{1,0:T(1,128)} %bitcast.21, ...), custom_call_target="tpu_custom_call" | custom-call | tf_op jit(solution)/shard_map/pallas_call | solution.py:180
  (9 shorter events, 0.3 us)
Async XLA Ops:
  0.0 16.3 %copy-start = (f32[4096,16]{0,1:T(8,128)S(1)}, f32[4096,16]{0,1:T(8,128)}, u32[]{:S(2)}) copy-start(f32[4096,16]{0,1:T(8,128)} %param.8) | copy-start | bytes 786436
  1.1 14.0 %collective-permute-start = (bf16[2,3,4096]{2,0,1:T(2,128)(2,1)S(1)}, bf16[2,3,4096]{2,0,1:T(2,128)(2,1)S(1)}, u32[]{:S(2)}, u32[]{:S(2)}) collective-permute-start(bf16[2,3,4096]{2,0,1:T(2,128)(2,1)S(1)} %get-tuple-element.14), channel_id=1, source_target_pairs={{0,1},{1,2},{2,3},{3,4},{4,5},{5,6},{6,7},{7,8},{8,9},{9,10},{10,1... | collective-permute-start | bytes 147464 | tf_op jit(solution)/shard_map/ppermute | solution.py:215
  18.1 8.7 %collective-permute-start.3 = (bf16[16,4096]{1,0:T(8,128)(2,1)S(1)}, bf16[16,4096]{1,0:T(8,128)(2,1)S(1)}, u32[]{:S(2)}, u32[]{:S(2)}) collective-permute-start(bf16[16,4096]{1,0:T(8,128)(2,1)S(1)} %get-tuple-element.16), channel_id=1, source_target_pairs={{0,3},{1,4},{2,5},{3,6},{4,7},{5,8},{6,9},{7,10},{8,11},{9,12},{10... | collective-permute-start | bytes 393224 | tf_op jit(solution)/shard_map/ppermute | solution.py:215
  21.2 7.2 %collective-permute-start.2 = (bf16[16,4096]{1,0:T(8,128)(2,1)S(1)}, bf16[16,4096]{1,0:T(8,128)(2,1)S(1)}, u32[]{:S(2)}, u32[]{:S(2)}) collective-permute-start(bf16[16,4096]{1,0:T(8,128)(2,1)S(1)} %get-tuple-element.16), channel_id=1, source_target_pairs={{0,2},{1,3},{2,4},{3,5},{4,6},{5,7},{6,8},{7,9},{8,10},{9,11},{10,... | collective-permute-start | bytes 393224 | tf_op jit(solution)/shard_map/ppermute | solution.py:215
  23.1 8.5 %collective-permute-start.1 = (bf16[16,4096]{1,0:T(8,128)(2,1)S(1)}, bf16[16,4096]{1,0:T(8,128)(2,1)S(1)}, u32[]{:S(2)}, u32[]{:S(2)}) collective-permute-start(bf16[16,4096]{1,0:T(8,128)(2,1)S(1)} %get-tuple-element.16), channel_id=1, source_target_pairs={{0,1},{1,2},{2,3},{3,4},{4,5},{5,6},{6,7},{7,8},{8,9},{9,10},{10,1... | collective-permute-start | bytes 393224 | tf_op jit(solution)/shard_map/ppermute | solution.py:215
  31.8 10.0 %collective-permute-start.6 = (bf16[16,4096]{1,0:T(8,128)(2,1)S(1)}, bf16[16,4096]{1,0:T(8,128)(2,1)S(1)}, u32[]{:S(2)}, u32[]{:S(2)}) collective-permute-start(bf16[16,4096]{1,0:T(8,128)(2,1)S(1)} %fusion.12), channel_id=1, source_target_pairs={{0,9},{1,10},{2,11},{3,12},{4,13},{5,14},{6,15},{7,16},{8,17},{9,1... | collective-permute-start | bytes 393224 | tf_op jit(solution)/shard_map/ppermute | solution.py:215
  34.9 7.0 %collective-permute-start.5 = (bf16[16,4096]{1,0:T(8,128)(2,1)S(1)}, bf16[16,4096]{1,0:T(8,128)(2,1)S(1)}, u32[]{:S(2)}, u32[]{:S(2)}) collective-permute-start(bf16[16,4096]{1,0:T(8,128)(2,1)S(1)} %fusion.12), channel_id=1, source_target_pairs={{0,6},{1,7},{2,8},{3,9},{4,10},{5,11},{6,12},{7,13},{8,14},{9,15},... | collective-permute-start | bytes 393224 | tf_op jit(solution)/shard_map/ppermute | solution.py:215
  37.0 11.4 %collective-permute-start.4 = (bf16[16,4096]{1,0:T(8,128)(2,1)S(1)}, bf16[16,4096]{1,0:T(8,128)(2,1)S(1)}, u32[]{:S(2)}, u32[]{:S(2)}) collective-permute-start(bf16[16,4096]{1,0:T(8,128)(2,1)S(1)} %fusion.12), channel_id=1, source_target_pairs={{0,3},{1,4},{2,5},{3,6},{4,7},{5,8},{6,9},{7,10},{8,11},{9,12},{10... | collective-permute-start | bytes 393224 | tf_op jit(solution)/shard_map/ppermute | solution.py:215
  48.8 2.6 %collective-permute-start.8 = (bf16[16,4096]{1,0:T(8,128)(2,1)S(1)}, bf16[16,4096]{1,0:T(8,128)(2,1)S(1)}, u32[]{:S(2)}, u32[]{:S(2)}) collective-permute-start(bf16[16,4096]{1,0:T(8,128)(2,1)S(1)} %get-tuple-element.9), channel_id=1, source_target_pairs={{0,24},{1,25},{2,26},{3,27},{4,28},{5,29},{6,30},{7,31}} | collective-permute-start | bytes 393224 | tf_op jit(solution)/shard_map/ppermute | solution.py:215
  49.4 9.4 %collective-permute-start.7 = (bf16[16,4096]{1,0:T(8,128)(2,1)S(1)}, bf16[16,4096]{1,0:T(8,128)(2,1)S(1)}, u32[]{:S(2)}, u32[]{:S(2)}) collective-permute-start(bf16[16,4096]{1,0:T(8,128)(2,1)S(1)} %get-tuple-element.9), channel_id=1, source_target_pairs={{0,12},{1,13},{2,14},{3,15},{4,16},{5,17},{6,18},{7,19},{8,20},{9,... | collective-permute-start | bytes 393224 | tf_op jit(solution)/shard_map/ppermute | solution.py:215

commit v11 on v9

--- a/solution.py
+++ b/solution.py
@@ -250,12 +250,12 @@
         return jnp.exp(-rate_t * float(tok_rows * steps))
 
     def gather_window(value, spacing, count):
-        sent = value.astype(jnp.bfloat16)
+        sent = value
         total = None
         for k in range(1, count + 1):
             if k * spacing >= devices:
                 break
-            term = decay_pow((k - 1) * spacing) * shift(sent, k * spacing).astype(jnp.float32)
+            term = decay_pow((k - 1) * spacing) * shift(sent, k * spacing)
             total = term if total is None else total + term
         return total
 

time: 74.6 us -> 102 us (1.37)
  waiting for transfers between devices: 21.7 us -> 47.6 us
  starting transfers between devices: 21.8 us -> 23.2 us
    ppermute x9, waiting for transfers between devices: 21.7 us -> 47.6 us  [shift(): return lax.ppermute(value, axes, pairs)]
    convert_element_type x3 -> x0, other arithmetic: 2.32 us -> none  [gather_window(): sent = value.astype(jnp.bfloat16)]
    add x0 -> x2, other arithmetic: none -> 1.98 us  [the longest x1 1.85 us: body(): local = local + local_fix]
    ppermute x9, starting transfers between devices: 21.8 us -> 23.2 us  [shift(): return lax.ppermute(value, axes, pairs)]
  transfers between devices with their start and end apart: 9 -> 9, of which waited for: 5 -> 5; matrix products, arithmetic and copies ran while one was open for 2% -> 2% of each run, Pallas kernels for 12% -> 9%
where the time goes in v11:
time: 102 us; the launch traced here: 101 us
  waiting for transfers between devices  47.6 us (47%)
  starting transfers between devices  23.2 us (23%)
  Pallas kernels  23.1 us (23%)
  other arithmetic  5.16 us (5%)
  local copies, waits for them, and re-layouts  1.6 us (2%)
    ppermute x9, waiting for transfers between devices, shift(): return lax.ppermute(value, axes, pairs)  47.6 us
    ppermute x9, starting transfers between devices, shift(): return lax.ppermute(value, axes, pairs)  23.2 us
    pallas_call x1, Pallas kernels, run_out(): pl.pallas_call(out_kernel, grid=(width // BLOCK,), in_specs=[pl.BlockSpec...  14.5 us
    pallas_call x1, Pallas kernels, run_state(): pl.pallas_call(state_kernel, grid=(width // BLOCK,), in_specs=[pl.BlockSp...  8.59 us
  transfers between devices with their start and end apart: 9, of which 5 were waited for; matrix products, arithmetic and copies ran while one was open for 2% of the time, Pallas kernels for 9%

profile of v11, /device:TPU:16, one launch (start us, length us, event | category | flops | bytes accessed | tf_op | source)
XLA Modules:
  0.0 100.8 jit_solution(5010002881246459848)
XLA Ops:
  0.0 1.1 %slice_convert_fusion = (f32[2,3,4096]{2,0,1:T(2,128)S(1)}, bf16[2,3,4096]{2,0,1:T(2,128)(2,1)S(1)}) fusion(bf16[128,3,4096]{2,0,1:T(8,128)(2,1)} %param.5), kind=kLoop, calls=%fused_computation.12 | loop fusion | flops 24576 | bytes 245760 | tf_op jit(solution)/shard_map/convert_element_type | solution.py:224
  1.1 3.4 %collective-permute-start = (bf16[2,3,4096]{2,0,1:T(2,128)(2,1)S(1)}, bf16[2,3,4096]{2,0,1:T(2,128)(2,1)S(1)}, u32[]{:S(2)}, u32[]{:S(2)}) collective-permute-start(bf16[2,3,4096]{2,0,1:T(2,128)(2,1)S(1)} %get-tuple-element.12), channel_id=1, source_target_pairs={{0,1},{1,2},{2,3},{3,4},{4,5},{5,6},{6,7},{7,8},{8,9},{9,10},{10,1... | collective-permute-start | bytes 147464 | tf_op jit(solution)/shard_map/ppermute | solution.py:215
  4.6 0.9 fusion.13
  5.5 0.7 broadcast_in_dim.2.halo_ref
  6.2 8.6 %shard_map.55 = (f32[16,8,4096]{2,1,0:T(8,128)}, f32[16,4096]{1,0:T(8,128)}) custom-call(bf16[3,128,4096]{2,1,0:T(8,128)(2,1)} %bitcast.13, f32[3,2,4096]{2,1,0:T(2,128)} %broadcast_in_dim.2.halo_ref, f32[3,3,4096]{2,1,0:T(4,128)} %f_ref.3, f32[16,4096]{1,0:T(8,128)} %bitcast.15), custom_call_target="tpu_custom_call" | custom-call | tf_op jit(solution)/shard_map/pallas_call | solution.py:151
  14.8 0.7 fusion.14
  15.5 0.2 multiply_add_fusion.4
  15.9 1.8 %add_add_fusion = (f32[16,4096]{1,0:T(8,128)S(1)}, f32[16,4096]{1,0:T(8,128)}) fusion(f32[16,4096]{1,0:T(8,128)} %get-tuple-element.8, f32[4096]{0:T(1024)S(1)} %bitcast.18, f32[4096]{0:T(1024)S(1)} %bitcast.19, f32[4096,16]{0,1:T(8,128)S(1)} %copy-done), kind=kLoop, calls=%fused_computation.3 | loop fusion | flops 786432 | bytes 1081344 | tf_op jit(solution)/shard_map/add | solution.py:247
  17.7 3.0 %collective-permute-start.3 = (f32[16,4096]{1,0:T(8,128)S(1)}, f32[16,4096]{1,0:T(8,128)S(1)}, u32[]{:S(2)}, u32[]{:S(2)}) collective-permute-start(f32[16,4096]{1,0:T(8,128)S(1)} %get-tuple-element.14), channel_id=1, source_target_pairs={{0,3},{1,4},{2,5},{3,6},{4,7},{5,8},{6,9},{7,10},{8,11},{9,12},{10... | collective-permute-start | bytes 786440 | tf_op jit(solution)/shard_map/ppermute | solution.py:215
  20.8 1.9 %collective-permute-start.2 = (f32[16,4096]{1,0:T(8,128)S(1)}, f32[16,4096]{1,0:T(8,128)S(1)}, u32[]{:S(2)}, u32[]{:S(2)}) collective-permute-start(f32[16,4096]{1,0:T(8,128)S(1)} %get-tuple-element.14), channel_id=1, source_target_pairs={{0,2},{1,3},{2,4},{3,5},{4,6},{5,7},{6,8},{7,9},{8,10},{9,11},{10,... | collective-permute-start | bytes 786440 | tf_op jit(solution)/shard_map/ppermute | solution.py:215
  22.7 3.7 %collective-permute-start.1 = (f32[16,4096]{1,0:T(8,128)S(1)}, f32[16,4096]{1,0:T(8,128)S(1)}, u32[]{:S(2)}, u32[]{:S(2)}) collective-permute-start(f32[16,4096]{1,0:T(8,128)S(1)} %get-tuple-element.14), channel_id=1, source_target_pairs={{0,1},{1,2},{2,3},{3,4},{4,5},{5,6},{6,7},{7,8},{8,9},{9,10},{10,1... | collective-permute-start | bytes 786440 | tf_op jit(solution)/shard_map/ppermute | solution.py:215
  26.4 4.0 %collective-permute-done.3 = f32[16,4096]{1,0:T(8,128)S(1)} collective-permute-done((f32[16,4096]{1,0:T(8,128)S(1)}, f32[16,4096]{1,0:T(8,128)S(1)}, u32[]{:S(2)}, u32[]{:S(2)}) %collective-permute-start.3) | collective-permute-done | bytes 262176 | tf_op jit(solution)/shard_map/ppermute | solution.py:215
  30.5 4.4 %collective-permute-done.1 = f32[16,4096]{1,0:T(8,128)S(1)} collective-permute-done((f32[16,4096]{1,0:T(8,128)S(1)}, f32[16,4096]{1,0:T(8,128)S(1)}, u32[]{:S(2)}, u32[]{:S(2)}) %collective-permute-start.1) | collective-permute-done | bytes 262176 | tf_op jit(solution)/shard_map/ppermute | solution.py:215
  35.0 3.6 %collective-permute-start.6 = (f32[16,4096]{1,0:T(8,128)S(1)}, f32[16,4096]{1,0:T(8,128)S(1)}, u32[]{:S(2)}, u32[]{:S(2)}) collective-permute-start(f32[16,4096]{1,0:T(8,128)S(1)} %multiply_add_fusion.2), channel_id=1, source_target_pairs={{0,9},{1,10},{2,11},{3,12},{4,13},{5,14},{6,15},{7,16},{8,17},{9,1... | collective-permute-start | bytes 786440 | tf_op jit(solution)/shard_map/ppermute | solution.py:215
  38.6 1.9 %collective-permute-start.5 = (f32[16,4096]{1,0:T(8,128)S(1)}, f32[16,4096]{1,0:T(8,128)S(1)}, u32[]{:S(2)}, u32[]{:S(2)}) collective-permute-start(f32[16,4096]{1,0:T(8,128)S(1)} %multiply_add_fusion.2), channel_id=1, source_target_pairs={{0,6},{1,7},{2,8},{3,9},{4,10},{5,11},{6,12},{7,13},{8,14},{9,15},... | collective-permute-start | bytes 786440 | tf_op jit(solution)/shard_map/ppermute | solution.py:215
  40.5 3.0 %collective-permute-start.4 = (f32[16,4096]{1,0:T(8,128)S(1)}, f32[16,4096]{1,0:T(8,128)S(1)}, u32[]{:S(2)}, u32[]{:S(2)}) collective-permute-start(f32[16,4096]{1,0:T(8,128)S(1)} %multiply_add_fusion.2), channel_id=1, source_target_pairs={{0,3},{1,4},{2,5},{3,6},{4,7},{5,8},{6,9},{7,10},{8,11},{9,12},{10... | collective-permute-start | bytes 786440 | tf_op jit(solution)/shard_map/ppermute | solution.py:215
  43.5 4.7 %collective-permute-done.6 = f32[16,4096]{1,0:T(8,128)S(1)} collective-permute-done((f32[16,4096]{1,0:T(8,128)S(1)}, f32[16,4096]{1,0:T(8,128)S(1)}, u32[]{:S(2)}, u32[]{:S(2)}) %collective-permute-start.6) | collective-permute-done | bytes 262176 | tf_op jit(solution)/shard_map/ppermute | solution.py:215
  48.2 23.9 %collective-permute-done.4 = f32[16,4096]{1,0:T(8,128)S(1)} collective-permute-done((f32[16,4096]{1,0:T(8,128)S(1)}, f32[16,4096]{1,0:T(8,128)S(1)}, u32[]{:S(2)}, u32[]{:S(2)}) %collective-permute-start.4) | collective-permute-done | bytes 262176 | tf_op jit(solution)/shard_map/ppermute | solution.py:215
  72.1 0.2 multiply_add_fusion.1
  72.2 0.7 collective-permute-start.8
  72.9 1.9 %collective-permute-start.7 = (f32[16,4096]{1,0:T(8,128)S(1)}, f32[16,4096]{1,0:T(8,128)S(1)}, u32[]{:S(2)}, u32[]{:S(2)}) collective-permute-start(f32[16,4096]{1,0:T(8,128)S(1)} %multiply_add_fusion.1), channel_id=1, source_target_pairs={{0,12},{1,13},{2,14},{3,15},{4,16},{5,17},{6,18},{7,19},{8,20},{9,... | collective-permute-start | bytes 786440 | tf_op jit(solution)/shard_map/ppermute | solution.py:215
  74.9 10.6 %collective-permute-done.7 = f32[16,4096]{1,0:T(8,128)S(1)} collective-permute-done((f32[16,4096]{1,0:T(8,128)S(1)}, f32[16,4096]{1,0:T(8,128)S(1)}, u32[]{:S(2)}, u32[]{:S(2)}) %collective-permute-start.7) | collective-permute-done | bytes 262176 | tf_op jit(solution)/shard_map/ppermute | solution.py:215
  85.5 0.8 multiply_add_fusion.hin_ref
  86.3 14.5 %shard_map.56 = bf16[128,4096]{1,0:T(8,128)(2,1)} custom-call(bf16[3,128,4096]{2,1,0:T(8,128)(2,1)} %bitcast.14, f32[3,2,4096]{2,1,0:T(2,128)} %get-tuple-element.21.halo_ref, f32[3,3,4096]{2,1,0:T(4,128)} %f_ref.3, f32[16,4096]{1,0:T(8,128)} %bitcast.16, f32[16,4096]{1,0:T(8,128)} %bitcast.17, f32[1,4096]{1,0:T(1,128)} %bitcast.20, ...), custom_call_target="tpu_custom_call" | custom-call | tf_op jit(solution)/shard_map/pallas_call | solution.py:180
  (9 shorter events, 0.3 us)
Async XLA Ops:
  0.0 15.9 %copy-start = (f32[4096,16]{0,1:T(8,128)S(1)}, f32[4096,16]{0,1:T(8,128)}, u32[]{:S(2)}) copy-start(f32[4096,16]{0,1:T(8,128)} %param.8) | copy-start | bytes 786436
  1.1 13.6 %collective-permute-start = (bf16[2,3,4096]{2,0,1:T(2,128)(2,1)S(1)}, bf16[2,3,4096]{2,0,1:T(2,128)(2,1)S(1)}, u32[]{:S(2)}, u32[]{:S(2)}) collective-permute-start(bf16[2,3,4096]{2,0,1:T(2,128)(2,1)S(1)} %get-tuple-element.12), channel_id=1, source_target_pairs={{0,1},{1,2},{2,3},{3,4},{4,5},{5,6},{6,7},{7,8},{8,9},{9,10},{10,1... | collective-permute-start | bytes 147464 | tf_op jit(solution)/shard_map/ppermute | solution.py:215
  17.7 12.7 %collective-permute-start.3 = (f32[16,4096]{1,0:T(8,128)S(1)}, f32[16,4096]{1,0:T(8,128)S(1)}, u32[]{:S(2)}, u32[]{:S(2)}) collective-permute-start(f32[16,4096]{1,0:T(8,128)S(1)} %get-tuple-element.14), channel_id=1, source_target_pairs={{0,3},{1,4},{2,5},{3,6},{4,7},{5,8},{6,9},{7,10},{8,11},{9,12},{10... | collective-permute-start | bytes 786440 | tf_op jit(solution)/shard_map/ppermute | solution.py:215
  20.8 9.7 %collective-permute-start.2 = (f32[16,4096]{1,0:T(8,128)S(1)}, f32[16,4096]{1,0:T(8,128)S(1)}, u32[]{:S(2)}, u32[]{:S(2)}) collective-permute-start(f32[16,4096]{1,0:T(8,128)S(1)} %get-tuple-element.14), channel_id=1, source_target_pairs={{0,2},{1,3},{2,4},{3,5},{4,6},{5,7},{6,8},{7,9},{8,10},{9,11},{10,... | collective-permute-start | bytes 786440 | tf_op jit(solution)/shard_map/ppermute | solution.py:215
  22.7 12.2 %collective-permute-start.1 = (f32[16,4096]{1,0:T(8,128)S(1)}, f32[16,4096]{1,0:T(8,128)S(1)}, u32[]{:S(2)}, u32[]{:S(2)}) collective-permute-start(f32[16,4096]{1,0:T(8,128)S(1)} %get-tuple-element.14), channel_id=1, source_target_pairs={{0,1},{1,2},{2,3},{3,4},{4,5},{5,6},{6,7},{7,8},{8,9},{9,10},{10,1... | collective-permute-start | bytes 786440 | tf_op jit(solution)/shard_map/ppermute | solution.py:215
  35.0 13.2 %collective-permute-start.6 = (f32[16,4096]{1,0:T(8,128)S(1)}, f32[16,4096]{1,0:T(8,128)S(1)}, u32[]{:S(2)}, u32[]{:S(2)}) collective-permute-start(f32[16,4096]{1,0:T(8,128)S(1)} %multiply_add_fusion.2), channel_id=1, source_target_pairs={{0,9},{1,10},{2,11},{3,12},{4,13},{5,14},{6,15},{7,16},{8,17},{9,1... | collective-permute-start | bytes 786440 | tf_op jit(solution)/shard_map/ppermute | solution.py:215
  38.6 9.6 %collective-permute-start.5 = (f32[16,4096]{1,0:T(8,128)S(1)}, f32[16,4096]{1,0:T(8,128)S(1)}, u32[]{:S(2)}, u32[]{:S(2)}) collective-permute-start(f32[16,4096]{1,0:T(8,128)S(1)} %multiply_add_fusion.2), channel_id=1, source_target_pairs={{0,6},{1,7},{2,8},{3,9},{4,10},{5,11},{6,12},{7,13},{8,14},{9,15},... | collective-permute-start | bytes 786440 | tf_op jit(solution)/shard_map/ppermute | solution.py:215
  40.5 31.5 %collective-permute-start.4 = (f32[16,4096]{1,0:T(8,128)S(1)}, f32[16,4096]{1,0:T(8,128)S(1)}, u32[]{:S(2)}, u32[]{:S(2)}) collective-permute-start(f32[16,4096]{1,0:T(8,128)S(1)} %multiply_add_fusion.2), channel_id=1, source_target_pairs={{0,3},{1,4},{2,5},{3,6},{4,7},{5,8},{6,9},{7,10},{8,11},{9,12},{10... | collective-permute-start | bytes 786440 | tf_op jit(solution)/shard_map/ppermute | solution.py:215
  72.2 2.6 %collective-permute-start.8 = (f32[16,4096]{1,0:T(8,128)S(1)}, f32[16,4096]{1,0:T(8,128)S(1)}, u32[]{:S(2)}, u32[]{:S(2)}) collective-permute-start(f32[16,4096]{1,0:T(8,128)S(1)} %multiply_add_fusion.1), channel_id=1, source_target_pairs={{0,24},{1,25},{2,26},{3,27},{4,28},{5,29},{6,30},{7,31}} | collective-permute-start | bytes 786440 | tf_op jit(solution)/shard_map/ppermute | solution.py:215
  72.9 12.5 %collective-permute-start.7 = (f32[16,4096]{1,0:T(8,128)S(1)}, f32[16,4096]{1,0:T(8,128)S(1)}, u32[]{:S(2)}, u32[]{:S(2)}) collective-permute-start(f32[16,4096]{1,0:T(8,128)S(1)} %multiply_add_fusion.1), channel_id=1, source_target_pairs={{0,12},{1,13},{2,14},{3,15},{4,16},{5,17},{6,18},{7,19},{8,20},{9,... | collective-permute-start | bytes 786440 | tf_op jit(solution)/shard_map/ppermute | solution.py:215

commit v12 on v11

--- a/solution.py
+++ b/solution.py
@@ -9,6 +9,7 @@
 SUB = 8
 BLOCK = 1024
 FIRST_WINDOW = 3
+LATER_WINDOW = 4
 UNROLL = 8
 
 
@@ -246,26 +247,60 @@
         ends_fix = to_seg if ends_fix is None else ends_fix + to_seg
     local = local + local_fix
 
-    def decay_pow(steps):
-        return jnp.exp(-rate_t * float(tok_rows * steps))
+    group = lax.axis_size("tp")
+    spans = lax.axis_size("ctx")
+    member = lax.axis_index("tp")
+    piece = width // group
+
+    def exchange(value, k):
+        return lax.ppermute(value, "tp", [(q, (q + k) % group) for q in range(group)])
+
+    def powers(rates_part, count):
+        return jnp.exp(-rates_part * (float(tok_rows) * count))
+
+    inside = None
+    total = powers(rate_t, (group - 1 - member).astype(jnp.float32)) * local
+    for k in range(1, group):
+        other = exchange(local, k)
+        source = (member - k) % group
+        total = total + powers(rate_t, (group - 1 - source).astype(jnp.float32)) * other
+        term = jnp.where(k <= member, powers(rate_t, float(k - 1)) * other, 0.0)
+        inside = term if inside is None else inside + term
+    if inside is None:
+        inside = jnp.zeros_like(local)
+
+    first_channel = member * piece
+    rate_part = lax.dynamic_slice_in_dim(rate_t, first_channel, piece, 1)
+    total_part = lax.dynamic_slice_in_dim(total, first_channel, piece, 1)
+
+    def span_shift(value, offset):
+        return lax.ppermute(value, "ctx", [(j, j + offset) for j in range(spans - offset)])
 
     def gather_window(value, spacing, count):
-        sent = value
-        total = None
+        gathered = None
         for k in range(1, count + 1):
-            if k * spacing >= devices:
+            if k * spacing >= spans:
                 break
-            term = decay_pow((k - 1) * spacing) * shift(sent, k * spacing)
-            total = term if total is None else total + term
-        return total
-
-    first = min(FIRST_WINDOW, devices - 1)
-    carried = gather_window(local, 1, first)
-    window = first
-    while window < devices - 1:
-        count = min(-(-(devices - 1) // window) - 1, FIRST_WINDOW)
-        carried = carried + decay_pow(window) * gather_window(carried, window, count)
-        window *= count + 1
+            term = powers(rate_part, float(group * (k - 1) * spacing)) * span_shift(value, k * spacing)
+            gathered = term if gathered is None else gathered + term
+        return gathered
+
+    if spans > 1:
+        first = min(FIRST_WINDOW, spans - 1)
+        before = gather_window(total_part, 1, first)
+        window = first
+        while window < spans - 1:
+            count = min(-(-(spans - 1) // window) - 1, LATER_WINDOW)
+            before = before + powers(rate_part, float(group * window)) * gather_window(before, window, count)
+            window *= count + 1
+    else:
+        before = jnp.zeros_like(total_part)
+
+    whole = jnp.zeros_like(local)
+    for k in range(group):
+        part = before if k == 0 else exchange(before, k)
+        whole = lax.dynamic_update_slice_in_dim(whole, part, ((member - k) % group) * piece, 1)
+    carried = powers(rate_t, member.astype(jnp.float32)) * whole + inside
 
     return run_out(x, halo, short_filter, rate_t, residue_t, skip.reshape(1, width), ends, ends_fix, carried)
 

time: 102 us -> 77.1 us (0.76)
  waiting for transfers between devices: 47.6 us -> 27.7 us
  starting transfers between devices: 23.2 us -> 18.5 us
    ppermute x9 -> x1, waiting for transfers between devices: 47.6 us -> 0.01 us  [shift(): return lax.ppermute(value, axes, pairs)]
    ppermute x0 -> x9, waiting for transfers between devices: none -> 27.7 us  [the longest x7 14.7 us: span_shift(): lax.ppermute(value, 'ctx', [(j, j + offset) for j in range(spans - offset)])]
    ppermute x9 -> x1, starting transfers between devices: 23.2 us -> 3.43 us  [shift(): return lax.ppermute(value, axes, pairs)]
    ppermute x0 -> x9, starting transfers between devices: none -> 15 us  [the longest x7 14.3 us: span_shift(): lax.ppermute(value, 'ctx', [(j, j + offset) for j in range(spans - offset)])]
  transfers between devices with their start and end apart: 9 -> 10, of which waited for: 5 -> 6; matrix products, arithmetic and copies ran while one was open for 2% -> 2% of each run, Pallas kernels for 9% -> 11%
where the time goes in v12:
time: 77.1 us; the launch traced here: 76.1 us
  waiting for transfers between devices  27.7 us (36%)
  Pallas kernels  23 us (30%)
  starting transfers between devices  18.5 us (24%)
  other arithmetic  5.09 us (7%)
  local copies, waits for them, and re-layouts  1.64 us (2%)
    ppermute x7, waiting for transfers between devices, span_shift(): lax.ppermute(value, 'ctx', [(j, j + offset) for j in range(spans - offset)])  14.7 us
    pallas_call x1, Pallas kernels, run_out(): pl.pallas_call(out_kernel, grid=(width // BLOCK,), in_specs=[pl.BlockSpec...  14.5 us
    ppermute x7, starting transfers between devices, span_shift(): lax.ppermute(value, 'ctx', [(j, j + offset) for j in range(spans - offset)])  14.3 us
    ppermute x2, waiting for transfers between devices, exchange(): lax.ppermute(value, 'tp', [(q, (q + k) % group) for q in range(group)])  13 us
    pallas_call x1, Pallas kernels, run_state(): pl.pallas_call(state_kernel, grid=(width // BLOCK,), in_specs=[pl.BlockSp...  8.55 us
    ppermute x1, starting transfers between devices, shift(): return lax.ppermute(value, axes, pairs)  3.43 us
    add x1, other arithmetic, body(): local = local + local_fix  1.84 us
  transfers between devices with their start and end apart: 10, of which 6 were waited for; matrix products, arithmetic and copies ran while one was open for 2% of the time, Pallas kernels for 11%

profile of v12, /device:TPU:16, one launch (start us, length us, event | category | flops | bytes accessed | tf_op | source)
XLA Modules:
  0.0 76.1 jit_solution(407014542246566151)
XLA Ops:
  0.0 1.1 %slice_convert_fusion = (f32[2,3,4096]{2,0,1:T(2,128)S(1)}, bf16[2,3,4096]{2,0,1:T(2,128)(2,1)S(1)}) fusion(bf16[128,3,4096]{2,0,1:T(8,128)(2,1)} %param.5), kind=kLoop, calls=%fused_computation.28 | loop fusion | flops 24576 | bytes 245760 | tf_op jit(solution)/shard_map/convert_element_type | solution.py:225
  1.1 3.4 %collective-permute-start = (bf16[2,3,4096]{2,0,1:T(2,128)(2,1)S(1)}, bf16[2,3,4096]{2,0,1:T(2,128)(2,1)S(1)}, u32[]{:S(2)}, u32[]{:S(2)}) collective-permute-start(bf16[2,3,4096]{2,0,1:T(2,128)(2,1)S(1)} %get-tuple-element.14), channel_id=1, source_target_pairs={{0,1},{1,2},{2,3},{3,4},{4,5},{5,6},{6,7},{7,8},{8,9},{9,10},{10,1... | collective-permute-start | bytes 147464 | tf_op jit(solution)/shard_map/ppermute | solution.py:216
  4.6 0.9 %fusion.22 = (f32[1,3,4096]{2,1,0:T(4,128)S(1)}, f32[1,3,4096]{2,1,0:T(4,128)S(1)}, f32[1,3,4096]{2,1,0:T(4,128)S(1)}) fusion(f32[3,3,4096]{2,1,0:T(4,128)} %f_ref.3), kind=kLoop, calls=%fused_computation.49 | loop fusion | bytes 294912 | tf_op jit(solution)/shard_map/slice | solution.py:231
  5.5 0.7 broadcast_in_dim.3.halo_ref
  6.2 8.5 %shard_map.55 = (f32[16,8,4096]{2,1,0:T(8,128)}, f32[16,4096]{1,0:T(8,128)}) custom-call(bf16[3,128,4096]{2,1,0:T(8,128)(2,1)} %bitcast.57, f32[3,2,4096]{2,1,0:T(2,128)} %broadcast_in_dim.3.halo_ref, f32[3,3,4096]{2,1,0:T(4,128)} %f_ref.3, f32[16,4096]{1,0:T(8,128)} %bitcast.59), custom_call_target="tpu_custom_call" | custom-call | tf_op jit(solution)/shard_map/pallas_call | solution.py:152
  14.7 0.7 fusion.23
  15.4 0.2 multiply_add_fusion.1
  15.8 1.8 %add_add_fusion = (f32[16,4096]{1,0:T(8,128)S(1)}, f32[16,4096]{1,0:T(8,128)}, f32[16,4096]{1,0:T(8,128)S(1)}) fusion(f32[16,4096]{1,0:T(8,128)} %get-tuple-element.8, f32[4096]{0:T(1024)S(1)} %bitcast.62, f32[4096]{0:T(1024)S(1)} %bitcast.63, f32[4096,16]{0,1:T(8,128)S(1)} %copy-done), kind=kLoop, calls=%fused_computation.1 | loop fusion | flops 786432 | bytes 1343488 | tf_op jit(solution)/shard_map/add | solution.py:248
  17.7 8.0 %collective-permute-done.1 = f32[16,4096]{1,0:T(8,128)S(1)} collective-permute-done((f32[16,4096]{1,0:T(8,128)S(1)}, f32[16,4096]{1,0:T(8,128)S(1)}, u32[]{:S(2)}, u32[]{:S(2)}) %collective-permute-start.1) | collective-permute-done | bytes 262176 | tf_op jit(solution)/shard_map/ppermute | solution.py:256
  25.7 2.1 %collective-permute-start.4 = (f32[16,2048]{1,0:T(8,128)S(1)}, f32[16,2048]{1,0:T(8,128)S(1)}, u32[]{:S(2)}, u32[]{:S(2)}) collective-permute-start(f32[16,2048]{1,0:T(8,128)S(1)} %fusion), channel_id=1, source_target_pairs={{0,6},{2,8},{4,10},{6,12},{8,14},{10,16},{12,18},{14,20},{16,22},{... | collective-permute-start | bytes 393224 | tf_op jit(solution)/shard_map/ppermute | solution.py:277
  27.8 3.3 %collective-permute-start.3 = (f32[16,2048]{1,0:T(8,128)S(1)}, f32[16,2048]{1,0:T(8,128)S(1)}, u32[]{:S(2)}, u32[]{:S(2)}) collective-permute-start(f32[16,2048]{1,0:T(8,128)S(1)} %fusion), channel_id=1, source_target_pairs={{0,4},{2,6},{4,8},{6,10},{8,12},{10,14},{12,16},{14,18},{16,20},{1... | collective-permute-start | bytes 393224 | tf_op jit(solution)/shard_map/ppermute | solution.py:277
  31.1 3.0 %collective-permute-start.2 = (f32[16,2048]{1,0:T(8,128)S(1)}, f32[16,2048]{1,0:T(8,128)S(1)}, u32[]{:S(2)}, u32[]{:S(2)}) collective-permute-start(f32[16,2048]{1,0:T(8,128)S(1)} %fusion), channel_id=1, source_target_pairs={{0,2},{2,4},{4,6},{6,8},{8,10},{10,12},{12,14},{14,16},{16,18},{18... | collective-permute-start | bytes 393224 | tf_op jit(solution)/shard_map/ppermute | solution.py:277
  34.2 2.3 %collective-permute-done.3 = f32[16,2048]{1,0:T(8,128)S(1)} collective-permute-done((f32[16,2048]{1,0:T(8,128)S(1)}, f32[16,2048]{1,0:T(8,128)S(1)}, u32[]{:S(2)}, u32[]{:S(2)}) %collective-permute-start.3) | collective-permute-done | bytes 131104 | tf_op jit(solution)/shard_map/ppermute | solution.py:277
  36.5 1.9 %collective-permute-done.2 = f32[16,2048]{1,0:T(8,128)S(1)} collective-permute-done((f32[16,2048]{1,0:T(8,128)S(1)}, f32[16,2048]{1,0:T(8,128)S(1)}, u32[]{:S(2)}, u32[]{:S(2)}) %collective-permute-start.2) | collective-permute-done | bytes 131104 | tf_op jit(solution)/shard_map/ppermute | solution.py:277
  38.5 0.7 collective-permute-start.8
  39.1 0.7 collective-permute-start.7
  39.8 2.6 %collective-permute-start.6 = (f32[16,2048]{1,0:T(8,128)S(1)}, f32[16,2048]{1,0:T(8,128)S(1)}, u32[]{:S(2)}, u32[]{:S(2)}) collective-permute-start(f32[16,2048]{1,0:T(8,128)S(1)} %fusion.6), channel_id=1, source_target_pairs={{0,12},{2,14},{4,16},{6,18},{8,20},{10,22},{12,24},{14,26},{16,28}... | collective-permute-start | bytes 393224 | tf_op jit(solution)/shard_map/ppermute | solution.py:277
  42.4 1.9 %collective-permute-start.5 = (f32[16,2048]{1,0:T(8,128)S(1)}, f32[16,2048]{1,0:T(8,128)S(1)}, u32[]{:S(2)}, u32[]{:S(2)}) collective-permute-start(f32[16,2048]{1,0:T(8,128)S(1)} %fusion.6), channel_id=1, source_target_pairs={{0,6},{2,8},{4,10},{6,12},{8,14},{10,16},{12,18},{14,20},{16,22},{... | collective-permute-start | bytes 393224 | tf_op jit(solution)/shard_map/ppermute | solution.py:277
  44.4 5.5 %collective-permute-done.6 = f32[16,2048]{1,0:T(8,128)S(1)} collective-permute-done((f32[16,2048]{1,0:T(8,128)S(1)}, f32[16,2048]{1,0:T(8,128)S(1)}, u32[]{:S(2)}, u32[]{:S(2)}) %collective-permute-start.6) | collective-permute-done | bytes 131104 | tf_op jit(solution)/shard_map/ppermute | solution.py:277
  49.9 5.0 %collective-permute-done.5 = f32[16,2048]{1,0:T(8,128)S(1)} collective-permute-done((f32[16,2048]{1,0:T(8,128)S(1)}, f32[16,2048]{1,0:T(8,128)S(1)}, u32[]{:S(2)}, u32[]{:S(2)}) %collective-permute-start.5) | collective-permute-done | bytes 131104 | tf_op jit(solution)/shard_map/ppermute | solution.py:277
  55.0 0.8 %collective-permute-start.9 = (f32[16,2048]{1,0:T(8,128)S(1)}, f32[16,2048]{1,0:T(8,128)S(1)}, u32[]{:S(2)}, u32[]{:S(2)}) collective-permute-start(f32[16,2048]{1,0:T(8,128)S(1)} %get-tuple-element.10), channel_id=1, source_target_pairs={{0,1},{1,0},{2,3},{3,2},{4,5},{5,4},{6,7},{7,6},{8,9},{9,8},{10,11... | collective-permute-start | bytes 393224 | tf_op jit(solution)/shard_map/ppermute | solution.py:256
  55.8 5.0 %collective-permute-done.9 = f32[16,2048]{1,0:T(8,128)S(1)} collective-permute-done((f32[16,2048]{1,0:T(8,128)S(1)}, f32[16,2048]{1,0:T(8,128)S(1)}, u32[]{:S(2)}, u32[]{:S(2)}) %collective-permute-start.9) | collective-permute-done | bytes 131104 | tf_op jit(solution)/shard_map/ppermute | solution.py:256
  60.8 0.8 %select_add_fusion.hin_ref = f32[16,4096]{1,0:T(8,128)} fusion(f32[16,4096]{1,0:T(8,128)S(1)} %collective-permute-done.1, f32[16,4096]{1,0:T(8,128)S(1)} %constant_dynamic-update-slice_fusion, f32[]{:T(128)S(6)} %mul.259, pred[]{:T(512)S(6)} %ge.3, f32[4096,16]{0,1:T(8,128)S(1)} %copy-done), kind=kLoop, calls=%fused_computation | loop fusion | flops 458752 | bytes 1048581 | tf_op jit(solution)/shard_map/add | solution.py:303
  61.6 14.5 %shard_map.56 = bf16[128,4096]{1,0:T(8,128)(2,1)} custom-call(bf16[3,128,4096]{2,1,0:T(8,128)(2,1)} %bitcast.58, f32[3,2,4096]{2,1,0:T(2,128)} %get-tuple-element.24.halo_ref, f32[3,3,4096]{2,1,0:T(4,128)} %f_ref.3, f32[16,4096]{1,0:T(8,128)} %bitcast.60, f32[16,4096]{1,0:T(8,128)} %bitcast.61, f32[1,4096]{1,0:T(1,128)} %bitcast.64, ...), custom_call_target="tpu_custom_call" | custom-call | tf_op jit(solution)/shard_map/pallas_call | solution.py:181
  (14 shorter events, 0.4 us)
Async XLA Ops:
  0.0 15.8 %copy-start = (f32[4096,16]{0,1:T(8,128)S(1)}, f32[4096,16]{0,1:T(8,128)}, u32[]{:S(2)}) copy-start(f32[4096,16]{0,1:T(8,128)} %param.8) | copy-start | bytes 786436
  1.1 13.6 %collective-permute-start = (bf16[2,3,4096]{2,0,1:T(2,128)(2,1)S(1)}, bf16[2,3,4096]{2,0,1:T(2,128)(2,1)S(1)}, u32[]{:S(2)}, u32[]{:S(2)}) collective-permute-start(bf16[2,3,4096]{2,0,1:T(2,128)(2,1)S(1)} %get-tuple-element.14), channel_id=1, source_target_pairs={{0,1},{1,2},{2,3},{3,4},{4,5},{5,6},{6,7},{7,8},{8,9},{9,10},{10,1... | collective-permute-start | bytes 147464 | tf_op jit(solution)/shard_map/ppermute | solution.py:216
  17.7 8.0 %collective-permute-start.1 = (f32[16,4096]{1,0:T(8,128)S(1)}, f32[16,4096]{1,0:T(8,128)S(1)}, u32[]{:S(2)}, u32[]{:S(2)}) collective-permute-start(f32[16,4096]{1,0:T(8,128)S(1)} %get-tuple-element.16), channel_id=1, source_target_pairs={{0,1},{1,0},{2,3},{3,2},{4,5},{5,4},{6,7},{7,6},{8,9},{9,8},{10,11... | collective-permute-start | bytes 786440 | tf_op jit(solution)/shard_map/ppermute | solution.py:256
  25.7 8.4 %collective-permute-start.4 = (f32[16,2048]{1,0:T(8,128)S(1)}, f32[16,2048]{1,0:T(8,128)S(1)}, u32[]{:S(2)}, u32[]{:S(2)}) collective-permute-start(f32[16,2048]{1,0:T(8,128)S(1)} %fusion), channel_id=1, source_target_pairs={{0,6},{2,8},{4,10},{6,12},{8,14},{10,16},{12,18},{14,20},{16,22},{... | collective-permute-start | bytes 393224 | tf_op jit(solution)/shard_map/ppermute | solution.py:277
  27.8 8.6 %collective-permute-start.3 = (f32[16,2048]{1,0:T(8,128)S(1)}, f32[16,2048]{1,0:T(8,128)S(1)}, u32[]{:S(2)}, u32[]{:S(2)}) collective-permute-start(f32[16,2048]{1,0:T(8,128)S(1)} %fusion), channel_id=1, source_target_pairs={{0,4},{2,6},{4,8},{6,10},{8,12},{10,14},{12,16},{14,18},{16,20},{1... | collective-permute-start | bytes 393224 | tf_op jit(solution)/shard_map/ppermute | solution.py:277
  31.1 7.2 %collective-permute-start.2 = (f32[16,2048]{1,0:T(8,128)S(1)}, f32[16,2048]{1,0:T(8,128)S(1)}, u32[]{:S(2)}, u32[]{:S(2)}) collective-permute-start(f32[16,2048]{1,0:T(8,128)S(1)} %fusion), channel_id=1, source_target_pairs={{0,2},{2,4},{4,6},{6,8},{8,10},{10,12},{12,14},{14,16},{16,18},{18... | collective-permute-start | bytes 393224 | tf_op jit(solution)/shard_map/ppermute | solution.py:277
  38.5 5.9 %collective-permute-start.8 = (f32[16,2048]{1,0:T(8,128)S(1)}, f32[16,2048]{1,0:T(8,128)S(1)}, u32[]{:S(2)}, u32[]{:S(2)}) collective-permute-start(f32[16,2048]{1,0:T(8,128)S(1)} %fusion.6), channel_id=1, source_target_pairs={{0,24},{2,26},{4,28},{6,30},{1,25},{3,27},{5,29},{7,31}} | collective-permute-start | bytes 393224 | tf_op jit(solution)/shard_map/ppermute | solution.py:277
  39.1 5.3 %collective-permute-start.7 = (f32[16,2048]{1,0:T(8,128)S(1)}, f32[16,2048]{1,0:T(8,128)S(1)}, u32[]{:S(2)}, u32[]{:S(2)}) collective-permute-start(f32[16,2048]{1,0:T(8,128)S(1)} %fusion.6), channel_id=1, source_target_pairs={{0,18},{2,20},{4,22},{6,24},{8,26},{10,28},{12,30},{1,19},{3,21},{... | collective-permute-start | bytes 393224 | tf_op jit(solution)/shard_map/ppermute | solution.py:277
  39.8 10.1 %collective-permute-start.6 = (f32[16,2048]{1,0:T(8,128)S(1)}, f32[16,2048]{1,0:T(8,128)S(1)}, u32[]{:S(2)}, u32[]{:S(2)}) collective-permute-start(f32[16,2048]{1,0:T(8,128)S(1)} %fusion.6), channel_id=1, source_target_pairs={{0,12},{2,14},{4,16},{6,18},{8,20},{10,22},{12,24},{14,26},{16,28}... | collective-permute-start | bytes 393224 | tf_op jit(solution)/shard_map/ppermute | solution.py:277
  42.4 12.4 %collective-permute-start.5 = (f32[16,2048]{1,0:T(8,128)S(1)}, f32[16,2048]{1,0:T(8,128)S(1)}, u32[]{:S(2)}, u32[]{:S(2)}) collective-permute-start(f32[16,2048]{1,0:T(8,128)S(1)} %fusion.6), channel_id=1, source_target_pairs={{0,6},{2,8},{4,10},{6,12},{8,14},{10,16},{12,18},{14,20},{16,22},{... | collective-permute-start | bytes 393224 | tf_op jit(solution)/shard_map/ppermute | solution.py:277
  55.0 5.8 %collective-permute-start.9 = (f32[16,2048]{1,0:T(8,128)S(1)}, f32[16,2048]{1,0:T(8,128)S(1)}, u32[]{:S(2)}, u32[]{:S(2)}) collective-permute-start(f32[16,2048]{1,0:T(8,128)S(1)} %get-tuple-element.10), channel_id=1, source_target_pairs={{0,1},{1,0},{2,3},{3,2},{4,5},{5,4},{6,7},{7,6},{8,9},{9,8},{10,11... | collective-permute-start | bytes 393224 | tf_op jit(solution)/shard_map/ppermute | solution.py:256

commit v13 on v12

--- a/solution.py
+++ b/solution.py
@@ -8,8 +8,8 @@
 LANES = 128
 SUB = 8
 BLOCK = 1024
-FIRST_WINDOW = 3
-LATER_WINDOW = 4
+FIRST_WINDOW = 2
+LATER_WINDOW = 2
 UNROLL = 8
 
 

time: 77.1 us -> 80.5 us (1.044)
  the two profiles are of different devices: /device:TPU:16 before, /device:TPU:24 now
where the time goes in v13:
time: 80.5 us; the launch traced here: 80.1 us
  waiting for transfers between devices  35.2 us (44%)
  Pallas kernels  23 us (29%)
  starting transfers between devices  15 us (19%)
  other arithmetic  5.09 us (6%)
  local copies, waits for them, and re-layouts  1.63 us (2%)
    ppermute x6, waiting for transfers between devices, span_shift(): lax.ppermute(value, 'ctx', [(j, j + offset) for j in range(spans - offset)])  22.5 us
    pallas_call x1, Pallas kernels, run_out(): pl.pallas_call(out_kernel, grid=(width // BLOCK,), in_specs=[pl.BlockSpec...  14.5 us
    ppermute x2, waiting for transfers between devices, exchange(): lax.ppermute(value, 'tp', [(q, (q + k) % group) for q in range(group)])  12.7 us
    ppermute x6, starting transfers between devices, span_shift(): lax.ppermute(value, 'ctx', [(j, j + offset) for j in range(spans - offset)])  10.9 us
    pallas_call x1, Pallas kernels, run_state(): pl.pallas_call(state_kernel, grid=(width // BLOCK,), in_specs=[pl.BlockSp...  8.53 us
    ppermute x1, starting transfers between devices, shift(): return lax.ppermute(value, axes, pairs)  3.43 us
    add x1, other arithmetic, body(): local = local + local_fix  1.84 us
  transfers between devices with their start and end apart: 9, of which 8 were waited for; matrix products, arithmetic and copies ran while one was open for 2% of the time, Pallas kernels for 11%

profile of v13, /device:TPU:24, one launch (start us, length us, event | category | flops | bytes accessed | tf_op | source)
XLA Modules:
  0.0 80.1 jit_solution(1617819037185907597)
XLA Ops:
  0.0 1.1 %slice_convert_fusion = (f32[2,3,4096]{2,0,1:T(2,128)S(1)}, bf16[2,3,4096]{2,0,1:T(2,128)(2,1)S(1)}) fusion(bf16[128,3,4096]{2,0,1:T(8,128)(2,1)} %param.5), kind=kLoop, calls=%fused_computation.27 | loop fusion | flops 24576 | bytes 245760 | tf_op jit(solution)/shard_map/convert_element_type | solution.py:225
  1.1 3.4 %collective-permute-start = (bf16[2,3,4096]{2,0,1:T(2,128)(2,1)S(1)}, bf16[2,3,4096]{2,0,1:T(2,128)(2,1)S(1)}, u32[]{:S(2)}, u32[]{:S(2)}) collective-permute-start(bf16[2,3,4096]{2,0,1:T(2,128)(2,1)S(1)} %get-tuple-element.14), channel_id=1, source_target_pairs={{0,1},{1,2},{2,3},{3,4},{4,5},{5,6},{6,7},{7,8},{8,9},{9,10},{10,1... | collective-permute-start | bytes 147464 | tf_op jit(solution)/shard_map/ppermute | solution.py:216
  4.6 0.9 %fusion.20 = (f32[1,3,4096]{2,1,0:T(4,128)S(1)}, f32[1,3,4096]{2,1,0:T(4,128)S(1)}, f32[1,3,4096]{2,1,0:T(4,128)S(1)}) fusion(f32[3,3,4096]{2,1,0:T(4,128)} %f_ref.3), kind=kLoop, calls=%fused_computation.48 | loop fusion | bytes 294912 | tf_op jit(solution)/shard_map/slice | solution.py:231
  5.5 0.7 broadcast_in_dim.3.halo_ref
  6.2 8.5 %shard_map.55 = (f32[16,8,4096]{2,1,0:T(8,128)}, f32[16,4096]{1,0:T(8,128)}) custom-call(bf16[3,128,4096]{2,1,0:T(8,128)(2,1)} %bitcast.49, f32[3,2,4096]{2,1,0:T(2,128)} %broadcast_in_dim.3.halo_ref, f32[3,3,4096]{2,1,0:T(4,128)} %f_ref.3, f32[16,4096]{1,0:T(8,128)} %bitcast.51), custom_call_target="tpu_custom_call" | custom-call | tf_op jit(solution)/shard_map/pallas_call | solution.py:152
  14.7 0.7 fusion.21
  15.8 1.8 %add_add_fusion = (f32[16,4096]{1,0:T(8,128)S(1)}, f32[16,4096]{1,0:T(8,128)}, f32[16,4096]{1,0:T(8,128)S(1)}) fusion(f32[16,4096]{1,0:T(8,128)} %get-tuple-element.8, f32[4096]{0:T(1024)S(1)} %bitcast.54, f32[4096]{0:T(1024)S(1)} %bitcast.55, f32[4096,16]{0,1:T(8,128)S(1)} %copy-done), kind=kLoop, calls=%fused_computation.1 | loop fusion | flops 786432 | bytes 1343488 | tf_op jit(solution)/shard_map/add | solution.py:248
  17.7 8.0 %collective-permute-done.1 = f32[16,4096]{1,0:T(8,128)S(1)} collective-permute-done((f32[16,4096]{1,0:T(8,128)S(1)}, f32[16,4096]{1,0:T(8,128)S(1)}, u32[]{:S(2)}, u32[]{:S(2)}) %collective-permute-start.1) | collective-permute-done | bytes 262176 | tf_op jit(solution)/shard_map/ppermute | solution.py:256
  25.7 1.9 %collective-permute-start.2 = (f32[16,2048]{1,0:T(8,128)S(1)}, f32[16,2048]{1,0:T(8,128)S(1)}, u32[]{:S(2)}, u32[]{:S(2)}) collective-permute-start(f32[16,2048]{1,0:T(8,128)S(1)} %fusion), channel_id=1, source_target_pairs={{0,2},{2,4},{4,6},{6,8},{8,10},{10,12},{12,14},{14,16},{16,18},{18... | collective-permute-start | bytes 393224 | tf_op jit(solution)/shard_map/ppermute | solution.py:277
  27.6 3.1 %collective-permute-start.3 = (f32[16,2048]{1,0:T(8,128)S(1)}, f32[16,2048]{1,0:T(8,128)S(1)}, u32[]{:S(2)}, u32[]{:S(2)}) collective-permute-start(f32[16,2048]{1,0:T(8,128)S(1)} %fusion), channel_id=1, source_target_pairs={{0,4},{2,6},{4,8},{6,10},{8,12},{10,14},{12,16},{14,18},{16,20},{1... | collective-permute-start | bytes 393224 | tf_op jit(solution)/shard_map/ppermute | solution.py:277
  30.8 2.1 %collective-permute-done.2 = f32[16,2048]{1,0:T(8,128)S(1)} collective-permute-done((f32[16,2048]{1,0:T(8,128)S(1)}, f32[16,2048]{1,0:T(8,128)S(1)}, u32[]{:S(2)}, u32[]{:S(2)}) %collective-permute-start.2) | collective-permute-done | bytes 131104 | tf_op jit(solution)/shard_map/ppermute | solution.py:277
  32.9 3.6 %collective-permute-done.3 = f32[16,2048]{1,0:T(8,128)S(1)} collective-permute-done((f32[16,2048]{1,0:T(8,128)S(1)}, f32[16,2048]{1,0:T(8,128)S(1)}, u32[]{:S(2)}, u32[]{:S(2)}) %collective-permute-start.3) | collective-permute-done | bytes 131104 | tf_op jit(solution)/shard_map/ppermute | solution.py:277
  36.6 1.3 %collective-permute-start.5 = (f32[16,2048]{1,0:T(8,128)S(1)}, f32[16,2048]{1,0:T(8,128)S(1)}, u32[]{:S(2)}, u32[]{:S(2)}) collective-permute-start(f32[16,2048]{1,0:T(8,128)S(1)} %fusion.5), channel_id=1, source_target_pairs={{0,8},{2,10},{4,12},{6,14},{8,16},{10,18},{12,20},{14,22},{16,24},... | collective-permute-start | bytes 393224 | tf_op jit(solution)/shard_map/ppermute | solution.py:277
  37.9 2.0 %collective-permute-start.4 = (f32[16,2048]{1,0:T(8,128)S(1)}, f32[16,2048]{1,0:T(8,128)S(1)}, u32[]{:S(2)}, u32[]{:S(2)}) collective-permute-start(f32[16,2048]{1,0:T(8,128)S(1)} %fusion.5), channel_id=1, source_target_pairs={{0,4},{2,6},{4,8},{6,10},{8,12},{10,14},{12,16},{14,18},{16,20},{1... | collective-permute-start | bytes 393224 | tf_op jit(solution)/shard_map/ppermute | solution.py:277
  39.9 4.1 %collective-permute-done.5 = f32[16,2048]{1,0:T(8,128)S(1)} collective-permute-done((f32[16,2048]{1,0:T(8,128)S(1)}, f32[16,2048]{1,0:T(8,128)S(1)}, u32[]{:S(2)}, u32[]{:S(2)}) %collective-permute-start.5) | collective-permute-done | bytes 131104 | tf_op jit(solution)/shard_map/ppermute | solution.py:277
  44.0 2.2 %collective-permute-done.4 = f32[16,2048]{1,0:T(8,128)S(1)} collective-permute-done((f32[16,2048]{1,0:T(8,128)S(1)}, f32[16,2048]{1,0:T(8,128)S(1)}, u32[]{:S(2)}, u32[]{:S(2)}) %collective-permute-start.4) | collective-permute-done | bytes 131104 | tf_op jit(solution)/shard_map/ppermute | solution.py:277
  46.3 1.3 %collective-permute-start.7 = (f32[16,2048]{1,0:T(8,128)S(1)}, f32[16,2048]{1,0:T(8,128)S(1)}, u32[]{:S(2)}, u32[]{:S(2)}) collective-permute-start(f32[16,2048]{1,0:T(8,128)S(1)} %fusion.4), channel_id=1, source_target_pairs={{0,24},{2,26},{4,28},{6,30},{1,25},{3,27},{5,29},{7,31}} | collective-permute-start | bytes 393224 | tf_op jit(solution)/shard_map/ppermute | solution.py:277
  47.6 1.3 %collective-permute-start.6 = (f32[16,2048]{1,0:T(8,128)S(1)}, f32[16,2048]{1,0:T(8,128)S(1)}, u32[]{:S(2)}, u32[]{:S(2)}) collective-permute-start(f32[16,2048]{1,0:T(8,128)S(1)} %fusion.4), channel_id=1, source_target_pairs={{0,12},{2,14},{4,16},{6,18},{8,20},{10,22},{12,24},{14,26},{16,28}... | collective-permute-start | bytes 393224 | tf_op jit(solution)/shard_map/ppermute | solution.py:277
  48.9 7.2 %collective-permute-done.7 = f32[16,2048]{1,0:T(8,128)S(1)} collective-permute-done((f32[16,2048]{1,0:T(8,128)S(1)}, f32[16,2048]{1,0:T(8,128)S(1)}, u32[]{:S(2)}, u32[]{:S(2)}) %collective-permute-start.7) | collective-permute-done | bytes 131104 | tf_op jit(solution)/shard_map/ppermute | solution.py:277
  56.1 3.3 %collective-permute-done.6 = f32[16,2048]{1,0:T(8,128)S(1)} collective-permute-done((f32[16,2048]{1,0:T(8,128)S(1)}, f32[16,2048]{1,0:T(8,128)S(1)}, u32[]{:S(2)}, u32[]{:S(2)}) %collective-permute-start.6) | collective-permute-done | bytes 131104 | tf_op jit(solution)/shard_map/ppermute | solution.py:277
  59.5 0.7 collective-permute-start.8
  60.1 4.7 %collective-permute-done.8 = f32[16,2048]{1,0:T(8,128)S(1)} collective-permute-done((f32[16,2048]{1,0:T(8,128)S(1)}, f32[16,2048]{1,0:T(8,128)S(1)}, u32[]{:S(2)}, u32[]{:S(2)}) %collective-permute-start.8) | collective-permute-done | bytes 131104 | tf_op jit(solution)/shard_map/ppermute | solution.py:256
  64.8 0.8 %select_add_fusion.hin_ref = f32[16,4096]{1,0:T(8,128)} fusion(f32[16,4096]{1,0:T(8,128)S(1)} %collective-permute-done.1, f32[16,4096]{1,0:T(8,128)S(1)} %constant_dynamic-update-slice_fusion, f32[]{:T(128)S(6)} %mul.244, pred[]{:T(512)S(6)} %ge.3, f32[4096,16]{0,1:T(8,128)S(1)} %copy-done), kind=kLoop, calls=%fused_computation | loop fusion | flops 458752 | bytes 1048581 | tf_op jit(solution)/shard_map/add | solution.py:303
  65.6 14.5 %shard_map.56 = bf16[128,4096]{1,0:T(8,128)(2,1)} custom-call(bf16[3,128,4096]{2,1,0:T(8,128)(2,1)} %bitcast.50, f32[3,2,4096]{2,1,0:T(2,128)} %get-tuple-element.24.halo_ref, f32[3,3,4096]{2,1,0:T(4,128)} %f_ref.3, f32[16,4096]{1,0:T(8,128)} %bitcast.52, f32[16,4096]{1,0:T(8,128)} %bitcast.53, f32[1,4096]{1,0:T(1,128)} %bitcast.56, ...), custom_call_target="tpu_custom_call" | custom-call | tf_op jit(solution)/shard_map/pallas_call | solution.py:181
  (13 shorter events, 0.7 us)
Async XLA Ops:
  0.0 15.8 %copy-start = (f32[4096,16]{0,1:T(8,128)S(1)}, f32[4096,16]{0,1:T(8,128)}, u32[]{:S(2)}) copy-start(f32[4096,16]{0,1:T(8,128)} %param.8) | copy-start | bytes 786436
  1.1 13.6 %collective-permute-start = (bf16[2,3,4096]{2,0,1:T(2,128)(2,1)S(1)}, bf16[2,3,4096]{2,0,1:T(2,128)(2,1)S(1)}, u32[]{:S(2)}, u32[]{:S(2)}) collective-permute-start(bf16[2,3,4096]{2,0,1:T(2,128)(2,1)S(1)} %get-tuple-element.14), channel_id=1, source_target_pairs={{0,1},{1,2},{2,3},{3,4},{4,5},{5,6},{6,7},{7,8},{8,9},{9,10},{10,1... | collective-permute-start | bytes 147464 | tf_op jit(solution)/shard_map/ppermute | solution.py:216
  17.6 8.0 %collective-permute-start.1 = (f32[16,4096]{1,0:T(8,128)S(1)}, f32[16,4096]{1,0:T(8,128)S(1)}, u32[]{:S(2)}, u32[]{:S(2)}) collective-permute-start(f32[16,4096]{1,0:T(8,128)S(1)} %get-tuple-element.16), channel_id=1, source_target_pairs={{0,1},{1,0},{2,3},{3,2},{4,5},{5,4},{6,7},{7,6},{8,9},{9,8},{10,11... | collective-permute-start | bytes 786440 | tf_op jit(solution)/shard_map/ppermute | solution.py:256
  25.7 7.2 %collective-permute-start.2 = (f32[16,2048]{1,0:T(8,128)S(1)}, f32[16,2048]{1,0:T(8,128)S(1)}, u32[]{:S(2)}, u32[]{:S(2)}) collective-permute-start(f32[16,2048]{1,0:T(8,128)S(1)} %fusion), channel_id=1, source_target_pairs={{0,2},{2,4},{4,6},{6,8},{8,10},{10,12},{12,14},{14,16},{16,18},{18... | collective-permute-start | bytes 393224 | tf_op jit(solution)/shard_map/ppermute | solution.py:277
  27.6 8.9 %collective-permute-start.3 = (f32[16,2048]{1,0:T(8,128)S(1)}, f32[16,2048]{1,0:T(8,128)S(1)}, u32[]{:S(2)}, u32[]{:S(2)}) collective-permute-start(f32[16,2048]{1,0:T(8,128)S(1)} %fusion), channel_id=1, source_target_pairs={{0,4},{2,6},{4,8},{6,10},{8,12},{10,14},{12,16},{14,18},{16,20},{1... | collective-permute-start | bytes 393224 | tf_op jit(solution)/shard_map/ppermute | solution.py:277
  36.6 7.4 %collective-permute-start.5 = (f32[16,2048]{1,0:T(8,128)S(1)}, f32[16,2048]{1,0:T(8,128)S(1)}, u32[]{:S(2)}, u32[]{:S(2)}) collective-permute-start(f32[16,2048]{1,0:T(8,128)S(1)} %fusion.5), channel_id=1, source_target_pairs={{0,8},{2,10},{4,12},{6,14},{8,16},{10,18},{12,20},{14,22},{16,24},... | collective-permute-start | bytes 393224 | tf_op jit(solution)/shard_map/ppermute | solution.py:277
  37.9 8.3 %collective-permute-start.4 = (f32[16,2048]{1,0:T(8,128)S(1)}, f32[16,2048]{1,0:T(8,128)S(1)}, u32[]{:S(2)}, u32[]{:S(2)}) collective-permute-start(f32[16,2048]{1,0:T(8,128)S(1)} %fusion.5), channel_id=1, source_target_pairs={{0,4},{2,6},{4,8},{6,10},{8,12},{10,14},{12,16},{14,18},{16,20},{1... | collective-permute-start | bytes 393224 | tf_op jit(solution)/shard_map/ppermute | solution.py:277
  46.3 9.8 %collective-permute-start.7 = (f32[16,2048]{1,0:T(8,128)S(1)}, f32[16,2048]{1,0:T(8,128)S(1)}, u32[]{:S(2)}, u32[]{:S(2)}) collective-permute-start(f32[16,2048]{1,0:T(8,128)S(1)} %fusion.4), channel_id=1, source_target_pairs={{0,24},{2,26},{4,28},{6,30},{1,25},{3,27},{5,29},{7,31}} | collective-permute-start | bytes 393224 | tf_op jit(solution)/shard_map/ppermute | solution.py:277
  47.6 11.8 %collective-permute-start.6 = (f32[16,2048]{1,0:T(8,128)S(1)}, f32[16,2048]{1,0:T(8,128)S(1)}, u32[]{:S(2)}, u32[]{:S(2)}) collective-permute-start(f32[16,2048]{1,0:T(8,128)S(1)} %fusion.4), channel_id=1, source_target_pairs={{0,12},{2,14},{4,16},{6,18},{8,20},{10,22},{12,24},{14,26},{16,28}... | collective-permute-start | bytes 393224 | tf_op jit(solution)/shard_map/ppermute | solution.py:277
  59.5 5.3 %collective-permute-start.8 = (f32[16,2048]{1,0:T(8,128)S(1)}, f32[16,2048]{1,0:T(8,128)S(1)}, u32[]{:S(2)}, u32[]{:S(2)}) collective-permute-start(f32[16,2048]{1,0:T(8,128)S(1)} %get-tuple-element.10), channel_id=1, source_target_pairs={{0,1},{1,0},{2,3},{3,2},{4,5},{5,4},{6,7},{7,6},{8,9},{9,8},{10,11... | collective-permute-start | bytes 393224 | tf_op jit(solution)/shard_map/ppermute | solution.py:256

commit v14 on v12

--- a/solution.py
+++ b/solution.py
@@ -174,34 +174,57 @@
     )(x, halo, f, rate_t)
 
 
-def run_out(x, halo, f, rate_t, residue_t, skip, ends, fix, hin):
+def run_out_part(x, halo, f, rate_t, residue_t, skip, ends, fix, hin, first_block, prior=None):
     streams_count, rows, width = x.shape
     taps = f.shape[0]
     modes = rate_t.shape[0]
-    return pl.pallas_call(
-        out_kernel,
-        grid=(width // BLOCK,),
-        in_specs=[
-            pl.BlockSpec((streams_count, rows, BLOCK), lambda i: (0, 0, i)),
-            pl.BlockSpec((streams_count, taps - 1, BLOCK), lambda i: (0, 0, i)),
-            pl.BlockSpec((taps, streams_count, BLOCK), lambda i: (0, 0, i)),
-            pl.BlockSpec((modes, BLOCK), lambda i: (0, i)),
-            pl.BlockSpec((modes, BLOCK), lambda i: (0, i)),
-            pl.BlockSpec((1, BLOCK), lambda i: (0, i)),
-            pl.BlockSpec((modes, SUB, BLOCK), lambda i: (0, 0, i)),
-            pl.BlockSpec((modes, BLOCK), lambda i: (0, i)),
-            pl.BlockSpec((modes, BLOCK), lambda i: (0, i)),
-        ],
-        out_specs=pl.BlockSpec((rows, BLOCK), lambda i: (0, i)),
-        out_shape=jax.ShapeDtypeStruct((rows, width), jnp.bfloat16),
+    block = min(BLOCK, hin.shape[1])
+
+    def at(i, off):
+        return off[0] + i
+
+    in_specs = [
+        pl.BlockSpec((streams_count, rows, block), lambda i, off: (0, 0, at(i, off))),
+        pl.BlockSpec((streams_count, taps - 1, block), lambda i, off: (0, 0, at(i, off))),
+        pl.BlockSpec((taps, streams_count, block), lambda i, off: (0, 0, at(i, off))),
+        pl.BlockSpec((modes, block), lambda i, off: (0, at(i, off))),
+        pl.BlockSpec((modes, block), lambda i, off: (0, at(i, off))),
+        pl.BlockSpec((1, block), lambda i, off: (0, at(i, off))),
+        pl.BlockSpec((modes, SUB, block), lambda i, off: (0, 0, at(i, off))),
+        pl.BlockSpec((modes, block), lambda i, off: (0, at(i, off))),
+        pl.BlockSpec((modes, block), lambda i, off: (0, i)),
+    ]
+    operands = [x, halo, f, rate_t, residue_t, skip, ends, fix, hin]
+    count = len(operands)
+    aliases = {}
+    if prior is not None:
+        in_specs.append(pl.BlockSpec(memory_space=pl.ANY))
+        operands.append(prior)
+        aliases = {len(operands): 0}
+
+    def kernel(off_ref, *refs):
+        out_kernel(*refs[:count], *refs[len(operands) :])
+
+    grid_spec = pltpu.PrefetchScalarGridSpec(
+        num_scalar_prefetch=1,
+        grid=(hin.shape[1] // block,),
+        in_specs=in_specs,
+        out_specs=pl.BlockSpec((rows, block), lambda i, off: (0, at(i, off))),
         scratch_shapes=[
-            pltpu.VMEM((streams_count, BLOCK // LANES, rows, LANES), jnp.float32),
-            pltpu.VMEM((BLOCK // LANES, rows, LANES), jnp.float32),
+            pltpu.VMEM((streams_count, block // LANES, rows, LANES), jnp.float32),
+            pltpu.VMEM((block // LANES, rows, LANES), jnp.float32),
             pltpu.VMEM((modes, SUB, LANES), jnp.float32),
             pltpu.VMEM((modes, SUB, LANES), jnp.float32),
             pltpu.VMEM((taps * streams_count, SUB, LANES), jnp.float32),
         ],
-    )(x, halo, f, rate_t, residue_t, skip, ends, fix, hin)
+    )
+    offset = jnp.reshape(first_block, (1,)).astype(jnp.int32)
+    return pl.pallas_call(
+        kernel,
+        grid_spec=grid_spec,
+        out_shape=jax.ShapeDtypeStruct((rows, width), jnp.bfloat16),
+        input_output_aliases=aliases,
+    )(offset, *operands)
 
 
 def body(streams, short_filter, skip, rates, residues):
@@ -296,13 +319,18 @@
     else:
         before = jnp.zeros_like(total_part)
 
-    whole = jnp.zeros_like(local)
+    out = None
     for k in range(group):
         part = before if k == 0 else exchange(before, k)
-        whole = lax.dynamic_update_slice_in_dim(whole, part, ((member - k) % group) * piece, 1)
-    carried = powers(rate_t, member.astype(jnp.float32)) * whole + inside
-
-    return run_out(x, halo, short_filter, rate_t, residue_t, skip.reshape(1, width), ends, ends_fix, carried)
+        slot = (member - k) % group
+        rate_slot = lax.dynamic_slice_in_dim(rate_t, slot * piece, piece, 1)
+        inside_slot = lax.dynamic_slice_in_dim(inside, slot * piece, piece, 1)
+        hin = powers(rate_slot, member.astype(jnp.float32)) * part + inside_slot
+        out = run_out_part(
+            x, halo, short_filter, rate_t, residue_t, skip.reshape(1, width), ends, ends_fix, hin,
+            slot * (piece // min(BLOCK, piece)), out,
+        )
+    return out
 
 
 def solution(mesh):

time: 77.1 us -> 78.1 us (1.013)
  the two profiles are of different devices: /device:TPU:16 before, /device:TPU:21 now
where the time goes in v14:
time: 78.1 us; the launch traced here: 77.7 us
  waiting for transfers between devices  25.6 us (33%)
  Pallas kernels  25.4 us (33%)
  starting transfers between devices  19.3 us (25%)
  other arithmetic  5.71 us (7%)
  local copies, waits for them, and re-layouts  1.61 us (2%)
    ppermute x7, waiting for transfers between devices, span_shift(): lax.ppermute(value, 'ctx', [(j, j + offset) for j in range(spans - offset)])  18.1 us
    pallas_call x2, Pallas kernels, run_out_part(): pl.pallas_call(kernel, grid_spec=grid_spec, out_shape=jax.ShapeDtypeStruc...  16.8 us
    ppermute x7, starting transfers between devices, span_shift(): lax.ppermute(value, 'ctx', [(j, j + offset) for j in range(spans - offset)])  14.4 us
    pallas_call x1, Pallas kernels, run_state(): pl.pallas_call(state_kernel, grid=(width // BLOCK,), in_specs=[pl.BlockSp...  8.57 us
    ppermute x2, waiting for transfers between devices, exchange(): lax.ppermute(value, 'tp', [(q, (q + k) % group) for q in range(group)])  7.46 us
    ppermute x1, starting transfers between devices, shift(): return lax.ppermute(value, axes, pairs)  3.62 us
    add x1, other arithmetic, body(): local = local + local_fix  1.82 us
  transfers between devices with their start and end apart: 10, of which 5 were waited for; matrix products, arithmetic and copies ran while one was open for 2% of the time, Pallas kernels for 22%

profile of v14, /device:TPU:21, one launch (start us, length us, event | category | flops | bytes accessed | tf_op | source)
XLA Modules:
  0.0 77.7 jit_solution(12480066056164675429)
XLA Ops:
  0.0 1.1 %slice_convert_fusion = (f32[2,3,4096]{2,0,1:T(2,128)S(1)}, bf16[2,3,4096]{2,0,1:T(2,128)(2,1)S(1)}) fusion(bf16[128,3,4096]{2,0,1:T(8,128)(2,1)} %param.5), kind=kLoop, calls=%fused_computation.32 | loop fusion | flops 24576 | bytes 245760 | tf_op jit(solution)/shard_map/convert_element_type | solution.py:248
  1.1 3.6 %collective-permute-start = (bf16[2,3,4096]{2,0,1:T(2,128)(2,1)S(1)}, bf16[2,3,4096]{2,0,1:T(2,128)(2,1)S(1)}, u32[]{:S(2)}, u32[]{:S(2)}) collective-permute-start(bf16[2,3,4096]{2,0,1:T(2,128)(2,1)S(1)} %get-tuple-element.14), channel_id=1, source_target_pairs={{0,1},{1,2},{2,3},{3,4},{4,5},{5,6},{6,7},{7,8},{8,9},{9,10},{10,1... | collective-permute-start | bytes 147464 | tf_op jit(solution)/shard_map/ppermute | solution.py:239
  4.8 0.9 %fusion.24 = (f32[1,3,4096]{2,1,0:T(4,128)S(1)}, f32[1,3,4096]{2,1,0:T(4,128)S(1)}, f32[1,3,4096]{2,1,0:T(4,128)S(1)}) fusion(f32[3,3,4096]{2,1,0:T(4,128)} %refs_2_.3), kind=kLoop, calls=%fused_computation.51 | loop fusion | bytes 294912 | tf_op jit(solution)/shard_map/slice | solution.py:254
  5.7 0.7 broadcast_in_dim.3.halo_ref
  6.4 8.6 %shard_map.55 = (f32[16,8,4096]{2,1,0:T(8,128)}, f32[16,4096]{1,0:T(8,128)}) custom-call(bf16[3,128,4096]{2,1,0:T(8,128)(2,1)} %bitcast.67, f32[3,2,4096]{2,1,0:T(2,128)} %broadcast_in_dim.3.halo_ref, f32[3,3,4096]{2,1,0:T(4,128)} %refs_2_.3, f32[16,4096]{1,0:T(8,128)} %bitcast.70), custom_call_target="tpu_custom_call" | custom-call | tf_op jit(solution)/shard_map/pallas_call | solution.py:152
  14.9 0.7 fusion.25
  16.1 1.8 %add_add_fusion = (f32[16,4096]{1,0:T(8,128)S(1)}, f32[16,4096]{1,0:T(8,128)}) fusion(f32[16,4096]{1,0:T(8,128)} %get-tuple-element.8, f32[4096]{0:T(1024)S(1)} %bitcast.77, f32[4096]{0:T(1024)S(1)} %bitcast.78, f32[4096,16]{0,1:T(8,128)S(1)} %copy-done), kind=kLoop, calls=%fused_computation.1 | loop fusion | flops 786432 | bytes 1081344 | tf_op jit(solution)/shard_map/add | solution.py:271
  17.9 7.5 %collective-permute-done.1 = f32[16,4096]{1,0:T(8,128)S(1)} collective-permute-done((f32[16,4096]{1,0:T(8,128)S(1)}, f32[16,4096]{1,0:T(8,128)S(1)}, u32[]{:S(2)}, u32[]{:S(2)}) %collective-permute-start.1) | collective-permute-done | bytes 262176 | tf_op jit(solution)/shard_map/ppermute | solution.py:279
  25.5 3.1 %collective-permute-start.3 = (f32[16,2048]{1,0:T(8,128)S(1)}, f32[16,2048]{1,0:T(8,128)S(1)}, u32[]{:S(2)}, u32[]{:S(2)}) collective-permute-start(f32[16,2048]{1,0:T(8,128)S(1)} %fusion), channel_id=1, source_target_pairs={{0,4},{2,6},{4,8},{6,10},{8,12},{10,14},{12,16},{14,18},{16,20},{1... | collective-permute-start | bytes 393224 | tf_op jit(solution)/shard_map/ppermute | solution.py:300
  28.6 3.5 %collective-permute-start.2 = (f32[16,2048]{1,0:T(8,128)S(1)}, f32[16,2048]{1,0:T(8,128)S(1)}, u32[]{:S(2)}, u32[]{:S(2)}) collective-permute-start(f32[16,2048]{1,0:T(8,128)S(1)} %fusion), channel_id=1, source_target_pairs={{0,2},{2,4},{4,6},{6,8},{8,10},{10,12},{12,14},{14,16},{16,18},{18... | collective-permute-start | bytes 393224 | tf_op jit(solution)/shard_map/ppermute | solution.py:300
  32.1 1.9 %collective-permute-start.4 = (f32[16,2048]{1,0:T(8,128)S(1)}, f32[16,2048]{1,0:T(8,128)S(1)}, u32[]{:S(2)}, u32[]{:S(2)}) collective-permute-start(f32[16,2048]{1,0:T(8,128)S(1)} %fusion), channel_id=1, source_target_pairs={{0,6},{2,8},{4,10},{6,12},{8,14},{10,16},{12,18},{14,20},{16,22},{... | collective-permute-start | bytes 393224 | tf_op jit(solution)/shard_map/ppermute | solution.py:300
  34.1 5.2 %collective-permute-done.4 = f32[16,2048]{1,0:T(8,128)S(1)} collective-permute-done((f32[16,2048]{1,0:T(8,128)S(1)}, f32[16,2048]{1,0:T(8,128)S(1)}, u32[]{:S(2)}, u32[]{:S(2)}) %collective-permute-start.4) | collective-permute-done | bytes 131104 | tf_op jit(solution)/shard_map/ppermute | solution.py:300
  39.4 0.7 collective-permute-start.8
  40.1 1.3 %collective-permute-start.7 = (f32[16,2048]{1,0:T(8,128)S(1)}, f32[16,2048]{1,0:T(8,128)S(1)}, u32[]{:S(2)}, u32[]{:S(2)}) collective-permute-start(f32[16,2048]{1,0:T(8,128)S(1)} %fusion.7), channel_id=1, source_target_pairs={{0,18},{2,20},{4,22},{6,24},{8,26},{10,28},{12,30},{1,19},{3,21},{... | collective-permute-start | bytes 393224 | tf_op jit(solution)/shard_map/ppermute | solution.py:300
  41.4 1.9 %collective-permute-start.6 = (f32[16,2048]{1,0:T(8,128)S(1)}, f32[16,2048]{1,0:T(8,128)S(1)}, u32[]{:S(2)}, u32[]{:S(2)}) collective-permute-start(f32[16,2048]{1,0:T(8,128)S(1)} %fusion.7), channel_id=1, source_target_pairs={{0,12},{2,14},{4,16},{6,18},{8,20},{10,22},{12,24},{14,26},{16,28}... | collective-permute-start | bytes 393224 | tf_op jit(solution)/shard_map/ppermute | solution.py:300
  43.3 1.9 %collective-permute-start.5 = (f32[16,2048]{1,0:T(8,128)S(1)}, f32[16,2048]{1,0:T(8,128)S(1)}, u32[]{:S(2)}, u32[]{:S(2)}) collective-permute-start(f32[16,2048]{1,0:T(8,128)S(1)} %fusion.7), channel_id=1, source_target_pairs={{0,6},{2,8},{4,10},{6,12},{8,14},{10,16},{12,18},{14,20},{16,22},{... | collective-permute-start | bytes 393224 | tf_op jit(solution)/shard_map/ppermute | solution.py:300
  45.3 4.4 %collective-permute-done.7 = f32[16,2048]{1,0:T(8,128)S(1)} collective-permute-done((f32[16,2048]{1,0:T(8,128)S(1)}, f32[16,2048]{1,0:T(8,128)S(1)}, u32[]{:S(2)}, u32[]{:S(2)}) %collective-permute-start.7) | collective-permute-done | bytes 131104 | tf_op jit(solution)/shard_map/ppermute | solution.py:300
  49.7 1.9 %collective-permute-done.6 = f32[16,2048]{1,0:T(8,128)S(1)} collective-permute-done((f32[16,2048]{1,0:T(8,128)S(1)}, f32[16,2048]{1,0:T(8,128)S(1)}, u32[]{:S(2)}, u32[]{:S(2)}) %collective-permute-start.6) | collective-permute-done | bytes 131104 | tf_op jit(solution)/shard_map/ppermute | solution.py:300
  51.6 6.5 %collective-permute-done.5 = f32[16,2048]{1,0:T(8,128)S(1)} collective-permute-done((f32[16,2048]{1,0:T(8,128)S(1)}, f32[16,2048]{1,0:T(8,128)S(1)}, u32[]{:S(2)}, u32[]{:S(2)}) %collective-permute-start.5) | collective-permute-done | bytes 131104 | tf_op jit(solution)/shard_map/ppermute | solution.py:300
  58.1 0.8 %fusion.1 = (f32[16,2048]{1,0:T(8,128)}, f32[16,2048]{1,0:T(8,128)S(1)}) fusion(f32[16,4096]{1,0:T(8,128)S(1)} %get-tuple-element.20, s32[]{:T(128)S(6)} %select_n.39, f32[4096,16]{0,1:T(8,128)S(1)} %copy-done, f32[]{:T(128)S(6)} %mul.282, f32[16,2048]{1,0:T(8,128)S(1)} %fusion.7, f32[16,2048]{1,0:T(8,128)S(1)} %collective-permute-done.8, ...), kind=kLoop, calls=%fused_computation.7 | loop fusion | flops 589824 | bytes 1310732 | tf_op jit(solution)/shard_map/add | solution.py:328
  58.9 1.3 %collective-permute-start.9 = (f32[16,2048]{1,0:T(8,128)S(1)}, f32[16,2048]{1,0:T(8,128)S(1)}, u32[]{:S(2)}, u32[]{:S(2)}) collective-permute-start(f32[16,2048]{1,0:T(8,128)S(1)} %get-tuple-element.10), channel_id=1, source_target_pairs={{0,1},{1,0},{2,3},{3,2},{4,5},{5,4},{6,7},{7,6},{8,9},{9,8},{10,11... | collective-permute-start | bytes 393224 | tf_op jit(solution)/shard_map/ppermute | solution.py:279
  60.2 8.4 %shard_map.56.refs_9_ = bf16[128,4096]{1,0:T(8,128)(2,1)} custom-call(s32[1]{0:T(128)} %bitcast.15.off_ref, bf16[3,128,4096]{2,1,0:T(8,128)(2,1)} %bitcast.68, f32[3,2,4096]{2,1,0:T(2,128)} %get-tuple-element.25.refs_1_, f32[3,3,4096]{2,1,0:T(4,128)} %refs_2_.3, f32[16,4096]{1,0:T(8,128)} %bitcast.71, f32[16,4096]{1,0:T(8,128)} %bitcast.73, ...), custom_call_target="tpu_custom_call" | custom-call | tf_op jit(solution)/shard_map/pallas_call | solution.py:222
  68.7 0.7 fusion.9.refs_8_
  69.4 8.4 %shard_map.57 = bf16[128,4096]{1,0:T(8,128)(2,1)} custom-call(s32[1]{0:T(128)} %bitcast.off_ref, bf16[3,128,4096]{2,1,0:T(8,128)(2,1)} %bitcast.69, f32[3,2,4096]{2,1,0:T(2,128)} %get-tuple-element.25.refs_1_, f32[3,3,4096]{2,1,0:T(4,128)} %refs_2_.3, f32[16,4096]{1,0:T(8,128)} %bitcast.72, f32[16,4096]{1,0:T(8,128)} %bitcast.74, ...), custom_call_target="tpu_custom_call", output_to_operand_aliasing={{}: (10, {})} | custom-call | tf_op jit(solution)/shard_map/pallas_call | solution.py:222
  (16 shorter events, 0.6 us)
Async XLA Ops:
  0.0 16.0 %copy-start = (f32[4096,16]{0,1:T(8,128)S(1)}, f32[4096,16]{0,1:T(8,128)}, u32[]{:S(2)}) copy-start(f32[4096,16]{0,1:T(8,128)} %param.8) | copy-start | bytes 786436
  1.1 13.8 %collective-permute-start = (bf16[2,3,4096]{2,0,1:T(2,128)(2,1)S(1)}, bf16[2,3,4096]{2,0,1:T(2,128)(2,1)S(1)}, u32[]{:S(2)}, u32[]{:S(2)}) collective-permute-start(bf16[2,3,4096]{2,0,1:T(2,128)(2,1)S(1)} %get-tuple-element.14), channel_id=1, source_target_pairs={{0,1},{1,2},{2,3},{3,4},{4,5},{5,6},{6,7},{7,8},{8,9},{9,10},{10,1... | collective-permute-start | bytes 147464 | tf_op jit(solution)/shard_map/ppermute | solution.py:239
  17.9 7.5 %collective-permute-start.1 = (f32[16,4096]{1,0:T(8,128)S(1)}, f32[16,4096]{1,0:T(8,128)S(1)}, u32[]{:S(2)}, u32[]{:S(2)}) collective-permute-start(f32[16,4096]{1,0:T(8,128)S(1)} %get-tuple-element.16), channel_id=1, source_target_pairs={{0,1},{1,0},{2,3},{3,2},{4,5},{5,4},{6,7},{7,6},{8,9},{9,8},{10,11... | collective-permute-start | bytes 786440 | tf_op jit(solution)/shard_map/ppermute | solution.py:279
  25.5 8.6 %collective-permute-start.3 = (f32[16,2048]{1,0:T(8,128)S(1)}, f32[16,2048]{1,0:T(8,128)S(1)}, u32[]{:S(2)}, u32[]{:S(2)}) collective-permute-start(f32[16,2048]{1,0:T(8,128)S(1)} %fusion), channel_id=1, source_target_pairs={{0,4},{2,6},{4,8},{6,10},{8,12},{10,14},{12,16},{14,18},{16,20},{1... | collective-permute-start | bytes 393224 | tf_op jit(solution)/shard_map/ppermute | solution.py:300
  28.6 5.5 %collective-permute-start.2 = (f32[16,2048]{1,0:T(8,128)S(1)}, f32[16,2048]{1,0:T(8,128)S(1)}, u32[]{:S(2)}, u32[]{:S(2)}) collective-permute-start(f32[16,2048]{1,0:T(8,128)S(1)} %fusion), channel_id=1, source_target_pairs={{0,2},{2,4},{4,6},{6,8},{8,10},{10,12},{12,14},{14,16},{16,18},{18... | collective-permute-start | bytes 393224 | tf_op jit(solution)/shard_map/ppermute | solution.py:300
  32.1 7.2 %collective-permute-start.4 = (f32[16,2048]{1,0:T(8,128)S(1)}, f32[16,2048]{1,0:T(8,128)S(1)}, u32[]{:S(2)}, u32[]{:S(2)}) collective-permute-start(f32[16,2048]{1,0:T(8,128)S(1)} %fusion), channel_id=1, source_target_pairs={{0,6},{2,8},{4,10},{6,12},{8,14},{10,16},{12,18},{14,20},{16,22},{... | collective-permute-start | bytes 393224 | tf_op jit(solution)/shard_map/ppermute | solution.py:300
  39.4 5.9 %collective-permute-start.8 = (f32[16,2048]{1,0:T(8,128)S(1)}, f32[16,2048]{1,0:T(8,128)S(1)}, u32[]{:S(2)}, u32[]{:S(2)}) collective-permute-start(f32[16,2048]{1,0:T(8,128)S(1)} %fusion.7), channel_id=1, source_target_pairs={{0,24},{2,26},{4,28},{6,30},{1,25},{3,27},{5,29},{7,31}} | collective-permute-start | bytes 393224 | tf_op jit(solution)/shard_map/ppermute | solution.py:300
  40.1 9.6 %collective-permute-start.7 = (f32[16,2048]{1,0:T(8,128)S(1)}, f32[16,2048]{1,0:T(8,128)S(1)}, u32[]{:S(2)}, u32[]{:S(2)}) collective-permute-start(f32[16,2048]{1,0:T(8,128)S(1)} %fusion.7), channel_id=1, source_target_pairs={{0,18},{2,20},{4,22},{6,24},{8,26},{10,28},{12,30},{1,19},{3,21},{... | collective-permute-start | bytes 393224 | tf_op jit(solution)/shard_map/ppermute | solution.py:300
  41.4 10.2 %collective-permute-start.6 = (f32[16,2048]{1,0:T(8,128)S(1)}, f32[16,2048]{1,0:T(8,128)S(1)}, u32[]{:S(2)}, u32[]{:S(2)}) collective-permute-start(f32[16,2048]{1,0:T(8,128)S(1)} %fusion.7), channel_id=1, source_target_pairs={{0,12},{2,14},{4,16},{6,18},{8,20},{10,22},{12,24},{14,26},{16,28}... | collective-permute-start | bytes 393224 | tf_op jit(solution)/shard_map/ppermute | solution.py:300
  43.3 14.8 %collective-permute-start.5 = (f32[16,2048]{1,0:T(8,128)S(1)}, f32[16,2048]{1,0:T(8,128)S(1)}, u32[]{:S(2)}, u32[]{:S(2)}) collective-permute-start(f32[16,2048]{1,0:T(8,128)S(1)} %fusion.7), channel_id=1, source_target_pairs={{0,6},{2,8},{4,10},{6,12},{8,14},{10,16},{12,18},{14,20},{16,22},{... | collective-permute-start | bytes 393224 | tf_op jit(solution)/shard_map/ppermute | solution.py:300
  58.9 9.8 %collective-permute-start.9 = (f32[16,2048]{1,0:T(8,128)S(1)}, f32[16,2048]{1,0:T(8,128)S(1)}, u32[]{:S(2)}, u32[]{:S(2)}) collective-permute-start(f32[16,2048]{1,0:T(8,128)S(1)} %get-tuple-element.10), channel_id=1, source_target_pairs={{0,1},{1,0},{2,3},{3,2},{4,5},{5,4},{6,7},{7,6},{8,9},{9,8},{10,11... | collective-permute-start | bytes 393224 | tf_op jit(solution)/shard_map/ppermute | solution.py:279
  60.2 8.4 %copy-start.1 = (f32[4096,16]{0,1:T(8,128)S(1)}, f32[4096,16]{0,1:T(8,128)}, u32[]{:S(2)}) copy-start(f32[4096,16]{0,1:T(8,128)} %param.8) | copy-start | bytes 786436

commit v15 on v12

--- a/solution.py
+++ b/solution.py
@@ -215,12 +215,14 @@
         pairs = [(j, j + offset) for j in range(devices - offset)]
         return lax.ppermute(value, axes, pairs)
 
-    halo_rows = shift(streams[tok_rows - (taps - 1) :], 1).astype(jnp.float32)
-    halo = jnp.transpose(halo_rows, (1, 0, 2))
     x = jnp.transpose(streams, (1, 0, 2))
     rate_t = rates.T
     residue_t = residues.T
-    ends, local = run_state(x, jnp.zeros_like(halo), short_filter, rate_t)
+    zero_halo = jnp.zeros((streams_count, taps - 1, width), jnp.float32)
+    ends, local = run_state(x, zero_halo, short_filter, rate_t)
+    tail, local = lax.optimization_barrier((streams[tok_rows - (taps - 1) :], local))
+    halo_rows = shift(tail, 1).astype(jnp.float32)
+    halo = jnp.transpose(halo_rows, (1, 0, 2))
 
     head = streams[: taps - 1].astype(jnp.float32)
 

time: 77.1 us -> 78.3 us (1.016)
  waiting for transfers between devices: 27.7 us -> 29.5 us
  local copies, waits for them, and re-layouts: 1.64 us -> 0.73 us
    ppermute x1, waiting for transfers between devices: 0.01 us -> 3.72 us  [shift(): return lax.ppermute(value, axes, pairs)]
    ppermute x2, waiting for transfers between devices: 13 us -> 11.2 us  [exchange(): lax.ppermute(value, 'tp', [(q, (q + k) % group) for q in range(group)])]
    slice x1, local copies, waits for them, and re-layouts: 0.94 us -> 0.04 us  [head_gate(): feat = short_filter[0] * rows[t + taps - 1]]
  transfers between devices with their start and end apart: 10 -> 10, of which waited for: 6 -> 7; matrix products, arithmetic and copies ran while one was open for 2% -> 0% of each run, Pallas kernels for 11% -> 0%
where the time goes in v15:
time: 78.3 us; the launch traced here: 77.7 us
  waiting for transfers between devices  29.5 us (38%)
  Pallas kernels  23 us (29%)
  starting transfers between devices  19.2 us (25%)
  other arithmetic  5.08 us (6%)
    ppermute x7, waiting for transfers between devices, span_shift(): lax.ppermute(value, 'ctx', [(j, j + offset) for j in range(spans - offset)])  14.6 us
    ppermute x7, starting transfers between devices, span_shift(): lax.ppermute(value, 'ctx', [(j, j + offset) for j in range(spans - offset)])  14.5 us
    pallas_call x1, Pallas kernels, run_out(): pl.pallas_call(out_kernel, grid=(width // BLOCK,), in_specs=[pl.BlockSpec...  14.5 us
    ppermute x2, waiting for transfers between devices, exchange(): lax.ppermute(value, 'tp', [(q, (q + k) % group) for q in range(group)])  11.2 us
    pallas_call x1, Pallas kernels, run_state(): pl.pallas_call(state_kernel, grid=(width // BLOCK,), in_specs=[pl.BlockSp...  8.53 us
    ppermute x1, waiting for transfers between devices, shift(): return lax.ppermute(value, axes, pairs)  3.72 us
    ppermute x1, starting transfers between devices, shift(): return lax.ppermute(value, axes, pairs)  3.42 us
    add x1, other arithmetic, body(): local = local + local_fix  1.83 us
  transfers between devices with their start and end apart: 10, of which 7 were waited for; matrix products, arithmetic and copies ran while one was open for 0% of the time, Pallas kernels for 0%

profile of v15, /device:TPU:16, one launch (start us, length us, event | category | flops | bytes accessed | tf_op | source)
XLA Modules:
  0.0 77.7 jit_solution(6649662877182229742)
XLA Ops:
  0.0 1.1 %slice_convert_fusion = (f32[2,3,4096]{2,0,1:T(2,128)S(1)}, bf16[2,3,4096]{2,0,1:T(2,128)(2,1)S(1)}) fusion(bf16[128,3,4096]{2,0,1:T(8,128)(2,1)} %param.5), kind=kLoop, calls=%fused_computation.28 | loop fusion | flops 24576 | bytes 245760 | tf_op jit(solution)/shard_map/convert_element_type | solution.py:227
  1.1 0.7 broadcast_in_dim.3.halo_ref
  1.8 8.5 %shard_map.55 = (f32[16,8,4096]{2,1,0:T(8,128)}, f32[16,4096]{1,0:T(8,128)}) custom-call(bf16[3,128,4096]{2,1,0:T(8,128)(2,1)} %bitcast.57, f32[3,2,4096]{2,1,0:T(2,128)} %broadcast_in_dim.3.halo_ref, f32[3,3,4096]{2,1,0:T(4,128)} %f_ref.3, f32[16,4096]{1,0:T(8,128)} %bitcast.59), custom_call_target="tpu_custom_call" | custom-call | tf_op jit(solution)/shard_map/pallas_call | solution.py:152
  10.3 3.4 %collective-permute-start = (bf16[2,3,4096]{2,0,1:T(2,128)(2,1)S(1)}, bf16[2,3,4096]{2,0,1:T(2,128)(2,1)S(1)}, u32[]{:S(2)}, u32[]{:S(2)}) collective-permute-start(bf16[2,3,4096]{2,0,1:T(2,128)(2,1)S(1)} %get-tuple-element.10), channel_id=1, source_target_pairs={{0,1},{1,2},{2,3},{3,4},{4,5},{5,6},{6,7},{7,8},{8,9},{9,10},{10,1... | collective-permute-start | bytes 147464 | tf_op jit(solution)/shard_map/ppermute | solution.py:216
  13.8 3.7 %collective-permute-done = bf16[2,3,4096]{2,0,1:T(2,128)(2,1)S(1)} collective-permute-done((bf16[2,3,4096]{2,0,1:T(2,128)(2,1)S(1)}, bf16[2,3,4096]{2,0,1:T(2,128)(2,1)S(1)}, u32[]{:S(2)}, u32[]{:S(2)}) %collective-permute-start) | collective-permute-done | bytes 49184 | tf_op jit(solution)/shard_map/ppermute | solution.py:216
  17.5 0.7 fusion.23
  18.6 1.8 %add_add_fusion = (f32[16,4096]{1,0:T(8,128)S(1)}, f32[16,4096]{1,0:T(8,128)}, f32[16,4096]{1,0:T(8,128)S(1)}) fusion(f32[16,4096]{1,0:T(8,128)} %get-tuple-element.12, f32[4096]{0:T(1024)S(1)} %bitcast.62, f32[4096]{0:T(1024)S(1)} %bitcast.63, f32[4096,16]{0,1:T(8,128)S(1)} %copy-done), kind=kLoop, calls=%fused_computation.1 | loop fusion | flops 786432 | bytes 1343488 | tf_op jit(solution)/shard_map/add | solution.py:250
  20.5 0.3 collective-permute-start.1
  20.8 6.1 %collective-permute-done.1 = f32[16,4096]{1,0:T(8,128)S(1)} collective-permute-done((f32[16,4096]{1,0:T(8,128)S(1)}, f32[16,4096]{1,0:T(8,128)S(1)}, u32[]{:S(2)}, u32[]{:S(2)}) %collective-permute-start.1) | collective-permute-done | bytes 262176 | tf_op jit(solution)/shard_map/ppermute | solution.py:258
  26.9 1.9 %collective-permute-start.4 = (f32[16,2048]{1,0:T(8,128)S(1)}, f32[16,2048]{1,0:T(8,128)S(1)}, u32[]{:S(2)}, u32[]{:S(2)}) collective-permute-start(f32[16,2048]{1,0:T(8,128)S(1)} %fusion), channel_id=1, source_target_pairs={{0,6},{2,8},{4,10},{6,12},{8,14},{10,16},{12,18},{14,20},{16,22},{... | collective-permute-start | bytes 393224 | tf_op jit(solution)/shard_map/ppermute | solution.py:279
  28.8 3.3 %collective-permute-start.3 = (f32[16,2048]{1,0:T(8,128)S(1)}, f32[16,2048]{1,0:T(8,128)S(1)}, u32[]{:S(2)}, u32[]{:S(2)}) collective-permute-start(f32[16,2048]{1,0:T(8,128)S(1)} %fusion), channel_id=1, source_target_pairs={{0,4},{2,6},{4,8},{6,10},{8,12},{10,14},{12,16},{14,18},{16,20},{1... | collective-permute-start | bytes 393224 | tf_op jit(solution)/shard_map/ppermute | solution.py:279
  32.2 3.3 %collective-permute-start.2 = (f32[16,2048]{1,0:T(8,128)S(1)}, f32[16,2048]{1,0:T(8,128)S(1)}, u32[]{:S(2)}, u32[]{:S(2)}) collective-permute-start(f32[16,2048]{1,0:T(8,128)S(1)} %fusion), channel_id=1, source_target_pairs={{0,2},{2,4},{4,6},{6,8},{8,10},{10,12},{12,14},{14,16},{16,18},{18... | collective-permute-start | bytes 393224 | tf_op jit(solution)/shard_map/ppermute | solution.py:279
  35.5 1.8 %collective-permute-done.3 = f32[16,2048]{1,0:T(8,128)S(1)} collective-permute-done((f32[16,2048]{1,0:T(8,128)S(1)}, f32[16,2048]{1,0:T(8,128)S(1)}, u32[]{:S(2)}, u32[]{:S(2)}) %collective-permute-start.3) | collective-permute-done | bytes 131104 | tf_op jit(solution)/shard_map/ppermute | solution.py:279
  37.3 2.1 %collective-permute-done.2 = f32[16,2048]{1,0:T(8,128)S(1)} collective-permute-done((f32[16,2048]{1,0:T(8,128)S(1)}, f32[16,2048]{1,0:T(8,128)S(1)}, u32[]{:S(2)}, u32[]{:S(2)}) %collective-permute-start.2) | collective-permute-done | bytes 131104 | tf_op jit(solution)/shard_map/ppermute | solution.py:279
  39.5 0.7 collective-permute-start.8
  40.1 0.7 collective-permute-start.7
  40.8 2.7 %collective-permute-start.6 = (f32[16,2048]{1,0:T(8,128)S(1)}, f32[16,2048]{1,0:T(8,128)S(1)}, u32[]{:S(2)}, u32[]{:S(2)}) collective-permute-start(f32[16,2048]{1,0:T(8,128)S(1)} %fusion.6), channel_id=1, source_target_pairs={{0,12},{2,14},{4,16},{6,18},{8,20},{10,22},{12,24},{14,26},{16,28}... | collective-permute-start | bytes 393224 | tf_op jit(solution)/shard_map/ppermute | solution.py:279
  43.5 1.9 %collective-permute-start.5 = (f32[16,2048]{1,0:T(8,128)S(1)}, f32[16,2048]{1,0:T(8,128)S(1)}, u32[]{:S(2)}, u32[]{:S(2)}) collective-permute-start(f32[16,2048]{1,0:T(8,128)S(1)} %fusion.6), channel_id=1, source_target_pairs={{0,6},{2,8},{4,10},{6,12},{8,14},{10,16},{12,18},{14,20},{16,22},{... | collective-permute-start | bytes 393224 | tf_op jit(solution)/shard_map/ppermute | solution.py:279
  45.5 5.4 %collective-permute-done.6 = f32[16,2048]{1,0:T(8,128)S(1)} collective-permute-done((f32[16,2048]{1,0:T(8,128)S(1)}, f32[16,2048]{1,0:T(8,128)S(1)}, u32[]{:S(2)}, u32[]{:S(2)}) %collective-permute-start.6) | collective-permute-done | bytes 131104 | tf_op jit(solution)/shard_map/ppermute | solution.py:279
  50.9 5.2 %collective-permute-done.5 = f32[16,2048]{1,0:T(8,128)S(1)} collective-permute-done((f32[16,2048]{1,0:T(8,128)S(1)}, f32[16,2048]{1,0:T(8,128)S(1)}, u32[]{:S(2)}, u32[]{:S(2)}) %collective-permute-start.5) | collective-permute-done | bytes 131104 | tf_op jit(solution)/shard_map/ppermute | solution.py:279
  56.3 1.0 %collective-permute-start.9 = (f32[16,2048]{1,0:T(8,128)S(1)}, f32[16,2048]{1,0:T(8,128)S(1)}, u32[]{:S(2)}, u32[]{:S(2)}) collective-permute-start(f32[16,2048]{1,0:T(8,128)S(1)} %get-tuple-element.14), channel_id=1, source_target_pairs={{0,1},{1,0},{2,3},{3,2},{4,5},{5,4},{6,7},{7,6},{8,9},{9,8},{10,11... | collective-permute-start | bytes 393224 | tf_op jit(solution)/shard_map/ppermute | solution.py:258
  57.3 5.1 %collective-permute-done.9 = f32[16,2048]{1,0:T(8,128)S(1)} collective-permute-done((f32[16,2048]{1,0:T(8,128)S(1)}, f32[16,2048]{1,0:T(8,128)S(1)}, u32[]{:S(2)}, u32[]{:S(2)}) %collective-permute-start.9) | collective-permute-done | bytes 131104 | tf_op jit(solution)/shard_map/ppermute | solution.py:258
  62.4 0.8 %select_add_fusion.hin_ref = f32[16,4096]{1,0:T(8,128)} fusion(f32[16,4096]{1,0:T(8,128)S(1)} %collective-permute-done.1, f32[16,4096]{1,0:T(8,128)S(1)} %constant_dynamic-update-slice_fusion, f32[]{:T(128)S(6)} %mul.259, pred[]{:T(512)S(6)} %ge.3, f32[4096,16]{0,1:T(8,128)S(1)} %copy-done), kind=kLoop, calls=%fused_computation | loop fusion | flops 458752 | bytes 1048581 | tf_op jit(solution)/shard_map/add | solution.py:305
  63.2 14.5 %shard_map.56 = bf16[128,4096]{1,0:T(8,128)(2,1)} custom-call(bf16[3,128,4096]{2,1,0:T(8,128)(2,1)} %bitcast.58, f32[3,2,4096]{2,1,0:T(2,128)} %get-tuple-element.28.halo_ref, f32[3,3,4096]{2,1,0:T(4,128)} %f_ref.3, f32[16,4096]{1,0:T(8,128)} %bitcast.60, f32[16,4096]{1,0:T(8,128)} %bitcast.61, f32[1,4096]{1,0:T(1,128)} %bitcast.64, ...), custom_call_target="tpu_custom_call" | custom-call | tf_op jit(solution)/shard_map/pallas_call | solution.py:181
  (16 shorter events, 0.7 us)
Async XLA Ops:
  0.0 13.8 %copy-start.1 = (f32[3,3,4096]{2,1,0:T(4,128)S(1)}, f32[3,3,4096]{2,1,0:T(4,128)}, u32[]{:S(2)}) copy-start(f32[3,3,4096]{2,1,0:T(4,128)} %f_ref.3) | copy-start | bytes 442372
  0.0 18.6 %copy-start = (f32[4096,16]{0,1:T(8,128)S(1)}, f32[4096,16]{0,1:T(8,128)}, u32[]{:S(2)}) copy-start(f32[4096,16]{0,1:T(8,128)} %param.8) | copy-start | bytes 786436
  10.3 7.2 %collective-permute-start = (bf16[2,3,4096]{2,0,1:T(2,128)(2,1)S(1)}, bf16[2,3,4096]{2,0,1:T(2,128)(2,1)S(1)}, u32[]{:S(2)}, u32[]{:S(2)}) collective-permute-start(bf16[2,3,4096]{2,0,1:T(2,128)(2,1)S(1)} %get-tuple-element.10), channel_id=1, source_target_pairs={{0,1},{1,2},{2,3},{3,4},{4,5},{5,6},{6,7},{7,8},{8,9},{9,10},{10,1... | collective-permute-start | bytes 147464 | tf_op jit(solution)/shard_map/ppermute | solution.py:216
  20.5 6.4 %collective-permute-start.1 = (f32[16,4096]{1,0:T(8,128)S(1)}, f32[16,4096]{1,0:T(8,128)S(1)}, u32[]{:S(2)}, u32[]{:S(2)}) collective-permute-start(f32[16,4096]{1,0:T(8,128)S(1)} %get-tuple-element.20), channel_id=1, source_target_pairs={{0,1},{1,0},{2,3},{3,2},{4,5},{5,4},{6,7},{7,6},{8,9},{9,8},{10,11... | collective-permute-start | bytes 786440 | tf_op jit(solution)/shard_map/ppermute | solution.py:258
  26.9 8.6 %collective-permute-start.4 = (f32[16,2048]{1,0:T(8,128)S(1)}, f32[16,2048]{1,0:T(8,128)S(1)}, u32[]{:S(2)}, u32[]{:S(2)}) collective-permute-start(f32[16,2048]{1,0:T(8,128)S(1)} %fusion), channel_id=1, source_target_pairs={{0,6},{2,8},{4,10},{6,12},{8,14},{10,16},{12,18},{14,20},{16,22},{... | collective-permute-start | bytes 393224 | tf_op jit(solution)/shard_map/ppermute | solution.py:279
  28.8 8.5 %collective-permute-start.3 = (f32[16,2048]{1,0:T(8,128)S(1)}, f32[16,2048]{1,0:T(8,128)S(1)}, u32[]{:S(2)}, u32[]{:S(2)}) collective-permute-start(f32[16,2048]{1,0:T(8,128)S(1)} %fusion), channel_id=1, source_target_pairs={{0,4},{2,6},{4,8},{6,10},{8,12},{10,14},{12,16},{14,18},{16,20},{1... | collective-permute-start | bytes 393224 | tf_op jit(solution)/shard_map/ppermute | solution.py:279
  32.2 7.2 %collective-permute-start.2 = (f32[16,2048]{1,0:T(8,128)S(1)}, f32[16,2048]{1,0:T(8,128)S(1)}, u32[]{:S(2)}, u32[]{:S(2)}) collective-permute-start(f32[16,2048]{1,0:T(8,128)S(1)} %fusion), channel_id=1, source_target_pairs={{0,2},{2,4},{4,6},{6,8},{8,10},{10,12},{12,14},{14,16},{16,18},{18... | collective-permute-start | bytes 393224 | tf_op jit(solution)/shard_map/ppermute | solution.py:279
  39.5 6.0 %collective-permute-start.8 = (f32[16,2048]{1,0:T(8,128)S(1)}, f32[16,2048]{1,0:T(8,128)S(1)}, u32[]{:S(2)}, u32[]{:S(2)}) collective-permute-start(f32[16,2048]{1,0:T(8,128)S(1)} %fusion.6), channel_id=1, source_target_pairs={{0,24},{2,26},{4,28},{6,30},{1,25},{3,27},{5,29},{7,31}} | collective-permute-start | bytes 393224 | tf_op jit(solution)/shard_map/ppermute | solution.py:279
  40.1 5.3 %collective-permute-start.7 = (f32[16,2048]{1,0:T(8,128)S(1)}, f32[16,2048]{1,0:T(8,128)S(1)}, u32[]{:S(2)}, u32[]{:S(2)}) collective-permute-start(f32[16,2048]{1,0:T(8,128)S(1)} %fusion.6), channel_id=1, source_target_pairs={{0,18},{2,20},{4,22},{6,24},{8,26},{10,28},{12,30},{1,19},{3,21},{... | collective-permute-start | bytes 393224 | tf_op jit(solution)/shard_map/ppermute | solution.py:279
  40.8 10.1 %collective-permute-start.6 = (f32[16,2048]{1,0:T(8,128)S(1)}, f32[16,2048]{1,0:T(8,128)S(1)}, u32[]{:S(2)}, u32[]{:S(2)}) collective-permute-start(f32[16,2048]{1,0:T(8,128)S(1)} %fusion.6), channel_id=1, source_target_pairs={{0,12},{2,14},{4,16},{6,18},{8,20},{10,22},{12,24},{14,26},{16,28}... | collective-permute-start | bytes 393224 | tf_op jit(solution)/shard_map/ppermute | solution.py:279
  43.5 12.6 %collective-permute-start.5 = (f32[16,2048]{1,0:T(8,128)S(1)}, f32[16,2048]{1,0:T(8,128)S(1)}, u32[]{:S(2)}, u32[]{:S(2)}) collective-permute-start(f32[16,2048]{1,0:T(8,128)S(1)} %fusion.6), channel_id=1, source_target_pairs={{0,6},{2,8},{4,10},{6,12},{8,14},{10,16},{12,18},{14,20},{16,22},{... | collective-permute-start | bytes 393224 | tf_op jit(solution)/shard_map/ppermute | solution.py:279
  56.3 6.1 %collective-permute-start.9 = (f32[16,2048]{1,0:T(8,128)S(1)}, f32[16,2048]{1,0:T(8,128)S(1)}, u32[]{:S(2)}, u32[]{:S(2)}) collective-permute-start(f32[16,2048]{1,0:T(8,128)S(1)} %get-tuple-element.14), channel_id=1, source_target_pairs={{0,1},{1,0},{2,3},{3,2},{4,5},{5,4},{6,7},{7,6},{8,9},{9,8},{10,11... | collective-permute-start | bytes 393224 | tf_op jit(solution)/shard_map/ppermute | solution.py:258

commit v16 on v13

--- a/solution.py
+++ b/solution.py
@@ -8,8 +8,8 @@
 LANES = 128
 SUB = 8
 BLOCK = 1024
-FIRST_WINDOW = 2
-LATER_WINDOW = 2
+FIRST_WINDOW = 4
+LATER_WINDOW = 3
 UNROLL = 8
 
 

time: 80.5 us -> 77.3 us (0.960)
  the two profiles are of different devices: /device:TPU:24 before, /device:TPU:16 now
where the time goes in v16:
time: 77.3 us; the launch traced here: 76.9 us
  waiting for transfers between devices  27.8 us (36%)
  Pallas kernels  23 us (30%)
  starting transfers between devices  19.1 us (25%)
  other arithmetic  5.09 us (7%)
  local copies, waits for them, and re-layouts  1.64 us (2%)
    ppermute x7, starting transfers between devices, span_shift(): lax.ppermute(value, 'ctx', [(j, j + offset) for j in range(spans - offset)])  15.3 us
    ppermute x7, waiting for transfers between devices, span_shift(): lax.ppermute(value, 'ctx', [(j, j + offset) for j in range(spans - offset)])  14.8 us
    pallas_call x1, Pallas kernels, run_out(): pl.pallas_call(out_kernel, grid=(width // BLOCK,), in_specs=[pl.BlockSpec...  14.5 us
    ppermute x2, waiting for transfers between devices, exchange(): lax.ppermute(value, 'tp', [(q, (q + k) % group) for q in range(group)])  13.1 us
    pallas_call x1, Pallas kernels, run_state(): pl.pallas_call(state_kernel, grid=(width // BLOCK,), in_specs=[pl.BlockSp...  8.55 us
    ppermute x1, starting transfers between devices, shift(): return lax.ppermute(value, axes, pairs)  3.43 us
    add x1, other arithmetic, body(): local = local + local_fix  1.84 us
  transfers between devices with their start and end apart: 10, of which 6 were waited for; matrix products, arithmetic and copies ran while one was open for 2% of the time, Pallas kernels for 11%

profile of v16, /device:TPU:16, one launch (start us, length us, event | category | flops | bytes accessed | tf_op | source)
XLA Modules:
  0.0 76.9 jit_solution(17204058803663112147)
XLA Ops:
  0.0 1.1 %slice_convert_fusion = (f32[2,3,4096]{2,0,1:T(2,128)S(1)}, bf16[2,3,4096]{2,0,1:T(2,128)(2,1)S(1)}) fusion(bf16[128,3,4096]{2,0,1:T(8,128)(2,1)} %param.5), kind=kLoop, calls=%fused_computation.28 | loop fusion | flops 24576 | bytes 245760 | tf_op jit(solution)/shard_map/convert_element_type | solution.py:225
  1.1 3.4 %collective-permute-start = (bf16[2,3,4096]{2,0,1:T(2,128)(2,1)S(1)}, bf16[2,3,4096]{2,0,1:T(2,128)(2,1)S(1)}, u32[]{:S(2)}, u32[]{:S(2)}) collective-permute-start(bf16[2,3,4096]{2,0,1:T(2,128)(2,1)S(1)} %get-tuple-element.14), channel_id=1, source_target_pairs={{0,1},{1,2},{2,3},{3,4},{4,5},{5,6},{6,7},{7,8},{8,9},{9,10},{10,1... | collective-permute-start | bytes 147464 | tf_op jit(solution)/shard_map/ppermute | solution.py:216
  4.6 0.9 %fusion.22 = (f32[1,3,4096]{2,1,0:T(4,128)S(1)}, f32[1,3,4096]{2,1,0:T(4,128)S(1)}, f32[1,3,4096]{2,1,0:T(4,128)S(1)}) fusion(f32[3,3,4096]{2,1,0:T(4,128)} %f_ref.3), kind=kLoop, calls=%fused_computation.49 | loop fusion | bytes 294912 | tf_op jit(solution)/shard_map/slice | solution.py:231
  5.5 0.7 broadcast_in_dim.3.halo_ref
  6.2 8.5 %shard_map.55 = (f32[16,8,4096]{2,1,0:T(8,128)}, f32[16,4096]{1,0:T(8,128)}) custom-call(bf16[3,128,4096]{2,1,0:T(8,128)(2,1)} %bitcast.56, f32[3,2,4096]{2,1,0:T(2,128)} %broadcast_in_dim.3.halo_ref, f32[3,3,4096]{2,1,0:T(4,128)} %f_ref.3, f32[16,4096]{1,0:T(8,128)} %bitcast.58), custom_call_target="tpu_custom_call" | custom-call | tf_op jit(solution)/shard_map/pallas_call | solution.py:152
  14.7 0.7 fusion.23
  15.4 0.2 multiply_add_fusion.1
  15.8 1.8 %add_add_fusion = (f32[16,4096]{1,0:T(8,128)S(1)}, f32[16,4096]{1,0:T(8,128)}, f32[16,4096]{1,0:T(8,128)S(1)}) fusion(f32[16,4096]{1,0:T(8,128)} %get-tuple-element.8, f32[4096]{0:T(1024)S(1)} %bitcast.61, f32[4096]{0:T(1024)S(1)} %bitcast.62, f32[4096,16]{0,1:T(8,128)S(1)} %copy-done), kind=kLoop, calls=%fused_computation.1 | loop fusion | flops 786432 | bytes 1343488 | tf_op jit(solution)/shard_map/add | solution.py:248
  17.7 8.0 %collective-permute-done.1 = f32[16,4096]{1,0:T(8,128)S(1)} collective-permute-done((f32[16,4096]{1,0:T(8,128)S(1)}, f32[16,4096]{1,0:T(8,128)S(1)}, u32[]{:S(2)}, u32[]{:S(2)}) %collective-permute-start.1) | collective-permute-done | bytes 262176 | tf_op jit(solution)/shard_map/ppermute | solution.py:256
  25.7 3.5 %collective-permute-start.5 = (f32[16,2048]{1,0:T(8,128)S(1)}, f32[16,2048]{1,0:T(8,128)S(1)}, u32[]{:S(2)}, u32[]{:S(2)}) collective-permute-start(f32[16,2048]{1,0:T(8,128)S(1)} %fusion), channel_id=1, source_target_pairs={{0,8},{2,10},{4,12},{6,14},{8,16},{10,18},{12,20},{14,22},{16,24},... | collective-permute-start | bytes 393224 | tf_op jit(solution)/shard_map/ppermute | solution.py:277
  29.2 1.9 %collective-permute-start.4 = (f32[16,2048]{1,0:T(8,128)S(1)}, f32[16,2048]{1,0:T(8,128)S(1)}, u32[]{:S(2)}, u32[]{:S(2)}) collective-permute-start(f32[16,2048]{1,0:T(8,128)S(1)} %fusion), channel_id=1, source_target_pairs={{0,6},{2,8},{4,10},{6,12},{8,14},{10,16},{12,18},{14,20},{16,22},{... | collective-permute-start | bytes 393224 | tf_op jit(solution)/shard_map/ppermute | solution.py:277
  31.2 3.1 %collective-permute-start.3 = (f32[16,2048]{1,0:T(8,128)S(1)}, f32[16,2048]{1,0:T(8,128)S(1)}, u32[]{:S(2)}, u32[]{:S(2)}) collective-permute-start(f32[16,2048]{1,0:T(8,128)S(1)} %fusion), channel_id=1, source_target_pairs={{0,4},{2,6},{4,8},{6,10},{8,12},{10,14},{12,16},{14,18},{16,20},{1... | collective-permute-start | bytes 393224 | tf_op jit(solution)/shard_map/ppermute | solution.py:277
  34.3 1.9 %collective-permute-start.2 = (f32[16,2048]{1,0:T(8,128)S(1)}, f32[16,2048]{1,0:T(8,128)S(1)}, u32[]{:S(2)}, u32[]{:S(2)}) collective-permute-start(f32[16,2048]{1,0:T(8,128)S(1)} %fusion), channel_id=1, source_target_pairs={{0,2},{2,4},{4,6},{6,8},{8,10},{10,12},{12,14},{14,16},{16,18},{18... | collective-permute-start | bytes 393224 | tf_op jit(solution)/shard_map/ppermute | solution.py:277
  36.3 3.5 %collective-permute-done.3 = f32[16,2048]{1,0:T(8,128)S(1)} collective-permute-done((f32[16,2048]{1,0:T(8,128)S(1)}, f32[16,2048]{1,0:T(8,128)S(1)}, u32[]{:S(2)}, u32[]{:S(2)}) %collective-permute-start.3) | collective-permute-done | bytes 131104 | tf_op jit(solution)/shard_map/ppermute | solution.py:277
  39.7 1.8 %collective-permute-done.2 = f32[16,2048]{1,0:T(8,128)S(1)} collective-permute-done((f32[16,2048]{1,0:T(8,128)S(1)}, f32[16,2048]{1,0:T(8,128)S(1)}, u32[]{:S(2)}, u32[]{:S(2)}) %collective-permute-start.2) | collective-permute-done | bytes 131104 | tf_op jit(solution)/shard_map/ppermute | solution.py:277
  41.6 0.7 collective-permute-start.8
  42.3 1.3 %collective-permute-start.7 = (f32[16,2048]{1,0:T(8,128)S(1)}, f32[16,2048]{1,0:T(8,128)S(1)}, u32[]{:S(2)}, u32[]{:S(2)}) collective-permute-start(f32[16,2048]{1,0:T(8,128)S(1)} %fusion.5), channel_id=1, source_target_pairs={{0,16},{2,18},{4,20},{6,22},{8,24},{10,26},{12,28},{14,30},{1,17},... | collective-permute-start | bytes 393224 | tf_op jit(solution)/shard_map/ppermute | solution.py:277
  43.6 2.9 %collective-permute-start.6 = (f32[16,2048]{1,0:T(8,128)S(1)}, f32[16,2048]{1,0:T(8,128)S(1)}, u32[]{:S(2)}, u32[]{:S(2)}) collective-permute-start(f32[16,2048]{1,0:T(8,128)S(1)} %fusion.5), channel_id=1, source_target_pairs={{0,8},{2,10},{4,12},{6,14},{8,16},{10,18},{12,20},{14,22},{16,24},... | collective-permute-start | bytes 393224 | tf_op jit(solution)/shard_map/ppermute | solution.py:277
  46.5 5.5 %collective-permute-done.7 = f32[16,2048]{1,0:T(8,128)S(1)} collective-permute-done((f32[16,2048]{1,0:T(8,128)S(1)}, f32[16,2048]{1,0:T(8,128)S(1)}, u32[]{:S(2)}, u32[]{:S(2)}) %collective-permute-start.7) | collective-permute-done | bytes 131104 | tf_op jit(solution)/shard_map/ppermute | solution.py:277
  52.0 4.0 %collective-permute-done.6 = f32[16,2048]{1,0:T(8,128)S(1)} collective-permute-done((f32[16,2048]{1,0:T(8,128)S(1)}, f32[16,2048]{1,0:T(8,128)S(1)}, u32[]{:S(2)}, u32[]{:S(2)}) %collective-permute-start.6) | collective-permute-done | bytes 131104 | tf_op jit(solution)/shard_map/ppermute | solution.py:277
  56.2 0.4 collective-permute-start.9
  56.5 5.0 %collective-permute-done.9 = f32[16,2048]{1,0:T(8,128)S(1)} collective-permute-done((f32[16,2048]{1,0:T(8,128)S(1)}, f32[16,2048]{1,0:T(8,128)S(1)}, u32[]{:S(2)}, u32[]{:S(2)}) %collective-permute-start.9) | collective-permute-done | bytes 131104 | tf_op jit(solution)/shard_map/ppermute | solution.py:256
  61.6 0.8 %select_add_fusion.hin_ref = f32[16,4096]{1,0:T(8,128)} fusion(f32[16,4096]{1,0:T(8,128)S(1)} %collective-permute-done.1, f32[16,4096]{1,0:T(8,128)S(1)} %constant_dynamic-update-slice_fusion, f32[]{:T(128)S(6)} %mul.259, pred[]{:T(512)S(6)} %ge.3, f32[4096,16]{0,1:T(8,128)S(1)} %copy-done), kind=kLoop, calls=%fused_computation | loop fusion | flops 458752 | bytes 1048581 | tf_op jit(solution)/shard_map/add | solution.py:303
  62.4 14.5 %shard_map.56 = bf16[128,4096]{1,0:T(8,128)(2,1)} custom-call(bf16[3,128,4096]{2,1,0:T(8,128)(2,1)} %bitcast.57, f32[3,2,4096]{2,1,0:T(2,128)} %get-tuple-element.24.halo_ref, f32[3,3,4096]{2,1,0:T(4,128)} %f_ref.3, f32[16,4096]{1,0:T(8,128)} %bitcast.59, f32[16,4096]{1,0:T(8,128)} %bitcast.60, f32[1,4096]{1,0:T(1,128)} %bitcast.63, ...), custom_call_target="tpu_custom_call" | custom-call | tf_op jit(solution)/shard_map/pallas_call | solution.py:181
  (14 shorter events, 0.4 us)
Async XLA Ops:
  0.0 15.8 %copy-start = (f32[4096,16]{0,1:T(8,128)S(1)}, f32[4096,16]{0,1:T(8,128)}, u32[]{:S(2)}) copy-start(f32[4096,16]{0,1:T(8,128)} %param.8) | copy-start | bytes 786436
  1.1 13.6 %collective-permute-start = (bf16[2,3,4096]{2,0,1:T(2,128)(2,1)S(1)}, bf16[2,3,4096]{2,0,1:T(2,128)(2,1)S(1)}, u32[]{:S(2)}, u32[]{:S(2)}) collective-permute-start(bf16[2,3,4096]{2,0,1:T(2,128)(2,1)S(1)} %get-tuple-element.14), channel_id=1, source_target_pairs={{0,1},{1,2},{2,3},{3,4},{4,5},{5,6},{6,7},{7,8},{8,9},{9,10},{10,1... | collective-permute-start | bytes 147464 | tf_op jit(solution)/shard_map/ppermute | solution.py:216
  17.7 8.0 %collective-permute-start.1 = (f32[16,4096]{1,0:T(8,128)S(1)}, f32[16,4096]{1,0:T(8,128)S(1)}, u32[]{:S(2)}, u32[]{:S(2)}) collective-permute-start(f32[16,4096]{1,0:T(8,128)S(1)} %get-tuple-element.16), channel_id=1, source_target_pairs={{0,1},{1,0},{2,3},{3,2},{4,5},{5,4},{6,7},{7,6},{8,9},{9,8},{10,11... | collective-permute-start | bytes 786440 | tf_op jit(solution)/shard_map/ppermute | solution.py:256
  25.7 10.5 %collective-permute-start.5 = (f32[16,2048]{1,0:T(8,128)S(1)}, f32[16,2048]{1,0:T(8,128)S(1)}, u32[]{:S(2)}, u32[]{:S(2)}) collective-permute-start(f32[16,2048]{1,0:T(8,128)S(1)} %fusion), channel_id=1, source_target_pairs={{0,8},{2,10},{4,12},{6,14},{8,16},{10,18},{12,20},{14,22},{16,24},... | collective-permute-start | bytes 393224 | tf_op jit(solution)/shard_map/ppermute | solution.py:277
  29.2 7.0 %collective-permute-start.4 = (f32[16,2048]{1,0:T(8,128)S(1)}, f32[16,2048]{1,0:T(8,128)S(1)}, u32[]{:S(2)}, u32[]{:S(2)}) collective-permute-start(f32[16,2048]{1,0:T(8,128)S(1)} %fusion), channel_id=1, source_target_pairs={{0,6},{2,8},{4,10},{6,12},{8,14},{10,16},{12,18},{14,20},{16,22},{... | collective-permute-start | bytes 393224 | tf_op jit(solution)/shard_map/ppermute | solution.py:277
  31.2 8.6 %collective-permute-start.3 = (f32[16,2048]{1,0:T(8,128)S(1)}, f32[16,2048]{1,0:T(8,128)S(1)}, u32[]{:S(2)}, u32[]{:S(2)}) collective-permute-start(f32[16,2048]{1,0:T(8,128)S(1)} %fusion), channel_id=1, source_target_pairs={{0,4},{2,6},{4,8},{6,10},{8,12},{10,14},{12,16},{14,18},{16,20},{1... | collective-permute-start | bytes 393224 | tf_op jit(solution)/shard_map/ppermute | solution.py:277
  34.3 7.2 %collective-permute-start.2 = (f32[16,2048]{1,0:T(8,128)S(1)}, f32[16,2048]{1,0:T(8,128)S(1)}, u32[]{:S(2)}, u32[]{:S(2)}) collective-permute-start(f32[16,2048]{1,0:T(8,128)S(1)} %fusion), channel_id=1, source_target_pairs={{0,2},{2,4},{4,6},{6,8},{8,10},{10,12},{12,14},{14,16},{16,18},{18... | collective-permute-start | bytes 393224 | tf_op jit(solution)/shard_map/ppermute | solution.py:277
  41.6 4.9 %collective-permute-start.8 = (f32[16,2048]{1,0:T(8,128)S(1)}, f32[16,2048]{1,0:T(8,128)S(1)}, u32[]{:S(2)}, u32[]{:S(2)}) collective-permute-start(f32[16,2048]{1,0:T(8,128)S(1)} %fusion.5), channel_id=1, source_target_pairs={{0,24},{2,26},{4,28},{6,30},{1,25},{3,27},{5,29},{7,31}} | collective-permute-start | bytes 393224 | tf_op jit(solution)/shard_map/ppermute | solution.py:277
  42.3 9.7 %collective-permute-start.7 = (f32[16,2048]{1,0:T(8,128)S(1)}, f32[16,2048]{1,0:T(8,128)S(1)}, u32[]{:S(2)}, u32[]{:S(2)}) collective-permute-start(f32[16,2048]{1,0:T(8,128)S(1)} %fusion.5), channel_id=1, source_target_pairs={{0,16},{2,18},{4,20},{6,22},{8,24},{10,26},{12,28},{14,30},{1,17},... | collective-permute-start | bytes 393224 | tf_op jit(solution)/shard_map/ppermute | solution.py:277
  43.6 12.5 %collective-permute-start.6 = (f32[16,2048]{1,0:T(8,128)S(1)}, f32[16,2048]{1,0:T(8,128)S(1)}, u32[]{:S(2)}, u32[]{:S(2)}) collective-permute-start(f32[16,2048]{1,0:T(8,128)S(1)} %fusion.5), channel_id=1, source_target_pairs={{0,8},{2,10},{4,12},{6,14},{8,16},{10,18},{12,20},{14,22},{16,24},... | collective-permute-start | bytes 393224 | tf_op jit(solution)/shard_map/ppermute | solution.py:277
  56.2 5.4 %collective-permute-start.9 = (f32[16,2048]{1,0:T(8,128)S(1)}, f32[16,2048]{1,0:T(8,128)S(1)}, u32[]{:S(2)}, u32[]{:S(2)}) collective-permute-start(f32[16,2048]{1,0:T(8,128)S(1)} %get-tuple-element.10), channel_id=1, source_target_pairs={{0,1},{1,0},{2,3},{3,2},{4,5},{5,4},{6,7},{7,6},{8,9},{9,8},{10,11... | collective-permute-start | bytes 393224 | tf_op jit(solution)/shard_map/ppermute | solution.py:256

commit v17 on v12

--- a/solution.py
+++ b/solution.py
@@ -258,20 +258,23 @@
     def powers(rates_part, count):
         return jnp.exp(-rates_part * (float(tok_rows) * count))
 
-    inside = None
-    total = powers(rate_t, (group - 1 - member).astype(jnp.float32)) * local
-    for k in range(1, group):
-        other = exchange(local, k)
-        source = (member - k) % group
-        total = total + powers(rate_t, (group - 1 - source).astype(jnp.float32)) * other
-        term = jnp.where(k <= member, powers(rate_t, float(k - 1)) * other, 0.0)
-        inside = term if inside is None else inside + term
-    if inside is None:
-        inside = jnp.zeros_like(local)
+    def cut(value, slot):
+        return lax.dynamic_slice_in_dim(value, slot * piece, piece, 1)
 
     first_channel = member * piece
     rate_part = lax.dynamic_slice_in_dim(rate_t, first_channel, piece, 1)
-    total_part = lax.dynamic_slice_in_dim(total, first_channel, piece, 1)
+    pieces = {0: cut(local, member)}
+    for k in range(1, group):
+        pieces[k] = exchange(cut(local, (member + k) % group), k)
+    sources = {k: (member - k) % group for k in range(group)}
+
+    def level(count):
+        return count.astype(jnp.float32) if hasattr(count, "astype") else float(count)
+
+    total_part = None
+    for k in range(group):
+        term = powers(rate_part, level(group - 1 - sources[k])) * pieces[k]
+        total_part = term if total_part is None else total_part + term
 
     def span_shift(value, offset):
         return lax.ppermute(value, "ctx", [(j, j + offset) for j in range(spans - offset)])
@@ -296,11 +299,20 @@
     else:
         before = jnp.zeros_like(total_part)
 
-    whole = jnp.zeros_like(local)
+    whole = None
     for k in range(group):
-        part = before if k == 0 else exchange(before, k)
-        whole = lax.dynamic_update_slice_in_dim(whole, part, ((member - k) % group) * piece, 1)
-    carried = powers(rate_t, member.astype(jnp.float32)) * whole + inside
+        target = (member + k) % group
+        start = powers(rate_part, level(target)) * before
+        for j in range(group):
+            ahead = target - 1 - sources[j]
+            term = powers(rate_part, level(jnp.maximum(ahead, 0))) * pieces[j]
+            start = start + jnp.where(sources[j] < target, term, 0.0)
+        got = start if k == 0 else exchange(start, k)
+        slot = (member - k) % group
+        if whole is None:
+            whole = jnp.zeros_like(local)
+        whole = lax.dynamic_update_slice_in_dim(whole, got, slot * piece, 1)
+    carried = whole
 
     return run_out(x, halo, short_filter, rate_t, residue_t, skip.reshape(1, width), ends, ends_fix, carried)
 

time: 77.1 us -> 77.1 us (level)
  the two profiles are of different devices: /device:TPU:16 before, /device:TPU:24 now
where the time goes in v17:
time: 77.1 us; the launch traced here: 76.7 us
  waiting for transfers between devices  29 us (38%)
  Pallas kernels  23 us (30%)
  starting transfers between devices  17.7 us (23%)
  other arithmetic  4.39 us (6%)
  local copies, waits for them, and re-layouts  2.34 us (3%)
    ppermute x7, waiting for transfers between devices, span_shift(): lax.ppermute(value, 'ctx', [(j, j + offset) for j in range(spans - offset)])  19.1 us
    pallas_call x1, Pallas kernels, run_out(): pl.pallas_call(out_kernel, grid=(width // BLOCK,), in_specs=[pl.BlockSpec...  14.5 us
    ppermute x7, starting transfers between devices, span_shift(): lax.ppermute(value, 'ctx', [(j, j + offset) for j in range(spans - offset)])  13.4 us
    ppermute x2, waiting for transfers between devices, exchange(): lax.ppermute(value, 'tp', [(q, (q + k) % group) for q in range(group)])  9.97 us
    pallas_call x1, Pallas kernels, run_state(): pl.pallas_call(state_kernel, grid=(width // BLOCK,), in_specs=[pl.BlockSp...  8.53 us
    ppermute x1, starting transfers between devices, shift(): return lax.ppermute(value, axes, pairs)  3.43 us
    add x1, other arithmetic, body(): local = local + local_fix  1.83 us
  transfers between devices with their start and end apart: 10, of which 7 were waited for; matrix products, arithmetic and copies ran while one was open for 2% of the time, Pallas kernels for 11%

profile of v17, /device:TPU:24, one launch (start us, length us, event | category | flops | bytes accessed | tf_op | source)
XLA Modules:
  0.0 76.7 jit_solution(6619713512404638565)
XLA Ops:
  0.0 1.1 %slice_convert_fusion = (f32[2,3,4096]{2,0,1:T(2,128)S(1)}, bf16[2,3,4096]{2,0,1:T(2,128)(2,1)S(1)}) fusion(bf16[128,3,4096]{2,0,1:T(8,128)(2,1)} %param.5), kind=kLoop, calls=%fused_computation.39 | loop fusion | flops 24576 | bytes 245760 | tf_op jit(solution)/shard_map/convert_element_type | solution.py:225
  1.1 3.4 %collective-permute-start = (bf16[2,3,4096]{2,0,1:T(2,128)(2,1)S(1)}, bf16[2,3,4096]{2,0,1:T(2,128)(2,1)S(1)}, u32[]{:S(2)}, u32[]{:S(2)}) collective-permute-start(bf16[2,3,4096]{2,0,1:T(2,128)(2,1)S(1)} %get-tuple-element.14), channel_id=1, source_target_pairs={{0,1},{1,2},{2,3},{3,4},{4,5},{5,6},{6,7},{7,8},{8,9},{9,10},{10,1... | collective-permute-start | bytes 147464 | tf_op jit(solution)/shard_map/ppermute | solution.py:216
  4.6 0.9 %fusion.29 = (f32[1,3,4096]{2,1,0:T(4,128)S(1)}, f32[1,3,4096]{2,1,0:T(4,128)S(1)}, f32[1,3,4096]{2,1,0:T(4,128)S(1)}) fusion(f32[3,3,4096]{2,1,0:T(4,128)} %f_ref.3), kind=kLoop, calls=%fused_computation.59 | loop fusion | bytes 294912 | tf_op jit(solution)/shard_map/slice | solution.py:231
  5.5 0.7 broadcast_in_dim.13.halo_ref
  6.2 8.5 %shard_map.55 = (f32[16,8,4096]{2,1,0:T(8,128)}, f32[16,4096]{1,0:T(8,128)}) custom-call(bf16[3,128,4096]{2,1,0:T(8,128)(2,1)} %bitcast.90, f32[3,2,4096]{2,1,0:T(2,128)} %broadcast_in_dim.13.halo_ref, f32[3,3,4096]{2,1,0:T(4,128)} %f_ref.3, f32[16,4096]{1,0:T(8,128)} %bitcast.92), custom_call_target="tpu_custom_call" | custom-call | tf_op jit(solution)/shard_map/pallas_call | solution.py:152
  14.7 0.7 fusion.30
  15.4 0.2 multiply_add_fusion.1
  15.8 1.8 %add_add_fusion = (f32[16,4096]{1,0:T(8,128)S(1)}, f32[16,4096]{1,0:T(8,128)}) fusion(f32[16,4096]{1,0:T(8,128)} %get-tuple-element.8, f32[4096]{0:T(1024)S(1)} %bitcast.95, f32[4096]{0:T(1024)S(1)} %bitcast.96, f32[4096,16]{0,1:T(8,128)S(1)} %copy-done), kind=kLoop, calls=%fused_computation | loop fusion | flops 786432 | bytes 1081344 | tf_op jit(solution)/shard_map/add | solution.py:248
  17.8 5.2 %collective-permute-done.1 = f32[16,2048]{1,0:T(8,128)S(1)} collective-permute-done((f32[16,2048]{1,0:T(8,128)S(1)}, f32[16,2048]{1,0:T(8,128)S(1)}, u32[]{:S(2)}, u32[]{:S(2)}) %collective-permute-start.1) | collective-permute-done | bytes 131104 | tf_op jit(solution)/shard_map/ppermute | solution.py:256
  23.0 1.9 %collective-permute-start.2 = (f32[16,2048]{1,0:T(8,128)S(1)}, f32[16,2048]{1,0:T(8,128)S(1)}, u32[]{:S(2)}, u32[]{:S(2)}) collective-permute-start(f32[16,2048]{1,0:T(8,128)S(1)} %fusion.14), channel_id=1, source_target_pairs={{0,2},{2,4},{4,6},{6,8},{8,10},{10,12},{12,14},{14,16},{16,18},{18... | collective-permute-start | bytes 393224 | tf_op jit(solution)/shard_map/ppermute | solution.py:280
  24.9 3.2 %collective-permute-start.3 = (f32[16,2048]{1,0:T(8,128)S(1)}, f32[16,2048]{1,0:T(8,128)S(1)}, u32[]{:S(2)}, u32[]{:S(2)}) collective-permute-start(f32[16,2048]{1,0:T(8,128)S(1)} %fusion.14), channel_id=1, source_target_pairs={{0,4},{2,6},{4,8},{6,10},{8,12},{10,14},{12,16},{14,18},{16,20},{1... | collective-permute-start | bytes 393224 | tf_op jit(solution)/shard_map/ppermute | solution.py:280
  28.1 1.9 %collective-permute-start.4 = (f32[16,2048]{1,0:T(8,128)S(1)}, f32[16,2048]{1,0:T(8,128)S(1)}, u32[]{:S(2)}, u32[]{:S(2)}) collective-permute-start(f32[16,2048]{1,0:T(8,128)S(1)} %fusion.14), channel_id=1, source_target_pairs={{0,6},{2,8},{4,10},{6,12},{8,14},{10,16},{12,18},{14,20},{16,22},{... | collective-permute-start | bytes 393224 | tf_op jit(solution)/shard_map/ppermute | solution.py:280
  30.2 3.6 %collective-permute-done.3 = f32[16,2048]{1,0:T(8,128)S(1)} collective-permute-done((f32[16,2048]{1,0:T(8,128)S(1)}, f32[16,2048]{1,0:T(8,128)S(1)}, u32[]{:S(2)}, u32[]{:S(2)}) %collective-permute-start.3) | collective-permute-done | bytes 131104 | tf_op jit(solution)/shard_map/ppermute | solution.py:280
  33.8 0.6 collective-permute-done.4
  34.5 2.5 %collective-permute-start.5 = (f32[16,2048]{1,0:T(8,128)S(1)}, f32[16,2048]{1,0:T(8,128)S(1)}, u32[]{:S(2)}, u32[]{:S(2)}) collective-permute-start(f32[16,2048]{1,0:T(8,128)S(1)} %fusion.12), channel_id=1, source_target_pairs={{0,6},{2,8},{4,10},{6,12},{8,14},{10,16},{12,18},{14,20},{16,22},{... | collective-permute-start | bytes 393224 | tf_op jit(solution)/shard_map/ppermute | solution.py:280
  37.0 1.3 %collective-permute-start.6 = (f32[16,2048]{1,0:T(8,128)S(1)}, f32[16,2048]{1,0:T(8,128)S(1)}, u32[]{:S(2)}, u32[]{:S(2)}) collective-permute-start(f32[16,2048]{1,0:T(8,128)S(1)} %fusion.12), channel_id=1, source_target_pairs={{0,12},{2,14},{4,16},{6,18},{8,20},{10,22},{12,24},{14,26},{16,28}... | collective-permute-start | bytes 393224 | tf_op jit(solution)/shard_map/ppermute | solution.py:280
  38.3 1.3 %collective-permute-start.7 = (f32[16,2048]{1,0:T(8,128)S(1)}, f32[16,2048]{1,0:T(8,128)S(1)}, u32[]{:S(2)}, u32[]{:S(2)}) collective-permute-start(f32[16,2048]{1,0:T(8,128)S(1)} %fusion.12), channel_id=1, source_target_pairs={{0,18},{2,20},{4,22},{6,24},{8,26},{10,28},{12,30},{1,19},{3,21},{... | collective-permute-start | bytes 393224 | tf_op jit(solution)/shard_map/ppermute | solution.py:280
  39.6 1.3 %collective-permute-start.8 = (f32[16,2048]{1,0:T(8,128)S(1)}, f32[16,2048]{1,0:T(8,128)S(1)}, u32[]{:S(2)}, u32[]{:S(2)}) collective-permute-start(f32[16,2048]{1,0:T(8,128)S(1)} %fusion.12), channel_id=1, source_target_pairs={{0,24},{2,26},{4,28},{6,30},{1,25},{3,27},{5,29},{7,31}} | collective-permute-start | bytes 393224 | tf_op jit(solution)/shard_map/ppermute | solution.py:280
  40.9 0.7 collective-permute-done.5
  41.6 14.0 %collective-permute-done.6 = f32[16,2048]{1,0:T(8,128)S(1)} collective-permute-done((f32[16,2048]{1,0:T(8,128)S(1)}, f32[16,2048]{1,0:T(8,128)S(1)}, u32[]{:S(2)}, u32[]{:S(2)}) %collective-permute-start.6) | collective-permute-done | bytes 131104 | tf_op jit(solution)/shard_map/ppermute | solution.py:280
  55.8 0.8 %collective-permute-start.9 = (f32[16,2048]{1,0:T(8,128)S(1)}, f32[16,2048]{1,0:T(8,128)S(1)}, u32[]{:S(2)}, u32[]{:S(2)}) collective-permute-start(f32[16,2048]{1,0:T(8,128)S(1)} %get-tuple-element.9), channel_id=1, source_target_pairs={{0,1},{1,0},{2,3},{3,2},{4,5},{5,4},{6,7},{7,6},{8,9},{9,8},{10,11... | collective-permute-start | bytes 393224 | tf_op jit(solution)/shard_map/ppermute | solution.py:256
  56.7 4.8 %collective-permute-done.9 = f32[16,2048]{1,0:T(8,128)S(1)} collective-permute-done((f32[16,2048]{1,0:T(8,128)S(1)}, f32[16,2048]{1,0:T(8,128)S(1)}, u32[]{:S(2)}, u32[]{:S(2)}) %collective-permute-start.9) | collective-permute-done | bytes 131104 | tf_op jit(solution)/shard_map/ppermute | solution.py:256
  61.6 0.7 copy-done.1
  62.2 14.5 %shard_map.56 = bf16[128,4096]{1,0:T(8,128)(2,1)} custom-call(bf16[3,128,4096]{2,1,0:T(8,128)(2,1)} %bitcast.91, f32[3,2,4096]{2,1,0:T(2,128)} %get-tuple-element.23.halo_ref, f32[3,3,4096]{2,1,0:T(4,128)} %f_ref.3, f32[16,4096]{1,0:T(8,128)} %bitcast.93, f32[16,4096]{1,0:T(8,128)} %bitcast.94, f32[1,4096]{1,0:T(1,128)} %bitcast.97, ...), custom_call_target="tpu_custom_call" | custom-call | tf_op jit(solution)/shard_map/pallas_call | solution.py:181
  (17 shorter events, 0.8 us)
Async XLA Ops:
  0.0 15.8 %copy-start = (f32[4096,16]{0,1:T(8,128)S(1)}, f32[4096,16]{0,1:T(8,128)}, u32[]{:S(2)}) copy-start(f32[4096,16]{0,1:T(8,128)} %param.8) | copy-start | bytes 786436
  1.1 13.6 %collective-permute-start = (bf16[2,3,4096]{2,0,1:T(2,128)(2,1)S(1)}, bf16[2,3,4096]{2,0,1:T(2,128)(2,1)S(1)}, u32[]{:S(2)}, u32[]{:S(2)}) collective-permute-start(bf16[2,3,4096]{2,0,1:T(2,128)(2,1)S(1)} %get-tuple-element.14), channel_id=1, source_target_pairs={{0,1},{1,2},{2,3},{3,4},{4,5},{5,6},{6,7},{7,8},{8,9},{9,10},{10,1... | collective-permute-start | bytes 147464 | tf_op jit(solution)/shard_map/ppermute | solution.py:216
  17.7 5.3 %collective-permute-start.1 = (f32[16,2048]{1,0:T(8,128)S(1)}, f32[16,2048]{1,0:T(8,128)S(1)}, u32[]{:S(2)}, u32[]{:S(2)}) collective-permute-start(f32[16,2048]{1,0:T(8,128)S(1)} %constant_dynamic-slice_fusion), channel_id=1, source_target_pairs={{0,1},{1,0},{2,3},{3,2},{4,5},{5,4},{6,7},{7,6},{8,9},{9,8},{10,11... | collective-permute-start | bytes 393224 | tf_op jit(solution)/shard_map/ppermute | solution.py:256
  23.0 7.2 %collective-permute-start.2 = (f32[16,2048]{1,0:T(8,128)S(1)}, f32[16,2048]{1,0:T(8,128)S(1)}, u32[]{:S(2)}, u32[]{:S(2)}) collective-permute-start(f32[16,2048]{1,0:T(8,128)S(1)} %fusion.14), channel_id=1, source_target_pairs={{0,2},{2,4},{4,6},{6,8},{8,10},{10,12},{12,14},{14,16},{16,18},{18... | collective-permute-start | bytes 393224 | tf_op jit(solution)/shard_map/ppermute | solution.py:280
  24.9 8.9 %collective-permute-start.3 = (f32[16,2048]{1,0:T(8,128)S(1)}, f32[16,2048]{1,0:T(8,128)S(1)}, u32[]{:S(2)}, u32[]{:S(2)}) collective-permute-start(f32[16,2048]{1,0:T(8,128)S(1)} %fusion.14), channel_id=1, source_target_pairs={{0,4},{2,6},{4,8},{6,10},{8,12},{10,14},{12,16},{14,18},{16,20},{1... | collective-permute-start | bytes 393224 | tf_op jit(solution)/shard_map/ppermute | solution.py:280
  28.1 6.3 %collective-permute-start.4 = (f32[16,2048]{1,0:T(8,128)S(1)}, f32[16,2048]{1,0:T(8,128)S(1)}, u32[]{:S(2)}, u32[]{:S(2)}) collective-permute-start(f32[16,2048]{1,0:T(8,128)S(1)} %fusion.14), channel_id=1, source_target_pairs={{0,6},{2,8},{4,10},{6,12},{8,14},{10,16},{12,18},{14,20},{16,22},{... | collective-permute-start | bytes 393224 | tf_op jit(solution)/shard_map/ppermute | solution.py:280
  34.5 7.1 %collective-permute-start.5 = (f32[16,2048]{1,0:T(8,128)S(1)}, f32[16,2048]{1,0:T(8,128)S(1)}, u32[]{:S(2)}, u32[]{:S(2)}) collective-permute-start(f32[16,2048]{1,0:T(8,128)S(1)} %fusion.12), channel_id=1, source_target_pairs={{0,6},{2,8},{4,10},{6,12},{8,14},{10,16},{12,18},{14,20},{16,22},{... | collective-permute-start | bytes 393224 | tf_op jit(solution)/shard_map/ppermute | solution.py:280
  37.0 18.6 %collective-permute-start.6 = (f32[16,2048]{1,0:T(8,128)S(1)}, f32[16,2048]{1,0:T(8,128)S(1)}, u32[]{:S(2)}, u32[]{:S(2)}) collective-permute-start(f32[16,2048]{1,0:T(8,128)S(1)} %fusion.12), channel_id=1, source_target_pairs={{0,12},{2,14},{4,16},{6,18},{8,20},{10,22},{12,24},{14,26},{16,28}... | collective-permute-start | bytes 393224 | tf_op jit(solution)/shard_map/ppermute | solution.py:280
  38.3 17.3 %collective-permute-start.7 = (f32[16,2048]{1,0:T(8,128)S(1)}, f32[16,2048]{1,0:T(8,128)S(1)}, u32[]{:S(2)}, u32[]{:S(2)}) collective-permute-start(f32[16,2048]{1,0:T(8,128)S(1)} %fusion.12), channel_id=1, source_target_pairs={{0,18},{2,20},{4,22},{6,24},{8,26},{10,28},{12,30},{1,19},{3,21},{... | collective-permute-start | bytes 393224 | tf_op jit(solution)/shard_map/ppermute | solution.py:280
  39.6 16.0 %collective-permute-start.8 = (f32[16,2048]{1,0:T(8,128)S(1)}, f32[16,2048]{1,0:T(8,128)S(1)}, u32[]{:S(2)}, u32[]{:S(2)}) collective-permute-start(f32[16,2048]{1,0:T(8,128)S(1)} %fusion.12), channel_id=1, source_target_pairs={{0,24},{2,26},{4,28},{6,30},{1,25},{3,27},{5,29},{7,31}} | collective-permute-start | bytes 393224 | tf_op jit(solution)/shard_map/ppermute | solution.py:280
  55.8 5.7 %collective-permute-start.9 = (f32[16,2048]{1,0:T(8,128)S(1)}, f32[16,2048]{1,0:T(8,128)S(1)}, u32[]{:S(2)}, u32[]{:S(2)}) collective-permute-start(f32[16,2048]{1,0:T(8,128)S(1)} %get-tuple-element.9), channel_id=1, source_target_pairs={{0,1},{1,0},{2,3},{3,2},{4,5},{5,4},{6,7},{7,6},{8,9},{9,8},{10,11... | collective-permute-start | bytes 393224 | tf_op jit(solution)/shard_map/ppermute | solution.py:256
  61.5 0.7 copy-start.1

commit v18 on v12

--- a/solution.py
+++ b/solution.py
@@ -10,7 +10,7 @@
 BLOCK = 1024
 FIRST_WINDOW = 3
 LATER_WINDOW = 4
-UNROLL = 8
+UNROLL = 16
 
 
 def lane_slice(c):

time: 77.1 us -> 74.8 us (0.970)
  Pallas kernels: 23 us -> 20.7 us
    pallas_call x1, Pallas kernels: 14.5 us -> 13.1 us  [run_out(): pl.pallas_call(out_kernel, grid=(width // BLOCK,), in_specs=[pl.BlockSpec...]
    pallas_call x1, Pallas kernels: 8.55 us -> 7.56 us  [run_state(): pl.pallas_call(state_kernel, grid=(width // BLOCK,), in_specs=[pl.BlockSp...]
  transfers between devices with their start and end apart: 10 -> 10, of which waited for: 6 -> 6; matrix products, arithmetic and copies ran while one was open for 2% -> 2% of each run, Pallas kernels for 11% -> 10%
where the time goes in v18:
time: 74.8 us; the launch traced here: 73.7 us
  waiting for transfers between devices  27.7 us (37%)
  Pallas kernels  20.7 us (28%)
  starting transfers between devices  18.5 us (25%)
  other arithmetic  5.09 us (7%)
  local copies, waits for them, and re-layouts  1.64 us (2%)
    ppermute x7, waiting for transfers between devices, span_shift(): lax.ppermute(value, 'ctx', [(j, j + offset) for j in range(spans - offset)])  14.7 us
    ppermute x7, starting transfers between devices, span_shift(): lax.ppermute(value, 'ctx', [(j, j + offset) for j in range(spans - offset)])  14.3 us
    pallas_call x1, Pallas kernels, run_out(): pl.pallas_call(out_kernel, grid=(width // BLOCK,), in_specs=[pl.BlockSpec...  13.1 us
    ppermute x2, waiting for transfers between devices, exchange(): lax.ppermute(value, 'tp', [(q, (q + k) % group) for q in range(group)])  13 us
    pallas_call x1, Pallas kernels, run_state(): pl.pallas_call(state_kernel, grid=(width // BLOCK,), in_specs=[pl.BlockSp...  7.56 us
    ppermute x1, starting transfers between devices, shift(): return lax.ppermute(value, axes, pairs)  3.43 us
    add x1, other arithmetic, body(): local = local + local_fix  1.84 us
  transfers between devices with their start and end apart: 10, of which 6 were waited for; matrix products, arithmetic and copies ran while one was open for 2% of the time, Pallas kernels for 10%

profile of v18, /device:TPU:16, one launch (start us, length us, event | category | flops | bytes accessed | tf_op | source)
XLA Modules:
  0.0 73.7 jit_solution(7928755896955462969)
XLA Ops:
  0.0 1.1 %slice_convert_fusion = (f32[2,3,4096]{2,0,1:T(2,128)S(1)}, bf16[2,3,4096]{2,0,1:T(2,128)(2,1)S(1)}) fusion(bf16[128,3,4096]{2,0,1:T(8,128)(2,1)} %param.5), kind=kLoop, calls=%fused_computation.28 | loop fusion | flops 24576 | bytes 245760 | tf_op jit(solution)/shard_map/convert_element_type | solution.py:225
  1.1 3.4 %collective-permute-start = (bf16[2,3,4096]{2,0,1:T(2,128)(2,1)S(1)}, bf16[2,3,4096]{2,0,1:T(2,128)(2,1)S(1)}, u32[]{:S(2)}, u32[]{:S(2)}) collective-permute-start(bf16[2,3,4096]{2,0,1:T(2,128)(2,1)S(1)} %get-tuple-element.14), channel_id=1, source_target_pairs={{0,1},{1,2},{2,3},{3,4},{4,5},{5,6},{6,7},{7,8},{8,9},{9,10},{10,1... | collective-permute-start | bytes 147464 | tf_op jit(solution)/shard_map/ppermute | solution.py:216
  4.6 0.9 %fusion.22 = (f32[1,3,4096]{2,1,0:T(4,128)S(1)}, f32[1,3,4096]{2,1,0:T(4,128)S(1)}, f32[1,3,4096]{2,1,0:T(4,128)S(1)}) fusion(f32[3,3,4096]{2,1,0:T(4,128)} %f_ref.3), kind=kLoop, calls=%fused_computation.49 | loop fusion | bytes 294912 | tf_op jit(solution)/shard_map/slice | solution.py:231
  5.5 0.7 broadcast_in_dim.3.halo_ref
  6.2 7.6 %shard_map.55 = (f32[16,8,4096]{2,1,0:T(8,128)}, f32[16,4096]{1,0:T(8,128)}) custom-call(bf16[3,128,4096]{2,1,0:T(8,128)(2,1)} %bitcast.57, f32[3,2,4096]{2,1,0:T(2,128)} %broadcast_in_dim.3.halo_ref, f32[3,3,4096]{2,1,0:T(4,128)} %f_ref.3, f32[16,4096]{1,0:T(8,128)} %bitcast.59), custom_call_target="tpu_custom_call" | custom-call | tf_op jit(solution)/shard_map/pallas_call | solution.py:152
  13.7 0.7 fusion.23
  14.4 0.2 multiply_add_fusion.1
  14.8 1.8 %add_add_fusion = (f32[16,4096]{1,0:T(8,128)S(1)}, f32[16,4096]{1,0:T(8,128)}, f32[16,4096]{1,0:T(8,128)S(1)}) fusion(f32[16,4096]{1,0:T(8,128)} %get-tuple-element.8, f32[4096]{0:T(1024)S(1)} %bitcast.62, f32[4096]{0:T(1024)S(1)} %bitcast.63, f32[4096,16]{0,1:T(8,128)S(1)} %copy-done), kind=kLoop, calls=%fused_computation.1 | loop fusion | flops 786432 | bytes 1343488 | tf_op jit(solution)/shard_map/add | solution.py:248
  16.7 8.0 %collective-permute-done.1 = f32[16,4096]{1,0:T(8,128)S(1)} collective-permute-done((f32[16,4096]{1,0:T(8,128)S(1)}, f32[16,4096]{1,0:T(8,128)S(1)}, u32[]{:S(2)}, u32[]{:S(2)}) %collective-permute-start.1) | collective-permute-done | bytes 262176 | tf_op jit(solution)/shard_map/ppermute | solution.py:256
  24.8 2.1 %collective-permute-start.4 = (f32[16,2048]{1,0:T(8,128)S(1)}, f32[16,2048]{1,0:T(8,128)S(1)}, u32[]{:S(2)}, u32[]{:S(2)}) collective-permute-start(f32[16,2048]{1,0:T(8,128)S(1)} %fusion), channel_id=1, source_target_pairs={{0,6},{2,8},{4,10},{6,12},{8,14},{10,16},{12,18},{14,20},{16,22},{... | collective-permute-start | bytes 393224 | tf_op jit(solution)/shard_map/ppermute | solution.py:277
  26.8 3.3 %collective-permute-start.3 = (f32[16,2048]{1,0:T(8,128)S(1)}, f32[16,2048]{1,0:T(8,128)S(1)}, u32[]{:S(2)}, u32[]{:S(2)}) collective-permute-start(f32[16,2048]{1,0:T(8,128)S(1)} %fusion), channel_id=1, source_target_pairs={{0,4},{2,6},{4,8},{6,10},{8,12},{10,14},{12,16},{14,18},{16,20},{1... | collective-permute-start | bytes 393224 | tf_op jit(solution)/shard_map/ppermute | solution.py:277
  30.2 3.0 %collective-permute-start.2 = (f32[16,2048]{1,0:T(8,128)S(1)}, f32[16,2048]{1,0:T(8,128)S(1)}, u32[]{:S(2)}, u32[]{:S(2)}) collective-permute-start(f32[16,2048]{1,0:T(8,128)S(1)} %fusion), channel_id=1, source_target_pairs={{0,2},{2,4},{4,6},{6,8},{8,10},{10,12},{12,14},{14,16},{16,18},{18... | collective-permute-start | bytes 393224 | tf_op jit(solution)/shard_map/ppermute | solution.py:277
  33.2 2.3 %collective-permute-done.3 = f32[16,2048]{1,0:T(8,128)S(1)} collective-permute-done((f32[16,2048]{1,0:T(8,128)S(1)}, f32[16,2048]{1,0:T(8,128)S(1)}, u32[]{:S(2)}, u32[]{:S(2)}) %collective-permute-start.3) | collective-permute-done | bytes 131104 | tf_op jit(solution)/shard_map/ppermute | solution.py:277
  35.5 1.9 %collective-permute-done.2 = f32[16,2048]{1,0:T(8,128)S(1)} collective-permute-done((f32[16,2048]{1,0:T(8,128)S(1)}, f32[16,2048]{1,0:T(8,128)S(1)}, u32[]{:S(2)}, u32[]{:S(2)}) %collective-permute-start.2) | collective-permute-done | bytes 131104 | tf_op jit(solution)/shard_map/ppermute | solution.py:277
  37.5 0.7 collective-permute-start.8
  38.1 0.7 collective-permute-start.7
  38.8 2.6 %collective-permute-start.6 = (f32[16,2048]{1,0:T(8,128)S(1)}, f32[16,2048]{1,0:T(8,128)S(1)}, u32[]{:S(2)}, u32[]{:S(2)}) collective-permute-start(f32[16,2048]{1,0:T(8,128)S(1)} %fusion.6), channel_id=1, source_target_pairs={{0,12},{2,14},{4,16},{6,18},{8,20},{10,22},{12,24},{14,26},{16,28}... | collective-permute-start | bytes 393224 | tf_op jit(solution)/shard_map/ppermute | solution.py:277
  41.4 1.9 %collective-permute-start.5 = (f32[16,2048]{1,0:T(8,128)S(1)}, f32[16,2048]{1,0:T(8,128)S(1)}, u32[]{:S(2)}, u32[]{:S(2)}) collective-permute-start(f32[16,2048]{1,0:T(8,128)S(1)} %fusion.6), channel_id=1, source_target_pairs={{0,6},{2,8},{4,10},{6,12},{8,14},{10,16},{12,18},{14,20},{16,22},{... | collective-permute-start | bytes 393224 | tf_op jit(solution)/shard_map/ppermute | solution.py:277
  43.4 5.5 %collective-permute-done.6 = f32[16,2048]{1,0:T(8,128)S(1)} collective-permute-done((f32[16,2048]{1,0:T(8,128)S(1)}, f32[16,2048]{1,0:T(8,128)S(1)}, u32[]{:S(2)}, u32[]{:S(2)}) %collective-permute-start.6) | collective-permute-done | bytes 131104 | tf_op jit(solution)/shard_map/ppermute | solution.py:277
  48.9 5.0 %collective-permute-done.5 = f32[16,2048]{1,0:T(8,128)S(1)} collective-permute-done((f32[16,2048]{1,0:T(8,128)S(1)}, f32[16,2048]{1,0:T(8,128)S(1)}, u32[]{:S(2)}, u32[]{:S(2)}) %collective-permute-start.5) | collective-permute-done | bytes 131104 | tf_op jit(solution)/shard_map/ppermute | solution.py:277
  54.0 0.8 %collective-permute-start.9 = (f32[16,2048]{1,0:T(8,128)S(1)}, f32[16,2048]{1,0:T(8,128)S(1)}, u32[]{:S(2)}, u32[]{:S(2)}) collective-permute-start(f32[16,2048]{1,0:T(8,128)S(1)} %get-tuple-element.10), channel_id=1, source_target_pairs={{0,1},{1,0},{2,3},{3,2},{4,5},{5,4},{6,7},{7,6},{8,9},{9,8},{10,11... | collective-permute-start | bytes 393224 | tf_op jit(solution)/shard_map/ppermute | solution.py:256
  54.8 5.0 %collective-permute-done.9 = f32[16,2048]{1,0:T(8,128)S(1)} collective-permute-done((f32[16,2048]{1,0:T(8,128)S(1)}, f32[16,2048]{1,0:T(8,128)S(1)}, u32[]{:S(2)}, u32[]{:S(2)}) %collective-permute-start.9) | collective-permute-done | bytes 131104 | tf_op jit(solution)/shard_map/ppermute | solution.py:256
  59.8 0.8 %select_add_fusion.hin_ref = f32[16,4096]{1,0:T(8,128)} fusion(f32[16,4096]{1,0:T(8,128)S(1)} %collective-permute-done.1, f32[16,4096]{1,0:T(8,128)S(1)} %constant_dynamic-update-slice_fusion, f32[]{:T(128)S(6)} %mul.259, pred[]{:T(512)S(6)} %ge.3, f32[4096,16]{0,1:T(8,128)S(1)} %copy-done), kind=kLoop, calls=%fused_computation | loop fusion | flops 458752 | bytes 1048581 | tf_op jit(solution)/shard_map/add | solution.py:303
  60.6 13.1 %shard_map.56 = bf16[128,4096]{1,0:T(8,128)(2,1)} custom-call(bf16[3,128,4096]{2,1,0:T(8,128)(2,1)} %bitcast.58, f32[3,2,4096]{2,1,0:T(2,128)} %get-tuple-element.24.halo_ref, f32[3,3,4096]{2,1,0:T(4,128)} %f_ref.3, f32[16,4096]{1,0:T(8,128)} %bitcast.60, f32[16,4096]{1,0:T(8,128)} %bitcast.61, f32[1,4096]{1,0:T(1,128)} %bitcast.64, ...), custom_call_target="tpu_custom_call" | custom-call | tf_op jit(solution)/shard_map/pallas_call | solution.py:181
  (14 shorter events, 0.4 us)
Async XLA Ops:
  0.0 14.8 %copy-start = (f32[4096,16]{0,1:T(8,128)S(1)}, f32[4096,16]{0,1:T(8,128)}, u32[]{:S(2)}) copy-start(f32[4096,16]{0,1:T(8,128)} %param.8) | copy-start | bytes 786436
  1.1 12.6 %collective-permute-start = (bf16[2,3,4096]{2,0,1:T(2,128)(2,1)S(1)}, bf16[2,3,4096]{2,0,1:T(2,128)(2,1)S(1)}, u32[]{:S(2)}, u32[]{:S(2)}) collective-permute-start(bf16[2,3,4096]{2,0,1:T(2,128)(2,1)S(1)} %get-tuple-element.14), channel_id=1, source_target_pairs={{0,1},{1,2},{2,3},{3,4},{4,5},{5,6},{6,7},{7,8},{8,9},{9,10},{10,1... | collective-permute-start | bytes 147464 | tf_op jit(solution)/shard_map/ppermute | solution.py:216
  16.7 8.0 %collective-permute-start.1 = (f32[16,4096]{1,0:T(8,128)S(1)}, f32[16,4096]{1,0:T(8,128)S(1)}, u32[]{:S(2)}, u32[]{:S(2)}) collective-permute-start(f32[16,4096]{1,0:T(8,128)S(1)} %get-tuple-element.16), channel_id=1, source_target_pairs={{0,1},{1,0},{2,3},{3,2},{4,5},{5,4},{6,7},{7,6},{8,9},{9,8},{10,11... | collective-permute-start | bytes 786440 | tf_op jit(solution)/shard_map/ppermute | solution.py:256
  24.8 8.4 %collective-permute-start.4 = (f32[16,2048]{1,0:T(8,128)S(1)}, f32[16,2048]{1,0:T(8,128)S(1)}, u32[]{:S(2)}, u32[]{:S(2)}) collective-permute-start(f32[16,2048]{1,0:T(8,128)S(1)} %fusion), channel_id=1, source_target_pairs={{0,6},{2,8},{4,10},{6,12},{8,14},{10,16},{12,18},{14,20},{16,22},{... | collective-permute-start | bytes 393224 | tf_op jit(solution)/shard_map/ppermute | solution.py:277
  26.8 8.6 %collective-permute-start.3 = (f32[16,2048]{1,0:T(8,128)S(1)}, f32[16,2048]{1,0:T(8,128)S(1)}, u32[]{:S(2)}, u32[]{:S(2)}) collective-permute-start(f32[16,2048]{1,0:T(8,128)S(1)} %fusion), channel_id=1, source_target_pairs={{0,4},{2,6},{4,8},{6,10},{8,12},{10,14},{12,16},{14,18},{16,20},{1... | collective-permute-start | bytes 393224 | tf_op jit(solution)/shard_map/ppermute | solution.py:277
  30.2 7.2 %collective-permute-start.2 = (f32[16,2048]{1,0:T(8,128)S(1)}, f32[16,2048]{1,0:T(8,128)S(1)}, u32[]{:S(2)}, u32[]{:S(2)}) collective-permute-start(f32[16,2048]{1,0:T(8,128)S(1)} %fusion), channel_id=1, source_target_pairs={{0,2},{2,4},{4,6},{6,8},{8,10},{10,12},{12,14},{14,16},{16,18},{18... | collective-permute-start | bytes 393224 | tf_op jit(solution)/shard_map/ppermute | solution.py:277
  37.5 5.9 %collective-permute-start.8 = (f32[16,2048]{1,0:T(8,128)S(1)}, f32[16,2048]{1,0:T(8,128)S(1)}, u32[]{:S(2)}, u32[]{:S(2)}) collective-permute-start(f32[16,2048]{1,0:T(8,128)S(1)} %fusion.6), channel_id=1, source_target_pairs={{0,24},{2,26},{4,28},{6,30},{1,25},{3,27},{5,29},{7,31}} | collective-permute-start | bytes 393224 | tf_op jit(solution)/shard_map/ppermute | solution.py:277
  38.1 5.3 %collective-permute-start.7 = (f32[16,2048]{1,0:T(8,128)S(1)}, f32[16,2048]{1,0:T(8,128)S(1)}, u32[]{:S(2)}, u32[]{:S(2)}) collective-permute-start(f32[16,2048]{1,0:T(8,128)S(1)} %fusion.6), channel_id=1, source_target_pairs={{0,18},{2,20},{4,22},{6,24},{8,26},{10,28},{12,30},{1,19},{3,21},{... | collective-permute-start | bytes 393224 | tf_op jit(solution)/shard_map/ppermute | solution.py:277
  38.8 10.1 %collective-permute-start.6 = (f32[16,2048]{1,0:T(8,128)S(1)}, f32[16,2048]{1,0:T(8,128)S(1)}, u32[]{:S(2)}, u32[]{:S(2)}) collective-permute-start(f32[16,2048]{1,0:T(8,128)S(1)} %fusion.6), channel_id=1, source_target_pairs={{0,12},{2,14},{4,16},{6,18},{8,20},{10,22},{12,24},{14,26},{16,28}... | collective-permute-start | bytes 393224 | tf_op jit(solution)/shard_map/ppermute | solution.py:277
  41.4 12.4 %collective-permute-start.5 = (f32[16,2048]{1,0:T(8,128)S(1)}, f32[16,2048]{1,0:T(8,128)S(1)}, u32[]{:S(2)}, u32[]{:S(2)}) collective-permute-start(f32[16,2048]{1,0:T(8,128)S(1)} %fusion.6), channel_id=1, source_target_pairs={{0,6},{2,8},{4,10},{6,12},{8,14},{10,16},{12,18},{14,20},{16,22},{... | collective-permute-start | bytes 393224 | tf_op jit(solution)/shard_map/ppermute | solution.py:277
  54.0 5.8 %collective-permute-start.9 = (f32[16,2048]{1,0:T(8,128)S(1)}, f32[16,2048]{1,0:T(8,128)S(1)}, u32[]{:S(2)}, u32[]{:S(2)}) collective-permute-start(f32[16,2048]{1,0:T(8,128)S(1)} %get-tuple-element.10), channel_id=1, source_target_pairs={{0,1},{1,0},{2,3},{3,2},{4,5},{5,4},{6,7},{7,6},{8,9},{9,8},{10,11... | collective-permute-start | bytes 393224 | tf_op jit(solution)/shard_map/ppermute | solution.py:256

commit v19 on v18

--- a/solution.py
+++ b/solution.py
@@ -89,7 +89,7 @@
             h_ref[pl.ds(m, 1), lanes] = jnp.sum(weight * states[m], axis=0, keepdims=True)
         return carry
 
-    lax.fori_loop(0, block // LANES, lane_group, 0)
+    lax.fori_loop(0, block // LANES, lane_group, 0, unroll=2)
 
 
 def out_kernel(
@@ -140,7 +140,7 @@
         lax.fori_loop(0, seg, step, init, unroll=UNROLL)
         return carry
 
-    lax.fori_loop(0, block // LANES, lane_group, 0)
+    lax.fori_loop(0, block // LANES, lane_group, 0, unroll=2)
     for c in range(block // LANES):
         o_ref[:, c * LANES : (c + 1) * LANES] = ys[c].astype(o_ref.dtype)
 

time: 74.8 us -> 74.5 us (level)
  no operation moved by 1% of the time
where the time goes in v19:
time: 74.5 us; the launch traced here: 73.4 us
  waiting for transfers between devices  27.7 us (37%)
  Pallas kernels  20.4 us (27%)
  starting transfers between devices  18.5 us (25%)
  other arithmetic  5.09 us (7%)
  local copies, waits for them, and re-layouts  1.64 us (2%)
    ppermute x7, waiting for transfers between devices, span_shift(): lax.ppermute(value, 'ctx', [(j, j + offset) for j in range(spans - offset)])  14.7 us
    ppermute x7, starting transfers between devices, span_shift(): lax.ppermute(value, 'ctx', [(j, j + offset) for j in range(spans - offset)])  14.3 us
    ppermute x2, waiting for transfers between devices, exchange(): lax.ppermute(value, 'tp', [(q, (q + k) % group) for q in range(group)])  13 us
    pallas_call x1, Pallas kernels, run_out(): pl.pallas_call(out_kernel, grid=(width // BLOCK,), in_specs=[pl.BlockSpec...  13 us
    pallas_call x1, Pallas kernels, run_state(): pl.pallas_call(state_kernel, grid=(width // BLOCK,), in_specs=[pl.BlockSp...  7.39 us
    ppermute x1, starting transfers between devices, shift(): return lax.ppermute(value, axes, pairs)  3.43 us
    add x1, other arithmetic, body(): local = local + local_fix  1.84 us
  transfers between devices with their start and end apart: 10, of which 6 were waited for; matrix products, arithmetic and copies ran while one was open for 2% of the time, Pallas kernels for 10%

profile of v19, /device:TPU:16, one launch (start us, length us, event | category | flops | bytes accessed | tf_op | source)
XLA Modules:
  0.0 73.4 jit_solution(8266248134459422061)
XLA Ops:
  0.0 1.1 %slice_convert_fusion = (f32[2,3,4096]{2,0,1:T(2,128)S(1)}, bf16[2,3,4096]{2,0,1:T(2,128)(2,1)S(1)}) fusion(bf16[128,3,4096]{2,0,1:T(8,128)(2,1)} %param.5), kind=kLoop, calls=%fused_computation.28 | loop fusion | flops 24576 | bytes 245760 | tf_op jit(solution)/shard_map/convert_element_type | solution.py:225
  1.1 3.4 %collective-permute-start = (bf16[2,3,4096]{2,0,1:T(2,128)(2,1)S(1)}, bf16[2,3,4096]{2,0,1:T(2,128)(2,1)S(1)}, u32[]{:S(2)}, u32[]{:S(2)}) collective-permute-start(bf16[2,3,4096]{2,0,1:T(2,128)(2,1)S(1)} %get-tuple-element.14), channel_id=1, source_target_pairs={{0,1},{1,2},{2,3},{3,4},{4,5},{5,6},{6,7},{7,8},{8,9},{9,10},{10,1... | collective-permute-start | bytes 147464 | tf_op jit(solution)/shard_map/ppermute | solution.py:216
  4.6 0.9 %fusion.22 = (f32[1,3,4096]{2,1,0:T(4,128)S(1)}, f32[1,3,4096]{2,1,0:T(4,128)S(1)}, f32[1,3,4096]{2,1,0:T(4,128)S(1)}) fusion(f32[3,3,4096]{2,1,0:T(4,128)} %f_ref.3), kind=kLoop, calls=%fused_computation.49 | loop fusion | bytes 294912 | tf_op jit(solution)/shard_map/slice | solution.py:231
  5.5 0.7 broadcast_in_dim.3.halo_ref
  6.2 7.4 %shard_map.55 = (f32[16,8,4096]{2,1,0:T(8,128)}, f32[16,4096]{1,0:T(8,128)}) custom-call(bf16[3,128,4096]{2,1,0:T(8,128)(2,1)} %bitcast.57, f32[3,2,4096]{2,1,0:T(2,128)} %broadcast_in_dim.3.halo_ref, f32[3,3,4096]{2,1,0:T(4,128)} %f_ref.3, f32[16,4096]{1,0:T(8,128)} %bitcast.59), custom_call_target="tpu_custom_call" | custom-call | tf_op jit(solution)/shard_map/pallas_call | solution.py:152
  13.6 0.7 fusion.23
  14.3 0.2 multiply_add_fusion.1
  14.7 1.8 %add_add_fusion = (f32[16,4096]{1,0:T(8,128)S(1)}, f32[16,4096]{1,0:T(8,128)}, f32[16,4096]{1,0:T(8,128)S(1)}) fusion(f32[16,4096]{1,0:T(8,128)} %get-tuple-element.8, f32[4096]{0:T(1024)S(1)} %bitcast.62, f32[4096]{0:T(1024)S(1)} %bitcast.63, f32[4096,16]{0,1:T(8,128)S(1)} %copy-done), kind=kLoop, calls=%fused_computation.1 | loop fusion | flops 786432 | bytes 1343488 | tf_op jit(solution)/shard_map/add | solution.py:248
  16.5 8.0 %collective-permute-done.1 = f32[16,4096]{1,0:T(8,128)S(1)} collective-permute-done((f32[16,4096]{1,0:T(8,128)S(1)}, f32[16,4096]{1,0:T(8,128)S(1)}, u32[]{:S(2)}, u32[]{:S(2)}) %collective-permute-start.1) | collective-permute-done | bytes 262176 | tf_op jit(solution)/shard_map/ppermute | solution.py:256
  24.6 2.1 %collective-permute-start.4 = (f32[16,2048]{1,0:T(8,128)S(1)}, f32[16,2048]{1,0:T(8,128)S(1)}, u32[]{:S(2)}, u32[]{:S(2)}) collective-permute-start(f32[16,2048]{1,0:T(8,128)S(1)} %fusion), channel_id=1, source_target_pairs={{0,6},{2,8},{4,10},{6,12},{8,14},{10,16},{12,18},{14,20},{16,22},{... | collective-permute-start | bytes 393224 | tf_op jit(solution)/shard_map/ppermute | solution.py:277
  26.6 3.3 %collective-permute-start.3 = (f32[16,2048]{1,0:T(8,128)S(1)}, f32[16,2048]{1,0:T(8,128)S(1)}, u32[]{:S(2)}, u32[]{:S(2)}) collective-permute-start(f32[16,2048]{1,0:T(8,128)S(1)} %fusion), channel_id=1, source_target_pairs={{0,4},{2,6},{4,8},{6,10},{8,12},{10,14},{12,16},{14,18},{16,20},{1... | collective-permute-start | bytes 393224 | tf_op jit(solution)/shard_map/ppermute | solution.py:277
  30.0 3.0 %collective-permute-start.2 = (f32[16,2048]{1,0:T(8,128)S(1)}, f32[16,2048]{1,0:T(8,128)S(1)}, u32[]{:S(2)}, u32[]{:S(2)}) collective-permute-start(f32[16,2048]{1,0:T(8,128)S(1)} %fusion), channel_id=1, source_target_pairs={{0,2},{2,4},{4,6},{6,8},{8,10},{10,12},{12,14},{14,16},{16,18},{18... | collective-permute-start | bytes 393224 | tf_op jit(solution)/shard_map/ppermute | solution.py:277
  33.0 2.3 %collective-permute-done.3 = f32[16,2048]{1,0:T(8,128)S(1)} collective-permute-done((f32[16,2048]{1,0:T(8,128)S(1)}, f32[16,2048]{1,0:T(8,128)S(1)}, u32[]{:S(2)}, u32[]{:S(2)}) %collective-permute-start.3) | collective-permute-done | bytes 131104 | tf_op jit(solution)/shard_map/ppermute | solution.py:277
  35.3 1.9 %collective-permute-done.2 = f32[16,2048]{1,0:T(8,128)S(1)} collective-permute-done((f32[16,2048]{1,0:T(8,128)S(1)}, f32[16,2048]{1,0:T(8,128)S(1)}, u32[]{:S(2)}, u32[]{:S(2)}) %collective-permute-start.2) | collective-permute-done | bytes 131104 | tf_op jit(solution)/shard_map/ppermute | solution.py:277
  37.3 0.7 collective-permute-start.8
  38.0 0.7 collective-permute-start.7
  38.6 2.6 %collective-permute-start.6 = (f32[16,2048]{1,0:T(8,128)S(1)}, f32[16,2048]{1,0:T(8,128)S(1)}, u32[]{:S(2)}, u32[]{:S(2)}) collective-permute-start(f32[16,2048]{1,0:T(8,128)S(1)} %fusion.6), channel_id=1, source_target_pairs={{0,12},{2,14},{4,16},{6,18},{8,20},{10,22},{12,24},{14,26},{16,28}... | collective-permute-start | bytes 393224 | tf_op jit(solution)/shard_map/ppermute | solution.py:277
  41.3 1.9 %collective-permute-start.5 = (f32[16,2048]{1,0:T(8,128)S(1)}, f32[16,2048]{1,0:T(8,128)S(1)}, u32[]{:S(2)}, u32[]{:S(2)}) collective-permute-start(f32[16,2048]{1,0:T(8,128)S(1)} %fusion.6), channel_id=1, source_target_pairs={{0,6},{2,8},{4,10},{6,12},{8,14},{10,16},{12,18},{14,20},{16,22},{... | collective-permute-start | bytes 393224 | tf_op jit(solution)/shard_map/ppermute | solution.py:277
  43.2 5.5 %collective-permute-done.6 = f32[16,2048]{1,0:T(8,128)S(1)} collective-permute-done((f32[16,2048]{1,0:T(8,128)S(1)}, f32[16,2048]{1,0:T(8,128)S(1)}, u32[]{:S(2)}, u32[]{:S(2)}) %collective-permute-start.6) | collective-permute-done | bytes 131104 | tf_op jit(solution)/shard_map/ppermute | solution.py:277
  48.7 5.0 %collective-permute-done.5 = f32[16,2048]{1,0:T(8,128)S(1)} collective-permute-done((f32[16,2048]{1,0:T(8,128)S(1)}, f32[16,2048]{1,0:T(8,128)S(1)}, u32[]{:S(2)}, u32[]{:S(2)}) %collective-permute-start.5) | collective-permute-done | bytes 131104 | tf_op jit(solution)/shard_map/ppermute | solution.py:277
  53.9 0.8 %collective-permute-start.9 = (f32[16,2048]{1,0:T(8,128)S(1)}, f32[16,2048]{1,0:T(8,128)S(1)}, u32[]{:S(2)}, u32[]{:S(2)}) collective-permute-start(f32[16,2048]{1,0:T(8,128)S(1)} %get-tuple-element.10), channel_id=1, source_target_pairs={{0,1},{1,0},{2,3},{3,2},{4,5},{5,4},{6,7},{7,6},{8,9},{9,8},{10,11... | collective-permute-start | bytes 393224 | tf_op jit(solution)/shard_map/ppermute | solution.py:256
  54.6 5.0 %collective-permute-done.9 = f32[16,2048]{1,0:T(8,128)S(1)} collective-permute-done((f32[16,2048]{1,0:T(8,128)S(1)}, f32[16,2048]{1,0:T(8,128)S(1)}, u32[]{:S(2)}, u32[]{:S(2)}) %collective-permute-start.9) | collective-permute-done | bytes 131104 | tf_op jit(solution)/shard_map/ppermute | solution.py:256
  59.6 0.8 %select_add_fusion.hin_ref = f32[16,4096]{1,0:T(8,128)} fusion(f32[16,4096]{1,0:T(8,128)S(1)} %collective-permute-done.1, f32[16,4096]{1,0:T(8,128)S(1)} %constant_dynamic-update-slice_fusion, f32[]{:T(128)S(6)} %mul.259, pred[]{:T(512)S(6)} %ge.3, f32[4096,16]{0,1:T(8,128)S(1)} %copy-done), kind=kLoop, calls=%fused_computation | loop fusion | flops 458752 | bytes 1048581 | tf_op jit(solution)/shard_map/add | solution.py:303
  60.4 13.0 %shard_map.56 = bf16[128,4096]{1,0:T(8,128)(2,1)} custom-call(bf16[3,128,4096]{2,1,0:T(8,128)(2,1)} %bitcast.58, f32[3,2,4096]{2,1,0:T(2,128)} %get-tuple-element.24.halo_ref, f32[3,3,4096]{2,1,0:T(4,128)} %f_ref.3, f32[16,4096]{1,0:T(8,128)} %bitcast.60, f32[16,4096]{1,0:T(8,128)} %bitcast.61, f32[1,4096]{1,0:T(1,128)} %bitcast.64, ...), custom_call_target="tpu_custom_call" | custom-call | tf_op jit(solution)/shard_map/pallas_call | solution.py:181
  (14 shorter events, 0.4 us)
Async XLA Ops:
  0.0 14.7 %copy-start = (f32[4096,16]{0,1:T(8,128)S(1)}, f32[4096,16]{0,1:T(8,128)}, u32[]{:S(2)}) copy-start(f32[4096,16]{0,1:T(8,128)} %param.8) | copy-start | bytes 786436
  1.1 12.4 %collective-permute-start = (bf16[2,3,4096]{2,0,1:T(2,128)(2,1)S(1)}, bf16[2,3,4096]{2,0,1:T(2,128)(2,1)S(1)}, u32[]{:S(2)}, u32[]{:S(2)}) collective-permute-start(bf16[2,3,4096]{2,0,1:T(2,128)(2,1)S(1)} %get-tuple-element.14), channel_id=1, source_target_pairs={{0,1},{1,2},{2,3},{3,4},{4,5},{5,6},{6,7},{7,8},{8,9},{9,10},{10,1... | collective-permute-start | bytes 147464 | tf_op jit(solution)/shard_map/ppermute | solution.py:216
  16.5 8.0 %collective-permute-start.1 = (f32[16,4096]{1,0:T(8,128)S(1)}, f32[16,4096]{1,0:T(8,128)S(1)}, u32[]{:S(2)}, u32[]{:S(2)}) collective-permute-start(f32[16,4096]{1,0:T(8,128)S(1)} %get-tuple-element.16), channel_id=1, source_target_pairs={{0,1},{1,0},{2,3},{3,2},{4,5},{5,4},{6,7},{7,6},{8,9},{9,8},{10,11... | collective-permute-start | bytes 786440 | tf_op jit(solution)/shard_map/ppermute | solution.py:256
  24.6 8.4 %collective-permute-start.4 = (f32[16,2048]{1,0:T(8,128)S(1)}, f32[16,2048]{1,0:T(8,128)S(1)}, u32[]{:S(2)}, u32[]{:S(2)}) collective-permute-start(f32[16,2048]{1,0:T(8,128)S(1)} %fusion), channel_id=1, source_target_pairs={{0,6},{2,8},{4,10},{6,12},{8,14},{10,16},{12,18},{14,20},{16,22},{... | collective-permute-start | bytes 393224 | tf_op jit(solution)/shard_map/ppermute | solution.py:277
  26.6 8.6 %collective-permute-start.3 = (f32[16,2048]{1,0:T(8,128)S(1)}, f32[16,2048]{1,0:T(8,128)S(1)}, u32[]{:S(2)}, u32[]{:S(2)}) collective-permute-start(f32[16,2048]{1,0:T(8,128)S(1)} %fusion), channel_id=1, source_target_pairs={{0,4},{2,6},{4,8},{6,10},{8,12},{10,14},{12,16},{14,18},{16,20},{1... | collective-permute-start | bytes 393224 | tf_op jit(solution)/shard_map/ppermute | solution.py:277
  30.0 7.2 %collective-permute-start.2 = (f32[16,2048]{1,0:T(8,128)S(1)}, f32[16,2048]{1,0:T(8,128)S(1)}, u32[]{:S(2)}, u32[]{:S(2)}) collective-permute-start(f32[16,2048]{1,0:T(8,128)S(1)} %fusion), channel_id=1, source_target_pairs={{0,2},{2,4},{4,6},{6,8},{8,10},{10,12},{12,14},{14,16},{16,18},{18... | collective-permute-start | bytes 393224 | tf_op jit(solution)/shard_map/ppermute | solution.py:277
  37.3 5.9 %collective-permute-start.8 = (f32[16,2048]{1,0:T(8,128)S(1)}, f32[16,2048]{1,0:T(8,128)S(1)}, u32[]{:S(2)}, u32[]{:S(2)}) collective-permute-start(f32[16,2048]{1,0:T(8,128)S(1)} %fusion.6), channel_id=1, source_target_pairs={{0,24},{2,26},{4,28},{6,30},{1,25},{3,27},{5,29},{7,31}} | collective-permute-start | bytes 393224 | tf_op jit(solution)/shard_map/ppermute | solution.py:277
  38.0 5.3 %collective-permute-start.7 = (f32[16,2048]{1,0:T(8,128)S(1)}, f32[16,2048]{1,0:T(8,128)S(1)}, u32[]{:S(2)}, u32[]{:S(2)}) collective-permute-start(f32[16,2048]{1,0:T(8,128)S(1)} %fusion.6), channel_id=1, source_target_pairs={{0,18},{2,20},{4,22},{6,24},{8,26},{10,28},{12,30},{1,19},{3,21},{... | collective-permute-start | bytes 393224 | tf_op jit(solution)/shard_map/ppermute | solution.py:277
  38.6 10.1 %collective-permute-start.6 = (f32[16,2048]{1,0:T(8,128)S(1)}, f32[16,2048]{1,0:T(8,128)S(1)}, u32[]{:S(2)}, u32[]{:S(2)}) collective-permute-start(f32[16,2048]{1,0:T(8,128)S(1)} %fusion.6), channel_id=1, source_target_pairs={{0,12},{2,14},{4,16},{6,18},{8,20},{10,22},{12,24},{14,26},{16,28}... | collective-permute-start | bytes 393224 | tf_op jit(solution)/shard_map/ppermute | solution.py:277
  41.3 12.4 %collective-permute-start.5 = (f32[16,2048]{1,0:T(8,128)S(1)}, f32[16,2048]{1,0:T(8,128)S(1)}, u32[]{:S(2)}, u32[]{:S(2)}) collective-permute-start(f32[16,2048]{1,0:T(8,128)S(1)} %fusion.6), channel_id=1, source_target_pairs={{0,6},{2,8},{4,10},{6,12},{8,14},{10,16},{12,18},{14,20},{16,22},{... | collective-permute-start | bytes 393224 | tf_op jit(solution)/shard_map/ppermute | solution.py:277
  53.9 5.8 %collective-permute-start.9 = (f32[16,2048]{1,0:T(8,128)S(1)}, f32[16,2048]{1,0:T(8,128)S(1)}, u32[]{:S(2)}, u32[]{:S(2)}) collective-permute-start(f32[16,2048]{1,0:T(8,128)S(1)} %get-tuple-element.10), channel_id=1, source_target_pairs={{0,1},{1,0},{2,3},{3,2},{4,5},{5,4},{6,7},{7,6},{8,9},{9,8},{10,11... | collective-permute-start | bytes 393224 | tf_op jit(solution)/shard_map/ppermute | solution.py:256

commit v20 on v18

--- a/solution.py
+++ b/solution.py
@@ -113,12 +113,14 @@
             rsc[m] = row(r_ref, m, lanes)
             ends = seg_ref[m, :, lanes] + jnp.where(sub == 0, row(fix_ref, m, lanes), 0.0)
             carried = jnp.where(sub >= 1, pltpu.roll(ends, 1, 0), 0.0)
+            factor = jnp.exp(-rate * float(seg))
+            lead = jnp.ones_like(factor)
             offset = 1
             while offset < SUB:
-                factor = jnp.exp(-rate * float(seg * offset))
                 carried = carried + jnp.where(sub >= offset, factor * pltpu.roll(carried, offset, 0), 0.0)
+                lead = jnp.where((sub & offset) != 0, lead * factor, lead)
+                factor = factor * factor
                 offset *= 2
-            lead = jnp.exp(-rate * (sub.astype(jnp.float32) * float(seg)))
             starts.append(carried + lead * row(hin_ref, m, lanes))
         skip_rows = row(skip_ref, 0, lanes)
 

time: 74.8 us -> 74.6 us (level)
  no operation moved by 1% of the time
where the time goes in v20:
time: 74.6 us; the launch traced here: 73.5 us
  waiting for transfers between devices  27.7 us (37%)
  Pallas kernels  20.4 us (27%)
  starting transfers between devices  18.5 us (25%)
  other arithmetic  5.09 us (7%)
  local copies, waits for them, and re-layouts  1.64 us (2%)
    ppermute x7, waiting for transfers between devices, span_shift(): lax.ppermute(value, 'ctx', [(j, j + offset) for j in range(spans - offset)])  14.7 us
    ppermute x7, starting transfers between devices, span_shift(): lax.ppermute(value, 'ctx', [(j, j + offset) for j in range(spans - offset)])  14.3 us
    ppermute x2, waiting for transfers between devices, exchange(): lax.ppermute(value, 'tp', [(q, (q + k) % group) for q in range(group)])  13 us
    pallas_call x1, Pallas kernels, run_out(): pl.pallas_call(out_kernel, grid=(width // BLOCK,), in_specs=[pl.BlockSpec...  12.9 us
    pallas_call x1, Pallas kernels, run_state(): pl.pallas_call(state_kernel, grid=(width // BLOCK,), in_specs=[pl.BlockSp...  7.56 us
    ppermute x1, starting transfers between devices, shift(): return lax.ppermute(value, axes, pairs)  3.43 us
    add x1, other arithmetic, body(): local = local + local_fix  1.84 us
  transfers between devices with their start and end apart: 10, of which 6 were waited for; matrix products, arithmetic and copies ran while one was open for 2% of the time, Pallas kernels for 10%

profile of v20, /device:TPU:16, one launch (start us, length us, event | category | flops | bytes accessed | tf_op | source)
XLA Modules:
  0.0 73.5 jit_solution(16031021524157602692)
XLA Ops:
  0.0 1.1 %slice_convert_fusion = (f32[2,3,4096]{2,0,1:T(2,128)S(1)}, bf16[2,3,4096]{2,0,1:T(2,128)(2,1)S(1)}) fusion(bf16[128,3,4096]{2,0,1:T(8,128)(2,1)} %param.5), kind=kLoop, calls=%fused_computation.28 | loop fusion | flops 24576 | bytes 245760 | tf_op jit(solution)/shard_map/convert_element_type | solution.py:227
  1.1 3.4 %collective-permute-start = (bf16[2,3,4096]{2,0,1:T(2,128)(2,1)S(1)}, bf16[2,3,4096]{2,0,1:T(2,128)(2,1)S(1)}, u32[]{:S(2)}, u32[]{:S(2)}) collective-permute-start(bf16[2,3,4096]{2,0,1:T(2,128)(2,1)S(1)} %get-tuple-element.14), channel_id=1, source_target_pairs={{0,1},{1,2},{2,3},{3,4},{4,5},{5,6},{6,7},{7,8},{8,9},{9,10},{10,1... | collective-permute-start | bytes 147464 | tf_op jit(solution)/shard_map/ppermute | solution.py:218
  4.6 0.9 %fusion.22 = (f32[1,3,4096]{2,1,0:T(4,128)S(1)}, f32[1,3,4096]{2,1,0:T(4,128)S(1)}, f32[1,3,4096]{2,1,0:T(4,128)S(1)}) fusion(f32[3,3,4096]{2,1,0:T(4,128)} %f_ref.3), kind=kLoop, calls=%fused_computation.49 | loop fusion | bytes 294912 | tf_op jit(solution)/shard_map/slice | solution.py:233
  5.5 0.7 broadcast_in_dim.3.halo_ref
  6.2 7.6 %shard_map.55 = (f32[16,8,4096]{2,1,0:T(8,128)}, f32[16,4096]{1,0:T(8,128)}) custom-call(bf16[3,128,4096]{2,1,0:T(8,128)(2,1)} %bitcast.57, f32[3,2,4096]{2,1,0:T(2,128)} %broadcast_in_dim.3.halo_ref, f32[3,3,4096]{2,1,0:T(4,128)} %f_ref.3, f32[16,4096]{1,0:T(8,128)} %bitcast.59), custom_call_target="tpu_custom_call" | custom-call | tf_op jit(solution)/shard_map/pallas_call | solution.py:154
  13.7 0.7 fusion.23
  14.4 0.2 multiply_add_fusion.1
  14.8 1.8 %add_add_fusion = (f32[16,4096]{1,0:T(8,128)S(1)}, f32[16,4096]{1,0:T(8,128)}, f32[16,4096]{1,0:T(8,128)S(1)}) fusion(f32[16,4096]{1,0:T(8,128)} %get-tuple-element.8, f32[4096]{0:T(1024)S(1)} %bitcast.62, f32[4096]{0:T(1024)S(1)} %bitcast.63, f32[4096,16]{0,1:T(8,128)S(1)} %copy-done), kind=kLoop, calls=%fused_computation.1 | loop fusion | flops 786432 | bytes 1343488 | tf_op jit(solution)/shard_map/add | solution.py:250
  16.7 8.0 %collective-permute-done.1 = f32[16,4096]{1,0:T(8,128)S(1)} collective-permute-done((f32[16,4096]{1,0:T(8,128)S(1)}, f32[16,4096]{1,0:T(8,128)S(1)}, u32[]{:S(2)}, u32[]{:S(2)}) %collective-permute-start.1) | collective-permute-done | bytes 262176 | tf_op jit(solution)/shard_map/ppermute | solution.py:258
  24.8 2.1 %collective-permute-start.4 = (f32[16,2048]{1,0:T(8,128)S(1)}, f32[16,2048]{1,0:T(8,128)S(1)}, u32[]{:S(2)}, u32[]{:S(2)}) collective-permute-start(f32[16,2048]{1,0:T(8,128)S(1)} %fusion), channel_id=1, source_target_pairs={{0,6},{2,8},{4,10},{6,12},{8,14},{10,16},{12,18},{14,20},{16,22},{... | collective-permute-start | bytes 393224 | tf_op jit(solution)/shard_map/ppermute | solution.py:279
  26.8 3.3 %collective-permute-start.3 = (f32[16,2048]{1,0:T(8,128)S(1)}, f32[16,2048]{1,0:T(8,128)S(1)}, u32[]{:S(2)}, u32[]{:S(2)}) collective-permute-start(f32[16,2048]{1,0:T(8,128)S(1)} %fusion), channel_id=1, source_target_pairs={{0,4},{2,6},{4,8},{6,10},{8,12},{10,14},{12,16},{14,18},{16,20},{1... | collective-permute-start | bytes 393224 | tf_op jit(solution)/shard_map/ppermute | solution.py:279
  30.2 3.0 %collective-permute-start.2 = (f32[16,2048]{1,0:T(8,128)S(1)}, f32[16,2048]{1,0:T(8,128)S(1)}, u32[]{:S(2)}, u32[]{:S(2)}) collective-permute-start(f32[16,2048]{1,0:T(8,128)S(1)} %fusion), channel_id=1, source_target_pairs={{0,2},{2,4},{4,6},{6,8},{8,10},{10,12},{12,14},{14,16},{16,18},{18... | collective-permute-start | bytes 393224 | tf_op jit(solution)/shard_map/ppermute | solution.py:279
  33.2 2.3 %collective-permute-done.3 = f32[16,2048]{1,0:T(8,128)S(1)} collective-permute-done((f32[16,2048]{1,0:T(8,128)S(1)}, f32[16,2048]{1,0:T(8,128)S(1)}, u32[]{:S(2)}, u32[]{:S(2)}) %collective-permute-start.3) | collective-permute-done | bytes 131104 | tf_op jit(solution)/shard_map/ppermute | solution.py:279
  35.5 1.9 %collective-permute-done.2 = f32[16,2048]{1,0:T(8,128)S(1)} collective-permute-done((f32[16,2048]{1,0:T(8,128)S(1)}, f32[16,2048]{1,0:T(8,128)S(1)}, u32[]{:S(2)}, u32[]{:S(2)}) %collective-permute-start.2) | collective-permute-done | bytes 131104 | tf_op jit(solution)/shard_map/ppermute | solution.py:279
  37.5 0.7 collective-permute-start.8
  38.1 0.7 collective-permute-start.7
  38.8 2.6 %collective-permute-start.6 = (f32[16,2048]{1,0:T(8,128)S(1)}, f32[16,2048]{1,0:T(8,128)S(1)}, u32[]{:S(2)}, u32[]{:S(2)}) collective-permute-start(f32[16,2048]{1,0:T(8,128)S(1)} %fusion.6), channel_id=1, source_target_pairs={{0,12},{2,14},{4,16},{6,18},{8,20},{10,22},{12,24},{14,26},{16,28}... | collective-permute-start | bytes 393224 | tf_op jit(solution)/shard_map/ppermute | solution.py:279
  41.4 1.9 %collective-permute-start.5 = (f32[16,2048]{1,0:T(8,128)S(1)}, f32[16,2048]{1,0:T(8,128)S(1)}, u32[]{:S(2)}, u32[]{:S(2)}) collective-permute-start(f32[16,2048]{1,0:T(8,128)S(1)} %fusion.6), channel_id=1, source_target_pairs={{0,6},{2,8},{4,10},{6,12},{8,14},{10,16},{12,18},{14,20},{16,22},{... | collective-permute-start | bytes 393224 | tf_op jit(solution)/shard_map/ppermute | solution.py:279
  43.4 5.5 %collective-permute-done.6 = f32[16,2048]{1,0:T(8,128)S(1)} collective-permute-done((f32[16,2048]{1,0:T(8,128)S(1)}, f32[16,2048]{1,0:T(8,128)S(1)}, u32[]{:S(2)}, u32[]{:S(2)}) %collective-permute-start.6) | collective-permute-done | bytes 131104 | tf_op jit(solution)/shard_map/ppermute | solution.py:279
  48.9 5.0 %collective-permute-done.5 = f32[16,2048]{1,0:T(8,128)S(1)} collective-permute-done((f32[16,2048]{1,0:T(8,128)S(1)}, f32[16,2048]{1,0:T(8,128)S(1)}, u32[]{:S(2)}, u32[]{:S(2)}) %collective-permute-start.5) | collective-permute-done | bytes 131104 | tf_op jit(solution)/shard_map/ppermute | solution.py:279
  54.0 0.8 %collective-permute-start.9 = (f32[16,2048]{1,0:T(8,128)S(1)}, f32[16,2048]{1,0:T(8,128)S(1)}, u32[]{:S(2)}, u32[]{:S(2)}) collective-permute-start(f32[16,2048]{1,0:T(8,128)S(1)} %get-tuple-element.10), channel_id=1, source_target_pairs={{0,1},{1,0},{2,3},{3,2},{4,5},{5,4},{6,7},{7,6},{8,9},{9,8},{10,11... | collective-permute-start | bytes 393224 | tf_op jit(solution)/shard_map/ppermute | solution.py:258
  54.8 5.0 %collective-permute-done.9 = f32[16,2048]{1,0:T(8,128)S(1)} collective-permute-done((f32[16,2048]{1,0:T(8,128)S(1)}, f32[16,2048]{1,0:T(8,128)S(1)}, u32[]{:S(2)}, u32[]{:S(2)}) %collective-permute-start.9) | collective-permute-done | bytes 131104 | tf_op jit(solution)/shard_map/ppermute | solution.py:258
  59.8 0.8 %select_add_fusion.hin_ref = f32[16,4096]{1,0:T(8,128)} fusion(f32[16,4096]{1,0:T(8,128)S(1)} %collective-permute-done.1, f32[16,4096]{1,0:T(8,128)S(1)} %constant_dynamic-update-slice_fusion, f32[]{:T(128)S(6)} %mul.259, pred[]{:T(512)S(6)} %ge.3, f32[4096,16]{0,1:T(8,128)S(1)} %copy-done), kind=kLoop, calls=%fused_computation | loop fusion | flops 458752 | bytes 1048581 | tf_op jit(solution)/shard_map/add | solution.py:305
  60.6 12.9 %shard_map.56 = bf16[128,4096]{1,0:T(8,128)(2,1)} custom-call(bf16[3,128,4096]{2,1,0:T(8,128)(2,1)} %bitcast.58, f32[3,2,4096]{2,1,0:T(2,128)} %get-tuple-element.24.halo_ref, f32[3,3,4096]{2,1,0:T(4,128)} %f_ref.3, f32[16,4096]{1,0:T(8,128)} %bitcast.60, f32[16,4096]{1,0:T(8,128)} %bitcast.61, f32[1,4096]{1,0:T(1,128)} %bitcast.64, ...), custom_call_target="tpu_custom_call" | custom-call | tf_op jit(solution)/shard_map/pallas_call | solution.py:183
  (14 shorter events, 0.4 us)
Async XLA Ops:
  0.0 14.8 %copy-start = (f32[4096,16]{0,1:T(8,128)S(1)}, f32[4096,16]{0,1:T(8,128)}, u32[]{:S(2)}) copy-start(f32[4096,16]{0,1:T(8,128)} %param.8) | copy-start | bytes 786436
  1.1 12.6 %collective-permute-start = (bf16[2,3,4096]{2,0,1:T(2,128)(2,1)S(1)}, bf16[2,3,4096]{2,0,1:T(2,128)(2,1)S(1)}, u32[]{:S(2)}, u32[]{:S(2)}) collective-permute-start(bf16[2,3,4096]{2,0,1:T(2,128)(2,1)S(1)} %get-tuple-element.14), channel_id=1, source_target_pairs={{0,1},{1,2},{2,3},{3,4},{4,5},{5,6},{6,7},{7,8},{8,9},{9,10},{10,1... | collective-permute-start | bytes 147464 | tf_op jit(solution)/shard_map/ppermute | solution.py:218
  16.7 8.0 %collective-permute-start.1 = (f32[16,4096]{1,0:T(8,128)S(1)}, f32[16,4096]{1,0:T(8,128)S(1)}, u32[]{:S(2)}, u32[]{:S(2)}) collective-permute-start(f32[16,4096]{1,0:T(8,128)S(1)} %get-tuple-element.16), channel_id=1, source_target_pairs={{0,1},{1,0},{2,3},{3,2},{4,5},{5,4},{6,7},{7,6},{8,9},{9,8},{10,11... | collective-permute-start | bytes 786440 | tf_op jit(solution)/shard_map/ppermute | solution.py:258
  24.8 8.4 %collective-permute-start.4 = (f32[16,2048]{1,0:T(8,128)S(1)}, f32[16,2048]{1,0:T(8,128)S(1)}, u32[]{:S(2)}, u32[]{:S(2)}) collective-permute-start(f32[16,2048]{1,0:T(8,128)S(1)} %fusion), channel_id=1, source_target_pairs={{0,6},{2,8},{4,10},{6,12},{8,14},{10,16},{12,18},{14,20},{16,22},{... | collective-permute-start | bytes 393224 | tf_op jit(solution)/shard_map/ppermute | solution.py:279
  26.8 8.6 %collective-permute-start.3 = (f32[16,2048]{1,0:T(8,128)S(1)}, f32[16,2048]{1,0:T(8,128)S(1)}, u32[]{:S(2)}, u32[]{:S(2)}) collective-permute-start(f32[16,2048]{1,0:T(8,128)S(1)} %fusion), channel_id=1, source_target_pairs={{0,4},{2,6},{4,8},{6,10},{8,12},{10,14},{12,16},{14,18},{16,20},{1... | collective-permute-start | bytes 393224 | tf_op jit(solution)/shard_map/ppermute | solution.py:279
  30.2 7.2 %collective-permute-start.2 = (f32[16,2048]{1,0:T(8,128)S(1)}, f32[16,2048]{1,0:T(8,128)S(1)}, u32[]{:S(2)}, u32[]{:S(2)}) collective-permute-start(f32[16,2048]{1,0:T(8,128)S(1)} %fusion), channel_id=1, source_target_pairs={{0,2},{2,4},{4,6},{6,8},{8,10},{10,12},{12,14},{14,16},{16,18},{18... | collective-permute-start | bytes 393224 | tf_op jit(solution)/shard_map/ppermute | solution.py:279
  37.5 5.9 %collective-permute-start.8 = (f32[16,2048]{1,0:T(8,128)S(1)}, f32[16,2048]{1,0:T(8,128)S(1)}, u32[]{:S(2)}, u32[]{:S(2)}) collective-permute-start(f32[16,2048]{1,0:T(8,128)S(1)} %fusion.6), channel_id=1, source_target_pairs={{0,24},{2,26},{4,28},{6,30},{1,25},{3,27},{5,29},{7,31}} | collective-permute-start | bytes 393224 | tf_op jit(solution)/shard_map/ppermute | solution.py:279
  38.1 5.3 %collective-permute-start.7 = (f32[16,2048]{1,0:T(8,128)S(1)}, f32[16,2048]{1,0:T(8,128)S(1)}, u32[]{:S(2)}, u32[]{:S(2)}) collective-permute-start(f32[16,2048]{1,0:T(8,128)S(1)} %fusion.6), channel_id=1, source_target_pairs={{0,18},{2,20},{4,22},{6,24},{8,26},{10,28},{12,30},{1,19},{3,21},{... | collective-permute-start | bytes 393224 | tf_op jit(solution)/shard_map/ppermute | solution.py:279
  38.8 10.1 %collective-permute-start.6 = (f32[16,2048]{1,0:T(8,128)S(1)}, f32[16,2048]{1,0:T(8,128)S(1)}, u32[]{:S(2)}, u32[]{:S(2)}) collective-permute-start(f32[16,2048]{1,0:T(8,128)S(1)} %fusion.6), channel_id=1, source_target_pairs={{0,12},{2,14},{4,16},{6,18},{8,20},{10,22},{12,24},{14,26},{16,28}... | collective-permute-start | bytes 393224 | tf_op jit(solution)/shard_map/ppermute | solution.py:279
  41.4 12.4 %collective-permute-start.5 = (f32[16,2048]{1,0:T(8,128)S(1)}, f32[16,2048]{1,0:T(8,128)S(1)}, u32[]{:S(2)}, u32[]{:S(2)}) collective-permute-start(f32[16,2048]{1,0:T(8,128)S(1)} %fusion.6), channel_id=1, source_target_pairs={{0,6},{2,8},{4,10},{6,12},{8,14},{10,16},{12,18},{14,20},{16,22},{... | collective-permute-start | bytes 393224 | tf_op jit(solution)/shard_map/ppermute | solution.py:279
  54.0 5.8 %collective-permute-start.9 = (f32[16,2048]{1,0:T(8,128)S(1)}, f32[16,2048]{1,0:T(8,128)S(1)}, u32[]{:S(2)}, u32[]{:S(2)}) collective-permute-start(f32[16,2048]{1,0:T(8,128)S(1)} %get-tuple-element.10), channel_id=1, source_target_pairs={{0,1},{1,0},{2,3},{3,2},{4,5},{5,4},{6,7},{7,6},{8,9},{9,8},{10,11... | collective-permute-start | bytes 393224 | tf_op jit(solution)/shard_map/ppermute | solution.py:258

commit v21 on v20

--- a/solution.py
+++ b/solution.py
@@ -82,14 +82,20 @@
         zero = jnp.zeros((SUB, LANES), jnp.float32)
         init = (first_prev(xs, halo_ref, c, lanes, seg, taps, sub), (zero,) * modes)
         _, states = lax.fori_loop(0, seg, step, init, unroll=UNROLL)
-        later = (SUB - 1 - sub).astype(jnp.float32) * float(seg)
+        later = SUB - 1 - sub
         for m in range(modes):
             seg_ref[m, :, lanes] = states[m]
-            weight = jnp.exp(-row(a_ref, m, lanes) * later)
+            factor = jnp.exp(-row(a_ref, m, lanes) * float(seg))
+            weight = jnp.ones_like(factor)
+            bit = 1
+            while bit < SUB:
+                weight = jnp.where((later & bit) != 0, weight * factor, weight)
+                factor = factor * factor
+                bit *= 2
             h_ref[pl.ds(m, 1), lanes] = jnp.sum(weight * states[m], axis=0, keepdims=True)
         return carry
 
-    lax.fori_loop(0, block // LANES, lane_group, 0)
+    lax.fori_loop(0, block // LANES, lane_group, 0, unroll=2)
 
 
 def out_kernel(
@@ -142,7 +148,7 @@
         lax.fori_loop(0, seg, step, init, unroll=UNROLL)
         return carry
 
-    lax.fori_loop(0, block // LANES, lane_group, 0)
+    lax.fori_loop(0, block // LANES, lane_group, 0, unroll=2)
     for c in range(block // LANES):
         o_ref[:, c * LANES : (c + 1) * LANES] = ys[c].astype(o_ref.dtype)
 

time: 74.6 us -> 74.7 us (level)
  transfers between devices with their start and end apart: 10 -> 10, of which waited for: 6 -> 6; matrix products, arithmetic and copies ran while one was open for 2% -> 2% of each run, Pallas kernels for 10% -> 11%
where the time goes in v21:
time: 74.7 us; the launch traced here: 73.6 us
  waiting for transfers between devices  27.7 us (37%)
  Pallas kernels  20.6 us (28%)
  starting transfers between devices  18.5 us (25%)
  other arithmetic  5.09 us (7%)
  local copies, waits for them, and re-layouts  1.64 us (2%)
    ppermute x7, waiting for transfers between devices, span_shift(): lax.ppermute(value, 'ctx', [(j, j + offset) for j in range(spans - offset)])  14.7 us
    ppermute x7, starting transfers between devices, span_shift(): lax.ppermute(value, 'ctx', [(j, j + offset) for j in range(spans - offset)])  14.3 us
    ppermute x2, waiting for transfers between devices, exchange(): lax.ppermute(value, 'tp', [(q, (q + k) % group) for q in range(group)])  13 us
    pallas_call x1, Pallas kernels, run_out(): pl.pallas_call(out_kernel, grid=(width // BLOCK,), in_specs=[pl.BlockSpec...  12.8 us
    pallas_call x1, Pallas kernels, run_state(): pl.pallas_call(state_kernel, grid=(width // BLOCK,), in_specs=[pl.BlockSp...  7.82 us
    ppermute x1, starting transfers between devices, shift(): return lax.ppermute(value, axes, pairs)  3.43 us
    add x1, other arithmetic, body(): local = local + local_fix  1.84 us
  transfers between devices with their start and end apart: 10, of which 6 were waited for; matrix products, arithmetic and copies ran while one was open for 2% of the time, Pallas kernels for 11%

profile of v21, /device:TPU:16, one launch (start us, length us, event | category | flops | bytes accessed | tf_op | source)
XLA Modules:
  0.0 73.6 jit_solution(8632453353066367708)
XLA Ops:
  0.0 1.1 %slice_convert_fusion = (f32[2,3,4096]{2,0,1:T(2,128)S(1)}, bf16[2,3,4096]{2,0,1:T(2,128)(2,1)S(1)}) fusion(bf16[128,3,4096]{2,0,1:T(8,128)(2,1)} %param.5), kind=kLoop, calls=%fused_computation.28 | loop fusion | flops 24576 | bytes 245760 | tf_op jit(solution)/shard_map/convert_element_type | solution.py:233
  1.1 3.4 %collective-permute-start = (bf16[2,3,4096]{2,0,1:T(2,128)(2,1)S(1)}, bf16[2,3,4096]{2,0,1:T(2,128)(2,1)S(1)}, u32[]{:S(2)}, u32[]{:S(2)}) collective-permute-start(bf16[2,3,4096]{2,0,1:T(2,128)(2,1)S(1)} %get-tuple-element.14), channel_id=1, source_target_pairs={{0,1},{1,2},{2,3},{3,4},{4,5},{5,6},{6,7},{7,8},{8,9},{9,10},{10,1... | collective-permute-start | bytes 147464 | tf_op jit(solution)/shard_map/ppermute | solution.py:224
  4.6 0.9 %fusion.22 = (f32[1,3,4096]{2,1,0:T(4,128)S(1)}, f32[1,3,4096]{2,1,0:T(4,128)S(1)}, f32[1,3,4096]{2,1,0:T(4,128)S(1)}) fusion(f32[3,3,4096]{2,1,0:T(4,128)} %f_ref.3), kind=kLoop, calls=%fused_computation.49 | loop fusion | bytes 294912 | tf_op jit(solution)/shard_map/slice | solution.py:239
  5.5 0.7 broadcast_in_dim.3.halo_ref
  6.2 7.8 %shard_map.55 = (f32[16,8,4096]{2,1,0:T(8,128)}, f32[16,4096]{1,0:T(8,128)}) custom-call(bf16[3,128,4096]{2,1,0:T(8,128)(2,1)} %bitcast.57, f32[3,2,4096]{2,1,0:T(2,128)} %broadcast_in_dim.3.halo_ref, f32[3,3,4096]{2,1,0:T(4,128)} %f_ref.3, f32[16,4096]{1,0:T(8,128)} %bitcast.59), custom_call_target="tpu_custom_call" | custom-call | tf_op jit(solution)/shard_map/pallas_call | solution.py:160
  14.0 0.7 fusion.23
  14.7 0.2 multiply_add_fusion.1
  15.1 1.8 %add_add_fusion = (f32[16,4096]{1,0:T(8,128)S(1)}, f32[16,4096]{1,0:T(8,128)}, f32[16,4096]{1,0:T(8,128)S(1)}) fusion(f32[16,4096]{1,0:T(8,128)} %get-tuple-element.8, f32[4096]{0:T(1024)S(1)} %bitcast.62, f32[4096]{0:T(1024)S(1)} %bitcast.63, f32[4096,16]{0,1:T(8,128)S(1)} %copy-done), kind=kLoop, calls=%fused_computation.1 | loop fusion | flops 786432 | bytes 1343488 | tf_op jit(solution)/shard_map/add | solution.py:256
  17.0 8.0 %collective-permute-done.1 = f32[16,4096]{1,0:T(8,128)S(1)} collective-permute-done((f32[16,4096]{1,0:T(8,128)S(1)}, f32[16,4096]{1,0:T(8,128)S(1)}, u32[]{:S(2)}, u32[]{:S(2)}) %collective-permute-start.1) | collective-permute-done | bytes 262176 | tf_op jit(solution)/shard_map/ppermute | solution.py:264
  25.0 2.1 %collective-permute-start.4 = (f32[16,2048]{1,0:T(8,128)S(1)}, f32[16,2048]{1,0:T(8,128)S(1)}, u32[]{:S(2)}, u32[]{:S(2)}) collective-permute-start(f32[16,2048]{1,0:T(8,128)S(1)} %fusion), channel_id=1, source_target_pairs={{0,6},{2,8},{4,10},{6,12},{8,14},{10,16},{12,18},{14,20},{16,22},{... | collective-permute-start | bytes 393224 | tf_op jit(solution)/shard_map/ppermute | solution.py:285
  27.1 3.3 %collective-permute-start.3 = (f32[16,2048]{1,0:T(8,128)S(1)}, f32[16,2048]{1,0:T(8,128)S(1)}, u32[]{:S(2)}, u32[]{:S(2)}) collective-permute-start(f32[16,2048]{1,0:T(8,128)S(1)} %fusion), channel_id=1, source_target_pairs={{0,4},{2,6},{4,8},{6,10},{8,12},{10,14},{12,16},{14,18},{16,20},{1... | collective-permute-start | bytes 393224 | tf_op jit(solution)/shard_map/ppermute | solution.py:285
  30.4 3.0 %collective-permute-start.2 = (f32[16,2048]{1,0:T(8,128)S(1)}, f32[16,2048]{1,0:T(8,128)S(1)}, u32[]{:S(2)}, u32[]{:S(2)}) collective-permute-start(f32[16,2048]{1,0:T(8,128)S(1)} %fusion), channel_id=1, source_target_pairs={{0,2},{2,4},{4,6},{6,8},{8,10},{10,12},{12,14},{14,16},{16,18},{18... | collective-permute-start | bytes 393224 | tf_op jit(solution)/shard_map/ppermute | solution.py:285
  33.4 2.3 %collective-permute-done.3 = f32[16,2048]{1,0:T(8,128)S(1)} collective-permute-done((f32[16,2048]{1,0:T(8,128)S(1)}, f32[16,2048]{1,0:T(8,128)S(1)}, u32[]{:S(2)}, u32[]{:S(2)}) %collective-permute-start.3) | collective-permute-done | bytes 131104 | tf_op jit(solution)/shard_map/ppermute | solution.py:285
  35.7 1.9 %collective-permute-done.2 = f32[16,2048]{1,0:T(8,128)S(1)} collective-permute-done((f32[16,2048]{1,0:T(8,128)S(1)}, f32[16,2048]{1,0:T(8,128)S(1)}, u32[]{:S(2)}, u32[]{:S(2)}) %collective-permute-start.2) | collective-permute-done | bytes 131104 | tf_op jit(solution)/shard_map/ppermute | solution.py:285
  37.7 0.7 collective-permute-start.8
  38.4 0.7 collective-permute-start.7
  39.1 2.6 %collective-permute-start.6 = (f32[16,2048]{1,0:T(8,128)S(1)}, f32[16,2048]{1,0:T(8,128)S(1)}, u32[]{:S(2)}, u32[]{:S(2)}) collective-permute-start(f32[16,2048]{1,0:T(8,128)S(1)} %fusion.6), channel_id=1, source_target_pairs={{0,12},{2,14},{4,16},{6,18},{8,20},{10,22},{12,24},{14,26},{16,28}... | collective-permute-start | bytes 393224 | tf_op jit(solution)/shard_map/ppermute | solution.py:285
  41.7 1.9 %collective-permute-start.5 = (f32[16,2048]{1,0:T(8,128)S(1)}, f32[16,2048]{1,0:T(8,128)S(1)}, u32[]{:S(2)}, u32[]{:S(2)}) collective-permute-start(f32[16,2048]{1,0:T(8,128)S(1)} %fusion.6), channel_id=1, source_target_pairs={{0,6},{2,8},{4,10},{6,12},{8,14},{10,16},{12,18},{14,20},{16,22},{... | collective-permute-start | bytes 393224 | tf_op jit(solution)/shard_map/ppermute | solution.py:285
  43.7 5.5 %collective-permute-done.6 = f32[16,2048]{1,0:T(8,128)S(1)} collective-permute-done((f32[16,2048]{1,0:T(8,128)S(1)}, f32[16,2048]{1,0:T(8,128)S(1)}, u32[]{:S(2)}, u32[]{:S(2)}) %collective-permute-start.6) | collective-permute-done | bytes 131104 | tf_op jit(solution)/shard_map/ppermute | solution.py:285
  49.1 5.0 %collective-permute-done.5 = f32[16,2048]{1,0:T(8,128)S(1)} collective-permute-done((f32[16,2048]{1,0:T(8,128)S(1)}, f32[16,2048]{1,0:T(8,128)S(1)}, u32[]{:S(2)}, u32[]{:S(2)}) %collective-permute-start.5) | collective-permute-done | bytes 131104 | tf_op jit(solution)/shard_map/ppermute | solution.py:285
  54.3 0.8 %collective-permute-start.9 = (f32[16,2048]{1,0:T(8,128)S(1)}, f32[16,2048]{1,0:T(8,128)S(1)}, u32[]{:S(2)}, u32[]{:S(2)}) collective-permute-start(f32[16,2048]{1,0:T(8,128)S(1)} %get-tuple-element.10), channel_id=1, source_target_pairs={{0,1},{1,0},{2,3},{3,2},{4,5},{5,4},{6,7},{7,6},{8,9},{9,8},{10,11... | collective-permute-start | bytes 393224 | tf_op jit(solution)/shard_map/ppermute | solution.py:264
  55.1 5.0 %collective-permute-done.9 = f32[16,2048]{1,0:T(8,128)S(1)} collective-permute-done((f32[16,2048]{1,0:T(8,128)S(1)}, f32[16,2048]{1,0:T(8,128)S(1)}, u32[]{:S(2)}, u32[]{:S(2)}) %collective-permute-start.9) | collective-permute-done | bytes 131104 | tf_op jit(solution)/shard_map/ppermute | solution.py:264
  60.1 0.8 %select_add_fusion.hin_ref = f32[16,4096]{1,0:T(8,128)} fusion(f32[16,4096]{1,0:T(8,128)S(1)} %collective-permute-done.1, f32[16,4096]{1,0:T(8,128)S(1)} %constant_dynamic-update-slice_fusion, f32[]{:T(128)S(6)} %mul.259, pred[]{:T(512)S(6)} %ge.3, f32[4096,16]{0,1:T(8,128)S(1)} %copy-done), kind=kLoop, calls=%fused_computation | loop fusion | flops 458752 | bytes 1048581 | tf_op jit(solution)/shard_map/add | solution.py:311
  60.9 12.8 %shard_map.56 = bf16[128,4096]{1,0:T(8,128)(2,1)} custom-call(bf16[3,128,4096]{2,1,0:T(8,128)(2,1)} %bitcast.58, f32[3,2,4096]{2,1,0:T(2,128)} %get-tuple-element.24.halo_ref, f32[3,3,4096]{2,1,0:T(4,128)} %f_ref.3, f32[16,4096]{1,0:T(8,128)} %bitcast.60, f32[16,4096]{1,0:T(8,128)} %bitcast.61, f32[1,4096]{1,0:T(1,128)} %bitcast.64, ...), custom_call_target="tpu_custom_call" | custom-call | tf_op jit(solution)/shard_map/pallas_call | solution.py:189
  (14 shorter events, 0.4 us)
Async XLA Ops:
  0.0 15.1 %copy-start = (f32[4096,16]{0,1:T(8,128)S(1)}, f32[4096,16]{0,1:T(8,128)}, u32[]{:S(2)}) copy-start(f32[4096,16]{0,1:T(8,128)} %param.8) | copy-start | bytes 786436
  1.1 12.9 %collective-permute-start = (bf16[2,3,4096]{2,0,1:T(2,128)(2,1)S(1)}, bf16[2,3,4096]{2,0,1:T(2,128)(2,1)S(1)}, u32[]{:S(2)}, u32[]{:S(2)}) collective-permute-start(bf16[2,3,4096]{2,0,1:T(2,128)(2,1)S(1)} %get-tuple-element.14), channel_id=1, source_target_pairs={{0,1},{1,2},{2,3},{3,4},{4,5},{5,6},{6,7},{7,8},{8,9},{9,10},{10,1... | collective-permute-start | bytes 147464 | tf_op jit(solution)/shard_map/ppermute | solution.py:224
  17.0 8.0 %collective-permute-start.1 = (f32[16,4096]{1,0:T(8,128)S(1)}, f32[16,4096]{1,0:T(8,128)S(1)}, u32[]{:S(2)}, u32[]{:S(2)}) collective-permute-start(f32[16,4096]{1,0:T(8,128)S(1)} %get-tuple-element.16), channel_id=1, source_target_pairs={{0,1},{1,0},{2,3},{3,2},{4,5},{5,4},{6,7},{7,6},{8,9},{9,8},{10,11... | collective-permute-start | bytes 786440 | tf_op jit(solution)/shard_map/ppermute | solution.py:264
  25.0 8.4 %collective-permute-start.4 = (f32[16,2048]{1,0:T(8,128)S(1)}, f32[16,2048]{1,0:T(8,128)S(1)}, u32[]{:S(2)}, u32[]{:S(2)}) collective-permute-start(f32[16,2048]{1,0:T(8,128)S(1)} %fusion), channel_id=1, source_target_pairs={{0,6},{2,8},{4,10},{6,12},{8,14},{10,16},{12,18},{14,20},{16,22},{... | collective-permute-start | bytes 393224 | tf_op jit(solution)/shard_map/ppermute | solution.py:285
  27.1 8.6 %collective-permute-start.3 = (f32[16,2048]{1,0:T(8,128)S(1)}, f32[16,2048]{1,0:T(8,128)S(1)}, u32[]{:S(2)}, u32[]{:S(2)}) collective-permute-start(f32[16,2048]{1,0:T(8,128)S(1)} %fusion), channel_id=1, source_target_pairs={{0,4},{2,6},{4,8},{6,10},{8,12},{10,14},{12,16},{14,18},{16,20},{1... | collective-permute-start | bytes 393224 | tf_op jit(solution)/shard_map/ppermute | solution.py:285
  30.4 7.2 %collective-permute-start.2 = (f32[16,2048]{1,0:T(8,128)S(1)}, f32[16,2048]{1,0:T(8,128)S(1)}, u32[]{:S(2)}, u32[]{:S(2)}) collective-permute-start(f32[16,2048]{1,0:T(8,128)S(1)} %fusion), channel_id=1, source_target_pairs={{0,2},{2,4},{4,6},{6,8},{8,10},{10,12},{12,14},{14,16},{16,18},{18... | collective-permute-start | bytes 393224 | tf_op jit(solution)/shard_map/ppermute | solution.py:285
  37.7 5.9 %collective-permute-start.8 = (f32[16,2048]{1,0:T(8,128)S(1)}, f32[16,2048]{1,0:T(8,128)S(1)}, u32[]{:S(2)}, u32[]{:S(2)}) collective-permute-start(f32[16,2048]{1,0:T(8,128)S(1)} %fusion.6), channel_id=1, source_target_pairs={{0,24},{2,26},{4,28},{6,30},{1,25},{3,27},{5,29},{7,31}} | collective-permute-start | bytes 393224 | tf_op jit(solution)/shard_map/ppermute | solution.py:285
  38.4 5.3 %collective-permute-start.7 = (f32[16,2048]{1,0:T(8,128)S(1)}, f32[16,2048]{1,0:T(8,128)S(1)}, u32[]{:S(2)}, u32[]{:S(2)}) collective-permute-start(f32[16,2048]{1,0:T(8,128)S(1)} %fusion.6), channel_id=1, source_target_pairs={{0,18},{2,20},{4,22},{6,24},{8,26},{10,28},{12,30},{1,19},{3,21},{... | collective-permute-start | bytes 393224 | tf_op jit(solution)/shard_map/ppermute | solution.py:285
  39.1 10.1 %collective-permute-start.6 = (f32[16,2048]{1,0:T(8,128)S(1)}, f32[16,2048]{1,0:T(8,128)S(1)}, u32[]{:S(2)}, u32[]{:S(2)}) collective-permute-start(f32[16,2048]{1,0:T(8,128)S(1)} %fusion.6), channel_id=1, source_target_pairs={{0,12},{2,14},{4,16},{6,18},{8,20},{10,22},{12,24},{14,26},{16,28}... | collective-permute-start | bytes 393224 | tf_op jit(solution)/shard_map/ppermute | solution.py:285
  41.7 12.4 %collective-permute-start.5 = (f32[16,2048]{1,0:T(8,128)S(1)}, f32[16,2048]{1,0:T(8,128)S(1)}, u32[]{:S(2)}, u32[]{:S(2)}) collective-permute-start(f32[16,2048]{1,0:T(8,128)S(1)} %fusion.6), channel_id=1, source_target_pairs={{0,6},{2,8},{4,10},{6,12},{8,14},{10,16},{12,18},{14,20},{16,22},{... | collective-permute-start | bytes 393224 | tf_op jit(solution)/shard_map/ppermute | solution.py:285
  54.3 5.8 %collective-permute-start.9 = (f32[16,2048]{1,0:T(8,128)S(1)}, f32[16,2048]{1,0:T(8,128)S(1)}, u32[]{:S(2)}, u32[]{:S(2)}) collective-permute-start(f32[16,2048]{1,0:T(8,128)S(1)} %get-tuple-element.10), channel_id=1, source_target_pairs={{0,1},{1,0},{2,3},{3,2},{4,5},{5,4},{6,7},{7,6},{8,9},{9,8},{10,11... | collective-permute-start | bytes 393224 | tf_op jit(solution)/shard_map/ppermute | solution.py:264

commit v22 on v19

--- a/solution.py
+++ b/solution.py
@@ -7,7 +7,7 @@
 
 LANES = 128
 SUB = 8
-BLOCK = 1024
+BLOCK = 512
 FIRST_WINDOW = 3
 LATER_WINDOW = 4
 UNROLL = 16

time: 74.5 us -> 75.7 us (1.016)
  Pallas kernels: 20.4 us -> 21.5 us
    pallas_call x1, Pallas kernels: 7.39 us -> 8.6 us  [run_state(): pl.pallas_call(state_kernel, grid=(width // BLOCK,), in_specs=[pl.BlockSp...]
  transfers between devices with their start and end apart: 10 -> 10, of which waited for: 6 -> 6; matrix products, arithmetic and copies ran while one was open for 2% -> 2% of each run, Pallas kernels for 10% -> 12%
where the time goes in v22:
time: 75.7 us; the launch traced here: 74.5 us
  waiting for transfers between devices  27.7 us (37%)
  Pallas kernels  21.5 us (28%)
  starting transfers between devices  18.5 us (24%)
  other arithmetic  5.09 us (7%)
  local copies, waits for them, and re-layouts  1.64 us (2%)
    ppermute x7, waiting for transfers between devices, span_shift(): lax.ppermute(value, 'ctx', [(j, j + offset) for j in range(spans - offset)])  14.7 us
    ppermute x7, starting transfers between devices, span_shift(): lax.ppermute(value, 'ctx', [(j, j + offset) for j in range(spans - offset)])  14.3 us
    ppermute x2, waiting for transfers between devices, exchange(): lax.ppermute(value, 'tp', [(q, (q + k) % group) for q in range(group)])  13 us
    pallas_call x1, Pallas kernels, run_out(): pl.pallas_call(out_kernel, grid=(width // BLOCK,), in_specs=[pl.BlockSpec...  12.9 us
    pallas_call x1, Pallas kernels, run_state(): pl.pallas_call(state_kernel, grid=(width // BLOCK,), in_specs=[pl.BlockSp...  8.6 us
    ppermute x1, starting transfers between devices, shift(): return lax.ppermute(value, axes, pairs)  3.43 us
    add x1, other arithmetic, body(): local = local + local_fix  1.84 us
  transfers between devices with their start and end apart: 10, of which 6 were waited for; matrix products, arithmetic and copies ran while one was open for 2% of the time, Pallas kernels for 12%

profile of v22, /device:TPU:16, one launch (start us, length us, event | category | flops | bytes accessed | tf_op | source)
XLA Modules:
  0.0 74.5 jit_solution(325769310451667595)
XLA Ops:
  0.0 1.1 %slice_convert_fusion = (f32[2,3,4096]{2,0,1:T(2,128)S(1)}, bf16[2,3,4096]{2,0,1:T(2,128)(2,1)S(1)}) fusion(bf16[128,3,4096]{2,0,1:T(8,128)(2,1)} %param.5), kind=kLoop, calls=%fused_computation.28 | loop fusion | flops 24576 | bytes 245760 | tf_op jit(solution)/shard_map/convert_element_type | solution.py:225
  1.1 3.4 %collective-permute-start = (bf16[2,3,4096]{2,0,1:T(2,128)(2,1)S(1)}, bf16[2,3,4096]{2,0,1:T(2,128)(2,1)S(1)}, u32[]{:S(2)}, u32[]{:S(2)}) collective-permute-start(bf16[2,3,4096]{2,0,1:T(2,128)(2,1)S(1)} %get-tuple-element.14), channel_id=1, source_target_pairs={{0,1},{1,2},{2,3},{3,4},{4,5},{5,6},{6,7},{7,8},{8,9},{9,10},{10,1... | collective-permute-start | bytes 147464 | tf_op jit(solution)/shard_map/ppermute | solution.py:216
  4.6 0.9 %fusion.22 = (f32[1,3,4096]{2,1,0:T(4,128)S(1)}, f32[1,3,4096]{2,1,0:T(4,128)S(1)}, f32[1,3,4096]{2,1,0:T(4,128)S(1)}) fusion(f32[3,3,4096]{2,1,0:T(4,128)} %f_ref.3), kind=kLoop, calls=%fused_computation.49 | loop fusion | bytes 294912 | tf_op jit(solution)/shard_map/slice | solution.py:231
  5.5 0.7 broadcast_in_dim.3.halo_ref
  6.2 8.6 %shard_map.55 = (f32[16,8,4096]{2,1,0:T(8,128)}, f32[16,4096]{1,0:T(8,128)}) custom-call(bf16[3,128,4096]{2,1,0:T(8,128)(2,1)} %bitcast.57, f32[3,2,4096]{2,1,0:T(2,128)} %broadcast_in_dim.3.halo_ref, f32[3,3,4096]{2,1,0:T(4,128)} %f_ref.3, f32[16,4096]{1,0:T(8,128)} %bitcast.59), custom_call_target="tpu_custom_call" | custom-call | tf_op jit(solution)/shard_map/pallas_call | solution.py:152
  14.8 0.7 fusion.23
  15.5 0.2 multiply_add_fusion.1
  15.9 1.8 %add_add_fusion = (f32[16,4096]{1,0:T(8,128)S(1)}, f32[16,4096]{1,0:T(8,128)}, f32[16,4096]{1,0:T(8,128)S(1)}) fusion(f32[16,4096]{1,0:T(8,128)} %get-tuple-element.8, f32[4096]{0:T(1024)S(1)} %bitcast.62, f32[4096]{0:T(1024)S(1)} %bitcast.63, f32[4096,16]{0,1:T(8,128)S(1)} %copy-done), kind=kLoop, calls=%fused_computation.1 | loop fusion | flops 786432 | bytes 1343488 | tf_op jit(solution)/shard_map/add | solution.py:248
  17.7 8.0 %collective-permute-done.1 = f32[16,4096]{1,0:T(8,128)S(1)} collective-permute-done((f32[16,4096]{1,0:T(8,128)S(1)}, f32[16,4096]{1,0:T(8,128)S(1)}, u32[]{:S(2)}, u32[]{:S(2)}) %collective-permute-start.1) | collective-permute-done | bytes 262176 | tf_op jit(solution)/shard_map/ppermute | solution.py:256
  25.8 2.1 %collective-permute-start.4 = (f32[16,2048]{1,0:T(8,128)S(1)}, f32[16,2048]{1,0:T(8,128)S(1)}, u32[]{:S(2)}, u32[]{:S(2)}) collective-permute-start(f32[16,2048]{1,0:T(8,128)S(1)} %fusion), channel_id=1, source_target_pairs={{0,6},{2,8},{4,10},{6,12},{8,14},{10,16},{12,18},{14,20},{16,22},{... | collective-permute-start | bytes 393224 | tf_op jit(solution)/shard_map/ppermute | solution.py:277
  27.9 3.3 %collective-permute-start.3 = (f32[16,2048]{1,0:T(8,128)S(1)}, f32[16,2048]{1,0:T(8,128)S(1)}, u32[]{:S(2)}, u32[]{:S(2)}) collective-permute-start(f32[16,2048]{1,0:T(8,128)S(1)} %fusion), channel_id=1, source_target_pairs={{0,4},{2,6},{4,8},{6,10},{8,12},{10,14},{12,16},{14,18},{16,20},{1... | collective-permute-start | bytes 393224 | tf_op jit(solution)/shard_map/ppermute | solution.py:277
  31.2 3.0 %collective-permute-start.2 = (f32[16,2048]{1,0:T(8,128)S(1)}, f32[16,2048]{1,0:T(8,128)S(1)}, u32[]{:S(2)}, u32[]{:S(2)}) collective-permute-start(f32[16,2048]{1,0:T(8,128)S(1)} %fusion), channel_id=1, source_target_pairs={{0,2},{2,4},{4,6},{6,8},{8,10},{10,12},{12,14},{14,16},{16,18},{18... | collective-permute-start | bytes 393224 | tf_op jit(solution)/shard_map/ppermute | solution.py:277
  34.2 2.3 %collective-permute-done.3 = f32[16,2048]{1,0:T(8,128)S(1)} collective-permute-done((f32[16,2048]{1,0:T(8,128)S(1)}, f32[16,2048]{1,0:T(8,128)S(1)}, u32[]{:S(2)}, u32[]{:S(2)}) %collective-permute-start.3) | collective-permute-done | bytes 131104 | tf_op jit(solution)/shard_map/ppermute | solution.py:277
  36.5 1.9 %collective-permute-done.2 = f32[16,2048]{1,0:T(8,128)S(1)} collective-permute-done((f32[16,2048]{1,0:T(8,128)S(1)}, f32[16,2048]{1,0:T(8,128)S(1)}, u32[]{:S(2)}, u32[]{:S(2)}) %collective-permute-start.2) | collective-permute-done | bytes 131104 | tf_op jit(solution)/shard_map/ppermute | solution.py:277
  38.5 0.7 collective-permute-start.8
  39.2 0.7 collective-permute-start.7
  39.9 2.6 %collective-permute-start.6 = (f32[16,2048]{1,0:T(8,128)S(1)}, f32[16,2048]{1,0:T(8,128)S(1)}, u32[]{:S(2)}, u32[]{:S(2)}) collective-permute-start(f32[16,2048]{1,0:T(8,128)S(1)} %fusion.6), channel_id=1, source_target_pairs={{0,12},{2,14},{4,16},{6,18},{8,20},{10,22},{12,24},{14,26},{16,28}... | collective-permute-start | bytes 393224 | tf_op jit(solution)/shard_map/ppermute | solution.py:277
  42.5 1.9 %collective-permute-start.5 = (f32[16,2048]{1,0:T(8,128)S(1)}, f32[16,2048]{1,0:T(8,128)S(1)}, u32[]{:S(2)}, u32[]{:S(2)}) collective-permute-start(f32[16,2048]{1,0:T(8,128)S(1)} %fusion.6), channel_id=1, source_target_pairs={{0,6},{2,8},{4,10},{6,12},{8,14},{10,16},{12,18},{14,20},{16,22},{... | collective-permute-start | bytes 393224 | tf_op jit(solution)/shard_map/ppermute | solution.py:277
  44.5 5.5 %collective-permute-done.6 = f32[16,2048]{1,0:T(8,128)S(1)} collective-permute-done((f32[16,2048]{1,0:T(8,128)S(1)}, f32[16,2048]{1,0:T(8,128)S(1)}, u32[]{:S(2)}, u32[]{:S(2)}) %collective-permute-start.6) | collective-permute-done | bytes 131104 | tf_op jit(solution)/shard_map/ppermute | solution.py:277
  49.9 5.0 %collective-permute-done.5 = f32[16,2048]{1,0:T(8,128)S(1)} collective-permute-done((f32[16,2048]{1,0:T(8,128)S(1)}, f32[16,2048]{1,0:T(8,128)S(1)}, u32[]{:S(2)}, u32[]{:S(2)}) %collective-permute-start.5) | collective-permute-done | bytes 131104 | tf_op jit(solution)/shard_map/ppermute | solution.py:277
  55.1 0.8 %collective-permute-start.9 = (f32[16,2048]{1,0:T(8,128)S(1)}, f32[16,2048]{1,0:T(8,128)S(1)}, u32[]{:S(2)}, u32[]{:S(2)}) collective-permute-start(f32[16,2048]{1,0:T(8,128)S(1)} %get-tuple-element.10), channel_id=1, source_target_pairs={{0,1},{1,0},{2,3},{3,2},{4,5},{5,4},{6,7},{7,6},{8,9},{9,8},{10,11... | collective-permute-start | bytes 393224 | tf_op jit(solution)/shard_map/ppermute | solution.py:256
  55.8 5.0 %collective-permute-done.9 = f32[16,2048]{1,0:T(8,128)S(1)} collective-permute-done((f32[16,2048]{1,0:T(8,128)S(1)}, f32[16,2048]{1,0:T(8,128)S(1)}, u32[]{:S(2)}, u32[]{:S(2)}) %collective-permute-start.9) | collective-permute-done | bytes 131104 | tf_op jit(solution)/shard_map/ppermute | solution.py:256
  60.9 0.8 %select_add_fusion.hin_ref = f32[16,4096]{1,0:T(8,128)} fusion(f32[16,4096]{1,0:T(8,128)S(1)} %collective-permute-done.1, f32[16,4096]{1,0:T(8,128)S(1)} %constant_dynamic-update-slice_fusion, f32[]{:T(128)S(6)} %mul.259, pred[]{:T(512)S(6)} %ge.3, f32[4096,16]{0,1:T(8,128)S(1)} %copy-done), kind=kLoop, calls=%fused_computation | loop fusion | flops 458752 | bytes 1048581 | tf_op jit(solution)/shard_map/add | solution.py:303
  61.7 12.9 %shard_map.56 = bf16[128,4096]{1,0:T(8,128)(2,1)} custom-call(bf16[3,128,4096]{2,1,0:T(8,128)(2,1)} %bitcast.58, f32[3,2,4096]{2,1,0:T(2,128)} %get-tuple-element.24.halo_ref, f32[3,3,4096]{2,1,0:T(4,128)} %f_ref.3, f32[16,4096]{1,0:T(8,128)} %bitcast.60, f32[16,4096]{1,0:T(8,128)} %bitcast.61, f32[1,4096]{1,0:T(1,128)} %bitcast.64, ...), custom_call_target="tpu_custom_call" | custom-call | tf_op jit(solution)/shard_map/pallas_call | solution.py:181
  (14 shorter events, 0.4 us)
Async XLA Ops:
  0.0 15.9 %copy-start = (f32[4096,16]{0,1:T(8,128)S(1)}, f32[4096,16]{0,1:T(8,128)}, u32[]{:S(2)}) copy-start(f32[4096,16]{0,1:T(8,128)} %param.8) | copy-start | bytes 786436
  1.1 13.7 %collective-permute-start = (bf16[2,3,4096]{2,0,1:T(2,128)(2,1)S(1)}, bf16[2,3,4096]{2,0,1:T(2,128)(2,1)S(1)}, u32[]{:S(2)}, u32[]{:S(2)}) collective-permute-start(bf16[2,3,4096]{2,0,1:T(2,128)(2,1)S(1)} %get-tuple-element.14), channel_id=1, source_target_pairs={{0,1},{1,2},{2,3},{3,4},{4,5},{5,6},{6,7},{7,8},{8,9},{9,10},{10,1... | collective-permute-start | bytes 147464 | tf_op jit(solution)/shard_map/ppermute | solution.py:216
  17.7 8.0 %collective-permute-start.1 = (f32[16,4096]{1,0:T(8,128)S(1)}, f32[16,4096]{1,0:T(8,128)S(1)}, u32[]{:S(2)}, u32[]{:S(2)}) collective-permute-start(f32[16,4096]{1,0:T(8,128)S(1)} %get-tuple-element.16), channel_id=1, source_target_pairs={{0,1},{1,0},{2,3},{3,2},{4,5},{5,4},{6,7},{7,6},{8,9},{9,8},{10,11... | collective-permute-start | bytes 786440 | tf_op jit(solution)/shard_map/ppermute | solution.py:256
  25.8 8.4 %collective-permute-start.4 = (f32[16,2048]{1,0:T(8,128)S(1)}, f32[16,2048]{1,0:T(8,128)S(1)}, u32[]{:S(2)}, u32[]{:S(2)}) collective-permute-start(f32[16,2048]{1,0:T(8,128)S(1)} %fusion), channel_id=1, source_target_pairs={{0,6},{2,8},{4,10},{6,12},{8,14},{10,16},{12,18},{14,20},{16,22},{... | collective-permute-start | bytes 393224 | tf_op jit(solution)/shard_map/ppermute | solution.py:277
  27.9 8.6 %collective-permute-start.3 = (f32[16,2048]{1,0:T(8,128)S(1)}, f32[16,2048]{1,0:T(8,128)S(1)}, u32[]{:S(2)}, u32[]{:S(2)}) collective-permute-start(f32[16,2048]{1,0:T(8,128)S(1)} %fusion), channel_id=1, source_target_pairs={{0,4},{2,6},{4,8},{6,10},{8,12},{10,14},{12,16},{14,18},{16,20},{1... | collective-permute-start | bytes 393224 | tf_op jit(solution)/shard_map/ppermute | solution.py:277
  31.2 7.2 %collective-permute-start.2 = (f32[16,2048]{1,0:T(8,128)S(1)}, f32[16,2048]{1,0:T(8,128)S(1)}, u32[]{:S(2)}, u32[]{:S(2)}) collective-permute-start(f32[16,2048]{1,0:T(8,128)S(1)} %fusion), channel_id=1, source_target_pairs={{0,2},{2,4},{4,6},{6,8},{8,10},{10,12},{12,14},{14,16},{16,18},{18... | collective-permute-start | bytes 393224 | tf_op jit(solution)/shard_map/ppermute | solution.py:277
  38.5 5.9 %collective-permute-start.8 = (f32[16,2048]{1,0:T(8,128)S(1)}, f32[16,2048]{1,0:T(8,128)S(1)}, u32[]{:S(2)}, u32[]{:S(2)}) collective-permute-start(f32[16,2048]{1,0:T(8,128)S(1)} %fusion.6), channel_id=1, source_target_pairs={{0,24},{2,26},{4,28},{6,30},{1,25},{3,27},{5,29},{7,31}} | collective-permute-start | bytes 393224 | tf_op jit(solution)/shard_map/ppermute | solution.py:277
  39.2 5.3 %collective-permute-start.7 = (f32[16,2048]{1,0:T(8,128)S(1)}, f32[16,2048]{1,0:T(8,128)S(1)}, u32[]{:S(2)}, u32[]{:S(2)}) collective-permute-start(f32[16,2048]{1,0:T(8,128)S(1)} %fusion.6), channel_id=1, source_target_pairs={{0,18},{2,20},{4,22},{6,24},{8,26},{10,28},{12,30},{1,19},{3,21},{... | collective-permute-start | bytes 393224 | tf_op jit(solution)/shard_map/ppermute | solution.py:277
  39.9 10.1 %collective-permute-start.6 = (f32[16,2048]{1,0:T(8,128)S(1)}, f32[16,2048]{1,0:T(8,128)S(1)}, u32[]{:S(2)}, u32[]{:S(2)}) collective-permute-start(f32[16,2048]{1,0:T(8,128)S(1)} %fusion.6), channel_id=1, source_target_pairs={{0,12},{2,14},{4,16},{6,18},{8,20},{10,22},{12,24},{14,26},{16,28}... | collective-permute-start | bytes 393224 | tf_op jit(solution)/shard_map/ppermute | solution.py:277
  42.5 12.4 %collective-permute-start.5 = (f32[16,2048]{1,0:T(8,128)S(1)}, f32[16,2048]{1,0:T(8,128)S(1)}, u32[]{:S(2)}, u32[]{:S(2)}) collective-permute-start(f32[16,2048]{1,0:T(8,128)S(1)} %fusion.6), channel_id=1, source_target_pairs={{0,6},{2,8},{4,10},{6,12},{8,14},{10,16},{12,18},{14,20},{16,22},{... | collective-permute-start | bytes 393224 | tf_op jit(solution)/shard_map/ppermute | solution.py:277
  55.1 5.8 %collective-permute-start.9 = (f32[16,2048]{1,0:T(8,128)S(1)}, f32[16,2048]{1,0:T(8,128)S(1)}, u32[]{:S(2)}, u32[]{:S(2)}) collective-permute-start(f32[16,2048]{1,0:T(8,128)S(1)} %get-tuple-element.10), channel_id=1, source_target_pairs={{0,1},{1,0},{2,3},{3,2},{4,5},{5,4},{6,7},{7,6},{8,9},{9,8},{10,11... | collective-permute-start | bytes 393224 | tf_op jit(solution)/shard_map/ppermute | solution.py:256

commit v23 on v19

--- a/solution.py
+++ b/solution.py
@@ -8,8 +8,8 @@
 LANES = 128
 SUB = 8
 BLOCK = 1024
-FIRST_WINDOW = 3
-LATER_WINDOW = 4
+FIRST_WINDOW = 5
+LATER_WINDOW = 2
 UNROLL = 16
 
 

time: 74.5 us -> 77 us (1.034)
  the two profiles are of different devices: /device:TPU:16 before, /device:TPU:24 now
where the time goes in v23:
time: 77 us; the launch traced here: 76.5 us
  waiting for transfers between devices  32.7 us (42%)
  Pallas kernels  20.4 us (26%)
  starting transfers between devices  16.6 us (22%)
  other arithmetic  5.09 us (7%)
  local copies, waits for them, and re-layouts  1.64 us (2%)
    ppermute x7, waiting for transfers between devices, span_shift(): lax.ppermute(value, 'ctx', [(j, j + offset) for j in range(spans - offset)])  20.7 us
    pallas_call x1, Pallas kernels, run_out(): pl.pallas_call(out_kernel, grid=(width // BLOCK,), in_specs=[pl.BlockSpec...  13 us
    ppermute x7, starting transfers between devices, span_shift(): lax.ppermute(value, 'ctx', [(j, j + offset) for j in range(spans - offset)])  12.2 us
    ppermute x2, waiting for transfers between devices, exchange(): lax.ppermute(value, 'tp', [(q, (q + k) % group) for q in range(group)])  12 us
    pallas_call x1, Pallas kernels, run_state(): pl.pallas_call(state_kernel, grid=(width // BLOCK,), in_specs=[pl.BlockSp...  7.39 us
    ppermute x1, starting transfers between devices, shift(): return lax.ppermute(value, axes, pairs)  3.43 us
    add x1, other arithmetic, body(): local = local + local_fix  1.84 us
  transfers between devices with their start and end apart: 10, of which 7 were waited for; matrix products, arithmetic and copies ran while one was open for 2% of the time, Pallas kernels for 10%

profile of v23, /device:TPU:24, one launch (start us, length us, event | category | flops | bytes accessed | tf_op | source)
XLA Modules:
  0.0 76.5 jit_solution(2600842387392228889)
XLA Ops:
  0.0 1.1 %slice_convert_fusion = (f32[2,3,4096]{2,0,1:T(2,128)S(1)}, bf16[2,3,4096]{2,0,1:T(2,128)(2,1)S(1)}) fusion(bf16[128,3,4096]{2,0,1:T(8,128)(2,1)} %param.5), kind=kLoop, calls=%fused_computation.28 | loop fusion | flops 24576 | bytes 245760 | tf_op jit(solution)/shard_map/convert_element_type | solution.py:225
  1.1 3.4 %collective-permute-start = (bf16[2,3,4096]{2,0,1:T(2,128)(2,1)S(1)}, bf16[2,3,4096]{2,0,1:T(2,128)(2,1)S(1)}, u32[]{:S(2)}, u32[]{:S(2)}) collective-permute-start(bf16[2,3,4096]{2,0,1:T(2,128)(2,1)S(1)} %get-tuple-element.14), channel_id=1, source_target_pairs={{0,1},{1,2},{2,3},{3,4},{4,5},{5,6},{6,7},{7,8},{8,9},{9,10},{10,1... | collective-permute-start | bytes 147464 | tf_op jit(solution)/shard_map/ppermute | solution.py:216
  4.6 0.9 %fusion.21 = (f32[1,3,4096]{2,1,0:T(4,128)S(1)}, f32[1,3,4096]{2,1,0:T(4,128)S(1)}, f32[1,3,4096]{2,1,0:T(4,128)S(1)}) fusion(f32[3,3,4096]{2,1,0:T(4,128)} %f_ref.3), kind=kLoop, calls=%fused_computation.49 | loop fusion | bytes 294912 | tf_op jit(solution)/shard_map/slice | solution.py:231
  5.5 0.7 broadcast_in_dim.3.halo_ref
  6.2 7.4 %shard_map.55 = (f32[16,8,4096]{2,1,0:T(8,128)}, f32[16,4096]{1,0:T(8,128)}) custom-call(bf16[3,128,4096]{2,1,0:T(8,128)(2,1)} %bitcast.55, f32[3,2,4096]{2,1,0:T(2,128)} %broadcast_in_dim.3.halo_ref, f32[3,3,4096]{2,1,0:T(4,128)} %f_ref.3, f32[16,4096]{1,0:T(8,128)} %bitcast.57), custom_call_target="tpu_custom_call" | custom-call | tf_op jit(solution)/shard_map/pallas_call | solution.py:152
  13.6 0.7 fusion.22
  14.7 1.8 %add_add_fusion = (f32[16,4096]{1,0:T(8,128)S(1)}, f32[16,4096]{1,0:T(8,128)}, f32[16,4096]{1,0:T(8,128)S(1)}) fusion(f32[16,4096]{1,0:T(8,128)} %get-tuple-element.8, f32[4096]{0:T(1024)S(1)} %bitcast.60, f32[4096]{0:T(1024)S(1)} %bitcast.61, f32[4096,16]{0,1:T(8,128)S(1)} %copy-done), kind=kLoop, calls=%fused_computation.1 | loop fusion | flops 786432 | bytes 1343488 | tf_op jit(solution)/shard_map/add | solution.py:248
  16.5 8.0 %collective-permute-done.1 = f32[16,4096]{1,0:T(8,128)S(1)} collective-permute-done((f32[16,4096]{1,0:T(8,128)S(1)}, f32[16,4096]{1,0:T(8,128)S(1)}, u32[]{:S(2)}, u32[]{:S(2)}) %collective-permute-start.1) | collective-permute-done | bytes 262176 | tf_op jit(solution)/shard_map/ppermute | solution.py:256
  24.6 1.9 %collective-permute-start.2 = (f32[16,2048]{1,0:T(8,128)S(1)}, f32[16,2048]{1,0:T(8,128)S(1)}, u32[]{:S(2)}, u32[]{:S(2)}) collective-permute-start(f32[16,2048]{1,0:T(8,128)S(1)} %fusion), channel_id=1, source_target_pairs={{0,2},{2,4},{4,6},{6,8},{8,10},{10,12},{12,14},{14,16},{16,18},{18... | collective-permute-start | bytes 393224 | tf_op jit(solution)/shard_map/ppermute | solution.py:277
  26.5 3.1 %collective-permute-start.3 = (f32[16,2048]{1,0:T(8,128)S(1)}, f32[16,2048]{1,0:T(8,128)S(1)}, u32[]{:S(2)}, u32[]{:S(2)}) collective-permute-start(f32[16,2048]{1,0:T(8,128)S(1)} %fusion), channel_id=1, source_target_pairs={{0,4},{2,6},{4,8},{6,10},{8,12},{10,14},{12,16},{14,18},{16,20},{1... | collective-permute-start | bytes 393224 | tf_op jit(solution)/shard_map/ppermute | solution.py:277
  29.7 1.9 %collective-permute-start.4 = (f32[16,2048]{1,0:T(8,128)S(1)}, f32[16,2048]{1,0:T(8,128)S(1)}, u32[]{:S(2)}, u32[]{:S(2)}) collective-permute-start(f32[16,2048]{1,0:T(8,128)S(1)} %fusion), channel_id=1, source_target_pairs={{0,6},{2,8},{4,10},{6,12},{8,14},{10,16},{12,18},{14,20},{16,22},{... | collective-permute-start | bytes 393224 | tf_op jit(solution)/shard_map/ppermute | solution.py:277
  31.6 1.3 %collective-permute-start.5 = (f32[16,2048]{1,0:T(8,128)S(1)}, f32[16,2048]{1,0:T(8,128)S(1)}, u32[]{:S(2)}, u32[]{:S(2)}) collective-permute-start(f32[16,2048]{1,0:T(8,128)S(1)} %fusion), channel_id=1, source_target_pairs={{0,8},{2,10},{4,12},{6,14},{8,16},{10,18},{12,20},{14,22},{16,24},... | collective-permute-start | bytes 393224 | tf_op jit(solution)/shard_map/ppermute | solution.py:277
  32.9 1.3 %collective-permute-start.6 = (f32[16,2048]{1,0:T(8,128)S(1)}, f32[16,2048]{1,0:T(8,128)S(1)}, u32[]{:S(2)}, u32[]{:S(2)}) collective-permute-start(f32[16,2048]{1,0:T(8,128)S(1)} %fusion), channel_id=1, source_target_pairs={{0,10},{2,12},{4,14},{6,16},{8,18},{10,20},{12,22},{14,24},{16,26}... | collective-permute-start | bytes 393224 | tf_op jit(solution)/shard_map/ppermute | solution.py:277
  34.2 1.2 %collective-permute-done.3 = f32[16,2048]{1,0:T(8,128)S(1)} collective-permute-done((f32[16,2048]{1,0:T(8,128)S(1)}, f32[16,2048]{1,0:T(8,128)S(1)}, u32[]{:S(2)}, u32[]{:S(2)}) %collective-permute-start.3) | collective-permute-done | bytes 131104 | tf_op jit(solution)/shard_map/ppermute | solution.py:277
  35.4 0.6 collective-permute-done.4
  36.0 4.4 %collective-permute-done.5 = f32[16,2048]{1,0:T(8,128)S(1)} collective-permute-done((f32[16,2048]{1,0:T(8,128)S(1)}, f32[16,2048]{1,0:T(8,128)S(1)}, u32[]{:S(2)}, u32[]{:S(2)}) %collective-permute-start.5) | collective-permute-done | bytes 131104 | tf_op jit(solution)/shard_map/ppermute | solution.py:277
  40.4 4.6 %collective-permute-done.6 = f32[16,2048]{1,0:T(8,128)S(1)} collective-permute-done((f32[16,2048]{1,0:T(8,128)S(1)}, f32[16,2048]{1,0:T(8,128)S(1)}, u32[]{:S(2)}, u32[]{:S(2)}) %collective-permute-start.6) | collective-permute-done | bytes 131104 | tf_op jit(solution)/shard_map/ppermute | solution.py:277
  45.1 1.3 %collective-permute-start.7 = (f32[16,2048]{1,0:T(8,128)S(1)}, f32[16,2048]{1,0:T(8,128)S(1)}, u32[]{:S(2)}, u32[]{:S(2)}) collective-permute-start(f32[16,2048]{1,0:T(8,128)S(1)} %fusion.3), channel_id=1, source_target_pairs={{0,10},{2,12},{4,14},{6,16},{8,18},{10,20},{12,22},{14,24},{16,26}... | collective-permute-start | bytes 393224 | tf_op jit(solution)/shard_map/ppermute | solution.py:277
  46.4 1.3 %collective-permute-start.8 = (f32[16,2048]{1,0:T(8,128)S(1)}, f32[16,2048]{1,0:T(8,128)S(1)}, u32[]{:S(2)}, u32[]{:S(2)}) collective-permute-start(f32[16,2048]{1,0:T(8,128)S(1)} %fusion.3), channel_id=1, source_target_pairs={{0,20},{2,22},{4,24},{6,26},{8,28},{10,30},{1,21},{3,23},{5,25},{7... | collective-permute-start | bytes 393224 | tf_op jit(solution)/shard_map/ppermute | solution.py:277
  47.7 9.8 %collective-permute-done.7 = f32[16,2048]{1,0:T(8,128)S(1)} collective-permute-done((f32[16,2048]{1,0:T(8,128)S(1)}, f32[16,2048]{1,0:T(8,128)S(1)}, u32[]{:S(2)}, u32[]{:S(2)}) %collective-permute-start.7) | collective-permute-done | bytes 131104 | tf_op jit(solution)/shard_map/ppermute | solution.py:277
  57.7 1.0 %collective-permute-start.9 = (f32[16,2048]{1,0:T(8,128)S(1)}, f32[16,2048]{1,0:T(8,128)S(1)}, u32[]{:S(2)}, u32[]{:S(2)}) collective-permute-start(f32[16,2048]{1,0:T(8,128)S(1)} %get-tuple-element.10), channel_id=1, source_target_pairs={{0,1},{1,0},{2,3},{3,2},{4,5},{5,4},{6,7},{7,6},{8,9},{9,8},{10,11... | collective-permute-start | bytes 393224 | tf_op jit(solution)/shard_map/ppermute | solution.py:256
  58.7 4.0 %collective-permute-done.9 = f32[16,2048]{1,0:T(8,128)S(1)} collective-permute-done((f32[16,2048]{1,0:T(8,128)S(1)}, f32[16,2048]{1,0:T(8,128)S(1)}, u32[]{:S(2)}, u32[]{:S(2)}) %collective-permute-start.9) | collective-permute-done | bytes 131104 | tf_op jit(solution)/shard_map/ppermute | solution.py:256
  62.7 0.8 %select_add_fusion.hin_ref = f32[16,4096]{1,0:T(8,128)} fusion(f32[16,4096]{1,0:T(8,128)S(1)} %collective-permute-done.1, f32[16,4096]{1,0:T(8,128)S(1)} %constant_dynamic-update-slice_fusion, f32[]{:T(128)S(6)} %mul.259, pred[]{:T(512)S(6)} %ge.3, f32[4096,16]{0,1:T(8,128)S(1)} %copy-done), kind=kLoop, calls=%fused_computation | loop fusion | flops 458752 | bytes 1048581 | tf_op jit(solution)/shard_map/add | solution.py:303
  63.6 13.0 %shard_map.56 = bf16[128,4096]{1,0:T(8,128)(2,1)} custom-call(bf16[3,128,4096]{2,1,0:T(8,128)(2,1)} %bitcast.56, f32[3,2,4096]{2,1,0:T(2,128)} %get-tuple-element.24.halo_ref, f32[3,3,4096]{2,1,0:T(4,128)} %f_ref.3, f32[16,4096]{1,0:T(8,128)} %bitcast.58, f32[16,4096]{1,0:T(8,128)} %bitcast.59, f32[1,4096]{1,0:T(1,128)} %bitcast.62, ...), custom_call_target="tpu_custom_call" | custom-call | tf_op jit(solution)/shard_map/pallas_call | solution.py:181
  (14 shorter events, 0.7 us)
Async XLA Ops:
  0.0 14.7 %copy-start = (f32[4096,16]{0,1:T(8,128)S(1)}, f32[4096,16]{0,1:T(8,128)}, u32[]{:S(2)}) copy-start(f32[4096,16]{0,1:T(8,128)} %param.8) | copy-start | bytes 786436
  1.1 12.4 %collective-permute-start = (bf16[2,3,4096]{2,0,1:T(2,128)(2,1)S(1)}, bf16[2,3,4096]{2,0,1:T(2,128)(2,1)S(1)}, u32[]{:S(2)}, u32[]{:S(2)}) collective-permute-start(bf16[2,3,4096]{2,0,1:T(2,128)(2,1)S(1)} %get-tuple-element.14), channel_id=1, source_target_pairs={{0,1},{1,2},{2,3},{3,4},{4,5},{5,6},{6,7},{7,8},{8,9},{9,10},{10,1... | collective-permute-start | bytes 147464 | tf_op jit(solution)/shard_map/ppermute | solution.py:216
  16.5 8.0 %collective-permute-start.1 = (f32[16,4096]{1,0:T(8,128)S(1)}, f32[16,4096]{1,0:T(8,128)S(1)}, u32[]{:S(2)}, u32[]{:S(2)}) collective-permute-start(f32[16,4096]{1,0:T(8,128)S(1)} %get-tuple-element.16), channel_id=1, source_target_pairs={{0,1},{1,0},{2,3},{3,2},{4,5},{5,4},{6,7},{7,6},{8,9},{9,8},{10,11... | collective-permute-start | bytes 786440 | tf_op jit(solution)/shard_map/ppermute | solution.py:256
  24.6 9.6 %collective-permute-start.2 = (f32[16,2048]{1,0:T(8,128)S(1)}, f32[16,2048]{1,0:T(8,128)S(1)}, u32[]{:S(2)}, u32[]{:S(2)}) collective-permute-start(f32[16,2048]{1,0:T(8,128)S(1)} %fusion), channel_id=1, source_target_pairs={{0,2},{2,4},{4,6},{6,8},{8,10},{10,12},{12,14},{14,16},{16,18},{18... | collective-permute-start | bytes 393224 | tf_op jit(solution)/shard_map/ppermute | solution.py:277
  26.5 8.9 %collective-permute-start.3 = (f32[16,2048]{1,0:T(8,128)S(1)}, f32[16,2048]{1,0:T(8,128)S(1)}, u32[]{:S(2)}, u32[]{:S(2)}) collective-permute-start(f32[16,2048]{1,0:T(8,128)S(1)} %fusion), channel_id=1, source_target_pairs={{0,4},{2,6},{4,8},{6,10},{8,12},{10,14},{12,16},{14,18},{16,20},{1... | collective-permute-start | bytes 393224 | tf_op jit(solution)/shard_map/ppermute | solution.py:277
  29.7 6.3 %collective-permute-start.4 = (f32[16,2048]{1,0:T(8,128)S(1)}, f32[16,2048]{1,0:T(8,128)S(1)}, u32[]{:S(2)}, u32[]{:S(2)}) collective-permute-start(f32[16,2048]{1,0:T(8,128)S(1)} %fusion), channel_id=1, source_target_pairs={{0,6},{2,8},{4,10},{6,12},{8,14},{10,16},{12,18},{14,20},{16,22},{... | collective-permute-start | bytes 393224 | tf_op jit(solution)/shard_map/ppermute | solution.py:277
  31.6 8.8 %collective-permute-start.5 = (f32[16,2048]{1,0:T(8,128)S(1)}, f32[16,2048]{1,0:T(8,128)S(1)}, u32[]{:S(2)}, u32[]{:S(2)}) collective-permute-start(f32[16,2048]{1,0:T(8,128)S(1)} %fusion), channel_id=1, source_target_pairs={{0,8},{2,10},{4,12},{6,14},{8,16},{10,18},{12,20},{14,22},{16,24},... | collective-permute-start | bytes 393224 | tf_op jit(solution)/shard_map/ppermute | solution.py:277
  32.9 12.1 %collective-permute-start.6 = (f32[16,2048]{1,0:T(8,128)S(1)}, f32[16,2048]{1,0:T(8,128)S(1)}, u32[]{:S(2)}, u32[]{:S(2)}) collective-permute-start(f32[16,2048]{1,0:T(8,128)S(1)} %fusion), channel_id=1, source_target_pairs={{0,10},{2,12},{4,14},{6,16},{8,18},{10,20},{12,22},{14,24},{16,26}... | collective-permute-start | bytes 393224 | tf_op jit(solution)/shard_map/ppermute | solution.py:277
  45.1 12.5 %collective-permute-start.7 = (f32[16,2048]{1,0:T(8,128)S(1)}, f32[16,2048]{1,0:T(8,128)S(1)}, u32[]{:S(2)}, u32[]{:S(2)}) collective-permute-start(f32[16,2048]{1,0:T(8,128)S(1)} %fusion.3), channel_id=1, source_target_pairs={{0,10},{2,12},{4,14},{6,16},{8,18},{10,20},{12,22},{14,24},{16,26}... | collective-permute-start | bytes 393224 | tf_op jit(solution)/shard_map/ppermute | solution.py:277
  46.4 11.2 %collective-permute-start.8 = (f32[16,2048]{1,0:T(8,128)S(1)}, f32[16,2048]{1,0:T(8,128)S(1)}, u32[]{:S(2)}, u32[]{:S(2)}) collective-permute-start(f32[16,2048]{1,0:T(8,128)S(1)} %fusion.3), channel_id=1, source_target_pairs={{0,20},{2,22},{4,24},{6,26},{8,28},{10,30},{1,21},{3,23},{5,25},{7... | collective-permute-start | bytes 393224 | tf_op jit(solution)/shard_map/ppermute | solution.py:277
  57.7 5.0 %collective-permute-start.9 = (f32[16,2048]{1,0:T(8,128)S(1)}, f32[16,2048]{1,0:T(8,128)S(1)}, u32[]{:S(2)}, u32[]{:S(2)}) collective-permute-start(f32[16,2048]{1,0:T(8,128)S(1)} %get-tuple-element.10), channel_id=1, source_target_pairs={{0,1},{1,0},{2,3},{3,2},{4,5},{5,4},{6,7},{7,6},{8,9},{9,8},{10,11... | collective-permute-start | bytes 393224 | tf_op jit(solution)/shard_map/ppermute | solution.py:256

commit v24 on v19

--- a/solution.py
+++ b/solution.py
@@ -89,7 +89,7 @@
             h_ref[pl.ds(m, 1), lanes] = jnp.sum(weight * states[m], axis=0, keepdims=True)
         return carry
 
-    lax.fori_loop(0, block // LANES, lane_group, 0, unroll=2)
+    lax.fori_loop(0, block // LANES, lane_group, 0, unroll=4)
 
 
 def out_kernel(
@@ -140,7 +140,7 @@
         lax.fori_loop(0, seg, step, init, unroll=UNROLL)
         return carry
 
-    lax.fori_loop(0, block // LANES, lane_group, 0, unroll=2)
+    lax.fori_loop(0, block // LANES, lane_group, 0, unroll=4)
     for c in range(block // LANES):
         o_ref[:, c * LANES : (c + 1) * LANES] = ys[c].astype(o_ref.dtype)
 

time: 74.5 us -> 74.4 us (level)
  no operation moved by 1% of the time
where the time goes in v24:
time: 74.4 us; the launch traced here: 73.3 us
  waiting for transfers between devices  27.7 us (37%)
  Pallas kernels  20.3 us (27%)
  starting transfers between devices  18.5 us (25%)
  other arithmetic  5.09 us (7%)
  local copies, waits for them, and re-layouts  1.64 us (2%)
    ppermute x7, waiting for transfers between devices, span_shift(): lax.ppermute(value, 'ctx', [(j, j + offset) for j in range(spans - offset)])  14.7 us
    ppermute x7, starting transfers between devices, span_shift(): lax.ppermute(value, 'ctx', [(j, j + offset) for j in range(spans - offset)])  14.3 us
    ppermute x2, waiting for transfers between devices, exchange(): lax.ppermute(value, 'tp', [(q, (q + k) % group) for q in range(group)])  13 us
    pallas_call x1, Pallas kernels, run_out(): pl.pallas_call(out_kernel, grid=(width // BLOCK,), in_specs=[pl.BlockSpec...  12.9 us
    pallas_call x1, Pallas kernels, run_state(): pl.pallas_call(state_kernel, grid=(width // BLOCK,), in_specs=[pl.BlockSp...  7.34 us
    ppermute x1, starting transfers between devices, shift(): return lax.ppermute(value, axes, pairs)  3.43 us
    add x1, other arithmetic, body(): local = local + local_fix  1.84 us
  transfers between devices with their start and end apart: 10, of which 6 were waited for; matrix products, arithmetic and copies ran while one was open for 2% of the time, Pallas kernels for 10%

profile of v24, /device:TPU:16, one launch (start us, length us, event | category | flops | bytes accessed | tf_op | source)
XLA Modules:
  0.0 73.3 jit_solution(9478247809973617191)
XLA Ops:
  0.0 1.1 %slice_convert_fusion = (f32[2,3,4096]{2,0,1:T(2,128)S(1)}, bf16[2,3,4096]{2,0,1:T(2,128)(2,1)S(1)}) fusion(bf16[128,3,4096]{2,0,1:T(8,128)(2,1)} %param.5), kind=kLoop, calls=%fused_computation.28 | loop fusion | flops 24576 | bytes 245760 | tf_op jit(solution)/shard_map/convert_element_type | solution.py:225
  1.1 3.4 %collective-permute-start = (bf16[2,3,4096]{2,0,1:T(2,128)(2,1)S(1)}, bf16[2,3,4096]{2,0,1:T(2,128)(2,1)S(1)}, u32[]{:S(2)}, u32[]{:S(2)}) collective-permute-start(bf16[2,3,4096]{2,0,1:T(2,128)(2,1)S(1)} %get-tuple-element.14), channel_id=1, source_target_pairs={{0,1},{1,2},{2,3},{3,4},{4,5},{5,6},{6,7},{7,8},{8,9},{9,10},{10,1... | collective-permute-start | bytes 147464 | tf_op jit(solution)/shard_map/ppermute | solution.py:216
  4.6 0.9 %fusion.22 = (f32[1,3,4096]{2,1,0:T(4,128)S(1)}, f32[1,3,4096]{2,1,0:T(4,128)S(1)}, f32[1,3,4096]{2,1,0:T(4,128)S(1)}) fusion(f32[3,3,4096]{2,1,0:T(4,128)} %f_ref.3), kind=kLoop, calls=%fused_computation.49 | loop fusion | bytes 294912 | tf_op jit(solution)/shard_map/slice | solution.py:231
  5.5 0.7 broadcast_in_dim.3.halo_ref
  6.2 7.3 %shard_map.55 = (f32[16,8,4096]{2,1,0:T(8,128)}, f32[16,4096]{1,0:T(8,128)}) custom-call(bf16[3,128,4096]{2,1,0:T(8,128)(2,1)} %bitcast.57, f32[3,2,4096]{2,1,0:T(2,128)} %broadcast_in_dim.3.halo_ref, f32[3,3,4096]{2,1,0:T(4,128)} %f_ref.3, f32[16,4096]{1,0:T(8,128)} %bitcast.59), custom_call_target="tpu_custom_call" | custom-call | tf_op jit(solution)/shard_map/pallas_call | solution.py:152
  13.5 0.7 fusion.23
  14.2 0.2 multiply_add_fusion.1
  14.6 1.8 %add_add_fusion = (f32[16,4096]{1,0:T(8,128)S(1)}, f32[16,4096]{1,0:T(8,128)}, f32[16,4096]{1,0:T(8,128)S(1)}) fusion(f32[16,4096]{1,0:T(8,128)} %get-tuple-element.8, f32[4096]{0:T(1024)S(1)} %bitcast.62, f32[4096]{0:T(1024)S(1)} %bitcast.63, f32[4096,16]{0,1:T(8,128)S(1)} %copy-done), kind=kLoop, calls=%fused_computation.1 | loop fusion | flops 786432 | bytes 1343488 | tf_op jit(solution)/shard_map/add | solution.py:248
  16.5 8.0 %collective-permute-done.1 = f32[16,4096]{1,0:T(8,128)S(1)} collective-permute-done((f32[16,4096]{1,0:T(8,128)S(1)}, f32[16,4096]{1,0:T(8,128)S(1)}, u32[]{:S(2)}, u32[]{:S(2)}) %collective-permute-start.1) | collective-permute-done | bytes 262176 | tf_op jit(solution)/shard_map/ppermute | solution.py:256
  24.5 2.1 %collective-permute-start.4 = (f32[16,2048]{1,0:T(8,128)S(1)}, f32[16,2048]{1,0:T(8,128)S(1)}, u32[]{:S(2)}, u32[]{:S(2)}) collective-permute-start(f32[16,2048]{1,0:T(8,128)S(1)} %fusion), channel_id=1, source_target_pairs={{0,6},{2,8},{4,10},{6,12},{8,14},{10,16},{12,18},{14,20},{16,22},{... | collective-permute-start | bytes 393224 | tf_op jit(solution)/shard_map/ppermute | solution.py:277
  26.6 3.3 %collective-permute-start.3 = (f32[16,2048]{1,0:T(8,128)S(1)}, f32[16,2048]{1,0:T(8,128)S(1)}, u32[]{:S(2)}, u32[]{:S(2)}) collective-permute-start(f32[16,2048]{1,0:T(8,128)S(1)} %fusion), channel_id=1, source_target_pairs={{0,4},{2,6},{4,8},{6,10},{8,12},{10,14},{12,16},{14,18},{16,20},{1... | collective-permute-start | bytes 393224 | tf_op jit(solution)/shard_map/ppermute | solution.py:277
  29.9 3.0 %collective-permute-start.2 = (f32[16,2048]{1,0:T(8,128)S(1)}, f32[16,2048]{1,0:T(8,128)S(1)}, u32[]{:S(2)}, u32[]{:S(2)}) collective-permute-start(f32[16,2048]{1,0:T(8,128)S(1)} %fusion), channel_id=1, source_target_pairs={{0,2},{2,4},{4,6},{6,8},{8,10},{10,12},{12,14},{14,16},{16,18},{18... | collective-permute-start | bytes 393224 | tf_op jit(solution)/shard_map/ppermute | solution.py:277
  32.9 2.3 %collective-permute-done.3 = f32[16,2048]{1,0:T(8,128)S(1)} collective-permute-done((f32[16,2048]{1,0:T(8,128)S(1)}, f32[16,2048]{1,0:T(8,128)S(1)}, u32[]{:S(2)}, u32[]{:S(2)}) %collective-permute-start.3) | collective-permute-done | bytes 131104 | tf_op jit(solution)/shard_map/ppermute | solution.py:277
  35.3 1.9 %collective-permute-done.2 = f32[16,2048]{1,0:T(8,128)S(1)} collective-permute-done((f32[16,2048]{1,0:T(8,128)S(1)}, f32[16,2048]{1,0:T(8,128)S(1)}, u32[]{:S(2)}, u32[]{:S(2)}) %collective-permute-start.2) | collective-permute-done | bytes 131104 | tf_op jit(solution)/shard_map/ppermute | solution.py:277
  37.2 0.7 collective-permute-start.8
  37.9 0.7 collective-permute-start.7
  38.6 2.6 %collective-permute-start.6 = (f32[16,2048]{1,0:T(8,128)S(1)}, f32[16,2048]{1,0:T(8,128)S(1)}, u32[]{:S(2)}, u32[]{:S(2)}) collective-permute-start(f32[16,2048]{1,0:T(8,128)S(1)} %fusion.6), channel_id=1, source_target_pairs={{0,12},{2,14},{4,16},{6,18},{8,20},{10,22},{12,24},{14,26},{16,28}... | collective-permute-start | bytes 393224 | tf_op jit(solution)/shard_map/ppermute | solution.py:277
  41.2 1.9 %collective-permute-start.5 = (f32[16,2048]{1,0:T(8,128)S(1)}, f32[16,2048]{1,0:T(8,128)S(1)}, u32[]{:S(2)}, u32[]{:S(2)}) collective-permute-start(f32[16,2048]{1,0:T(8,128)S(1)} %fusion.6), channel_id=1, source_target_pairs={{0,6},{2,8},{4,10},{6,12},{8,14},{10,16},{12,18},{14,20},{16,22},{... | collective-permute-start | bytes 393224 | tf_op jit(solution)/shard_map/ppermute | solution.py:277
  43.2 5.5 %collective-permute-done.6 = f32[16,2048]{1,0:T(8,128)S(1)} collective-permute-done((f32[16,2048]{1,0:T(8,128)S(1)}, f32[16,2048]{1,0:T(8,128)S(1)}, u32[]{:S(2)}, u32[]{:S(2)}) %collective-permute-start.6) | collective-permute-done | bytes 131104 | tf_op jit(solution)/shard_map/ppermute | solution.py:277
  48.7 5.0 %collective-permute-done.5 = f32[16,2048]{1,0:T(8,128)S(1)} collective-permute-done((f32[16,2048]{1,0:T(8,128)S(1)}, f32[16,2048]{1,0:T(8,128)S(1)}, u32[]{:S(2)}, u32[]{:S(2)}) %collective-permute-start.5) | collective-permute-done | bytes 131104 | tf_op jit(solution)/shard_map/ppermute | solution.py:277
  53.8 0.8 %collective-permute-start.9 = (f32[16,2048]{1,0:T(8,128)S(1)}, f32[16,2048]{1,0:T(8,128)S(1)}, u32[]{:S(2)}, u32[]{:S(2)}) collective-permute-start(f32[16,2048]{1,0:T(8,128)S(1)} %get-tuple-element.10), channel_id=1, source_target_pairs={{0,1},{1,0},{2,3},{3,2},{4,5},{5,4},{6,7},{7,6},{8,9},{9,8},{10,11... | collective-permute-start | bytes 393224 | tf_op jit(solution)/shard_map/ppermute | solution.py:256
  54.6 5.0 %collective-permute-done.9 = f32[16,2048]{1,0:T(8,128)S(1)} collective-permute-done((f32[16,2048]{1,0:T(8,128)S(1)}, f32[16,2048]{1,0:T(8,128)S(1)}, u32[]{:S(2)}, u32[]{:S(2)}) %collective-permute-start.9) | collective-permute-done | bytes 131104 | tf_op jit(solution)/shard_map/ppermute | solution.py:256
  59.6 0.8 %select_add_fusion.hin_ref = f32[16,4096]{1,0:T(8,128)} fusion(f32[16,4096]{1,0:T(8,128)S(1)} %collective-permute-done.1, f32[16,4096]{1,0:T(8,128)S(1)} %constant_dynamic-update-slice_fusion, f32[]{:T(128)S(6)} %mul.259, pred[]{:T(512)S(6)} %ge.3, f32[4096,16]{0,1:T(8,128)S(1)} %copy-done), kind=kLoop, calls=%fused_computation | loop fusion | flops 458752 | bytes 1048581 | tf_op jit(solution)/shard_map/add | solution.py:303
  60.4 12.9 %shard_map.56 = bf16[128,4096]{1,0:T(8,128)(2,1)} custom-call(bf16[3,128,4096]{2,1,0:T(8,128)(2,1)} %bitcast.58, f32[3,2,4096]{2,1,0:T(2,128)} %get-tuple-element.24.halo_ref, f32[3,3,4096]{2,1,0:T(4,128)} %f_ref.3, f32[16,4096]{1,0:T(8,128)} %bitcast.60, f32[16,4096]{1,0:T(8,128)} %bitcast.61, f32[1,4096]{1,0:T(1,128)} %bitcast.64, ...), custom_call_target="tpu_custom_call" | custom-call | tf_op jit(solution)/shard_map/pallas_call | solution.py:181
  (14 shorter events, 0.4 us)
Async XLA Ops:
  0.0 14.6 %copy-start = (f32[4096,16]{0,1:T(8,128)S(1)}, f32[4096,16]{0,1:T(8,128)}, u32[]{:S(2)}) copy-start(f32[4096,16]{0,1:T(8,128)} %param.8) | copy-start | bytes 786436
  1.1 12.4 %collective-permute-start = (bf16[2,3,4096]{2,0,1:T(2,128)(2,1)S(1)}, bf16[2,3,4096]{2,0,1:T(2,128)(2,1)S(1)}, u32[]{:S(2)}, u32[]{:S(2)}) collective-permute-start(bf16[2,3,4096]{2,0,1:T(2,128)(2,1)S(1)} %get-tuple-element.14), channel_id=1, source_target_pairs={{0,1},{1,2},{2,3},{3,4},{4,5},{5,6},{6,7},{7,8},{8,9},{9,10},{10,1... | collective-permute-start | bytes 147464 | tf_op jit(solution)/shard_map/ppermute | solution.py:216
  16.5 8.0 %collective-permute-start.1 = (f32[16,4096]{1,0:T(8,128)S(1)}, f32[16,4096]{1,0:T(8,128)S(1)}, u32[]{:S(2)}, u32[]{:S(2)}) collective-permute-start(f32[16,4096]{1,0:T(8,128)S(1)} %get-tuple-element.16), channel_id=1, source_target_pairs={{0,1},{1,0},{2,3},{3,2},{4,5},{5,4},{6,7},{7,6},{8,9},{9,8},{10,11... | collective-permute-start | bytes 786440 | tf_op jit(solution)/shard_map/ppermute | solution.py:256
  24.5 8.4 %collective-permute-start.4 = (f32[16,2048]{1,0:T(8,128)S(1)}, f32[16,2048]{1,0:T(8,128)S(1)}, u32[]{:S(2)}, u32[]{:S(2)}) collective-permute-start(f32[16,2048]{1,0:T(8,128)S(1)} %fusion), channel_id=1, source_target_pairs={{0,6},{2,8},{4,10},{6,12},{8,14},{10,16},{12,18},{14,20},{16,22},{... | collective-permute-start | bytes 393224 | tf_op jit(solution)/shard_map/ppermute | solution.py:277
  26.6 8.6 %collective-permute-start.3 = (f32[16,2048]{1,0:T(8,128)S(1)}, f32[16,2048]{1,0:T(8,128)S(1)}, u32[]{:S(2)}, u32[]{:S(2)}) collective-permute-start(f32[16,2048]{1,0:T(8,128)S(1)} %fusion), channel_id=1, source_target_pairs={{0,4},{2,6},{4,8},{6,10},{8,12},{10,14},{12,16},{14,18},{16,20},{1... | collective-permute-start | bytes 393224 | tf_op jit(solution)/shard_map/ppermute | solution.py:277
  29.9 7.2 %collective-permute-start.2 = (f32[16,2048]{1,0:T(8,128)S(1)}, f32[16,2048]{1,0:T(8,128)S(1)}, u32[]{:S(2)}, u32[]{:S(2)}) collective-permute-start(f32[16,2048]{1,0:T(8,128)S(1)} %fusion), channel_id=1, source_target_pairs={{0,2},{2,4},{4,6},{6,8},{8,10},{10,12},{12,14},{14,16},{16,18},{18... | collective-permute-start | bytes 393224 | tf_op jit(solution)/shard_map/ppermute | solution.py:277
  37.2 5.9 %collective-permute-start.8 = (f32[16,2048]{1,0:T(8,128)S(1)}, f32[16,2048]{1,0:T(8,128)S(1)}, u32[]{:S(2)}, u32[]{:S(2)}) collective-permute-start(f32[16,2048]{1,0:T(8,128)S(1)} %fusion.6), channel_id=1, source_target_pairs={{0,24},{2,26},{4,28},{6,30},{1,25},{3,27},{5,29},{7,31}} | collective-permute-start | bytes 393224 | tf_op jit(solution)/shard_map/ppermute | solution.py:277
  37.9 5.3 %collective-permute-start.7 = (f32[16,2048]{1,0:T(8,128)S(1)}, f32[16,2048]{1,0:T(8,128)S(1)}, u32[]{:S(2)}, u32[]{:S(2)}) collective-permute-start(f32[16,2048]{1,0:T(8,128)S(1)} %fusion.6), channel_id=1, source_target_pairs={{0,18},{2,20},{4,22},{6,24},{8,26},{10,28},{12,30},{1,19},{3,21},{... | collective-permute-start | bytes 393224 | tf_op jit(solution)/shard_map/ppermute | solution.py:277
  38.6 10.1 %collective-permute-start.6 = (f32[16,2048]{1,0:T(8,128)S(1)}, f32[16,2048]{1,0:T(8,128)S(1)}, u32[]{:S(2)}, u32[]{:S(2)}) collective-permute-start(f32[16,2048]{1,0:T(8,128)S(1)} %fusion.6), channel_id=1, source_target_pairs={{0,12},{2,14},{4,16},{6,18},{8,20},{10,22},{12,24},{14,26},{16,28}... | collective-permute-start | bytes 393224 | tf_op jit(solution)/shard_map/ppermute | solution.py:277
  41.2 12.4 %collective-permute-start.5 = (f32[16,2048]{1,0:T(8,128)S(1)}, f32[16,2048]{1,0:T(8,128)S(1)}, u32[]{:S(2)}, u32[]{:S(2)}) collective-permute-start(f32[16,2048]{1,0:T(8,128)S(1)} %fusion.6), channel_id=1, source_target_pairs={{0,6},{2,8},{4,10},{6,12},{8,14},{10,16},{12,18},{14,20},{16,22},{... | collective-permute-start | bytes 393224 | tf_op jit(solution)/shard_map/ppermute | solution.py:277
  53.8 5.8 %collective-permute-start.9 = (f32[16,2048]{1,0:T(8,128)S(1)}, f32[16,2048]{1,0:T(8,128)S(1)}, u32[]{:S(2)}, u32[]{:S(2)}) collective-permute-start(f32[16,2048]{1,0:T(8,128)S(1)} %get-tuple-element.10), channel_id=1, source_target_pairs={{0,1},{1,0},{2,3},{3,2},{4,5},{5,4},{6,7},{7,6},{8,9},{9,8},{10,11... | collective-permute-start | bytes 393224 | tf_op jit(solution)/shard_map/ppermute | solution.py:256
